TPU v7x, 512 devices: a whole 4x8x8 slice. The times are simulated.
512 devices in a mesh: gx: 32 (over x, y), gy: 16 (over z, core).
Axes of the slice: x: 4, y: 8, z: 8, core: 2. Of those that a mesh axis runs over, the one named last changes fastest.
Arguments:
- right_side: bfloat16 [32, 16, 896, 128], P('gx', 'gy')
- schur_offdiag: bfloat16 [32, 16, 896, 896], P('gx', 'gy'), may hold values from -0.125 to 0.125
- schur_diag: float32 [32, 16, 896], P('gx', 'gy'), may hold values from 1.5 to 3
- trace_offdiag: bfloat16 [32, 16, 896, 896], P('gx', 'gy'), may hold values from -0.0390625 to 0.0390625
- trace_diag: float32 [32, 16, 896], P('gx', 'gy'), may hold values from 0.3 to 0.7
- couplings: bfloat16 [32, 16, 4, 128, 128], P('gx', 'gy'), may hold values from -0.375 to 0.375
- margin_rows: int32 [32, 16, 4, 128], P('gx', 'gy'), may hold values from 0 to 895, as said below
- deflation: bfloat16 [32, 16, 8, 896], P('gx', 'gy'), may hold values from -0.59765625 to 0.59765625
- coarse_inverse: float32 [4096, 4096], P(('gx', 'gy'))
- coarse_map: int32 [4096], replicated, may hold values from 0 to 4095, each once
Outputs:
- solution: float32 [32, 16, 896, 128], P('gx', 'gy')
- residual: float32 [32, 16, 896, 128], P('gx', 'gy')
Inputs may be any that keep to these rules, and one draw needn't show every extreme that they name: `margin_rows`: the 512 rows of one subdomain's four lists are all distinct. `coarse_map`: every coarse number appears once.
All inputs are finite; a program needn't handle non-finite values.
Results may differ from a plain program's by a relative error of at most 0.022.
Values may be sent and summed in bfloat16 or wider, within the bound.
No kernel may reach another device: no remote copies, remote signals or barrier semaphores. Data moves between devices by JAX's collectives and lax.ppermute only.
A program may use at most 64 MiB of HBM per device.

v0:
```python
import jax
import jax.numpy as jnp
from jax import lax
from jax.sharding import PartitionSpec as P

ITERS = 3


def from_behind(value, axis, steps):
    count = lax.axis_size(axis)
    leading, last = (max(0, -steps), min(count, count - steps))
    return lax.ppermute(value, axis, [(source, source + steps) for source in range(leading, last)])


def pass_columns(rows, offset):
    return from_behind(rows, "gx", offset)


def pass_lines(rows, offset):
    return from_behind(rows, "gy", offset)


def shards(
    right_side,
    schur_offdiag,
    schur_diag,
    trace_offdiag,
    trace_diag,
    couplings,
    margin_rows,
    deflation,
    coarse_inverse,
    coarse_map,
):
    rhs_wide = right_side[0, 0].astype(jnp.float32)
    schur_mat = schur_offdiag[0, 0]
    schur_scale = schur_diag[0, 0][:, None]
    trace_mat = trace_offdiag[0, 0]
    trace_scale = trace_diag[0, 0][:, None]
    coupling_blocks = couplings[0, 0]
    rows_lists = margin_rows[0, 0]
    flat_rows = rows_lists.reshape(-1)
    vectors = deflation[0, 0]
    vectors_wide = vectors.astype(jnp.float32).T
    coarse_cols = jnp.take(coarse_inverse, coarse_map, axis=1)

    def apply_schur(field):
        rounded = lax.optimization_barrier(field.astype(jnp.bfloat16))
        result = schur_scale * rounded.astype(jnp.float32) + jnp.dot(
            schur_mat, rounded, preferred_element_type=jnp.float32
        )
        sent_rows = rounded[rows_lists]
        received = jnp.stack(
            [
                pass_columns(sent_rows[1], 1),
                pass_columns(sent_rows[0], -1),
                pass_lines(sent_rows[3], 1),
                pass_lines(sent_rows[2], -1),
            ]
        )
        coupled = jnp.einsum(
            "dab,dbs->das", coupling_blocks, received, preferred_element_type=jnp.float32
        )
        return result.at[flat_rows].add(-coupled.reshape(-1, coupled.shape[-1]))

    def apply_prec(field):
        rounded = lax.optimization_barrier(field.astype(jnp.bfloat16))
        result = trace_scale * rounded.astype(jnp.float32) + jnp.dot(
            trace_mat, rounded, preferred_element_type=jnp.float32
        )
        coarse = jnp.dot(vectors, rounded, preferred_element_type=jnp.float32)
        stacked = lax.all_gather(coarse, ("gx", "gy"), axis=0, tiled=True)
        solved = jnp.dot(coarse_cols, stacked, precision=lax.Precision.HIGHEST)
        return result + jnp.dot(vectors_wide, solved, precision=lax.Precision.HIGHEST)

    solution = jnp.zeros(rhs_wide.shape, jnp.float32)
    direction = apply_prec(rhs_wide)
    for iteration in range(ITERS):
        image = apply_schur(direction)
        mapped = apply_prec(image)
        numer, denom = lax.psum(
            (jnp.sum(mapped * direction, axis=0), jnp.sum(mapped * mapped, axis=0)), ("gx", "gy")
        )
        alpha = numer / denom
        solution = solution + alpha * direction
        direction = direction - alpha * mapped
    residual = rhs_wide - apply_schur(solution)
    return (solution[None, None], residual[None, None])


def solution(mesh):
    return jax.shard_map(
        shards,
        mesh=mesh,
        in_specs=(
            P("gx", "gy", None, None),
            P("gx", "gy", None, None),
            P("gx", "gy", None),
            P("gx", "gy", None, None),
            P("gx", "gy", None),
            P("gx", "gy", None, None, None),
            P("gx", "gy", None, None),
            P("gx", "gy", None, None),
            P(("gx", "gy"), None),
            P(),
        ),
        out_specs=(P("gx", "gy", None, None), P("gx", "gy", None, None)),
        check_vma=False,
    )
```

profile of v0, /device:TPU:1, one launch (start us, length us, event | category | flops | bytes accessed | tf_op | source)
XLA Modules:
  0.0 899.7 jit_solution(9823042556222363306)
XLA Ops:
  7.3 1.8 fusion.129
  9.1 2.8 copy.24
  12.1 15.7 %gather_fusion = f32[4096,8]{1,0:T(8,128)} fusion(f32[8,4096]{0,1:T(8,128)} %copy.24, s32[4096]{0:T(1024)S(1)} %fusion.131), kind=kCustom, calls=%fused_computation | custom fusion | bytes 278528 | tf_op jit(solution)/shard_map/jit(_take)/gather | solution.py:45
  27.8 106.2 %all-gather.5.cloned.1.call-done = f32[4096,128]{1,0:T(8,128)} async-done(((f32[8,128]{1,0:T(8,128)}), f32[4096,128]{1,0:T(8,128)}) %all-gather.5.cloned.1.call-update) | async-done | bytes 2097168 | tf_op jit(solution)/shard_map/all_gather | solution.py:72
  134.0 6.4 fusion.4
  140.9 1.4 fusion.147
  142.2 1.9 gather_fusion.1
  144.1 0.9 fusion.146
  145.0 3.0 collective-permute-start
  148.0 1.3 collective-permute-start.1
  149.3 2.8 collective-permute-start.2
  152.2 1.9 collective-permute-start.3
  154.1 1.4 fusion.45
  155.5 1.9 collective-permute-done.3
  157.4 0.9 convolution_negate_fusion.3
  158.3 5.2 scatter_fusion
  163.5 1.0 convert_element_type.53
  165.5 114.8 %all-gather.7.cloned.1.call-done = f32[4096,128]{1,0:T(8,128)} async-done(((f32[8,128]{1,0:T(8,128)}), f32[4096,128]{1,0:T(8,128)}) %all-gather.7.cloned.1.call-update) | async-done | bytes 2097168 | tf_op jit(solution)/shard_map/all_gather | solution.py:72
  280.3 6.4 fusion.2
  287.2 1.4 multiply_reduce_fusion.4
  288.6 96.5 %all-reduce.2 = (f32[128]{0:T(128)S(1)}, f32[128]{0:T(128)S(1)}) all-reduce(f32[128]{0:T(128)S(1)} %get-tuple-element.7, f32[128]{0:T(128)S(1)} %get-tuple-element.6), channel_id=1, replica_groups=mesh['gx'=32,'gy'=16] {'gx','gy'}, use_global_device_ids=true, to_apply=%region_2.3 | all-reduce | flops 256 | bytes 2048 | tf_op jit(solution)/shard_map/psum | solution.py:81
  385.0 2.0 fusion.142
  387.0 1.9 gather_fusion.2
  388.9 0.9 fusion.145
  389.8 1.9 collective-permute-start.4
  391.6 1.3 collective-permute-start.5
  392.9 3.1 collective-permute-start.6
  396.0 1.9 collective-permute-start.7
  397.9 1.4 fusion.48
  399.3 1.9 collective-permute-done.7
  401.2 0.9 convolution_negate_fusion.2
  402.1 5.2 scatter_fusion.1
  407.3 1.0 convert_element_type.57
  408.3 0.7 convolution_bitcast_fusion.5
  409.4 114.0 %all-gather.9.cloned.1.call-done = f32[4096,128]{1,0:T(8,128)} async-done(((f32[8,128]{1,0:T(8,128)}), f32[4096,128]{1,0:T(8,128)}) %all-gather.9.cloned.1.call-update) | async-done | bytes 2097168 | tf_op jit(solution)/shard_map/all_gather | solution.py:72
  523.4 6.4 fusion
  530.3 1.4 multiply_reduce_fusion.2
  531.7 96.5 %all-reduce.1 = (f32[128]{0:T(128)S(1)}, f32[128]{0:T(128)S(1)}) all-reduce(f32[128]{0:T(128)S(1)} %get-tuple-element.5, f32[128]{0:T(128)S(1)} %get-tuple-element.4), channel_id=1, replica_groups=mesh['gx'=32,'gy'=16] {'gx','gy'}, use_global_device_ids=true, to_apply=%region_7.8 | all-reduce | flops 256 | bytes 2048 | tf_op jit(solution)/shard_map/psum | solution.py:81
  628.2 1.2 fusion.121
  629.4 1.9 gather_fusion.3
  631.3 0.9 fusion.144
  632.1 1.9 collective-permute-start.8
  634.0 1.3 collective-permute-start.9
  635.3 3.1 collective-permute-start.10
  638.4 1.9 collective-permute-start.11
  640.3 1.4 fusion.51
  641.7 1.9 collective-permute-done.11
  643.6 0.9 convolution_negate_fusion.1
  644.5 5.2 scatter_fusion.2
  649.7 1.0 convert_element_type.61
  651.5 114.3 %all-gather.11.cloned.1.call-done = f32[4096,128]{1,0:T(8,128)} async-done(((f32[8,128]{1,0:T(8,128)}), f32[4096,128]{1,0:T(8,128)}) %all-gather.11.cloned.1.call-update) | async-done | bytes 2097168 | tf_op jit(solution)/shard_map/all_gather | solution.py:72
  765.8 6.4 fusion.6
  773.4 96.5 %all-reduce = (f32[128]{0:T(128)S(1)}, f32[128]{0:T(128)S(1)}) all-reduce(f32[128]{0:T(128)S(1)} %get-tuple-element.3, f32[128]{0:T(128)S(1)} %get-tuple-element.2), channel_id=1, replica_groups=mesh['gx'=32,'gy'=16] {'gx','gy'}, use_global_device_ids=true, to_apply=%region_12.13 | all-reduce | flops 256 | bytes 2048 | tf_op jit(solution)/shard_map/psum | solution.py:81
  869.9 2.2 fusion.141
  872.1 1.9 gather_fusion.4
  874.0 0.9 fusion.143
  874.9 1.9 collective-permute-start.12
  876.7 1.3 collective-permute-start.13
  878.0 3.1 collective-permute-start.14
  881.1 1.9 collective-permute-start.15
  883.0 1.4 fusion.54
  884.4 1.9 collective-permute-done.15
  886.5 4.8 scatter_fusion.3
  891.3 1.8 subtract_bitcast_fusion
  (72 shorter events, 4.9 us)
Async XLA Ops:
  7.2 133.7 %copy-start = (bf16[1,1,896,896]{3,2,1,0:T(8,128)(2,1)S(1)}, bf16[1,1,896,896]{3,2,1,0:T(8,128)(2,1)}, u32[]{:S(2)}) copy-start(bf16[1,1,896,896]{3,2,1,0:T(8,128)(2,1)} %param.13) | copy-start | bytes 4816900
  7.2 4.8 copy-start.11
  7.2 4.8 copy-start.12
  7.2 4.8 copy-start.9
  7.2 20.6 %copy-start.10 = (s32[1,1,4,128]{3,2,1,0:T(4,128)S(1)}, s32[1,1,4,128]{3,2,1,0:T(4,128)}, u32[]{:S(2)}) copy-start(s32[1,1,4,128]{3,2,1,0:T(4,128)} %param.16) | copy-start | bytes 6148
  7.2 126.8 %all-gather.5.cloned.1.call-start = ((), (), s32[]{:S(2)}) async-start(), calls=%async_computation | async-start | bytes 2101248 | tf_op jit(solution)/shard_map/all_gather | solution.py:72
  9.1 271.2 %all-gather.7.cloned.1.call-start = ((), (), s32[]{:S(2)}) async-start(), calls=%async_computation.1 | async-start | bytes 2101248 | tf_op jit(solution)/shard_map/all_gather | solution.py:72
  27.8 112.6 %copy-start.8 = (bf16[1,1,8,896]{3,2,1,0:T(8,128)(2,1)S(1)}, bf16[1,1,8,896]{3,2,1,0:T(8,128)(2,1)}, u32[]{:S(2)}) copy-start(bf16[1,1,8,896]{3,2,1,0:T(8,128)(2,1)} %param.17) | copy-start | bytes 43012
  134.0 6.9 copy-start.6
  140.9 13.3 %copy-start.1 = (bf16[1,1,896,896]{3,2,1,0:T(8,128)(2,1)S(1)}, bf16[1,1,896,896]{3,2,1,0:T(8,128)(2,1)}, u32[]{:S(2)}) copy-start(bf16[1,1,896,896]{3,2,1,0:T(8,128)(2,1)} %param.11) | copy-start | bytes 4816900
  144.1 13.3 %copy-start.13 = (bf16[1,1,4,128,128]{4,3,2,1,0:T(8,128)(2,1)S(1)}, bf16[1,1,4,128,128]{4,3,2,1,0:T(8,128)(2,1)}, u32[]{:S(2)}) copy-start(bf16[1,1,4,128,128]{4,3,2,1,0:T(8,128)(2,1)} %param.15) | copy-start | bytes 393220
  145.0 10.5 %collective-permute-start = (bf16[128,128]{1,0:T(8,128)(2,1)S(1)}, bf16[128,128]{1,0:T(8,128)(2,1)S(1)}, u32[]{:S(2)}, u32[]{:S(2)}) collective-permute-start(bf16[128,128]{1,0:T(8,128)(2,1)S(1)} %get-tuple-element.30), channel_id=1, source_target_pairs={{0,16},{16,32},{32,48},{48,64},{64,80},{80,96},{96,112},{112,128},... | collective-permute-start | bytes 98312 | tf_op jit(solution)/shard_map/ppermute | solution.py:12
  148.0 7.5 collective-permute-start.1
  149.3 6.2 collective-permute-start.2
  152.2 5.2 collective-permute-start.3
  165.3 358.2 %all-gather.9.cloned.1.call-start = ((), (), s32[]{:S(2)}) async-start(), calls=%async_computation.2 | async-start | bytes 2101248 | tf_op jit(solution)/shard_map/all_gather | solution.py:72
  280.3 6.9 copy-start.5
  388.9 12.3 %copy-start.14 = (bf16[1,1,4,128,128]{4,3,2,1,0:T(8,128)(2,1)S(1)}, bf16[1,1,4,128,128]{4,3,2,1,0:T(8,128)(2,1)}, u32[]{:S(2)}) copy-start(bf16[1,1,4,128,128]{4,3,2,1,0:T(8,128)(2,1)} %param.15) | copy-start | bytes 393220
  389.8 9.5 %collective-permute-start.4 = (bf16[128,128]{1,0:T(8,128)(2,1)S(1)}, bf16[128,128]{1,0:T(8,128)(2,1)S(1)}, u32[]{:S(2)}, u32[]{:S(2)}) collective-permute-start(bf16[128,128]{1,0:T(8,128)(2,1)S(1)} %get-tuple-element.26), channel_id=1, source_target_pairs={{0,16},{16,32},{32,48},{48,64},{64,80},{80,96},{96,112},{112,128},... | collective-permute-start | bytes 98312 | tf_op jit(solution)/shard_map/ppermute | solution.py:12
  391.6 7.7 collective-permute-start.5
  392.9 6.4 collective-permute-start.6
  396.0 5.2 collective-permute-start.7
  409.1 356.7 %all-gather.11.cloned.1.call-start = ((), (), s32[]{:S(2)}) async-start(), calls=%async_computation.3 | async-start | bytes 2101248 | tf_op jit(solution)/shard_map/all_gather | solution.py:72
  523.4 6.9 copy-start.2
  631.3 12.3 %copy-start.15 = (bf16[1,1,4,128,128]{4,3,2,1,0:T(8,128)(2,1)S(1)}, bf16[1,1,4,128,128]{4,3,2,1,0:T(8,128)(2,1)}, u32[]{:S(2)}) copy-start(bf16[1,1,4,128,128]{4,3,2,1,0:T(8,128)(2,1)} %param.15) | copy-start | bytes 393220
  632.1 9.5 %collective-permute-start.8 = (bf16[128,128]{1,0:T(8,128)(2,1)S(1)}, bf16[128,128]{1,0:T(8,128)(2,1)S(1)}, u32[]{:S(2)}, u32[]{:S(2)}) collective-permute-start(bf16[128,128]{1,0:T(8,128)(2,1)S(1)} %get-tuple-element.22), channel_id=1, source_target_pairs={{0,16},{16,32},{32,48},{48,64},{64,80},{80,96},{96,112},{112,128},... | collective-permute-start | bytes 98312 | tf_op jit(solution)/shard_map/ppermute | solution.py:12
  634.0 7.7 collective-permute-start.9
  635.3 6.4 collective-permute-start.10
  638.4 5.2 collective-permute-start.11
  765.8 6.9 copy-start.3
  765.8 6.9 copy-start.4
  874.0 12.3 %copy-start.16 = (bf16[1,1,4,128,128]{4,3,2,1,0:T(8,128)(2,1)S(1)}, bf16[1,1,4,128,128]{4,3,2,1,0:T(8,128)(2,1)}, u32[]{:S(2)}) copy-start(bf16[1,1,4,128,128]{4,3,2,1,0:T(8,128)(2,1)} %param.15) | copy-start | bytes 393220
  874.9 9.5 %collective-permute-start.12 = (bf16[128,128]{1,0:T(8,128)(2,1)S(1)}, bf16[128,128]{1,0:T(8,128)(2,1)S(1)}, u32[]{:S(2)}, u32[]{:S(2)}) collective-permute-start(bf16[128,128]{1,0:T(8,128)(2,1)S(1)} %get-tuple-element.18), channel_id=1, source_target_pairs={{0,16},{16,32},{32,48},{48,64},{64,80},{80,96},{96,112},{112,128},... | collective-permute-start | bytes 98312 | tf_op jit(solution)/shard_map/ppermute | solution.py:12
  876.7 7.7 collective-permute-start.13
  878.0 6.4 collective-permute-start.14
  881.1 5.2 collective-permute-start.15
  886.5 4.8 copy-start.7
Sparse Core Ops, SparseCore 0:
  12.8 121.1 all-gather.4
  165.4 114.8 all-gather.6
  409.2 114.1 all-gather.8
  651.6 114.1 all-gather.10
where the time goes:
time: 904 us; the launch traced here: 900 us
  waiting for transfers between devices  457 us (51%)
  blocking collectives  289 us (32%)
  matrix products  44.5 us (5%)
  starting transfers between devices  34.1 us (4%)
  other arithmetic  30.7 us (3%)
  local copies, waits for them, and re-layouts  29.7 us (3%)
  between operations  14.2 us (2%)
    all_gather x4, waiting for transfers between devices, apply_prec(): stacked = lax.all_gather(coarse, ('gx', 'gy'), axis=0, tiled=True)  449 us
    psum x3, blocking collectives, shards(): lax.psum((jnp.sum(mapped * direction, axis=0), jnp.sum(mapped * mapped, a...  289 us
    ppermute x16, starting transfers between devices, from_behind(): lax.ppermute(value, axis, [(source, source + steps) for source in range(l...  33.5 us
    dot_general x4, matrix products, apply_prec(): solved = jnp.dot(coarse_cols, stacked, precision=lax.Precision.HIGHEST)  25.7 us
    scatter-add x4, other arithmetic, apply_schur(): return result.at[flat_rows].add(-coupled.reshape(-1, coupled.shape[-1]))  20.3 us
  transfers between devices with their start and end apart: 20, of which 8 were waited for; matrix products, arithmetic and copies ran while one was open for 3% of the time, Pallas kernels for 0%

commit v1 on v0

--- a/solution.py
+++ b/solution.py
@@ -10,6 +10,16 @@
     count = lax.axis_size(axis)
     leading, last = (max(0, -steps), min(count, count - steps))
     return lax.ppermute(value, axis, [(source, source + steps) for source in range(leading, last)])
+
+
+def total_over_mesh(value):
+    for axis in ("gy", "gx"):
+        count = lax.axis_size(axis)
+        step = 1
+        while step < count:
+            value = value + lax.ppermute(value, axis, [(i, i ^ step) for i in range(count)])
+            step *= 2
+    return value
 
 
 def pass_columns(rows, offset):
@@ -69,7 +79,9 @@
             trace_mat, rounded, preferred_element_type=jnp.float32
         )
         coarse = jnp.dot(vectors, rounded, preferred_element_type=jnp.float32)
-        stacked = lax.all_gather(coarse, ("gx", "gy"), axis=0, tiled=True)
+        stacked = lax.all_gather(
+            lax.all_gather(coarse, "gx", axis=0), "gy", axis=1
+        ).reshape(-1, coarse.shape[-1])
         solved = jnp.dot(coarse_cols, stacked, precision=lax.Precision.HIGHEST)
         return result + jnp.dot(vectors_wide, solved, precision=lax.Precision.HIGHEST)
 
@@ -78,8 +90,8 @@
     for iteration in range(ITERS):
         image = apply_schur(direction)
         mapped = apply_prec(image)
-        numer, denom = lax.psum(
-            (jnp.sum(mapped * direction, axis=0), jnp.sum(mapped * mapped, axis=0)), ("gx", "gy")
+        numer, denom = total_over_mesh(
+            jnp.stack([jnp.sum(mapped * direction, axis=0), jnp.sum(mapped * mapped, axis=0)])
         )
         alpha = numer / denom
         solution = solution + alpha * direction

time: 904 us -> 660 us (0.73)
  waiting for transfers between devices: 457 us -> 224 us
  blocking collectives: 289 us -> 141 us
  starting transfers between devices: 34.1 us -> 177 us
    psum x3 -> x0, blocking collectives: 289 us -> none  [shards(): lax.psum((jnp.sum(mapped * direction, axis=0), jnp.sum(mapped * mapped, a...]
    all_gather x4, waiting for transfers between devices: 449 us -> 181 us  [apply_prec(): lax.all_gather(lax.all_gather(coarse, 'gx', axis=0), 'gy', axis=1)]
    all_gather x0 -> x4, blocking collectives: none -> 141 us  [apply_prec(): lax.all_gather(coarse, 'gx', axis=0)]
    ppermute x0 -> x27, starting transfers between devices: none -> 110 us  [total_over_mesh(): lax.ppermute(value, axis, [(i, i ^ step) for i in range(count)])]
    ppermute x0 -> x27, waiting for transfers between devices: none -> 35.6 us  [total_over_mesh(): lax.ppermute(value, axis, [(i, i ^ step) for i in range(count)])]
    ppermute x16, starting transfers between devices: 33.5 us -> 66.8 us  [from_behind(): lax.ppermute(value, axis, [(source, source + steps) for source in range(l...]
  transfers between devices with their start and end apart: 20 -> 47, of which waited for: 8 -> 35; matrix products, arithmetic and copies ran while one was open for 3% -> 4% of each run, Pallas kernels for 0% -> 0%
where the time goes in v1:
time: 660 us; the launch traced here: 655 us
  waiting for transfers between devices  224 us (34%)
  starting transfers between devices  177 us (27%)
  blocking collectives  141 us (21%)
  matrix products  40.7 us (6%)
  local copies, waits for them, and re-layouts  29.7 us (4%)
  other arithmetic  27.4 us (4%)
  between operations  14.4 us (2%)
    all_gather x4, waiting for transfers between devices, apply_prec(): lax.all_gather(lax.all_gather(coarse, 'gx', axis=0), 'gy', axis=1)  181 us
    all_gather x4, blocking collectives, apply_prec(): lax.all_gather(coarse, 'gx', axis=0)  141 us
    ppermute x27, starting transfers between devices, total_over_mesh(): lax.ppermute(value, axis, [(i, i ^ step) for i in range(count)])  110 us
    ppermute x16, starting transfers between devices, from_behind(): lax.ppermute(value, axis, [(source, source + steps) for source in range(l...  66.8 us
    ppermute x27, waiting for transfers between devices, total_over_mesh(): lax.ppermute(value, axis, [(i, i ^ step) for i in range(count)])  35.6 us
    dot_general x4, matrix products, apply_prec(): solved = jnp.dot(coarse_cols, stacked, precision=lax.Precision.HIGHEST)  25.7 us
    scatter-add x4, other arithmetic, apply_schur(): return result.at[flat_rows].add(-coupled.reshape(-1, coupled.shape[-1]))  20.4 us
    gather x1, local copies, waits for them, and re-layouts, shards(): coarse_cols = jnp.take(coarse_inverse, coarse_map, axis=1)  15.8 us
  transfers between devices with their start and end apart: 47, of which 35 were waited for; matrix products, arithmetic and copies ran while one was open for 4% of the time, Pallas kernels for 0%

profile of v1, /device:TPU:1, one launch (start us, length us, event | category | flops | bytes accessed | tf_op | source)
XLA Modules:
  0.0 655.3 jit_solution(1789176798314529678)
XLA Ops:
  8.5 34.3 %all-gather = f32[256,128]{1,0:T(8,128)} all-gather(f32[8,128]{1,0:T(8,128)S(1)} %fusion.129), channel_id=2, replica_groups=mesh['gx'=32,'gy'=16] {'gx'}, dimensions={0}, use_global_device_ids=true | all-gather | bytes 135168 | tf_op jit(solution)/shard_map/all_gather | solution.py:83
  42.8 2.9 copy.12
  45.8 15.8 %gather_fusion = f32[4096,8]{1,0:T(8,128)} fusion(f32[8,4096]{0,1:T(8,128)} %copy.12, s32[4096]{0:T(1024)S(1)} %fusion.131), kind=kCustom, calls=%fused_computation | custom fusion | bytes 278528 | tf_op jit(solution)/shard_map/jit(_take)/gather | solution.py:55
  61.6 35.8 %all-gather.13.cloned.1.call-done = f32[32,128,128]{2,1,0:T(8,128)} async-done(((f32[32,8,128]{2,1,0:T(8,128)}), f32[32,128,128]{2,1,0:T(8,128)}) %all-gather.13.cloned.1.call-update) | async-done | bytes 2097168 | tf_op jit(solution)/shard_map/all_gather | solution.py:82
  97.4 6.4 fusion.4
  108.4 3.2 collective-permute-start
  112.9 3.4 collective-permute-start.2
  116.3 1.9 collective-permute-start.3
  119.6 1.9 collective-permute-done.3
  122.4 5.2 scatter_fusion
  128.8 35.7 %all-gather.2 = f32[256,128]{1,0:T(8,128)} all-gather(f32[8,128]{1,0:T(8,128)S(1)} %convolution_bitcast_fusion.6), channel_id=4, replica_groups=mesh['gx'=32,'gy'=16] {'gx'}, dimensions={0}, use_global_device_ids=true | all-gather | bytes 135168 | tf_op jit(solution)/shard_map/all_gather | solution.py:83
  164.7 48.2 %all-gather.15.cloned.1.call-done = f32[32,128,128]{2,1,0:T(8,128)} async-done(((f32[32,8,128]{2,1,0:T(8,128)}), f32[32,128,128]{2,1,0:T(8,128)}) %all-gather.15.cloned.1.call-update) | async-done | bytes 2097168 | tf_op jit(solution)/shard_map/all_gather | solution.py:82
  212.9 6.4 fusion.2
  220.4 2.2 collective-permute-start.4
  223.5 3.0 collective-permute-start.5
  227.8 3.9 collective-permute-start.6
  233.0 5.2 collective-permute-start.7
  238.2 3.0 collective-permute-done.7
  241.2 3.2 collective-permute-start.8
  245.5 4.1 collective-permute-start.9
  250.7 7.2 %collective-permute-start.10 = (f32[2,128]{1,0:T(2,128)S(1)}, f32[2,128]{1,0:T(2,128)S(1)}, u32[]{:S(2)}, u32[]{:S(2)}) collective-permute-start(f32[2,128]{1,0:T(2,128)S(1)} %add.179), channel_id=1, source_target_pairs={{0,64},{16,80},{32,96},{48,112},{64,0},{80,16},{96,32},{112,48},{1... | collective-permute-start | bytes 3080 | tf_op jit(solution)/shard_map/ppermute | solution.py:20
  258.9 3.2 collective-permute-start.11
  263.2 4.7 collective-permute-start.12
  272.7 3.2 collective-permute-start.13
  277.2 12.6 %collective-permute-start.15 = (bf16[128,128]{1,0:T(8,128)(2,1)S(1)}, bf16[128,128]{1,0:T(8,128)(2,1)S(1)}, u32[]{:S(2)}, u32[]{:S(2)}) collective-permute-start(bf16[128,128]{1,0:T(8,128)(2,1)S(1)} %get-tuple-element.21), channel_id=1, source_target_pairs={{0,1},{1,2},{2,3},{3,4},{4,5},{5,6},{6,7},{7,8},{8,9},{9,10},{10,1... | collective-permute-start | bytes 98312 | tf_op jit(solution)/shard_map/ppermute | solution.py:12
  289.8 1.9 collective-permute-start.16
  293.1 1.9 collective-permute-done.16
  295.9 5.2 scatter_fusion.1
  302.3 35.7 %all-gather.4 = f32[256,128]{1,0:T(8,128)} all-gather(f32[8,128]{1,0:T(8,128)S(1)} %convolution_bitcast_fusion.5), channel_id=6, replica_groups=mesh['gx'=32,'gy'=16] {'gx'}, dimensions={0}, use_global_device_ids=true | all-gather | bytes 135168 | tf_op jit(solution)/shard_map/all_gather | solution.py:83
  338.3 48.2 %all-gather.17.cloned.1.call-done = f32[32,128,128]{2,1,0:T(8,128)} async-done(((f32[32,8,128]{2,1,0:T(8,128)}), f32[32,128,128]{2,1,0:T(8,128)}) %all-gather.17.cloned.1.call-update) | async-done | bytes 2097168 | tf_op jit(solution)/shard_map/all_gather | solution.py:82
  386.4 6.4 fusion
  393.9 2.2 collective-permute-start.17
  397.0 3.0 collective-permute-start.18
  401.3 3.9 collective-permute-start.19
  406.5 5.2 collective-permute-start.20
  411.8 3.0 collective-permute-done.20
  414.7 3.2 collective-permute-start.21
  419.1 4.1 collective-permute-start.22
  424.3 7.2 %collective-permute-start.23 = (f32[2,128]{1,0:T(2,128)S(1)}, f32[2,128]{1,0:T(2,128)S(1)}, u32[]{:S(2)}, u32[]{:S(2)}) collective-permute-start(f32[2,128]{1,0:T(2,128)S(1)} %add.191), channel_id=1, source_target_pairs={{0,64},{16,80},{32,96},{48,112},{64,0},{80,16},{96,32},{112,48},{1... | collective-permute-start | bytes 3080 | tf_op jit(solution)/shard_map/ppermute | solution.py:20
  432.5 3.2 collective-permute-start.24
  436.8 4.7 collective-permute-start.25
  445.5 3.2 collective-permute-start.26
  450.0 12.6 %collective-permute-start.28 = (bf16[128,128]{1,0:T(8,128)(2,1)S(1)}, bf16[128,128]{1,0:T(8,128)(2,1)S(1)}, u32[]{:S(2)}, u32[]{:S(2)}) collective-permute-start(bf16[128,128]{1,0:T(8,128)(2,1)S(1)} %get-tuple-element.17), channel_id=1, source_target_pairs={{0,1},{1,2},{2,3},{3,4},{4,5},{5,6},{6,7},{7,8},{8,9},{9,10},{10,1... | collective-permute-start | bytes 98312 | tf_op jit(solution)/shard_map/ppermute | solution.py:12
  462.6 1.9 collective-permute-start.29
  465.9 1.9 collective-permute-done.29
  468.7 5.2 scatter_fusion.2
  475.1 35.8 %all-gather.6 = f32[256,128]{1,0:T(8,128)} all-gather(f32[8,128]{1,0:T(8,128)S(1)} %convolution_bitcast_fusion.4), channel_id=8, replica_groups=mesh['gx'=32,'gy'=16] {'gx'}, dimensions={0}, use_global_device_ids=true | all-gather | bytes 135168 | tf_op jit(solution)/shard_map/all_gather | solution.py:83
  510.9 48.7 %all-gather.19.cloned.1.call-done = f32[32,128,128]{2,1,0:T(8,128)} async-done(((f32[32,8,128]{2,1,0:T(8,128)}), f32[32,128,128]{2,1,0:T(8,128)}) %all-gather.19.cloned.1.call-update) | async-done | bytes 2097168 | tf_op jit(solution)/shard_map/all_gather | solution.py:82
  559.7 6.4 fusion.6
  567.3 2.2 collective-permute-start.30
  570.3 3.0 collective-permute-start.31
  574.6 3.9 collective-permute-start.32
  579.9 5.2 collective-permute-start.33
  585.1 3.0 collective-permute-done.33
  588.1 3.2 collective-permute-start.34
  592.4 4.1 collective-permute-start.35
  597.6 7.2 %collective-permute-start.36 = (f32[2,128]{1,0:T(2,128)S(1)}, f32[2,128]{1,0:T(2,128)S(1)}, u32[]{:S(2)}, u32[]{:S(2)}) collective-permute-start(f32[2,128]{1,0:T(2,128)S(1)} %add.204), channel_id=1, source_target_pairs={{0,64},{16,80},{32,96},{48,112},{64,0},{80,16},{96,32},{112,48},{1... | collective-permute-start | bytes 3080 | tf_op jit(solution)/shard_map/ppermute | solution.py:20
  605.8 3.2 collective-permute-start.37
  610.1 4.7 collective-permute-start.38
  619.6 3.2 collective-permute-start.39
  624.1 12.6 %collective-permute-start.41 = (bf16[128,128]{1,0:T(8,128)(2,1)S(1)}, bf16[128,128]{1,0:T(8,128)(2,1)S(1)}, u32[]{:S(2)}, u32[]{:S(2)}) collective-permute-start(bf16[128,128]{1,0:T(8,128)(2,1)S(1)} %get-tuple-element.13), channel_id=1, source_target_pairs={{0,1},{1,2},{2,3},{3,4},{4,5},{5,6},{6,7},{7,8},{8,9},{9,10},{10,1... | collective-permute-start | bytes 98312 | tf_op jit(solution)/shard_map/ppermute | solution.py:12
  636.7 1.9 collective-permute-start.42
  640.0 1.9 collective-permute-done.42
  642.1 4.8 scatter_fusion.3
  (161 shorter events, 65.7 us)
Async XLA Ops:
  7.2 97.0 %copy-start = (bf16[1,1,896,896]{3,2,1,0:T(8,128)(2,1)S(1)}, bf16[1,1,896,896]{3,2,1,0:T(8,128)(2,1)}, u32[]{:S(2)}) copy-start(bf16[1,1,896,896]{3,2,1,0:T(8,128)(2,1)} %param.13) | copy-start | bytes 4816900
  7.2 38.5 %copy-start.13 = (f32[1,1,896]{2,1,0:T(1,128)S(1)}, f32[1,1,896]{2,1,0:T(1,128)}, u32[]{:S(2)}) copy-start(f32[1,1,896]{2,1,0:T(1,128)} %param.14) | copy-start | bytes 10756
  7.2 38.5 %copy-start.14 = (f32[1,1,896]{2,1,0:T(1,128)S(1)}, f32[1,1,896]{2,1,0:T(1,128)}, u32[]{:S(2)}) copy-start(f32[1,1,896]{2,1,0:T(1,128)} %param.12) | copy-start | bytes 10756
  7.2 38.6 %copy-start.11 = (s32[4096]{0:T(1024)S(1)}, s32[4096]{0:T(1024)}, u32[]{:S(2)}) copy-start(s32[4096]{0:T(1024)} %param.19) | copy-start | bytes 49156
  7.2 54.3 %copy-start.12 = (s32[1,1,4,128]{3,2,1,0:T(4,128)S(1)}, s32[1,1,4,128]{3,2,1,0:T(4,128)}, u32[]{:S(2)}) copy-start(s32[1,1,4,128]{3,2,1,0:T(4,128)} %param.16) | copy-start | bytes 6148
  7.2 90.1 %all-gather.13.cloned.1.call-start = ((), (), s32[]{:S(2)}) async-start(), calls=%async_computation | async-start | bytes 2228224 | tf_op jit(solution)/shard_map/all_gather | solution.py:82
  42.8 170.1 %all-gather.15.cloned.1.call-start = ((), (), s32[]{:S(2)}) async-start(), calls=%async_computation.1 | async-start | bytes 2228224 | tf_op jit(solution)/shard_map/all_gather | solution.py:82
  97.4 6.9 %copy-start.8 = (bf16[1,1,896,128]{3,2,1,0:T(8,128)(2,1)S(1)}, bf16[1,1,896,128]{3,2,1,0:T(8,128)(2,1)}, u32[]{:S(2)}) copy-start(bf16[1,1,896,128]{3,2,1,0:T(8,128)(2,1)} %param.10) | copy-start | bytes 688132
  104.2 14.0 %copy-start.1 = (bf16[1,1,896,896]{3,2,1,0:T(8,128)(2,1)S(1)}, bf16[1,1,896,896]{3,2,1,0:T(8,128)(2,1)}, u32[]{:S(2)}) copy-start(bf16[1,1,896,896]{3,2,1,0:T(8,128)(2,1)} %param.11) | copy-start | bytes 4816900
  107.5 14.0 %copy-start.15 = (bf16[1,1,4,128,128]{4,3,2,1,0:T(8,128)(2,1)S(1)}, bf16[1,1,4,128,128]{4,3,2,1,0:T(8,128)(2,1)}, u32[]{:S(2)}) copy-start(bf16[1,1,4,128,128]{4,3,2,1,0:T(8,128)(2,1)} %param.15) | copy-start | bytes 393220
  108.4 11.2 %collective-permute-start = (bf16[128,128]{1,0:T(8,128)(2,1)S(1)}, bf16[128,128]{1,0:T(8,128)(2,1)S(1)}, u32[]{:S(2)}, u32[]{:S(2)}) collective-permute-start(bf16[128,128]{1,0:T(8,128)(2,1)S(1)} %get-tuple-element.24), channel_id=1, source_target_pairs={{0,16},{16,32},{32,48},{48,64},{64,80},{80,96},{96,112},{112,128},... | collective-permute-start | bytes 98312 | tf_op jit(solution)/shard_map/ppermute | solution.py:12
  111.6 8.0 %collective-permute-start.1 = (bf16[128,128]{1,0:T(8,128)(2,1)S(1)}, bf16[128,128]{1,0:T(8,128)(2,1)S(1)}, u32[]{:S(2)}, u32[]{:S(2)}) collective-permute-start(bf16[128,128]{1,0:T(8,128)(2,1)S(1)} %get-tuple-element.26), channel_id=1, source_target_pairs={{16,0},{32,16},{48,32},{64,48},{80,64},{96,80},{112,96},{128,112},... | collective-permute-start | bytes 98312 | tf_op jit(solution)/shard_map/ppermute | solution.py:12
  112.9 6.7 %collective-permute-start.2 = (bf16[128,128]{1,0:T(8,128)(2,1)S(1)}, bf16[128,128]{1,0:T(8,128)(2,1)S(1)}, u32[]{:S(2)}, u32[]{:S(2)}) collective-permute-start(bf16[128,128]{1,0:T(8,128)(2,1)S(1)} %get-tuple-element.25), channel_id=1, source_target_pairs={{0,1},{1,2},{2,3},{3,4},{4,5},{5,6},{6,7},{7,8},{8,9},{9,10},{10,1... | collective-permute-start | bytes 98312 | tf_op jit(solution)/shard_map/ppermute | solution.py:12
  116.3 5.2 collective-permute-start.3
  164.5 222.0 %all-gather.17.cloned.1.call-start = ((), (), s32[]{:S(2)}) async-start(), calls=%async_computation.2 | async-start | bytes 2228224 | tf_op jit(solution)/shard_map/all_gather | solution.py:82
  212.9 6.9 %copy-start.6 = (f32[896,128]{1,0:T(8,128)S(1)}, f32[896,128]{1,0:T(8,128)}, u32[]{:S(2)}) copy-start(f32[896,128]{1,0:T(8,128)} %get-tuple-element.29) | copy-start | bytes 1376260
  220.4 3.0 collective-permute-start.4
  223.5 4.3 collective-permute-start.5
  227.8 5.2 collective-permute-start.6
  233.0 8.2 %collective-permute-start.7 = (f32[2,128]{1,0:T(2,128)S(1)}, f32[2,128]{1,0:T(2,128)S(1)}, u32[]{:S(2)}, u32[]{:S(2)}) collective-permute-start(f32[2,128]{1,0:T(2,128)S(1)} %add.176), channel_id=1, source_target_pairs={{0,8},{1,9},{2,10},{3,11},{4,12},{5,13},{6,14},{7,15},{8,0},{9,1},... | collective-permute-start | bytes 3080 | tf_op jit(solution)/shard_map/ppermute | solution.py:20
  241.2 4.3 collective-permute-start.8
  245.5 5.2 collective-permute-start.9
  250.7 8.2 %collective-permute-start.10 = (f32[2,128]{1,0:T(2,128)S(1)}, f32[2,128]{1,0:T(2,128)S(1)}, u32[]{:S(2)}, u32[]{:S(2)}) collective-permute-start(f32[2,128]{1,0:T(2,128)S(1)} %add.179), channel_id=1, source_target_pairs={{0,64},{16,80},{32,96},{48,112},{64,0},{80,16},{96,32},{112,48},{1... | collective-permute-start | bytes 3080 | tf_op jit(solution)/shard_map/ppermute | solution.py:20
  258.9 4.3 collective-permute-start.11
  263.2 5.8 collective-permute-start.12
  271.8 23.2 %copy-start.16 = (bf16[1,1,4,128,128]{4,3,2,1,0:T(8,128)(2,1)S(1)}, bf16[1,1,4,128,128]{4,3,2,1,0:T(8,128)(2,1)}, u32[]{:S(2)}) copy-start(bf16[1,1,4,128,128]{4,3,2,1,0:T(8,128)(2,1)} %param.15) | copy-start | bytes 393220
  272.7 20.4 %collective-permute-start.13 = (bf16[128,128]{1,0:T(8,128)(2,1)S(1)}, bf16[128,128]{1,0:T(8,128)(2,1)S(1)}, u32[]{:S(2)}, u32[]{:S(2)}) collective-permute-start(bf16[128,128]{1,0:T(8,128)(2,1)S(1)} %get-tuple-element.20), channel_id=1, source_target_pairs={{0,16},{16,32},{32,48},{48,64},{64,80},{80,96},{96,112},{112,128},... | collective-permute-start | bytes 98312 | tf_op jit(solution)/shard_map/ppermute | solution.py:12
  275.9 17.2 %collective-permute-start.14 = (bf16[128,128]{1,0:T(8,128)(2,1)S(1)}, bf16[128,128]{1,0:T(8,128)(2,1)S(1)}, u32[]{:S(2)}, u32[]{:S(2)}) collective-permute-start(bf16[128,128]{1,0:T(8,128)(2,1)S(1)} %get-tuple-element.22), channel_id=1, source_target_pairs={{16,0},{32,16},{48,32},{64,48},{80,64},{96,80},{112,96},{128,112},... | collective-permute-start | bytes 98312 | tf_op jit(solution)/shard_map/ppermute | solution.py:12
  277.2 15.9 %collective-permute-start.15 = (bf16[128,128]{1,0:T(8,128)(2,1)S(1)}, bf16[128,128]{1,0:T(8,128)(2,1)S(1)}, u32[]{:S(2)}, u32[]{:S(2)}) collective-permute-start(bf16[128,128]{1,0:T(8,128)(2,1)S(1)} %get-tuple-element.21), channel_id=1, source_target_pairs={{0,1},{1,2},{2,3},{3,4},{4,5},{5,6},{6,7},{7,8},{8,9},{9,10},{10,1... | collective-permute-start | bytes 98312 | tf_op jit(solution)/shard_map/ppermute | solution.py:12
  289.8 5.2 collective-permute-start.16
  338.0 221.7 %all-gather.19.cloned.1.call-start = ((), (), s32[]{:S(2)}) async-start(), calls=%async_computation.3 | async-start | bytes 2228224 | tf_op jit(solution)/shard_map/all_gather | solution.py:82
  386.4 6.9 %copy-start.2 = (f32[896,128]{1,0:T(8,128)S(1)}, f32[896,128]{1,0:T(8,128)}, u32[]{:S(2)}) copy-start(f32[896,128]{1,0:T(8,128)} %get-tuple-element.11) | copy-start | bytes 1376260
  393.9 48.7 %copy-start.4 = (f32[896,128]{1,0:T(8,128)}, f32[896,128]{1,0:T(8,128)S(1)}, u32[]{:S(2)}) copy-start(f32[896,128]{1,0:T(8,128)S(1)} %get-tuple-element.31) | copy-start | bytes 1376260
  393.9 3.0 collective-permute-start.17
  397.0 4.3 collective-permute-start.18
  401.3 5.2 collective-permute-start.19
  406.5 8.2 %collective-permute-start.20 = (f32[2,128]{1,0:T(2,128)S(1)}, f32[2,128]{1,0:T(2,128)S(1)}, u32[]{:S(2)}, u32[]{:S(2)}) collective-permute-start(f32[2,128]{1,0:T(2,128)S(1)} %add.188), channel_id=1, source_target_pairs={{0,8},{1,9},{2,10},{3,11},{4,12},{5,13},{6,14},{7,15},{8,0},{9,1},... | collective-permute-start | bytes 3080 | tf_op jit(solution)/shard_map/ppermute | solution.py:20
  414.7 4.3 collective-permute-start.21
  419.1 5.2 collective-permute-start.22
  424.3 8.2 %collective-permute-start.23 = (f32[2,128]{1,0:T(2,128)S(1)}, f32[2,128]{1,0:T(2,128)S(1)}, u32[]{:S(2)}, u32[]{:S(2)}) collective-permute-start(f32[2,128]{1,0:T(2,128)S(1)} %add.191), channel_id=1, source_target_pairs={{0,64},{16,80},{32,96},{48,112},{64,0},{80,16},{96,32},{112,48},{1... | collective-permute-start | bytes 3080 | tf_op jit(solution)/shard_map/ppermute | solution.py:20
  432.5 4.3 collective-permute-start.24
  436.8 5.8 collective-permute-start.25
  444.6 23.2 %copy-start.17 = (bf16[1,1,4,128,128]{4,3,2,1,0:T(8,128)(2,1)S(1)}, bf16[1,1,4,128,128]{4,3,2,1,0:T(8,128)(2,1)}, u32[]{:S(2)}) copy-start(bf16[1,1,4,128,128]{4,3,2,1,0:T(8,128)(2,1)} %param.15) | copy-start | bytes 393220
  445.5 20.4 %collective-permute-start.26 = (bf16[128,128]{1,0:T(8,128)(2,1)S(1)}, bf16[128,128]{1,0:T(8,128)(2,1)S(1)}, u32[]{:S(2)}, u32[]{:S(2)}) collective-permute-start(bf16[128,128]{1,0:T(8,128)(2,1)S(1)} %get-tuple-element.16), channel_id=1, source_target_pairs={{0,16},{16,32},{32,48},{48,64},{64,80},{80,96},{96,112},{112,128},... | collective-permute-start | bytes 98312 | tf_op jit(solution)/shard_map/ppermute | solution.py:12
  448.7 17.2 %collective-permute-start.27 = (bf16[128,128]{1,0:T(8,128)(2,1)S(1)}, bf16[128,128]{1,0:T(8,128)(2,1)S(1)}, u32[]{:S(2)}, u32[]{:S(2)}) collective-permute-start(bf16[128,128]{1,0:T(8,128)(2,1)S(1)} %get-tuple-element.18), channel_id=1, source_target_pairs={{16,0},{32,16},{48,32},{64,48},{80,64},{96,80},{112,96},{128,112},... | collective-permute-start | bytes 98312 | tf_op jit(solution)/shard_map/ppermute | solution.py:12
  450.0 15.9 %collective-permute-start.28 = (bf16[128,128]{1,0:T(8,128)(2,1)S(1)}, bf16[128,128]{1,0:T(8,128)(2,1)S(1)}, u32[]{:S(2)}, u32[]{:S(2)}) collective-permute-start(bf16[128,128]{1,0:T(8,128)(2,1)S(1)} %get-tuple-element.17), channel_id=1, source_target_pairs={{0,1},{1,2},{2,3},{3,4},{4,5},{5,6},{6,7},{7,8},{8,9},{9,10},{10,1... | collective-permute-start | bytes 98312 | tf_op jit(solution)/shard_map/ppermute | solution.py:12
  462.6 5.2 collective-permute-start.29
  559.7 6.9 %copy-start.3 = (f32[896,128]{1,0:T(8,128)S(1)}, f32[896,128]{1,0:T(8,128)}, u32[]{:S(2)}) copy-start(f32[896,128]{1,0:T(8,128)} %get-tuple-element.11) | copy-start | bytes 1376260
  559.7 6.9 %copy-start.5 = (f32[896,128]{1,0:T(8,128)S(1)}, f32[896,128]{1,0:T(8,128)}, u32[]{:S(2)}) copy-start(f32[896,128]{1,0:T(8,128)} %copy-done.4) | copy-start | bytes 1376260
  566.1 49.8 %copy-start.7 = (f32[896,128]{1,0:T(8,128)S(1)}, f32[896,128]{1,0:T(8,128)}, u32[]{:S(2)}) copy-start(f32[896,128]{1,0:T(8,128)} %get-tuple-element.29) | copy-start | bytes 1376260
  567.3 3.0 collective-permute-start.30
  570.3 4.3 collective-permute-start.31
  574.6 5.2 collective-permute-start.32
  579.9 8.2 %collective-permute-start.33 = (f32[2,128]{1,0:T(2,128)S(1)}, f32[2,128]{1,0:T(2,128)S(1)}, u32[]{:S(2)}, u32[]{:S(2)}) collective-permute-start(f32[2,128]{1,0:T(2,128)S(1)} %add.201), channel_id=1, source_target_pairs={{0,8},{1,9},{2,10},{3,11},{4,12},{5,13},{6,14},{7,15},{8,0},{9,1},... | collective-permute-start | bytes 3080 | tf_op jit(solution)/shard_map/ppermute | solution.py:20
  588.1 4.3 collective-permute-start.34
  592.4 5.2 collective-permute-start.35
  597.6 8.2 %collective-permute-start.36 = (f32[2,128]{1,0:T(2,128)S(1)}, f32[2,128]{1,0:T(2,128)S(1)}, u32[]{:S(2)}, u32[]{:S(2)}) collective-permute-start(f32[2,128]{1,0:T(2,128)S(1)} %add.204), channel_id=1, source_target_pairs={{0,64},{16,80},{32,96},{48,112},{64,0},{80,16},{96,32},{112,48},{1... | collective-permute-start | bytes 3080 | tf_op jit(solution)/shard_map/ppermute | solution.py:20
  605.8 4.3 collective-permute-start.37
  610.1 5.8 collective-permute-start.38
  618.8 23.2 %copy-start.18 = (bf16[1,1,4,128,128]{4,3,2,1,0:T(8,128)(2,1)S(1)}, bf16[1,1,4,128,128]{4,3,2,1,0:T(8,128)(2,1)}, u32[]{:S(2)}) copy-start(bf16[1,1,4,128,128]{4,3,2,1,0:T(8,128)(2,1)} %param.15) | copy-start | bytes 393220
  619.6 20.4 %collective-permute-start.39 = (bf16[128,128]{1,0:T(8,128)(2,1)S(1)}, bf16[128,128]{1,0:T(8,128)(2,1)S(1)}, u32[]{:S(2)}, u32[]{:S(2)}) collective-permute-start(bf16[128,128]{1,0:T(8,128)(2,1)S(1)} %get-tuple-element.12), channel_id=1, source_target_pairs={{0,16},{16,32},{32,48},{48,64},{64,80},{80,96},{96,112},{112,128},... | collective-permute-start | bytes 98312 | tf_op jit(solution)/shard_map/ppermute | solution.py:12
  622.8 17.2 %collective-permute-start.40 = (bf16[128,128]{1,0:T(8,128)(2,1)S(1)}, bf16[128,128]{1,0:T(8,128)(2,1)S(1)}, u32[]{:S(2)}, u32[]{:S(2)}) collective-permute-start(bf16[128,128]{1,0:T(8,128)(2,1)S(1)} %get-tuple-element.14), channel_id=1, source_target_pairs={{16,0},{32,16},{48,32},{64,48},{80,64},{96,80},{112,96},{128,112},... | collective-permute-start | bytes 98312 | tf_op jit(solution)/shard_map/ppermute | solution.py:12
  624.1 15.9 %collective-permute-start.41 = (bf16[128,128]{1,0:T(8,128)(2,1)S(1)}, bf16[128,128]{1,0:T(8,128)(2,1)S(1)}, u32[]{:S(2)}, u32[]{:S(2)}) collective-permute-start(bf16[128,128]{1,0:T(8,128)(2,1)S(1)} %get-tuple-element.13), channel_id=1, source_target_pairs={{0,1},{1,2},{2,3},{3,4},{4,5},{5,6},{6,7},{7,8},{8,9},{9,10},{10,1... | collective-permute-start | bytes 98312 | tf_op jit(solution)/shard_map/ppermute | solution.py:12
  636.7 5.2 collective-permute-start.42
  (2 other events, 11.2 us)
Sparse Core Ops, SparseCore 0:
  42.9 54.4 all-gather.12
  164.6 48.2 all-gather.14
  338.1 48.2 all-gather.16
  511.0 48.5 all-gather.18

commit v2 on v1

--- a/solution.py
+++ b/solution.py
@@ -20,6 +20,20 @@
             value = value + lax.ppermute(value, axis, [(i, i ^ step) for i in range(count)])
             step *= 2
     return value
+
+
+def scatter_rows(stacked, axis, rows):
+    count = lax.axis_size(axis)
+    index = lax.axis_index(axis)
+    blocks = stacked.reshape(count, rows, stacked.shape[-1])
+    half = count // 2
+    while half >= 1:
+        upper = (index // half) % 2 == 1
+        keep = jnp.where(upper, blocks[half:], blocks[:half])
+        send = jnp.where(upper, blocks[:half], blocks[half:])
+        blocks = keep + lax.ppermute(send, axis, [(i, i ^ half) for i in range(count)])
+        half //= 2
+    return blocks[0]
 
 
 def pass_columns(rows, offset):
@@ -52,7 +66,12 @@
     flat_rows = rows_lists.reshape(-1)
     vectors = deflation[0, 0]
     vectors_wide = vectors.astype(jnp.float32).T
+    count_x, count_y = lax.axis_size("gx"), lax.axis_size("gy")
+    depth = vectors.shape[0]
     coarse_cols = jnp.take(coarse_inverse, coarse_map, axis=1)
+    coarse_block = lax.all_to_all(
+        coarse_cols.reshape(depth, count_x, count_y * depth), "gx", 1, 0, tiled=True
+    ).reshape(count_x * depth, count_y * depth)
 
     def apply_schur(field):
         rounded = lax.optimization_barrier(field.astype(jnp.bfloat16))
@@ -79,10 +98,9 @@
             trace_mat, rounded, preferred_element_type=jnp.float32
         )
         coarse = jnp.dot(vectors, rounded, preferred_element_type=jnp.float32)
-        stacked = lax.all_gather(
-            lax.all_gather(coarse, "gx", axis=0), "gy", axis=1
-        ).reshape(-1, coarse.shape[-1])
-        solved = jnp.dot(coarse_cols, stacked, precision=lax.Precision.HIGHEST)
+        line = lax.all_gather(coarse, "gy", axis=0, tiled=True)
+        partial = jnp.dot(coarse_block, line, precision=lax.Precision.HIGHEST)
+        solved = scatter_rows(partial, "gx", depth)
         return result + jnp.dot(vectors_wide, solved, precision=lax.Precision.HIGHEST)
 
     solution = jnp.zeros(rhs_wide.shape, jnp.float32)

time: 660 us -> 526 us (0.80)
  waiting for transfers between devices: 224 us -> 102 us
  starting transfers between devices: 177 us -> 269 us
  blocking collectives: 141 us -> 70.1 us
  matrix products: 40.7 us -> 16.6 us
  between operations: 14.4 us -> 1.74 us
    all_gather x4 -> x0, waiting for transfers between devices: 181 us -> none  [apply_prec(): lax.all_gather(lax.all_gather(coarse, 'gx', axis=0), 'gy', axis=1)]
    ppermute x0 -> x20, starting transfers between devices: none -> 87.5 us  [scatter_rows(): lax.ppermute(send, axis, [(i, i ^ half) for i in range(count)])]
    all_gather x4, blocking collectives: 141 us -> 70.1 us  [apply_prec(): line = lax.all_gather(coarse, 'gy', axis=0, tiled=True)]
    ppermute x0 -> x20, waiting for transfers between devices: none -> 41.7 us  [scatter_rows(): lax.ppermute(send, axis, [(i, i ^ half) for i in range(count)])]
    dot_general x4, matrix products: 25.7 us -> 1.04 us  [apply_prec(): partial = jnp.dot(coarse_block, line, precision=lax.Precision.HIGHEST)]
    ppermute x27, waiting for transfers between devices: 35.6 us -> 53.2 us  [total_over_mesh(): lax.ppermute(value, axis, [(i, i ^ step) for i in range(count)])]
    all_to_all x0 -> x1, starting transfers between devices: none -> 10.5 us  [shards(): lax.all_to_all(coarse_cols.reshape(depth, count_x, count_y * depth), 'gx'...]
    gather x1 -> x2, local copies, waits for them, and re-layouts: 15.8 us -> 18 us  [shards(): coarse_cols = jnp.take(coarse_inverse, coarse_map, axis=1)]
  transfers between devices with their start and end apart: 47 -> 64, of which waited for: 35 -> 50; matrix products, arithmetic and copies ran while one was open for 4% -> 2% of each run, Pallas kernels for 0% -> 0%
where the time goes in v2:
time: 526 us; the launch traced here: 519 us
  starting transfers between devices  269 us (51%)
  waiting for transfers between devices  102 us (19%)
  blocking collectives  70.1 us (13%)
  local copies, waits for them, and re-layouts  32 us (6%)
  other arithmetic  27.6 us (5%)
  matrix products  16.6 us (3%)
    ppermute x27, starting transfers between devices, total_over_mesh(): lax.ppermute(value, axis, [(i, i ^ step) for i in range(count)])  107 us
    ppermute x20, starting transfers between devices, scatter_rows(): lax.ppermute(send, axis, [(i, i ^ half) for i in range(count)])  87.5 us
    all_gather x4, blocking collectives, apply_prec(): line = lax.all_gather(coarse, 'gy', axis=0, tiled=True)  70.1 us
    ppermute x16, starting transfers between devices, from_behind(): lax.ppermute(value, axis, [(source, source + steps) for source in range(l...  63.5 us
    ppermute x27, waiting for transfers between devices, total_over_mesh(): lax.ppermute(value, axis, [(i, i ^ step) for i in range(count)])  53.2 us
    ppermute x20, waiting for transfers between devices, scatter_rows(): lax.ppermute(send, axis, [(i, i ^ half) for i in range(count)])  41.7 us
    scatter-add x4, other arithmetic, apply_schur(): return result.at[flat_rows].add(-coupled.reshape(-1, coupled.shape[-1]))  19.1 us
    gather x2, local copies, waits for them, and re-layouts, shards(): coarse_cols = jnp.take(coarse_inverse, coarse_map, axis=1)  18 us
  transfers between devices with their start and end apart: 64, of which 50 were waited for; matrix products, arithmetic and copies ran while one was open for 2% of the time, Pallas kernels for 0%

profile of v2, /device:TPU:1, one launch (start us, length us, event | category | flops | bytes accessed | tf_op | source)
XLA Modules:
  0.0 519.0 jit_solution(16364988911038670015)
XLA Ops:
  2.2 2.9 copy.37
  5.1 15.8 %gather_fusion = f32[4096,8]{1,0:T(8,128)} fusion(f32[8,4096]{0,1:T(8,128)} %copy.37, s32[4096]{0:T(1024)S(1)} %fusion.115), kind=kCustom, calls=%fused_computation | custom fusion | bytes 278528 | tf_op jit(solution)/shard_map/jit(_take)/gather | solution.py:71
  23.7 10.5 %all-to-all-start = ((f32[8,32,128]{2,0,1:T(8,128)}), f32[8,32,128]{2,0,1:T(8,128)S(1)}, u32[]{:S(2)}, u32[]{:S(2)}) async-start(f32[8,32,128]{2,0,1:T(8,128)} %broadcast_select_fusion), calls=%async_computation | async-start | bytes 262144 | tf_op jit(solution)/shard_map/all_to_all | solution.py:72
  34.5 24.1 %all_gather.12 = f32[128,128]{1,0:T(8,128)S(1)} all-gather(f32[8,128]{1,0:T(8,128)S(1)} %fusion.113), channel_id=1, replica_groups=mesh['gx'=32,'gy'=16] {'gy'}, dimensions={0}, use_global_device_ids=true | all-gather | bytes 69632 | tf_op jit(solution)/shard_map/all_gather | solution.py:101
  58.9 4.9 collective-permute-start
  66.0 3.3 collective-permute-start.1
  70.7 7.3 %collective-permute-start.2 = (f32[4,8,128]{2,1,0:T(8,128)S(1)}, f32[4,8,128]{2,1,0:T(8,128)S(1)}, u32[]{:S(2)}, u32[]{:S(2)}) collective-permute-start(f32[4,8,128]{2,1,0:T(8,128)S(1)} %slice_select_fusion.7), channel_id=1, source_target_pairs={{0,64},{16,80},{32,96},{48,112},{64,0},{80,16},{96,32},{112,48},{1... | collective-permute-start | bytes 49160 | tf_op jit(solution)/shard_map/ppermute | solution.py:34
  79.2 4.3 collective-permute-start.3
  84.5 3.2 collective-permute-start.4
  93.8 3.2 collective-permute-start.5
  98.4 6.6 %collective-permute-start.7 = (bf16[128,128]{1,0:T(8,128)(2,1)S(1)}, bf16[128,128]{1,0:T(8,128)(2,1)S(1)}, u32[]{:S(2)}, u32[]{:S(2)}) collective-permute-start(bf16[128,128]{1,0:T(8,128)(2,1)S(1)} %get-tuple-element.25), channel_id=1, source_target_pairs={{0,1},{1,2},{2,3},{3,4},{4,5},{5,6},{6,7},{7,8},{8,9},{9,10},{10,1... | collective-permute-start | bytes 98312 | tf_op jit(solution)/shard_map/ppermute | solution.py:12
  111.1 5.2 %scatter_fusion = f32[896,128]{1,0:T(8,128)} fusion(f32[896,128]{1,0:T(8,128)} %fusion.37, s32[512]{0:T(512)S(1)} %bitcast.261, f32[512,128]{1,0:T(8,128)} %bitcast.258), kind=kCustom, calls=%fused_computation.5 | custom fusion | flops 65536 | bytes 788480 | tf_op jit(solution)/shard_map/scatter-add | solution.py:93
  117.5 14.6 %all_gather.13 = f32[128,128]{1,0:T(8,128)S(1)} all-gather(f32[8,128]{1,0:T(8,128)S(1)} %convolution_bitcast_fusion.6), channel_id=1, replica_groups=mesh['gx'=32,'gy'=16] {'gy'}, dimensions={0}, use_global_device_ids=true | all-gather | bytes 69632 | tf_op jit(solution)/shard_map/all_gather | solution.py:101
  132.4 8.0 %collective-permute-start.9 = (f32[16,8,128]{2,1,0:T(8,128)S(1)}, f32[16,8,128]{2,1,0:T(8,128)S(1)}, u32[]{:S(2)}, u32[]{:S(2)}) collective-permute-start(f32[16,8,128]{2,1,0:T(8,128)S(1)} %select_bitcast_fusion.2), channel_id=1, source_target_pairs={{0,256},{16,272},{32,288},{48,304},{64,320},{80,336},{96,352},{112... | collective-permute-start | bytes 196616 | tf_op jit(solution)/shard_map/ppermute | solution.py:34
  142.9 3.1 collective-permute-start.10
  147.6 6.3 %collective-permute-start.11 = (f32[4,8,128]{2,1,0:T(8,128)S(1)}, f32[4,8,128]{2,1,0:T(8,128)S(1)}, u32[]{:S(2)}, u32[]{:S(2)}) collective-permute-start(f32[4,8,128]{2,1,0:T(8,128)S(1)} %slice_select_fusion.6), channel_id=1, source_target_pairs={{0,64},{16,80},{32,96},{48,112},{64,0},{80,16},{96,32},{112,48},{1... | collective-permute-start | bytes 49160 | tf_op jit(solution)/shard_map/ppermute | solution.py:34
  157.9 3.4 collective-permute-done.12
  166.1 7.2 %collective-permute-start.14 = (f32[2,128]{1,0:T(2,128)S(1)}, f32[2,128]{1,0:T(2,128)S(1)}, u32[]{:S(2)}, u32[]{:S(2)}) collective-permute-start(f32[2,128]{1,0:T(2,128)S(1)} %pad_maximum_fusion), channel_id=1, source_target_pairs={{0,1},{1,0},{2,3},{3,2},{4,5},{5,4},{6,7},{7,6},{8,9},{9,8},{10,11... | collective-permute-start | bytes 3080 | tf_op jit(solution)/shard_map/ppermute | solution.py:20
  178.4 3.1 collective-permute-start.16
  183.6 5.2 %collective-permute-start.17 = (f32[2,128]{1,0:T(2,128)S(1)}, f32[2,128]{1,0:T(2,128)S(1)}, u32[]{:S(2)}, u32[]{:S(2)}) collective-permute-start(f32[2,128]{1,0:T(2,128)S(1)} %add.287), channel_id=1, source_target_pairs={{0,8},{1,9},{2,10},{3,11},{4,12},{5,13},{6,14},{7,15},{8,0},{9,1},... | collective-permute-start | bytes 3080 | tf_op jit(solution)/shard_map/ppermute | solution.py:20
  188.8 3.0 collective-permute-done.17
  196.1 2.8 collective-permute-start.19
  198.9 2.4 collective-permute-done.19
  201.3 6.6 %collective-permute-start.20 = (f32[2,128]{1,0:T(2,128)S(1)}, f32[2,128]{1,0:T(2,128)S(1)}, u32[]{:S(2)}, u32[]{:S(2)}) collective-permute-start(f32[2,128]{1,0:T(2,128)S(1)} %add.290), channel_id=1, source_target_pairs={{0,64},{16,80},{32,96},{48,112},{64,0},{80,16},{96,32},{112,48},{1... | collective-permute-start | bytes 3080 | tf_op jit(solution)/shard_map/ppermute | solution.py:20
  209.5 3.4 collective-permute-start.21
  213.9 4.8 collective-permute-start.22
  226.8 11.3 %collective-permute-start.25 = (bf16[128,128]{1,0:T(8,128)(2,1)S(1)}, bf16[128,128]{1,0:T(8,128)(2,1)S(1)}, u32[]{:S(2)}, u32[]{:S(2)}) collective-permute-start(bf16[128,128]{1,0:T(8,128)(2,1)S(1)} %get-tuple-element.21), channel_id=1, source_target_pairs={{0,1},{1,2},{2,3},{3,4},{4,5},{5,6},{6,7},{7,8},{8,9},{9,10},{10,1... | collective-permute-start | bytes 98312 | tf_op jit(solution)/shard_map/ppermute | solution.py:12
  244.2 5.2 %scatter_fusion.1 = f32[896,128]{1,0:T(8,128)} fusion(f32[896,128]{1,0:T(8,128)} %fusion.40, s32[512]{0:T(512)S(1)} %bitcast.262, f32[512,128]{1,0:T(8,128)} %bitcast.259), kind=kCustom, calls=%fused_computation.6 | custom fusion | flops 65536 | bytes 788480 | tf_op jit(solution)/shard_map/scatter-add | solution.py:93
  250.6 15.7 %all_gather.14 = f32[128,128]{1,0:T(8,128)S(1)} all-gather(f32[8,128]{1,0:T(8,128)S(1)} %convolution_bitcast_fusion.5), channel_id=1, replica_groups=mesh['gx'=32,'gy'=16] {'gy'}, dimensions={0}, use_global_device_ids=true | all-gather | bytes 69632 | tf_op jit(solution)/shard_map/all_gather | solution.py:101
  266.6 9.7 %collective-permute-start.27 = (f32[16,8,128]{2,1,0:T(8,128)S(1)}, f32[16,8,128]{2,1,0:T(8,128)S(1)}, u32[]{:S(2)}, u32[]{:S(2)}) collective-permute-start(f32[16,8,128]{2,1,0:T(8,128)S(1)} %select_bitcast_fusion.1), channel_id=1, source_target_pairs={{0,256},{16,272},{32,288},{48,304},{64,320},{80,336},{96,352},{112... | collective-permute-start | bytes 196616 | tf_op jit(solution)/shard_map/ppermute | solution.py:34
  278.7 3.1 collective-permute-start.28
  283.4 5.4 %collective-permute-start.29 = (f32[4,8,128]{2,1,0:T(8,128)S(1)}, f32[4,8,128]{2,1,0:T(8,128)S(1)}, u32[]{:S(2)}, u32[]{:S(2)}) collective-permute-start(f32[4,8,128]{2,1,0:T(8,128)S(1)} %slice_select_fusion.5), channel_id=1, source_target_pairs={{0,64},{16,80},{32,96},{48,112},{64,0},{80,16},{96,32},{112,48},{1... | collective-permute-start | bytes 49160 | tf_op jit(solution)/shard_map/ppermute | solution.py:34
  288.8 3.0 collective-permute-done.29
  293.7 3.4 collective-permute-done.30
  301.9 7.3 %collective-permute-start.32 = (f32[2,128]{1,0:T(2,128)S(1)}, f32[2,128]{1,0:T(2,128)S(1)}, u32[]{:S(2)}, u32[]{:S(2)}) collective-permute-start(f32[2,128]{1,0:T(2,128)S(1)} %pad_maximum_fusion.1), channel_id=1, source_target_pairs={{0,1},{1,0},{2,3},{3,2},{4,5},{5,4},{6,7},{7,6},{8,9},{9,8},{10,11... | collective-permute-start | bytes 3080 | tf_op jit(solution)/shard_map/ppermute | solution.py:20
  314.3 2.7 collective-permute-start.34
  317.0 2.5 collective-permute-done.34
  319.5 5.3 %collective-permute-start.35 = (f32[2,128]{1,0:T(2,128)S(1)}, f32[2,128]{1,0:T(2,128)S(1)}, u32[]{:S(2)}, u32[]{:S(2)}) collective-permute-start(f32[2,128]{1,0:T(2,128)S(1)} %add.304), channel_id=1, source_target_pairs={{0,8},{1,9},{2,10},{3,11},{4,12},{5,13},{6,14},{7,15},{8,0},{9,1},... | collective-permute-start | bytes 3080 | tf_op jit(solution)/shard_map/ppermute | solution.py:20
  324.8 2.9 collective-permute-done.35
  334.0 3.3 collective-permute-done.37
  337.2 5.6 %collective-permute-start.38 = (f32[2,128]{1,0:T(2,128)S(1)}, f32[2,128]{1,0:T(2,128)S(1)}, u32[]{:S(2)}, u32[]{:S(2)}) collective-permute-start(f32[2,128]{1,0:T(2,128)S(1)} %add.307), channel_id=1, source_target_pairs={{0,64},{16,80},{32,96},{48,112},{64,0},{80,16},{96,32},{112,48},{1... | collective-permute-start | bytes 3080 | tf_op jit(solution)/shard_map/ppermute | solution.py:20
  342.8 2.6 collective-permute-done.38
  345.5 3.3 collective-permute-start.39
  349.8 4.8 collective-permute-start.40
  361.7 11.2 %collective-permute-start.43 = (bf16[128,128]{1,0:T(8,128)(2,1)S(1)}, bf16[128,128]{1,0:T(8,128)(2,1)S(1)}, u32[]{:S(2)}, u32[]{:S(2)}) collective-permute-start(bf16[128,128]{1,0:T(8,128)(2,1)S(1)} %get-tuple-element.17), channel_id=1, source_target_pairs={{0,1},{1,2},{2,3},{3,4},{4,5},{5,6},{6,7},{7,8},{8,9},{9,10},{10,1... | collective-permute-start | bytes 98312 | tf_op jit(solution)/shard_map/ppermute | solution.py:12
  378.9 5.2 %scatter_fusion.2 = f32[896,128]{1,0:T(8,128)} fusion(f32[896,128]{1,0:T(8,128)} %fusion.43, s32[512]{0:T(512)S(1)} %bitcast.263, f32[512,128]{1,0:T(8,128)} %bitcast.260), kind=kCustom, calls=%fused_computation.7 | custom fusion | flops 65536 | bytes 788480 | tf_op jit(solution)/shard_map/scatter-add | solution.py:93
  385.3 15.7 %all_gather.15 = f32[128,128]{1,0:T(8,128)S(1)} all-gather(f32[8,128]{1,0:T(8,128)S(1)} %convolution_bitcast_fusion.4), channel_id=1, replica_groups=mesh['gx'=32,'gy'=16] {'gy'}, dimensions={0}, use_global_device_ids=true | all-gather | bytes 69632 | tf_op jit(solution)/shard_map/all_gather | solution.py:101
  401.4 9.7 %collective-permute-start.45 = (f32[16,8,128]{2,1,0:T(8,128)S(1)}, f32[16,8,128]{2,1,0:T(8,128)S(1)}, u32[]{:S(2)}, u32[]{:S(2)}) collective-permute-start(f32[16,8,128]{2,1,0:T(8,128)S(1)} %select_bitcast_fusion), channel_id=1, source_target_pairs={{0,256},{16,272},{32,288},{48,304},{64,320},{80,336},{96,352},{112... | collective-permute-start | bytes 196616 | tf_op jit(solution)/shard_map/ppermute | solution.py:34
  413.5 3.0 collective-permute-start.46
  418.1 4.4 collective-permute-start.47
  422.6 4.0 collective-permute-done.47
  428.5 3.4 collective-permute-done.48
  436.8 7.2 %collective-permute-start.50 = (f32[2,128]{1,0:T(2,128)S(1)}, f32[2,128]{1,0:T(2,128)S(1)}, u32[]{:S(2)}, u32[]{:S(2)}) collective-permute-start(f32[2,128]{1,0:T(2,128)S(1)} %pad_maximum_fusion.2), channel_id=1, source_target_pairs={{0,1},{1,0},{2,3},{3,2},{4,5},{5,4},{6,7},{7,6},{8,9},{9,8},{10,11... | collective-permute-start | bytes 3080 | tf_op jit(solution)/shard_map/ppermute | solution.py:20
  444.8 2.5 collective-permute-start.51
  449.1 3.5 collective-permute-start.52
  454.3 5.6 %collective-permute-start.53 = (f32[2,128]{1,0:T(2,128)S(1)}, f32[2,128]{1,0:T(2,128)S(1)}, u32[]{:S(2)}, u32[]{:S(2)}) collective-permute-start(f32[2,128]{1,0:T(2,128)S(1)} %add.322), channel_id=1, source_target_pairs={{0,8},{1,9},{2,10},{3,11},{4,12},{5,13},{6,14},{7,15},{8,0},{9,1},... | collective-permute-start | bytes 3080 | tf_op jit(solution)/shard_map/ppermute | solution.py:20
  459.9 2.6 collective-permute-done.53
  468.8 3.3 collective-permute-done.55
  472.0 4.7 collective-permute-start.56
  476.8 3.5 collective-permute-done.56
  480.3 3.3 collective-permute-start.57
  484.6 4.9 collective-permute-start.58
  497.6 11.7 %collective-permute-start.61 = (bf16[128,128]{1,0:T(8,128)(2,1)S(1)}, bf16[128,128]{1,0:T(8,128)(2,1)S(1)}, u32[]{:S(2)}, u32[]{:S(2)}) collective-permute-start(bf16[128,128]{1,0:T(8,128)(2,1)S(1)} %get-tuple-element.13), channel_id=1, source_target_pairs={{0,1},{1,2},{2,3},{3,4},{4,5},{5,6},{6,7},{7,8},{8,9},{9,10},{10,1... | collective-permute-start | bytes 98312 | tf_op jit(solution)/shard_map/ppermute | solution.py:12
  514.7 3.5 scatter_fusion.3
  (237 shorter events, 142.3 us)
Async XLA Ops:
  23.7 34.8 %all-to-all-start = ((f32[8,32,128]{2,0,1:T(8,128)}), f32[8,32,128]{2,0,1:T(8,128)S(1)}, u32[]{:S(2)}, u32[]{:S(2)}) async-start(f32[8,32,128]{2,0,1:T(8,128)} %broadcast_select_fusion), calls=%async_computation | async-start | bytes 262144 | tf_op jit(solution)/shard_map/all_to_all | solution.py:72
  58.9 7.1 %collective-permute-start = (f32[16,8,128]{2,1,0:T(8,128)S(1)}, f32[16,8,128]{2,1,0:T(8,128)S(1)}, u32[]{:S(2)}, u32[]{:S(2)}) collective-permute-start(f32[16,8,128]{2,1,0:T(8,128)S(1)} %select_bitcast_fusion.3), channel_id=1, source_target_pairs={{0,256},{16,272},{32,288},{48,304},{64,320},{80,336},{96,352},{112... | collective-permute-start | bytes 196616 | tf_op jit(solution)/shard_map/ppermute | solution.py:34
  66.0 4.7 collective-permute-start.1
  70.7 8.5 %collective-permute-start.2 = (f32[4,8,128]{2,1,0:T(8,128)S(1)}, f32[4,8,128]{2,1,0:T(8,128)S(1)}, u32[]{:S(2)}, u32[]{:S(2)}) collective-permute-start(f32[4,8,128]{2,1,0:T(8,128)S(1)} %slice_select_fusion.7), channel_id=1, source_target_pairs={{0,64},{16,80},{32,96},{48,112},{64,0},{80,16},{96,32},{112,48},{1... | collective-permute-start | bytes 49160 | tf_op jit(solution)/shard_map/ppermute | solution.py:34
  79.2 5.3 %collective-permute-start.3 = (f32[2,8,128]{2,1,0:T(8,128)S(1)}, f32[2,8,128]{2,1,0:T(8,128)S(1)}, u32[]{:S(2)}, u32[]{:S(2)}) collective-permute-start(f32[2,8,128]{2,1,0:T(8,128)S(1)} %slice_select_fusion.11), channel_id=1, source_target_pairs={{0,32},{16,48},{32,0},{48,16},{64,96},{80,112},{96,64},{112,80},{1... | collective-permute-start | bytes 24584 | tf_op jit(solution)/shard_map/ppermute | solution.py:34
  84.5 4.3 collective-permute-start.4
  93.8 14.9 %collective-permute-start.5 = (bf16[128,128]{1,0:T(8,128)(2,1)S(1)}, bf16[128,128]{1,0:T(8,128)(2,1)S(1)}, u32[]{:S(2)}, u32[]{:S(2)}) collective-permute-start(bf16[128,128]{1,0:T(8,128)(2,1)S(1)} %get-tuple-element.24), channel_id=1, source_target_pairs={{0,16},{16,32},{32,48},{48,64},{64,80},{80,96},{96,112},{112,128},... | collective-permute-start | bytes 98312 | tf_op jit(solution)/shard_map/ppermute | solution.py:12
  97.1 11.6 %collective-permute-start.6 = (bf16[128,128]{1,0:T(8,128)(2,1)S(1)}, bf16[128,128]{1,0:T(8,128)(2,1)S(1)}, u32[]{:S(2)}, u32[]{:S(2)}) collective-permute-start(bf16[128,128]{1,0:T(8,128)(2,1)S(1)} %get-tuple-element.26), channel_id=1, source_target_pairs={{16,0},{32,16},{48,32},{64,48},{80,64},{96,80},{112,96},{128,112},... | collective-permute-start | bytes 98312 | tf_op jit(solution)/shard_map/ppermute | solution.py:12
  98.4 10.3 %collective-permute-start.7 = (bf16[128,128]{1,0:T(8,128)(2,1)S(1)}, bf16[128,128]{1,0:T(8,128)(2,1)S(1)}, u32[]{:S(2)}, u32[]{:S(2)}) collective-permute-start(bf16[128,128]{1,0:T(8,128)(2,1)S(1)} %get-tuple-element.25), channel_id=1, source_target_pairs={{0,1},{1,2},{2,3},{3,4},{4,5},{5,6},{6,7},{7,8},{8,9},{9,10},{10,1... | collective-permute-start | bytes 98312 | tf_op jit(solution)/shard_map/ppermute | solution.py:12
  105.0 5.2 %collective-permute-start.8 = (bf16[128,128]{1,0:T(8,128)(2,1)S(1)}, bf16[128,128]{1,0:T(8,128)(2,1)S(1)}, u32[]{:S(2)}, u32[]{:S(2)}) collective-permute-start(bf16[128,128]{1,0:T(8,128)(2,1)S(1)} %get-tuple-element.27), channel_id=1, source_target_pairs={{1,0},{2,1},{3,2},{4,3},{5,4},{6,5},{7,6},{8,7},{9,8},{10,9},{11,1... | collective-permute-start | bytes 98312 | tf_op jit(solution)/shard_map/ppermute | solution.py:12
  132.4 10.4 %collective-permute-start.9 = (f32[16,8,128]{2,1,0:T(8,128)S(1)}, f32[16,8,128]{2,1,0:T(8,128)S(1)}, u32[]{:S(2)}, u32[]{:S(2)}) collective-permute-start(f32[16,8,128]{2,1,0:T(8,128)S(1)} %select_bitcast_fusion.2), channel_id=1, source_target_pairs={{0,256},{16,272},{32,288},{48,304},{64,320},{80,336},{96,352},{112... | collective-permute-start | bytes 196616 | tf_op jit(solution)/shard_map/ppermute | solution.py:34
  142.9 4.7 collective-permute-start.10
  147.6 8.4 %collective-permute-start.11 = (f32[4,8,128]{2,1,0:T(8,128)S(1)}, f32[4,8,128]{2,1,0:T(8,128)S(1)}, u32[]{:S(2)}, u32[]{:S(2)}) collective-permute-start(f32[4,8,128]{2,1,0:T(8,128)S(1)} %slice_select_fusion.6), channel_id=1, source_target_pairs={{0,64},{16,80},{32,96},{48,112},{64,0},{80,16},{96,32},{112,48},{1... | collective-permute-start | bytes 49160 | tf_op jit(solution)/shard_map/ppermute | solution.py:34
  156.0 5.3 %collective-permute-start.12 = (f32[2,8,128]{2,1,0:T(8,128)S(1)}, f32[2,8,128]{2,1,0:T(8,128)S(1)}, u32[]{:S(2)}, u32[]{:S(2)}) collective-permute-start(f32[2,8,128]{2,1,0:T(8,128)S(1)} %slice_select_fusion.10), channel_id=1, source_target_pairs={{0,32},{16,48},{32,0},{48,16},{64,96},{80,112},{96,64},{112,80},{1... | collective-permute-start | bytes 24584 | tf_op jit(solution)/shard_map/ppermute | solution.py:34
  161.3 4.3 collective-permute-start.13
  166.1 8.0 %collective-permute-start.14 = (f32[2,128]{1,0:T(2,128)S(1)}, f32[2,128]{1,0:T(2,128)S(1)}, u32[]{:S(2)}, u32[]{:S(2)}) collective-permute-start(f32[2,128]{1,0:T(2,128)S(1)} %pad_maximum_fusion), channel_id=1, source_target_pairs={{0,1},{1,0},{2,3},{3,2},{4,5},{5,4},{6,7},{7,6},{8,9},{9,8},{10,11... | collective-permute-start | bytes 3080 | tf_op jit(solution)/shard_map/ppermute | solution.py:20
  174.0 4.3 collective-permute-start.15
  178.4 5.2 %collective-permute-start.16 = (f32[2,128]{1,0:T(2,128)S(1)}, f32[2,128]{1,0:T(2,128)S(1)}, u32[]{:S(2)}, u32[]{:S(2)}) collective-permute-start(f32[2,128]{1,0:T(2,128)S(1)} %fusion.176), channel_id=1, source_target_pairs={{0,4},{1,5},{2,6},{3,7},{4,0},{5,1},{6,2},{7,3},{8,12},{9,13},{10,... | collective-permute-start | bytes 3080 | tf_op jit(solution)/shard_map/ppermute | solution.py:20
  183.6 8.2 %collective-permute-start.17 = (f32[2,128]{1,0:T(2,128)S(1)}, f32[2,128]{1,0:T(2,128)S(1)}, u32[]{:S(2)}, u32[]{:S(2)}) collective-permute-start(f32[2,128]{1,0:T(2,128)S(1)} %add.287), channel_id=1, source_target_pairs={{0,8},{1,9},{2,10},{3,11},{4,12},{5,13},{6,14},{7,15},{8,0},{9,1},... | collective-permute-start | bytes 3080 | tf_op jit(solution)/shard_map/ppermute | solution.py:20
  191.8 4.3 collective-permute-start.18
  196.1 5.2 %collective-permute-start.19 = (f32[2,128]{1,0:T(2,128)S(1)}, f32[2,128]{1,0:T(2,128)S(1)}, u32[]{:S(2)}, u32[]{:S(2)}) collective-permute-start(f32[2,128]{1,0:T(2,128)S(1)} %add.289), channel_id=1, source_target_pairs={{0,32},{16,48},{32,0},{48,16},{64,96},{80,112},{96,64},{112,80},{1... | collective-permute-start | bytes 3080 | tf_op jit(solution)/shard_map/ppermute | solution.py:20
  201.3 8.2 %collective-permute-start.20 = (f32[2,128]{1,0:T(2,128)S(1)}, f32[2,128]{1,0:T(2,128)S(1)}, u32[]{:S(2)}, u32[]{:S(2)}) collective-permute-start(f32[2,128]{1,0:T(2,128)S(1)} %add.290), channel_id=1, source_target_pairs={{0,64},{16,80},{32,96},{48,112},{64,0},{80,16},{96,32},{112,48},{1... | collective-permute-start | bytes 3080 | tf_op jit(solution)/shard_map/ppermute | solution.py:20
  209.5 4.3 collective-permute-start.21
  213.9 5.8 %collective-permute-start.22 = (f32[2,128]{1,0:T(2,128)S(1)}, f32[2,128]{1,0:T(2,128)S(1)}, u32[]{:S(2)}, u32[]{:S(2)}) collective-permute-start(f32[2,128]{1,0:T(2,128)S(1)} %add.292), channel_id=1, source_target_pairs={{0,256},{16,272},{32,288},{48,304},{64,320},{80,336},{96,352},{112... | collective-permute-start | bytes 3080 | tf_op jit(solution)/shard_map/ppermute | solution.py:20
  223.3 18.1 %collective-permute-start.23 = (bf16[128,128]{1,0:T(8,128)(2,1)S(1)}, bf16[128,128]{1,0:T(8,128)(2,1)S(1)}, u32[]{:S(2)}, u32[]{:S(2)}) collective-permute-start(bf16[128,128]{1,0:T(8,128)(2,1)S(1)} %get-tuple-element.20), channel_id=1, source_target_pairs={{0,16},{16,32},{32,48},{48,64},{64,80},{80,96},{96,112},{112,128},... | collective-permute-start | bytes 98312 | tf_op jit(solution)/shard_map/ppermute | solution.py:12
  225.5 15.9 %collective-permute-start.24 = (bf16[128,128]{1,0:T(8,128)(2,1)S(1)}, bf16[128,128]{1,0:T(8,128)(2,1)S(1)}, u32[]{:S(2)}, u32[]{:S(2)}) collective-permute-start(bf16[128,128]{1,0:T(8,128)(2,1)S(1)} %get-tuple-element.22), channel_id=1, source_target_pairs={{16,0},{32,16},{48,32},{64,48},{80,64},{96,80},{112,96},{128,112},... | collective-permute-start | bytes 98312 | tf_op jit(solution)/shard_map/ppermute | solution.py:12
  226.8 14.6 %collective-permute-start.25 = (bf16[128,128]{1,0:T(8,128)(2,1)S(1)}, bf16[128,128]{1,0:T(8,128)(2,1)S(1)}, u32[]{:S(2)}, u32[]{:S(2)}) collective-permute-start(bf16[128,128]{1,0:T(8,128)(2,1)S(1)} %get-tuple-element.21), channel_id=1, source_target_pairs={{0,1},{1,2},{2,3},{3,4},{4,5},{5,6},{6,7},{7,8},{8,9},{9,10},{10,1... | collective-permute-start | bytes 98312 | tf_op jit(solution)/shard_map/ppermute | solution.py:12
  238.1 5.2 %collective-permute-start.26 = (bf16[128,128]{1,0:T(8,128)(2,1)S(1)}, bf16[128,128]{1,0:T(8,128)(2,1)S(1)}, u32[]{:S(2)}, u32[]{:S(2)}) collective-permute-start(bf16[128,128]{1,0:T(8,128)(2,1)S(1)} %get-tuple-element.23), channel_id=1, source_target_pairs={{1,0},{2,1},{3,2},{4,3},{5,4},{6,5},{7,6},{8,7},{9,8},{10,9},{11,1... | collective-permute-start | bytes 98312 | tf_op jit(solution)/shard_map/ppermute | solution.py:12
  266.6 12.0 %collective-permute-start.27 = (f32[16,8,128]{2,1,0:T(8,128)S(1)}, f32[16,8,128]{2,1,0:T(8,128)S(1)}, u32[]{:S(2)}, u32[]{:S(2)}) collective-permute-start(f32[16,8,128]{2,1,0:T(8,128)S(1)} %select_bitcast_fusion.1), channel_id=1, source_target_pairs={{0,256},{16,272},{32,288},{48,304},{64,320},{80,336},{96,352},{112... | collective-permute-start | bytes 196616 | tf_op jit(solution)/shard_map/ppermute | solution.py:34
  278.7 4.7 collective-permute-start.28
  283.4 8.4 %collective-permute-start.29 = (f32[4,8,128]{2,1,0:T(8,128)S(1)}, f32[4,8,128]{2,1,0:T(8,128)S(1)}, u32[]{:S(2)}, u32[]{:S(2)}) collective-permute-start(f32[4,8,128]{2,1,0:T(8,128)S(1)} %slice_select_fusion.5), channel_id=1, source_target_pairs={{0,64},{16,80},{32,96},{48,112},{64,0},{80,16},{96,32},{112,48},{1... | collective-permute-start | bytes 49160 | tf_op jit(solution)/shard_map/ppermute | solution.py:34
  291.8 5.3 %collective-permute-start.30 = (f32[2,8,128]{2,1,0:T(8,128)S(1)}, f32[2,8,128]{2,1,0:T(8,128)S(1)}, u32[]{:S(2)}, u32[]{:S(2)}) collective-permute-start(f32[2,8,128]{2,1,0:T(8,128)S(1)} %slice_select_fusion.9), channel_id=1, source_target_pairs={{0,32},{16,48},{32,0},{48,16},{64,96},{80,112},{96,64},{112,80},{1... | collective-permute-start | bytes 24584 | tf_op jit(solution)/shard_map/ppermute | solution.py:34
  297.1 4.3 collective-permute-start.31
  301.9 8.1 %collective-permute-start.32 = (f32[2,128]{1,0:T(2,128)S(1)}, f32[2,128]{1,0:T(2,128)S(1)}, u32[]{:S(2)}, u32[]{:S(2)}) collective-permute-start(f32[2,128]{1,0:T(2,128)S(1)} %pad_maximum_fusion.1), channel_id=1, source_target_pairs={{0,1},{1,0},{2,3},{3,2},{4,5},{5,4},{6,7},{7,6},{8,9},{9,8},{10,11... | collective-permute-start | bytes 3080 | tf_op jit(solution)/shard_map/ppermute | solution.py:20
  310.0 4.3 collective-permute-start.33
  314.3 5.2 %collective-permute-start.34 = (f32[2,128]{1,0:T(2,128)S(1)}, f32[2,128]{1,0:T(2,128)S(1)}, u32[]{:S(2)}, u32[]{:S(2)}) collective-permute-start(f32[2,128]{1,0:T(2,128)S(1)} %fusion.175), channel_id=1, source_target_pairs={{0,4},{1,5},{2,6},{3,7},{4,0},{5,1},{6,2},{7,3},{8,12},{9,13},{10,... | collective-permute-start | bytes 3080 | tf_op jit(solution)/shard_map/ppermute | solution.py:20
  319.5 8.2 %collective-permute-start.35 = (f32[2,128]{1,0:T(2,128)S(1)}, f32[2,128]{1,0:T(2,128)S(1)}, u32[]{:S(2)}, u32[]{:S(2)}) collective-permute-start(f32[2,128]{1,0:T(2,128)S(1)} %add.304), channel_id=1, source_target_pairs={{0,8},{1,9},{2,10},{3,11},{4,12},{5,13},{6,14},{7,15},{8,0},{9,1},... | collective-permute-start | bytes 3080 | tf_op jit(solution)/shard_map/ppermute | solution.py:20
  327.7 4.3 collective-permute-start.36
  332.0 5.2 %collective-permute-start.37 = (f32[2,128]{1,0:T(2,128)S(1)}, f32[2,128]{1,0:T(2,128)S(1)}, u32[]{:S(2)}, u32[]{:S(2)}) collective-permute-start(f32[2,128]{1,0:T(2,128)S(1)} %add.306), channel_id=1, source_target_pairs={{0,32},{16,48},{32,0},{48,16},{64,96},{80,112},{96,64},{112,80},{1... | collective-permute-start | bytes 3080 | tf_op jit(solution)/shard_map/ppermute | solution.py:20
  337.2 8.2 %collective-permute-start.38 = (f32[2,128]{1,0:T(2,128)S(1)}, f32[2,128]{1,0:T(2,128)S(1)}, u32[]{:S(2)}, u32[]{:S(2)}) collective-permute-start(f32[2,128]{1,0:T(2,128)S(1)} %add.307), channel_id=1, source_target_pairs={{0,64},{16,80},{32,96},{48,112},{64,0},{80,16},{96,32},{112,48},{1... | collective-permute-start | bytes 3080 | tf_op jit(solution)/shard_map/ppermute | solution.py:20
  345.5 4.3 collective-permute-start.39
  349.8 5.8 %collective-permute-start.40 = (f32[2,128]{1,0:T(2,128)S(1)}, f32[2,128]{1,0:T(2,128)S(1)}, u32[]{:S(2)}, u32[]{:S(2)}) collective-permute-start(f32[2,128]{1,0:T(2,128)S(1)} %add.309), channel_id=1, source_target_pairs={{0,256},{16,272},{32,288},{48,304},{64,320},{80,336},{96,352},{112... | collective-permute-start | bytes 3080 | tf_op jit(solution)/shard_map/ppermute | solution.py:20
  358.4 17.7 %collective-permute-start.41 = (bf16[128,128]{1,0:T(8,128)(2,1)S(1)}, bf16[128,128]{1,0:T(8,128)(2,1)S(1)}, u32[]{:S(2)}, u32[]{:S(2)}) collective-permute-start(bf16[128,128]{1,0:T(8,128)(2,1)S(1)} %get-tuple-element.16), channel_id=1, source_target_pairs={{0,16},{16,32},{32,48},{48,64},{64,80},{80,96},{96,112},{112,128},... | collective-permute-start | bytes 98312 | tf_op jit(solution)/shard_map/ppermute | solution.py:12
  360.4 15.8 %collective-permute-start.42 = (bf16[128,128]{1,0:T(8,128)(2,1)S(1)}, bf16[128,128]{1,0:T(8,128)(2,1)S(1)}, u32[]{:S(2)}, u32[]{:S(2)}) collective-permute-start(bf16[128,128]{1,0:T(8,128)(2,1)S(1)} %get-tuple-element.18), channel_id=1, source_target_pairs={{16,0},{32,16},{48,32},{64,48},{80,64},{96,80},{112,96},{128,112},... | collective-permute-start | bytes 98312 | tf_op jit(solution)/shard_map/ppermute | solution.py:12
  361.7 14.5 %collective-permute-start.43 = (bf16[128,128]{1,0:T(8,128)(2,1)S(1)}, bf16[128,128]{1,0:T(8,128)(2,1)S(1)}, u32[]{:S(2)}, u32[]{:S(2)}) collective-permute-start(bf16[128,128]{1,0:T(8,128)(2,1)S(1)} %get-tuple-element.17), channel_id=1, source_target_pairs={{0,1},{1,2},{2,3},{3,4},{4,5},{5,6},{6,7},{7,8},{8,9},{9,10},{10,1... | collective-permute-start | bytes 98312 | tf_op jit(solution)/shard_map/ppermute | solution.py:12
  372.8 5.2 %collective-permute-start.44 = (bf16[128,128]{1,0:T(8,128)(2,1)S(1)}, bf16[128,128]{1,0:T(8,128)(2,1)S(1)}, u32[]{:S(2)}, u32[]{:S(2)}) collective-permute-start(bf16[128,128]{1,0:T(8,128)(2,1)S(1)} %get-tuple-element.19), channel_id=1, source_target_pairs={{1,0},{2,1},{3,2},{4,3},{5,4},{6,5},{7,6},{8,7},{9,8},{10,9},{11,1... | collective-permute-start | bytes 98312 | tf_op jit(solution)/shard_map/ppermute | solution.py:12
  401.4 12.1 %collective-permute-start.45 = (f32[16,8,128]{2,1,0:T(8,128)S(1)}, f32[16,8,128]{2,1,0:T(8,128)S(1)}, u32[]{:S(2)}, u32[]{:S(2)}) collective-permute-start(f32[16,8,128]{2,1,0:T(8,128)S(1)} %select_bitcast_fusion), channel_id=1, source_target_pairs={{0,256},{16,272},{32,288},{48,304},{64,320},{80,336},{96,352},{112... | collective-permute-start | bytes 196616 | tf_op jit(solution)/shard_map/ppermute | solution.py:34
  413.5 4.7 collective-permute-start.46
  418.1 8.4 %collective-permute-start.47 = (f32[4,8,128]{2,1,0:T(8,128)S(1)}, f32[4,8,128]{2,1,0:T(8,128)S(1)}, u32[]{:S(2)}, u32[]{:S(2)}) collective-permute-start(f32[4,8,128]{2,1,0:T(8,128)S(1)} %slice_select_fusion.4), channel_id=1, source_target_pairs={{0,64},{16,80},{32,96},{48,112},{64,0},{80,16},{96,32},{112,48},{1... | collective-permute-start | bytes 49160 | tf_op jit(solution)/shard_map/ppermute | solution.py:34
  426.5 5.3 %collective-permute-start.48 = (f32[2,8,128]{2,1,0:T(8,128)S(1)}, f32[2,8,128]{2,1,0:T(8,128)S(1)}, u32[]{:S(2)}, u32[]{:S(2)}) collective-permute-start(f32[2,8,128]{2,1,0:T(8,128)S(1)} %slice_select_fusion.8), channel_id=1, source_target_pairs={{0,32},{16,48},{32,0},{48,16},{64,96},{80,112},{96,64},{112,80},{1... | collective-permute-start | bytes 24584 | tf_op jit(solution)/shard_map/ppermute | solution.py:34
  431.9 4.5 collective-permute-start.49
  436.8 8.0 %collective-permute-start.50 = (f32[2,128]{1,0:T(2,128)S(1)}, f32[2,128]{1,0:T(2,128)S(1)}, u32[]{:S(2)}, u32[]{:S(2)}) collective-permute-start(f32[2,128]{1,0:T(2,128)S(1)} %pad_maximum_fusion.2), channel_id=1, source_target_pairs={{0,1},{1,0},{2,3},{3,2},{4,5},{5,4},{6,7},{7,6},{8,9},{9,8},{10,11... | collective-permute-start | bytes 3080 | tf_op jit(solution)/shard_map/ppermute | solution.py:20
  444.8 4.3 collective-permute-start.51
  449.1 5.2 %collective-permute-start.52 = (f32[2,128]{1,0:T(2,128)S(1)}, f32[2,128]{1,0:T(2,128)S(1)}, u32[]{:S(2)}, u32[]{:S(2)}) collective-permute-start(f32[2,128]{1,0:T(2,128)S(1)} %fusion.174), channel_id=1, source_target_pairs={{0,4},{1,5},{2,6},{3,7},{4,0},{5,1},{6,2},{7,3},{8,12},{9,13},{10,... | collective-permute-start | bytes 3080 | tf_op jit(solution)/shard_map/ppermute | solution.py:20
  454.3 8.2 %collective-permute-start.53 = (f32[2,128]{1,0:T(2,128)S(1)}, f32[2,128]{1,0:T(2,128)S(1)}, u32[]{:S(2)}, u32[]{:S(2)}) collective-permute-start(f32[2,128]{1,0:T(2,128)S(1)} %add.322), channel_id=1, source_target_pairs={{0,8},{1,9},{2,10},{3,11},{4,12},{5,13},{6,14},{7,15},{8,0},{9,1},... | collective-permute-start | bytes 3080 | tf_op jit(solution)/shard_map/ppermute | solution.py:20
  462.5 4.3 collective-permute-start.54
  466.8 5.2 %collective-permute-start.55 = (f32[2,128]{1,0:T(2,128)S(1)}, f32[2,128]{1,0:T(2,128)S(1)}, u32[]{:S(2)}, u32[]{:S(2)}) collective-permute-start(f32[2,128]{1,0:T(2,128)S(1)} %add.324), channel_id=1, source_target_pairs={{0,32},{16,48},{32,0},{48,16},{64,96},{80,112},{96,64},{112,80},{1... | collective-permute-start | bytes 3080 | tf_op jit(solution)/shard_map/ppermute | solution.py:20
  472.0 8.2 %collective-permute-start.56 = (f32[2,128]{1,0:T(2,128)S(1)}, f32[2,128]{1,0:T(2,128)S(1)}, u32[]{:S(2)}, u32[]{:S(2)}) collective-permute-start(f32[2,128]{1,0:T(2,128)S(1)} %add.325), channel_id=1, source_target_pairs={{0,64},{16,80},{32,96},{48,112},{64,0},{80,16},{96,32},{112,48},{1... | collective-permute-start | bytes 3080 | tf_op jit(solution)/shard_map/ppermute | solution.py:20
  480.3 4.3 collective-permute-start.57
  484.6 5.8 %collective-permute-start.58 = (f32[2,128]{1,0:T(2,128)S(1)}, f32[2,128]{1,0:T(2,128)S(1)}, u32[]{:S(2)}, u32[]{:S(2)}) collective-permute-start(f32[2,128]{1,0:T(2,128)S(1)} %add.327), channel_id=1, source_target_pairs={{0,256},{16,272},{32,288},{48,304},{64,320},{80,336},{96,352},{112... | collective-permute-start | bytes 3080 | tf_op jit(solution)/shard_map/ppermute | solution.py:20
  494.1 18.5 %collective-permute-start.59 = (bf16[128,128]{1,0:T(8,128)(2,1)S(1)}, bf16[128,128]{1,0:T(8,128)(2,1)S(1)}, u32[]{:S(2)}, u32[]{:S(2)}) collective-permute-start(bf16[128,128]{1,0:T(8,128)(2,1)S(1)} %get-tuple-element.12), channel_id=1, source_target_pairs={{0,16},{16,32},{32,48},{48,64},{64,80},{80,96},{96,112},{112,128},... | collective-permute-start | bytes 98312 | tf_op jit(solution)/shard_map/ppermute | solution.py:12
  496.3 16.3 %collective-permute-start.60 = (bf16[128,128]{1,0:T(8,128)(2,1)S(1)}, bf16[128,128]{1,0:T(8,128)(2,1)S(1)}, u32[]{:S(2)}, u32[]{:S(2)}) collective-permute-start(bf16[128,128]{1,0:T(8,128)(2,1)S(1)} %get-tuple-element.14), channel_id=1, source_target_pairs={{16,0},{32,16},{48,32},{64,48},{80,64},{96,80},{112,96},{128,112},... | collective-permute-start | bytes 98312 | tf_op jit(solution)/shard_map/ppermute | solution.py:12
  497.6 15.0 %collective-permute-start.61 = (bf16[128,128]{1,0:T(8,128)(2,1)S(1)}, bf16[128,128]{1,0:T(8,128)(2,1)S(1)}, u32[]{:S(2)}, u32[]{:S(2)}) collective-permute-start(bf16[128,128]{1,0:T(8,128)(2,1)S(1)} %get-tuple-element.13), channel_id=1, source_target_pairs={{0,1},{1,2},{2,3},{3,4},{4,5},{5,6},{6,7},{7,8},{8,9},{9,10},{10,1... | collective-permute-start | bytes 98312 | tf_op jit(solution)/shard_map/ppermute | solution.py:12
  509.2 5.2 %collective-permute-start.62 = (bf16[128,128]{1,0:T(8,128)(2,1)S(1)}, bf16[128,128]{1,0:T(8,128)(2,1)S(1)}, u32[]{:S(2)}, u32[]{:S(2)}) collective-permute-start(bf16[128,128]{1,0:T(8,128)(2,1)S(1)} %get-tuple-element.15), channel_id=1, source_target_pairs={{1,0},{2,1},{3,2},{4,3},{5,4},{6,5},{7,6},{8,7},{9,8},{10,9},{11,1... | collective-permute-start | bytes 98312 | tf_op jit(solution)/shard_map/ppermute | solution.py:12
  (23 other events, 635.1 us)

commit v3 on v2

--- a/solution.py
+++ b/solution.py
@@ -12,13 +12,15 @@
     return lax.ppermute(value, axis, [(source, source + steps) for source in range(leading, last)])
 
 
-def total_over_mesh(value):
-    for axis in ("gy", "gx"):
-        count = lax.axis_size(axis)
-        step = 1
-        while step < count:
-            value = value + lax.ppermute(value, axis, [(i, i ^ step) for i in range(count)])
-            step *= 2
+def total_over_mesh(value, tie):
+    value = jnp.sum(lax.all_gather(value, "gy", axis=0), axis=0)
+    count = lax.axis_size("gx")
+    step = 1
+    while step < count:
+        if step == count // 2:
+            value = value + 0.0 * tie
+        value = value + lax.ppermute(value, "gx", [(i, i ^ step) for i in range(count)])
+        step *= 2
     return value
 
 
@@ -73,13 +75,8 @@
         coarse_cols.reshape(depth, count_x, count_y * depth), "gx", 1, 0, tiled=True
     ).reshape(count_x * depth, count_y * depth)
 
-    def apply_schur(field):
-        rounded = lax.optimization_barrier(field.astype(jnp.bfloat16))
-        result = schur_scale * rounded.astype(jnp.float32) + jnp.dot(
-            schur_mat, rounded, preferred_element_type=jnp.float32
-        )
-        sent_rows = rounded[rows_lists]
-        received = jnp.stack(
+    def exchange(sent_rows):
+        return jnp.stack(
             [
                 pass_columns(sent_rows[1], 1),
                 pass_columns(sent_rows[0], -1),
@@ -87,10 +84,27 @@
                 pass_lines(sent_rows[2], -1),
             ]
         )
+
+    def finish_schur(rounded, received):
+        result = schur_scale * rounded.astype(jnp.float32) + jnp.dot(
+            schur_mat, rounded, preferred_element_type=jnp.float32
+        )
         coupled = jnp.einsum(
             "dab,dbs->das", coupling_blocks, received, preferred_element_type=jnp.float32
         )
         return result.at[flat_rows].add(-coupled.reshape(-1, coupled.shape[-1]))
+
+    def apply_schur(field):
+        rounded = lax.optimization_barrier(field.astype(jnp.bfloat16))
+        return finish_schur(rounded, exchange(rounded[rows_lists]))
+
+    def send_early(base, step):
+        return exchange(jnp.stack([base[rows_lists], step[rows_lists]], axis=1))
+
+    def apply_schur_late(field, pair, coef):
+        rounded = lax.optimization_barrier(field.astype(jnp.bfloat16))
+        received = (pair[:, 0] + coef * pair[:, 1]).astype(jnp.bfloat16)
+        return finish_schur(rounded, received)
 
     def apply_prec(field):
         rounded = lax.optimization_barrier(field.astype(jnp.bfloat16))
@@ -105,16 +119,23 @@
 
     solution = jnp.zeros(rhs_wide.shape, jnp.float32)
     direction = apply_prec(rhs_wide)
+    image = apply_schur(direction)
     for iteration in range(ITERS):
-        image = apply_schur(direction)
         mapped = apply_prec(image)
+        if iteration + 1 < ITERS:
+            pair = send_early(direction, mapped)
+        else:
+            pair = send_early(solution, direction)
         numer, denom = total_over_mesh(
-            jnp.stack([jnp.sum(mapped * direction, axis=0), jnp.sum(mapped * mapped, axis=0)])
+            jnp.stack([jnp.sum(mapped * direction, axis=0), jnp.sum(mapped * mapped, axis=0)]),
+            jnp.sum(pair[:, 0, 0, 0]),
         )
         alpha = numer / denom
         solution = solution + alpha * direction
-        direction = direction - alpha * mapped
-    residual = rhs_wide - apply_schur(solution)
+        direction = direction + (-alpha) * mapped
+        if iteration + 1 < ITERS:
+            image = apply_schur_late(direction, pair, -alpha)
+    residual = rhs_wide - apply_schur_late(solution, pair, alpha)
     return (solution[None, None], residual[None, None])
 
 

time: 526 us -> 477 us (0.907)
  blocking collectives: 70.1 us -> 132 us
  waiting for transfers between devices: 102 us -> 50.1 us
  starting transfers between devices: 269 us -> 218 us
  matrix products: 16.6 us -> 10.9 us
    all_gather x0 -> x3, blocking collectives: none -> 50.6 us  [total_over_mesh(): value = jnp.sum(lax.all_gather(value, 'gy', axis=0), axis=0)]
    ppermute x27 -> x15, waiting for transfers between devices: 53.2 us -> 14.1 us  [total_over_mesh(): lax.ppermute(value, 'gx', [(i, i ^ step) for i in range(count)])]
    ppermute x27 -> x15, starting transfers between devices: 107 us -> 77.6 us  [total_over_mesh(): lax.ppermute(value, 'gx', [(i, i ^ step) for i in range(count)])]
    ppermute x16, starting transfers between devices: 63.5 us -> 51.5 us  [from_behind(): lax.ppermute(value, axis, [(source, source + steps) for source in range(l...]
    all_gather x4, blocking collectives: 70.1 us -> 81.4 us  [apply_prec(): line = lax.all_gather(coarse, 'gy', axis=0, tiled=True)]
    ppermute x20, starting transfers between devices: 87.5 us -> 77.9 us  [scatter_rows(): lax.ppermute(send, axis, [(i, i ^ half) for i in range(count)])]
    ppermute x20, waiting for transfers between devices: 41.7 us -> 35.1 us  [scatter_rows(): lax.ppermute(send, axis, [(i, i ^ half) for i in range(count)])]
    ppermute x16, waiting for transfers between devices: 7.31 us -> 0.88 us  [from_behind(): lax.ppermute(value, axis, [(source, source + steps) for source in range(l...]
  transfers between devices with their start and end apart: 64 -> 52, of which waited for: 50 -> 32; matrix products, arithmetic and copies ran while one was open for 2% -> 3% of each run, Pallas kernels for 0% -> 0%
where the time goes in v3:
time: 477 us; the launch traced here: 472 us
  starting transfers between devices  218 us (46%)
  blocking collectives  132 us (28%)
  waiting for transfers between devices  50.1 us (11%)
  local copies, waits for them, and re-layouts  30.6 us (6%)
  other arithmetic  26.5 us (6%)
  matrix products  10.9 us (2%)
    all_gather x4, blocking collectives, apply_prec(): line = lax.all_gather(coarse, 'gy', axis=0, tiled=True)  81.4 us
    ppermute x20, starting transfers between devices, scatter_rows(): lax.ppermute(send, axis, [(i, i ^ half) for i in range(count)])  77.9 us
    ppermute x15, starting transfers between devices, total_over_mesh(): lax.ppermute(value, 'gx', [(i, i ^ step) for i in range(count)])  77.6 us
    ppermute x16, starting transfers between devices, from_behind(): lax.ppermute(value, axis, [(source, source + steps) for source in range(l...  51.5 us
    all_gather x3, blocking collectives, total_over_mesh(): value = jnp.sum(lax.all_gather(value, 'gy', axis=0), axis=0)  50.6 us
    ppermute x20, waiting for transfers between devices, scatter_rows(): lax.ppermute(send, axis, [(i, i ^ half) for i in range(count)])  35.1 us
    gather x2, local copies, waits for them, and re-layouts, shards(): coarse_cols = jnp.take(coarse_inverse, coarse_map, axis=1)  17.9 us
    ppermute x15, waiting for transfers between devices, total_over_mesh(): lax.ppermute(value, 'gx', [(i, i ^ step) for i in range(count)])  14.1 us
  transfers between devices with their start and end apart: 52, of which 32 were waited for; matrix products, arithmetic and copies ran while one was open for 3% of the time, Pallas kernels for 0%

profile of v3, /device:TPU:1, one launch (start us, length us, event | category | flops | bytes accessed | tf_op | source)
XLA Modules:
  0.0 471.5 jit_solution(15103961335445536836)
XLA Ops:
  2.2 2.9 copy.67
  5.1 15.7 %gather_fusion = f32[4096,8]{1,0:T(8,128)} fusion(f32[8,4096]{0,1:T(8,128)} %copy.67, s32[4096]{0:T(1024)S(1)} %fusion.131), kind=kCustom, calls=%fused_computation | custom fusion | bytes 278528 | tf_op jit(solution)/shard_map/jit(_take)/gather | solution.py:73
  20.8 2.2 copy.68
  23.6 10.5 %all-to-all-start = ((f32[8,32,128]{2,0,1:T(8,128)}), f32[8,32,128]{2,0,1:T(8,128)S(1)}, u32[]{:S(2)}, u32[]{:S(2)}) async-start(f32[8,32,128]{2,0,1:T(8,128)} %broadcast_select_fusion), calls=%async_computation | async-start | bytes 262144 | tf_op jit(solution)/shard_map/all_to_all | solution.py:74
  34.4 24.1 %all_gather.30 = f32[128,128]{1,0:T(8,128)S(1)} all-gather(f32[8,128]{1,0:T(8,128)S(1)} %fusion.129), channel_id=1, replica_groups=mesh['gx'=32,'gy'=16] {'gy'}, dimensions={0}, use_global_device_ids=true | all-gather | bytes 69632 | tf_op jit(solution)/shard_map/all_gather | solution.py:115
  58.8 4.9 %collective-permute-start = (f32[16,8,128]{2,1,0:T(8,128)S(1)}, f32[16,8,128]{2,1,0:T(8,128)S(1)}, u32[]{:S(2)}, u32[]{:S(2)}) collective-permute-start(f32[16,8,128]{2,1,0:T(8,128)S(1)} %select_bitcast_fusion.3), channel_id=1, source_target_pairs={{0,256},{16,272},{32,288},{48,304},{64,320},{80,336},{96,352},{112... | collective-permute-start | bytes 196616 | tf_op jit(solution)/shard_map/ppermute | solution.py:36
  63.8 2.1 collective-permute-done
  65.9 3.3 collective-permute-start.1
  70.6 7.2 %collective-permute-start.2 = (f32[4,8,128]{2,1,0:T(8,128)S(1)}, f32[4,8,128]{2,1,0:T(8,128)S(1)}, u32[]{:S(2)}, u32[]{:S(2)}) collective-permute-start(f32[4,8,128]{2,1,0:T(8,128)S(1)} %slice_select_fusion.7), channel_id=1, source_target_pairs={{0,64},{16,80},{32,96},{48,112},{64,0},{80,16},{96,32},{112,48},{1... | collective-permute-start | bytes 49160 | tf_op jit(solution)/shard_map/ppermute | solution.py:36
  79.0 4.2 collective-permute-start.3
  84.3 3.3 collective-permute-start.4
  90.4 3.3 collective-permute-start.5
  95.0 6.7 %collective-permute-start.7 = (bf16[128,128]{1,0:T(8,128)(2,1)S(1)}, bf16[128,128]{1,0:T(8,128)(2,1)S(1)}, u32[]{:S(2)}, u32[]{:S(2)}) collective-permute-start(bf16[128,128]{1,0:T(8,128)(2,1)S(1)} %get-tuple-element.32), channel_id=1, source_target_pairs={{0,1},{1,2},{2,3},{3,4},{4,5},{5,6},{6,7},{7,8},{8,9},{9,10},{10,1... | collective-permute-start | bytes 98312 | tf_op jit(solution)/shard_map/ppermute | solution.py:12
  101.7 2.3 collective-permute-start.8
  104.1 2.0 fusion.37
  107.1 3.5 scatter_fusion
  110.8 15.0 %all_gather.31 = f32[128,128]{1,0:T(8,128)S(1)} all-gather(f32[8,128]{1,0:T(8,128)S(1)} %convolution_bitcast_fusion.6), channel_id=1, replica_groups=mesh['gx'=32,'gy'=16] {'gy'}, dimensions={0}, use_global_device_ids=true | all-gather | bytes 69632 | tf_op jit(solution)/shard_map/all_gather | solution.py:115
  126.1 8.1 %collective-permute-start.9 = (f32[16,8,128]{2,1,0:T(8,128)S(1)}, f32[16,8,128]{2,1,0:T(8,128)S(1)}, u32[]{:S(2)}, u32[]{:S(2)}) collective-permute-start(f32[16,8,128]{2,1,0:T(8,128)S(1)} %select_bitcast_fusion.2), channel_id=1, source_target_pairs={{0,256},{16,272},{32,288},{48,304},{64,320},{80,336},{96,352},{112... | collective-permute-start | bytes 196616 | tf_op jit(solution)/shard_map/ppermute | solution.py:36
  134.2 2.4 collective-permute-done.9
  136.6 3.0 collective-permute-start.10
  141.2 6.1 %collective-permute-start.11 = (f32[4,8,128]{2,1,0:T(8,128)S(1)}, f32[4,8,128]{2,1,0:T(8,128)S(1)}, u32[]{:S(2)}, u32[]{:S(2)}) collective-permute-start(f32[4,8,128]{2,1,0:T(8,128)S(1)} %slice_select_fusion.6), channel_id=1, source_target_pairs={{0,64},{16,80},{32,96},{48,112},{64,0},{80,16},{96,32},{112,48},{1... | collective-permute-start | bytes 49160 | tf_op jit(solution)/shard_map/ppermute | solution.py:36
  147.4 2.3 collective-permute-done.11
  152.6 2.3 collective-permute-done.12
  164.7 7.1 %collective-permute-start.20 = (f32[2,128,128]{2,1,0:T(8,128)}, f32[2,128,128]{2,1,0:T(8,128)S(1)}, u32[]{:S(2)}, u32[]{:S(2)}) collective-permute-start(f32[2,128,128]{2,1,0:T(8,128)} %get-tuple-element.29), channel_id=1, source_target_pairs={{0,1},{1,2},{2,3},{3,4},{4,5},{5,6},{6,7},{7,8},{8,9},{9,10},{10,1... | collective-permute-start | bytes 393224 | tf_op jit(solution)/shard_map/ppermute | solution.py:12
  173.8 17.3 %all-gather.3 = f32[16,2,128]{2,1,0:T(2,128)S(1)} all-gather(f32[1,2,128]{2,1,0:T(2,128)S(1)} %maximum_bitcast_fusion), channel_id=2, replica_groups=mesh['gx'=32,'gy'=16] {'gy'}, dimensions={0}, use_global_device_ids=true | all-gather | bytes 17408 | tf_op jit(solution)/shard_map/all_gather | solution.py:16
  191.2 4.3 collective-permute-start.14
  196.4 5.6 %collective-permute-start.15 = (f32[2,128]{1,0:T(2,128)S(1)}, f32[2,128]{1,0:T(2,128)S(1)}, u32[]{:S(2)}, u32[]{:S(2)}) collective-permute-start(f32[2,128]{1,0:T(2,128)S(1)} %add.285), channel_id=1, source_target_pairs={{0,32},{16,48},{32,0},{48,16},{64,96},{80,112},{96,64},{112,80},{1... | collective-permute-start | bytes 3080 | tf_op jit(solution)/shard_map/ppermute | solution.py:22
  202.9 8.1 %collective-permute-start.16 = (f32[2,128]{1,0:T(2,128)S(1)}, f32[2,128]{1,0:T(2,128)S(1)}, u32[]{:S(2)}, u32[]{:S(2)}) collective-permute-start(f32[2,128]{1,0:T(2,128)S(1)} %add.286), channel_id=1, source_target_pairs={{0,64},{16,80},{32,96},{48,112},{64,0},{80,16},{96,32},{112,48},{1... | collective-permute-start | bytes 3080 | tf_op jit(solution)/shard_map/ppermute | solution.py:22
  212.0 5.0 %collective-permute-start.17 = (f32[2,128]{1,0:T(2,128)S(1)}, f32[2,128]{1,0:T(2,128)S(1)}, u32[]{:S(2)}, u32[]{:S(2)}) collective-permute-start(f32[2,128]{1,0:T(2,128)S(1)} %add.287), channel_id=1, source_target_pairs={{0,128},{16,144},{32,160},{48,176},{64,192},{80,208},{96,224},{112... | collective-permute-start | bytes 3080 | tf_op jit(solution)/shard_map/ppermute | solution.py:22
  218.3 4.6 collective-permute-start.22
  225.1 3.7 scatter_fusion.1
  229.0 20.6 %all_gather.34 = f32[128,128]{1,0:T(8,128)S(1)} all-gather(f32[8,128]{1,0:T(8,128)S(1)} %convolution_bitcast_fusion.5), channel_id=1, replica_groups=mesh['gx'=32,'gy'=16] {'gy'}, dimensions={0}, use_global_device_ids=true | all-gather | bytes 69632 | tf_op jit(solution)/shard_map/all_gather | solution.py:115
  249.9 5.1 %collective-permute-start.23 = (f32[16,8,128]{2,1,0:T(8,128)S(1)}, f32[16,8,128]{2,1,0:T(8,128)S(1)}, u32[]{:S(2)}, u32[]{:S(2)}) collective-permute-start(f32[16,8,128]{2,1,0:T(8,128)S(1)} %select_bitcast_fusion.1), channel_id=1, source_target_pairs={{0,256},{16,272},{32,288},{48,304},{64,320},{80,336},{96,352},{112... | collective-permute-start | bytes 196616 | tf_op jit(solution)/shard_map/ppermute | solution.py:36
  255.0 2.4 collective-permute-done.23
  257.5 3.0 collective-permute-start.24
  262.1 5.3 %collective-permute-start.25 = (f32[4,8,128]{2,1,0:T(8,128)S(1)}, f32[4,8,128]{2,1,0:T(8,128)S(1)}, u32[]{:S(2)}, u32[]{:S(2)}) collective-permute-start(f32[4,8,128]{2,1,0:T(8,128)S(1)} %slice_select_fusion.5), channel_id=1, source_target_pairs={{0,64},{16,80},{32,96},{48,112},{64,0},{80,16},{96,32},{112,48},{1... | collective-permute-start | bytes 49160 | tf_op jit(solution)/shard_map/ppermute | solution.py:36
  267.4 3.2 collective-permute-done.25
  272.5 3.4 collective-permute-done.26
  284.1 3.2 collective-permute-start.32
  288.6 6.9 %collective-permute-start.34 = (f32[2,128,128]{2,1,0:T(8,128)}, f32[2,128,128]{2,1,0:T(8,128)S(1)}, u32[]{:S(2)}, u32[]{:S(2)}) collective-permute-start(f32[2,128,128]{2,1,0:T(8,128)} %get-tuple-element.25), channel_id=1, source_target_pairs={{0,1},{1,2},{2,3},{3,4},{4,5},{5,6},{6,7},{7,8},{8,9},{9,10},{10,1... | collective-permute-start | bytes 393224 | tf_op jit(solution)/shard_map/ppermute | solution.py:12
  297.4 16.1 %all-gather.4 = f32[16,2,128]{2,1,0:T(2,128)S(1)} all-gather(f32[1,2,128]{2,1,0:T(2,128)S(1)} %maximum_bitcast_fusion.1), channel_id=3, replica_groups=mesh['gx'=32,'gy'=16] {'gy'}, dimensions={0}, use_global_device_ids=true | all-gather | bytes 17408 | tf_op jit(solution)/shard_map/all_gather | solution.py:16
  313.5 4.3 collective-permute-start.28
  318.7 4.0 collective-permute-start.29
  323.9 7.9 %collective-permute-start.30 = (f32[2,128]{1,0:T(2,128)S(1)}, f32[2,128]{1,0:T(2,128)S(1)}, u32[]{:S(2)}, u32[]{:S(2)}) collective-permute-start(f32[2,128]{1,0:T(2,128)S(1)} %add.303), channel_id=1, source_target_pairs={{0,64},{16,80},{32,96},{48,112},{64,0},{80,16},{96,32},{112,48},{1... | collective-permute-start | bytes 3080 | tf_op jit(solution)/shard_map/ppermute | solution.py:22
  332.8 5.9 %collective-permute-start.31 = (f32[2,128]{1,0:T(2,128)S(1)}, f32[2,128]{1,0:T(2,128)S(1)}, u32[]{:S(2)}, u32[]{:S(2)}) collective-permute-start(f32[2,128]{1,0:T(2,128)S(1)} %add.304), channel_id=1, source_target_pairs={{0,128},{16,144},{32,160},{48,176},{64,192},{80,208},{96,224},{112... | collective-permute-start | bytes 3080 | tf_op jit(solution)/shard_map/ppermute | solution.py:22
  340.0 4.5 collective-permute-start.36
  347.9 3.5 scatter_fusion.2
  351.6 21.7 %all_gather.37 = f32[128,128]{1,0:T(8,128)S(1)} all-gather(f32[8,128]{1,0:T(8,128)S(1)} %convolution_bitcast_fusion.4), channel_id=1, replica_groups=mesh['gx'=32,'gy'=16] {'gy'}, dimensions={0}, use_global_device_ids=true | all-gather | bytes 69632 | tf_op jit(solution)/shard_map/all_gather | solution.py:115
  373.6 5.2 %collective-permute-start.37 = (f32[16,8,128]{2,1,0:T(8,128)S(1)}, f32[16,8,128]{2,1,0:T(8,128)S(1)}, u32[]{:S(2)}, u32[]{:S(2)}) collective-permute-start(f32[16,8,128]{2,1,0:T(8,128)S(1)} %select_bitcast_fusion), channel_id=1, source_target_pairs={{0,256},{16,272},{32,288},{48,304},{64,320},{80,336},{96,352},{112... | collective-permute-start | bytes 196616 | tf_op jit(solution)/shard_map/ppermute | solution.py:36
  378.7 2.3 collective-permute-done.37
  381.1 3.1 collective-permute-start.38
  385.7 4.5 collective-permute-start.39
  390.2 4.1 collective-permute-done.39
  403.3 3.3 collective-permute-start.46
  407.9 5.8 %collective-permute-start.48 = (f32[2,128,128]{2,1,0:T(8,128)}, f32[2,128,128]{2,1,0:T(8,128)S(1)}, u32[]{:S(2)}, u32[]{:S(2)}) collective-permute-start(f32[2,128,128]{2,1,0:T(8,128)} %get-tuple-element.21), channel_id=1, source_target_pairs={{0,1},{1,2},{2,3},{3,4},{4,5},{5,6},{6,7},{7,8},{8,9},{9,10},{10,1... | collective-permute-start | bytes 393224 | tf_op jit(solution)/shard_map/ppermute | solution.py:12
  413.7 2.0 collective-permute-start.49
  416.2 17.2 %all-gather.5 = f32[16,2,128]{2,1,0:T(2,128)S(1)} all-gather(f32[1,2,128]{2,1,0:T(2,128)S(1)} %maximum_bitcast_fusion.2), channel_id=4, replica_groups=mesh['gx'=32,'gy'=16] {'gy'}, dimensions={0}, use_global_device_ids=true | all-gather | bytes 17408 | tf_op jit(solution)/shard_map/all_gather | solution.py:16
  433.4 4.4 collective-permute-start.42
  438.8 3.3 collective-permute-start.43
  444.0 5.7 %collective-permute-start.44 = (f32[2,128]{1,0:T(2,128)S(1)}, f32[2,128]{1,0:T(2,128)S(1)}, u32[]{:S(2)}, u32[]{:S(2)}) collective-permute-start(f32[2,128]{1,0:T(2,128)S(1)} %add.321), channel_id=1, source_target_pairs={{0,64},{16,80},{32,96},{48,112},{64,0},{80,16},{96,32},{112,48},{1... | collective-permute-start | bytes 3080 | tf_op jit(solution)/shard_map/ppermute | solution.py:22
  449.8 2.5 collective-permute-done.44
  452.2 5.4 %collective-permute-start.45 = (f32[2,128]{1,0:T(2,128)S(1)}, f32[2,128]{1,0:T(2,128)S(1)}, u32[]{:S(2)}, u32[]{:S(2)}) collective-permute-start(f32[2,128]{1,0:T(2,128)S(1)} %add.322), channel_id=1, source_target_pairs={{0,128},{16,144},{32,160},{48,176},{64,192},{80,208},{96,224},{112... | collective-permute-start | bytes 3080 | tf_op jit(solution)/shard_map/ppermute | solution.py:22
  459.6 4.7 collective-permute-start.50
  467.2 3.5 scatter_fusion.3
  (208 shorter events, 76.9 us)
Async XLA Ops:
  0.6 68.5 %copy-start = (bf16[1,1,896,896]{3,2,1,0:T(8,128)(2,1)S(1)}, bf16[1,1,896,896]{3,2,1,0:T(8,128)(2,1)}, u32[]{:S(2)}) copy-start(bf16[1,1,896,896]{3,2,1,0:T(8,128)(2,1)} %param.13) | copy-start | bytes 4816900
  20.8 13.4 %copy-start.8 = (bf16[1,1,896,128]{3,2,1,0:T(8,128)(2,1)S(1)}, bf16[1,1,896,128]{3,2,1,0:T(8,128)(2,1)}, u32[]{:S(2)}) copy-start(bf16[1,1,896,128]{3,2,1,0:T(8,128)(2,1)} %param.10) | copy-start | bytes 688132
  20.8 13.4 %copy-start.15 = (bf16[1,1,8,896]{3,2,1,0:T(8,128)(2,1)S(1)}, bf16[1,1,8,896]{3,2,1,0:T(8,128)(2,1)}, u32[]{:S(2)}) copy-start(bf16[1,1,8,896]{3,2,1,0:T(8,128)(2,1)} %param.17) | copy-start | bytes 43012
  20.8 43.0 %copy-start.17 = (f32[1,1,896]{2,1,0:T(1,128)S(1)}, f32[1,1,896]{2,1,0:T(1,128)}, u32[]{:S(2)}) copy-start(f32[1,1,896]{2,1,0:T(1,128)} %param.14) | copy-start | bytes 10756
  23.6 34.8 %all-to-all-start = ((f32[8,32,128]{2,0,1:T(8,128)}), f32[8,32,128]{2,0,1:T(8,128)S(1)}, u32[]{:S(2)}, u32[]{:S(2)}) async-start(f32[8,32,128]{2,0,1:T(8,128)} %broadcast_select_fusion), calls=%async_computation | async-start | bytes 262144 | tf_op jit(solution)/shard_map/all_to_all | solution.py:74
  58.5 191.1 %copy-start.6 = (f32[8,32,128]{2,0,1:T(8,128)}, f32[8,32,128]{2,0,1:T(8,128)S(1)}, u32[]{:S(2)}) copy-start(f32[8,32,128]{2,0,1:T(8,128)S(1)} %all-to-all-done) | copy-start | bytes 393220
  58.7 19.0 %copy-start.16 = (s32[1,1,4,128]{3,2,1,0:T(4,128)S(1)}, s32[1,1,4,128]{3,2,1,0:T(4,128)}, u32[]{:S(2)}) copy-start(s32[1,1,4,128]{3,2,1,0:T(4,128)} %param.16) | copy-start | bytes 6148
  58.8 28.8 %copy-start.18 = (f32[1,1,896]{2,1,0:T(1,128)S(1)}, f32[1,1,896]{2,1,0:T(1,128)}, u32[]{:S(2)}) copy-start(f32[1,1,896]{2,1,0:T(1,128)} %param.12) | copy-start | bytes 10756
  58.8 7.1 %collective-permute-start = (f32[16,8,128]{2,1,0:T(8,128)S(1)}, f32[16,8,128]{2,1,0:T(8,128)S(1)}, u32[]{:S(2)}, u32[]{:S(2)}) collective-permute-start(f32[16,8,128]{2,1,0:T(8,128)S(1)} %select_bitcast_fusion.3), channel_id=1, source_target_pairs={{0,256},{16,272},{32,288},{48,304},{64,320},{80,336},{96,352},{112... | collective-permute-start | bytes 196616 | tf_op jit(solution)/shard_map/ppermute | solution.py:36
  65.9 4.7 collective-permute-start.1
  70.6 8.4 %collective-permute-start.2 = (f32[4,8,128]{2,1,0:T(8,128)S(1)}, f32[4,8,128]{2,1,0:T(8,128)S(1)}, u32[]{:S(2)}, u32[]{:S(2)}) collective-permute-start(f32[4,8,128]{2,1,0:T(8,128)S(1)} %slice_select_fusion.7), channel_id=1, source_target_pairs={{0,64},{16,80},{32,96},{48,112},{64,0},{80,16},{96,32},{112,48},{1... | collective-permute-start | bytes 49160 | tf_op jit(solution)/shard_map/ppermute | solution.py:36
  79.0 5.3 %collective-permute-start.3 = (f32[2,8,128]{2,1,0:T(8,128)S(1)}, f32[2,8,128]{2,1,0:T(8,128)S(1)}, u32[]{:S(2)}, u32[]{:S(2)}) collective-permute-start(f32[2,8,128]{2,1,0:T(8,128)S(1)} %slice_select_fusion.11), channel_id=1, source_target_pairs={{0,32},{16,48},{32,0},{48,16},{64,96},{80,112},{96,64},{112,80},{1... | collective-permute-start | bytes 24584 | tf_op jit(solution)/shard_map/ppermute | solution.py:36
  84.3 4.3 collective-permute-start.4
  89.0 17.9 %copy-start.10 = (bf16[1,1,4,128,128]{4,3,2,1,0:T(8,128)(2,1)S(1)}, bf16[1,1,4,128,128]{4,3,2,1,0:T(8,128)(2,1)}, u32[]{:S(2)}) copy-start(bf16[1,1,4,128,128]{4,3,2,1,0:T(8,128)(2,1)} %param.15) | copy-start | bytes 393220
  90.4 15.7 %collective-permute-start.5 = (bf16[128,128]{1,0:T(8,128)(2,1)S(1)}, bf16[128,128]{1,0:T(8,128)(2,1)S(1)}, u32[]{:S(2)}, u32[]{:S(2)}) collective-permute-start(bf16[128,128]{1,0:T(8,128)(2,1)S(1)} %get-tuple-element.31), channel_id=1, source_target_pairs={{0,16},{16,32},{32,48},{48,64},{64,80},{80,96},{96,112},{112,128},... | collective-permute-start | bytes 98312 | tf_op jit(solution)/shard_map/ppermute | solution.py:12
  93.7 12.4 %collective-permute-start.6 = (bf16[128,128]{1,0:T(8,128)(2,1)S(1)}, bf16[128,128]{1,0:T(8,128)(2,1)S(1)}, u32[]{:S(2)}, u32[]{:S(2)}) collective-permute-start(bf16[128,128]{1,0:T(8,128)(2,1)S(1)} %get-tuple-element.33), channel_id=1, source_target_pairs={{16,0},{32,16},{48,32},{64,48},{80,64},{96,80},{112,96},{128,112},... | collective-permute-start | bytes 98312 | tf_op jit(solution)/shard_map/ppermute | solution.py:12
  95.0 11.1 %collective-permute-start.7 = (bf16[128,128]{1,0:T(8,128)(2,1)S(1)}, bf16[128,128]{1,0:T(8,128)(2,1)S(1)}, u32[]{:S(2)}, u32[]{:S(2)}) collective-permute-start(bf16[128,128]{1,0:T(8,128)(2,1)S(1)} %get-tuple-element.32), channel_id=1, source_target_pairs={{0,1},{1,2},{2,3},{3,4},{4,5},{5,6},{6,7},{7,8},{8,9},{9,10},{10,1... | collective-permute-start | bytes 98312 | tf_op jit(solution)/shard_map/ppermute | solution.py:12
  101.7 5.2 %collective-permute-start.8 = (bf16[128,128]{1,0:T(8,128)(2,1)S(1)}, bf16[128,128]{1,0:T(8,128)(2,1)S(1)}, u32[]{:S(2)}, u32[]{:S(2)}) collective-permute-start(bf16[128,128]{1,0:T(8,128)(2,1)S(1)} %get-tuple-element.34), channel_id=1, source_target_pairs={{1,0},{2,1},{3,2},{4,3},{5,4},{6,5},{7,6},{8,7},{9,8},{10,9},{11,1... | collective-permute-start | bytes 98312 | tf_op jit(solution)/shard_map/ppermute | solution.py:12
  126.1 10.5 %collective-permute-start.9 = (f32[16,8,128]{2,1,0:T(8,128)S(1)}, f32[16,8,128]{2,1,0:T(8,128)S(1)}, u32[]{:S(2)}, u32[]{:S(2)}) collective-permute-start(f32[16,8,128]{2,1,0:T(8,128)S(1)} %select_bitcast_fusion.2), channel_id=1, source_target_pairs={{0,256},{16,272},{32,288},{48,304},{64,320},{80,336},{96,352},{112... | collective-permute-start | bytes 196616 | tf_op jit(solution)/shard_map/ppermute | solution.py:36
  136.6 4.7 collective-permute-start.10
  141.2 8.4 %collective-permute-start.11 = (f32[4,8,128]{2,1,0:T(8,128)S(1)}, f32[4,8,128]{2,1,0:T(8,128)S(1)}, u32[]{:S(2)}, u32[]{:S(2)}) collective-permute-start(f32[4,8,128]{2,1,0:T(8,128)S(1)} %slice_select_fusion.6), channel_id=1, source_target_pairs={{0,64},{16,80},{32,96},{48,112},{64,0},{80,16},{96,32},{112,48},{1... | collective-permute-start | bytes 49160 | tf_op jit(solution)/shard_map/ppermute | solution.py:36
  149.6 5.3 %collective-permute-start.12 = (f32[2,8,128]{2,1,0:T(8,128)S(1)}, f32[2,8,128]{2,1,0:T(8,128)S(1)}, u32[]{:S(2)}, u32[]{:S(2)}) collective-permute-start(f32[2,8,128]{2,1,0:T(8,128)S(1)} %slice_select_fusion.10), channel_id=1, source_target_pairs={{0,32},{16,48},{32,0},{48,16},{64,96},{80,112},{96,64},{112,80},{1... | collective-permute-start | bytes 24584 | tf_op jit(solution)/shard_map/ppermute | solution.py:36
  155.0 4.3 collective-permute-start.13
  161.5 55.4 %collective-permute-start.18 = (f32[2,128,128]{2,1,0:T(8,128)}, f32[2,128,128]{2,1,0:T(8,128)S(1)}, u32[]{:S(2)}, u32[]{:S(2)}) collective-permute-start(f32[2,128,128]{2,1,0:T(8,128)} %get-tuple-element.26), channel_id=1, source_target_pairs={{0,16},{16,32},{32,48},{48,64},{64,80},{80,96},{96,112},{112,128},... | collective-permute-start | bytes 393224 | tf_op jit(solution)/shard_map/ppermute | solution.py:12
  163.4 53.5 %collective-permute-start.19 = (f32[2,128,128]{2,1,0:T(8,128)}, f32[2,128,128]{2,1,0:T(8,128)S(1)}, u32[]{:S(2)}, u32[]{:S(2)}) collective-permute-start(f32[2,128,128]{2,1,0:T(8,128)} %get-tuple-element.27), channel_id=1, source_target_pairs={{16,0},{32,16},{48,32},{64,48},{80,64},{96,80},{112,96},{128,112},... | collective-permute-start | bytes 393224 | tf_op jit(solution)/shard_map/ppermute | solution.py:12
  164.7 52.2 %collective-permute-start.20 = (f32[2,128,128]{2,1,0:T(8,128)}, f32[2,128,128]{2,1,0:T(8,128)S(1)}, u32[]{:S(2)}, u32[]{:S(2)}) collective-permute-start(f32[2,128,128]{2,1,0:T(8,128)} %get-tuple-element.29), channel_id=1, source_target_pairs={{0,1},{1,2},{2,3},{3,4},{4,5},{5,6},{6,7},{7,8},{8,9},{9,10},{10,1... | collective-permute-start | bytes 393224 | tf_op jit(solution)/shard_map/ppermute | solution.py:12
  171.9 45.1 %collective-permute-start.21 = (f32[2,128,128]{2,1,0:T(8,128)S(1)}, f32[2,128,128]{2,1,0:T(8,128)S(1)}, u32[]{:S(2)}, u32[]{:S(2)}) collective-permute-start(f32[2,128,128]{2,1,0:T(8,128)S(1)} %get-tuple-element.28), channel_id=1, source_target_pairs={{1,0},{2,1},{3,2},{4,3},{5,4},{6,5},{7,6},{8,7},{9,8},{10,9},{11,1... | collective-permute-start | bytes 393224 | tf_op jit(solution)/shard_map/ppermute | solution.py:12
  191.2 5.2 %collective-permute-start.14 = (f32[2,128]{1,0:T(2,128)S(1)}, f32[2,128]{1,0:T(2,128)S(1)}, u32[]{:S(2)}, u32[]{:S(2)}) collective-permute-start(f32[2,128]{1,0:T(2,128)S(1)} %reduce_sum.110), channel_id=1, source_target_pairs={{0,16},{16,0},{32,48},{48,32},{64,80},{80,64},{96,112},{112,96},{1... | collective-permute-start | bytes 3080 | tf_op jit(solution)/shard_map/ppermute | solution.py:22
  196.4 6.6 %collective-permute-start.15 = (f32[2,128]{1,0:T(2,128)S(1)}, f32[2,128]{1,0:T(2,128)S(1)}, u32[]{:S(2)}, u32[]{:S(2)}) collective-permute-start(f32[2,128]{1,0:T(2,128)S(1)} %add.285), channel_id=1, source_target_pairs={{0,32},{16,48},{32,0},{48,16},{64,96},{80,112},{96,64},{112,80},{1... | collective-permute-start | bytes 3080 | tf_op jit(solution)/shard_map/ppermute | solution.py:22
  202.9 9.0 %collective-permute-start.16 = (f32[2,128]{1,0:T(2,128)S(1)}, f32[2,128]{1,0:T(2,128)S(1)}, u32[]{:S(2)}, u32[]{:S(2)}) collective-permute-start(f32[2,128]{1,0:T(2,128)S(1)} %add.286), channel_id=1, source_target_pairs={{0,64},{16,80},{32,96},{48,112},{64,0},{80,16},{96,32},{112,48},{1... | collective-permute-start | bytes 3080 | tf_op jit(solution)/shard_map/ppermute | solution.py:22
  212.0 6.3 %collective-permute-start.17 = (f32[2,128]{1,0:T(2,128)S(1)}, f32[2,128]{1,0:T(2,128)S(1)}, u32[]{:S(2)}, u32[]{:S(2)}) collective-permute-start(f32[2,128]{1,0:T(2,128)S(1)} %add.287), channel_id=1, source_target_pairs={{0,128},{16,144},{32,160},{48,176},{64,192},{80,208},{96,224},{112... | collective-permute-start | bytes 3080 | tf_op jit(solution)/shard_map/ppermute | solution.py:22
  218.3 5.9 %collective-permute-start.22 = (f32[2,128]{1,0:T(2,128)S(1)}, f32[2,128]{1,0:T(2,128)S(1)}, u32[]{:S(2)}, u32[]{:S(2)}) collective-permute-start(f32[2,128]{1,0:T(2,128)S(1)} %add_add_fusion.2), channel_id=1, source_target_pairs={{0,256},{16,272},{32,288},{48,304},{64,320},{80,336},{96,352},{112... | collective-permute-start | bytes 3080 | tf_op jit(solution)/shard_map/ppermute | solution.py:22
  249.9 7.5 %collective-permute-start.23 = (f32[16,8,128]{2,1,0:T(8,128)S(1)}, f32[16,8,128]{2,1,0:T(8,128)S(1)}, u32[]{:S(2)}, u32[]{:S(2)}) collective-permute-start(f32[16,8,128]{2,1,0:T(8,128)S(1)} %select_bitcast_fusion.1), channel_id=1, source_target_pairs={{0,256},{16,272},{32,288},{48,304},{64,320},{80,336},{96,352},{112... | collective-permute-start | bytes 196616 | tf_op jit(solution)/shard_map/ppermute | solution.py:36
  257.5 4.7 collective-permute-start.24
  262.1 8.5 %collective-permute-start.25 = (f32[4,8,128]{2,1,0:T(8,128)S(1)}, f32[4,8,128]{2,1,0:T(8,128)S(1)}, u32[]{:S(2)}, u32[]{:S(2)}) collective-permute-start(f32[4,8,128]{2,1,0:T(8,128)S(1)} %slice_select_fusion.5), channel_id=1, source_target_pairs={{0,64},{16,80},{32,96},{48,112},{64,0},{80,16},{96,32},{112,48},{1... | collective-permute-start | bytes 49160 | tf_op jit(solution)/shard_map/ppermute | solution.py:36
  270.6 5.3 %collective-permute-start.26 = (f32[2,8,128]{2,1,0:T(8,128)S(1)}, f32[2,8,128]{2,1,0:T(8,128)S(1)}, u32[]{:S(2)}, u32[]{:S(2)}) collective-permute-start(f32[2,8,128]{2,1,0:T(8,128)S(1)} %slice_select_fusion.9), channel_id=1, source_target_pairs={{0,32},{16,48},{32,0},{48,16},{64,96},{80,112},{96,64},{112,80},{1... | collective-permute-start | bytes 24584 | tf_op jit(solution)/shard_map/ppermute | solution.py:36
  275.9 4.3 collective-permute-start.27
  282.4 63.6 %copy-start.11 = (bf16[1,1,4,128,128]{4,3,2,1,0:T(8,128)(2,1)S(1)}, bf16[1,1,4,128,128]{4,3,2,1,0:T(8,128)(2,1)}, u32[]{:S(2)}) copy-start(bf16[1,1,4,128,128]{4,3,2,1,0:T(8,128)(2,1)} %param.15) | copy-start | bytes 393220
  284.1 54.6 %collective-permute-start.32 = (f32[2,128,128]{2,1,0:T(8,128)}, f32[2,128,128]{2,1,0:T(8,128)S(1)}, u32[]{:S(2)}, u32[]{:S(2)}) collective-permute-start(f32[2,128,128]{2,1,0:T(8,128)} %get-tuple-element.22), channel_id=1, source_target_pairs={{0,16},{16,32},{32,48},{48,64},{64,80},{80,96},{96,112},{112,128},... | collective-permute-start | bytes 393224 | tf_op jit(solution)/shard_map/ppermute | solution.py:12
  287.3 51.4 %collective-permute-start.33 = (f32[2,128,128]{2,1,0:T(8,128)}, f32[2,128,128]{2,1,0:T(8,128)S(1)}, u32[]{:S(2)}, u32[]{:S(2)}) collective-permute-start(f32[2,128,128]{2,1,0:T(8,128)} %get-tuple-element.23), channel_id=1, source_target_pairs={{16,0},{32,16},{48,32},{64,48},{80,64},{96,80},{112,96},{128,112},... | collective-permute-start | bytes 393224 | tf_op jit(solution)/shard_map/ppermute | solution.py:12
  288.6 50.1 %collective-permute-start.34 = (f32[2,128,128]{2,1,0:T(8,128)}, f32[2,128,128]{2,1,0:T(8,128)S(1)}, u32[]{:S(2)}, u32[]{:S(2)}) collective-permute-start(f32[2,128,128]{2,1,0:T(8,128)} %get-tuple-element.25), channel_id=1, source_target_pairs={{0,1},{1,2},{2,3},{3,4},{4,5},{5,6},{6,7},{7,8},{8,9},{9,10},{10,1... | collective-permute-start | bytes 393224 | tf_op jit(solution)/shard_map/ppermute | solution.py:12
  295.5 43.2 %collective-permute-start.35 = (f32[2,128,128]{2,1,0:T(8,128)}, f32[2,128,128]{2,1,0:T(8,128)S(1)}, u32[]{:S(2)}, u32[]{:S(2)}) collective-permute-start(f32[2,128,128]{2,1,0:T(8,128)} %get-tuple-element.24), channel_id=1, source_target_pairs={{1,0},{2,1},{3,2},{4,3},{5,4},{6,5},{7,6},{8,7},{9,8},{10,9},{11,1... | collective-permute-start | bytes 393224 | tf_op jit(solution)/shard_map/ppermute | solution.py:12
  313.5 5.2 %collective-permute-start.28 = (f32[2,128]{1,0:T(2,128)S(1)}, f32[2,128]{1,0:T(2,128)S(1)}, u32[]{:S(2)}, u32[]{:S(2)}) collective-permute-start(f32[2,128]{1,0:T(2,128)S(1)} %reduce_sum.114), channel_id=1, source_target_pairs={{0,16},{16,0},{32,48},{48,32},{64,80},{80,64},{96,112},{112,96},{1... | collective-permute-start | bytes 3080 | tf_op jit(solution)/shard_map/ppermute | solution.py:22
  318.7 5.2 %collective-permute-start.29 = (f32[2,128]{1,0:T(2,128)S(1)}, f32[2,128]{1,0:T(2,128)S(1)}, u32[]{:S(2)}, u32[]{:S(2)}) collective-permute-start(f32[2,128]{1,0:T(2,128)S(1)} %add.302), channel_id=1, source_target_pairs={{0,32},{16,48},{32,0},{48,16},{64,96},{80,112},{96,64},{112,80},{1... | collective-permute-start | bytes 3080 | tf_op jit(solution)/shard_map/ppermute | solution.py:22
  323.9 8.8 %collective-permute-start.30 = (f32[2,128]{1,0:T(2,128)S(1)}, f32[2,128]{1,0:T(2,128)S(1)}, u32[]{:S(2)}, u32[]{:S(2)}) collective-permute-start(f32[2,128]{1,0:T(2,128)S(1)} %add.303), channel_id=1, source_target_pairs={{0,64},{16,80},{32,96},{48,112},{64,0},{80,16},{96,32},{112,48},{1... | collective-permute-start | bytes 3080 | tf_op jit(solution)/shard_map/ppermute | solution.py:22
  332.8 7.2 %collective-permute-start.31 = (f32[2,128]{1,0:T(2,128)S(1)}, f32[2,128]{1,0:T(2,128)S(1)}, u32[]{:S(2)}, u32[]{:S(2)}) collective-permute-start(f32[2,128]{1,0:T(2,128)S(1)} %add.304), channel_id=1, source_target_pairs={{0,128},{16,144},{32,160},{48,176},{64,192},{80,208},{96,224},{112... | collective-permute-start | bytes 3080 | tf_op jit(solution)/shard_map/ppermute | solution.py:22
  340.0 5.9 %collective-permute-start.36 = (f32[2,128]{1,0:T(2,128)S(1)}, f32[2,128]{1,0:T(2,128)S(1)}, u32[]{:S(2)}, u32[]{:S(2)}) collective-permute-start(f32[2,128]{1,0:T(2,128)S(1)} %add_add_fusion.1), channel_id=1, source_target_pairs={{0,256},{16,272},{32,288},{48,304},{64,320},{80,336},{96,352},{112... | collective-permute-start | bytes 3080 | tf_op jit(solution)/shard_map/ppermute | solution.py:22
  347.9 25.4 %copy-start.7 = (f32[8,32,128]{2,0,1:T(8,128)S(1)}, f32[8,32,128]{2,0,1:T(8,128)}, u32[]{:S(2)}) copy-start(f32[8,32,128]{2,0,1:T(8,128)} %copy-done.6) | copy-start | bytes 393220
  373.6 7.4 %collective-permute-start.37 = (f32[16,8,128]{2,1,0:T(8,128)S(1)}, f32[16,8,128]{2,1,0:T(8,128)S(1)}, u32[]{:S(2)}, u32[]{:S(2)}) collective-permute-start(f32[16,8,128]{2,1,0:T(8,128)S(1)} %select_bitcast_fusion), channel_id=1, source_target_pairs={{0,256},{16,272},{32,288},{48,304},{64,320},{80,336},{96,352},{112... | collective-permute-start | bytes 196616 | tf_op jit(solution)/shard_map/ppermute | solution.py:36
  381.1 4.7 collective-permute-start.38
  385.7 8.6 %collective-permute-start.39 = (f32[4,8,128]{2,1,0:T(8,128)S(1)}, f32[4,8,128]{2,1,0:T(8,128)S(1)}, u32[]{:S(2)}, u32[]{:S(2)}) collective-permute-start(f32[4,8,128]{2,1,0:T(8,128)S(1)} %slice_select_fusion.4), channel_id=1, source_target_pairs={{0,64},{16,80},{32,96},{48,112},{64,0},{80,16},{96,32},{112,48},{1... | collective-permute-start | bytes 49160 | tf_op jit(solution)/shard_map/ppermute | solution.py:36
  394.3 5.3 %collective-permute-start.40 = (f32[2,8,128]{2,1,0:T(8,128)S(1)}, f32[2,8,128]{2,1,0:T(8,128)S(1)}, u32[]{:S(2)}, u32[]{:S(2)}) collective-permute-start(f32[2,8,128]{2,1,0:T(8,128)S(1)} %slice_select_fusion.8), channel_id=1, source_target_pairs={{0,32},{16,48},{32,0},{48,16},{64,96},{80,112},{96,64},{112,80},{1... | collective-permute-start | bytes 24584 | tf_op jit(solution)/shard_map/ppermute | solution.py:36
  399.6 16.1 %collective-permute-start.41 = (f32[1,8,128]{2,1,0:T(8,128)S(1)}, f32[1,8,128]{2,1,0:T(8,128)S(1)}, u32[]{:S(2)}, u32[]{:S(2)}) collective-permute-start(f32[1,8,128]{2,1,0:T(8,128)S(1)} %slice_select_fusion.12), channel_id=1, source_target_pairs={{0,16},{16,0},{32,48},{48,32},{64,80},{80,64},{96,112},{112,96},{1... | collective-permute-start | bytes 12296 | tf_op jit(solution)/shard_map/ppermute | solution.py:36
  403.3 54.3 %collective-permute-start.46 = (f32[2,128,128]{2,1,0:T(8,128)}, f32[2,128,128]{2,1,0:T(8,128)S(1)}, u32[]{:S(2)}, u32[]{:S(2)}) collective-permute-start(f32[2,128,128]{2,1,0:T(8,128)} %get-tuple-element.18), channel_id=1, source_target_pairs={{0,16},{16,32},{32,48},{48,64},{64,80},{80,96},{96,112},{112,128},... | collective-permute-start | bytes 393224 | tf_op jit(solution)/shard_map/ppermute | solution.py:12
  406.6 51.0 %collective-permute-start.47 = (f32[2,128,128]{2,1,0:T(8,128)}, f32[2,128,128]{2,1,0:T(8,128)S(1)}, u32[]{:S(2)}, u32[]{:S(2)}) collective-permute-start(f32[2,128,128]{2,1,0:T(8,128)} %get-tuple-element.19), channel_id=1, source_target_pairs={{16,0},{32,16},{48,32},{64,48},{80,64},{96,80},{112,96},{128,112},... | collective-permute-start | bytes 393224 | tf_op jit(solution)/shard_map/ppermute | solution.py:12
  407.9 49.7 %collective-permute-start.48 = (f32[2,128,128]{2,1,0:T(8,128)}, f32[2,128,128]{2,1,0:T(8,128)S(1)}, u32[]{:S(2)}, u32[]{:S(2)}) collective-permute-start(f32[2,128,128]{2,1,0:T(8,128)} %get-tuple-element.21), channel_id=1, source_target_pairs={{0,1},{1,2},{2,3},{3,4},{4,5},{5,6},{6,7},{7,8},{8,9},{9,10},{10,1... | collective-permute-start | bytes 393224 | tf_op jit(solution)/shard_map/ppermute | solution.py:12
  413.7 43.9 %collective-permute-start.49 = (f32[2,128,128]{2,1,0:T(8,128)}, f32[2,128,128]{2,1,0:T(8,128)}, u32[]{:S(2)}, u32[]{:S(2)}) collective-permute-start(f32[2,128,128]{2,1,0:T(8,128)} %get-tuple-element.20), channel_id=1, source_target_pairs={{1,0},{2,1},{3,2},{4,3},{5,4},{6,5},{7,6},{8,7},{9,8},{10,9},{11,1... | collective-permute-start | bytes 393224 | tf_op jit(solution)/shard_map/ppermute | solution.py:12
  433.4 33.0 %copy-start.12 = (bf16[1,1,4,128,128]{4,3,2,1,0:T(8,128)(2,1)S(1)}, bf16[1,1,4,128,128]{4,3,2,1,0:T(8,128)(2,1)}, u32[]{:S(2)}) copy-start(bf16[1,1,4,128,128]{4,3,2,1,0:T(8,128)(2,1)} %param.15) | copy-start | bytes 393220
  433.4 5.4 %collective-permute-start.42 = (f32[2,128]{1,0:T(2,128)S(1)}, f32[2,128]{1,0:T(2,128)S(1)}, u32[]{:S(2)}, u32[]{:S(2)}) collective-permute-start(f32[2,128]{1,0:T(2,128)S(1)} %reduce_sum.118), channel_id=1, source_target_pairs={{0,16},{16,0},{32,48},{48,32},{64,80},{80,64},{96,112},{112,96},{1... | collective-permute-start | bytes 3080 | tf_op jit(solution)/shard_map/ppermute | solution.py:22
  438.8 5.2 %collective-permute-start.43 = (f32[2,128]{1,0:T(2,128)S(1)}, f32[2,128]{1,0:T(2,128)S(1)}, u32[]{:S(2)}, u32[]{:S(2)}) collective-permute-start(f32[2,128]{1,0:T(2,128)S(1)} %add.320), channel_id=1, source_target_pairs={{0,32},{16,48},{32,0},{48,16},{64,96},{80,112},{96,64},{112,80},{1... | collective-permute-start | bytes 3080 | tf_op jit(solution)/shard_map/ppermute | solution.py:22
  444.0 8.2 %collective-permute-start.44 = (f32[2,128]{1,0:T(2,128)S(1)}, f32[2,128]{1,0:T(2,128)S(1)}, u32[]{:S(2)}, u32[]{:S(2)}) collective-permute-start(f32[2,128]{1,0:T(2,128)S(1)} %add.321), channel_id=1, source_target_pairs={{0,64},{16,80},{32,96},{48,112},{64,0},{80,16},{96,32},{112,48},{1... | collective-permute-start | bytes 3080 | tf_op jit(solution)/shard_map/ppermute | solution.py:22
  452.2 7.3 %collective-permute-start.45 = (f32[2,128]{1,0:T(2,128)S(1)}, f32[2,128]{1,0:T(2,128)S(1)}, u32[]{:S(2)}, u32[]{:S(2)}) collective-permute-start(f32[2,128]{1,0:T(2,128)S(1)} %add.322), channel_id=1, source_target_pairs={{0,128},{16,144},{32,160},{48,176},{64,192},{80,208},{96,224},{112... | collective-permute-start | bytes 3080 | tf_op jit(solution)/shard_map/ppermute | solution.py:22
  459.6 7.0 %copy-start.3 = (bf16[1,1,896,896]{3,2,1,0:T(8,128)(2,1)S(1)}, bf16[1,1,896,896]{3,2,1,0:T(8,128)(2,1)}, u32[]{:S(2)}) copy-start(bf16[1,1,896,896]{3,2,1,0:T(8,128)(2,1)} %param.11) | copy-start | bytes 4816900
  459.6 5.9 %collective-permute-start.50 = (f32[2,128]{1,0:T(2,128)S(1)}, f32[2,128]{1,0:T(2,128)S(1)}, u32[]{:S(2)}, u32[]{:S(2)}) collective-permute-start(f32[2,128]{1,0:T(2,128)S(1)} %add_add_fusion), channel_id=1, source_target_pairs={{0,256},{16,272},{32,288},{48,304},{64,320},{80,336},{96,352},{112... | collective-permute-start | bytes 3080 | tf_op jit(solution)/shard_map/ppermute | solution.py:22
  (7 other events, 25.1 us)

commit v4 on v3

--- a/solution.py
+++ b/solution.py
@@ -12,15 +12,31 @@
     return lax.ppermute(value, axis, [(source, source + steps) for source in range(leading, last)])
 
 
+def digit_sizes(count):
+    sizes, size = [], count
+    while size > 1:
+        radix = 4 if size % 4 == 0 else 2
+        size //= radix
+        sizes.append((radix, size))
+    return sizes
+
+
 def total_over_mesh(value, tie):
     value = jnp.sum(lax.all_gather(value, "gy", axis=0), axis=0)
     count = lax.axis_size("gx")
-    step = 1
-    while step < count:
-        if step == count // 2:
+    index = lax.axis_index("gx")
+    sizes = digit_sizes(count)
+    for position, (radix, size) in enumerate(sizes):
+        if position == len(sizes) - 1:
             value = value + 0.0 * tie
-        value = value + lax.ppermute(value, "gx", [(i, i ^ step) for i in range(count)])
-        step *= 2
+        parts = [value] + [
+            lax.ppermute(value, "gx", [(i, i ^ (j * size)) for i in range(count)]) for j in range(1, radix)
+        ]
+        own = (index // size) % radix
+        ordered = jnp.stack(parts)[jnp.arange(radix) ^ own]
+        while ordered.shape[0] > 1:
+            ordered = ordered[0::2] + ordered[1::2]
+        value = ordered[0]
     return value
 
 
@@ -28,13 +44,14 @@
     count = lax.axis_size(axis)
     index = lax.axis_index(axis)
     blocks = stacked.reshape(count, rows, stacked.shape[-1])
-    half = count // 2
-    while half >= 1:
-        upper = (index // half) % 2 == 1
-        keep = jnp.where(upper, blocks[half:], blocks[:half])
-        send = jnp.where(upper, blocks[:half], blocks[half:])
-        blocks = keep + lax.ppermute(send, axis, [(i, i ^ half) for i in range(count)])
-        half //= 2
+    for radix, size in digit_sizes(count):
+        own = (index // size) % radix
+        quarters = blocks.reshape((radix, size) + blocks.shape[1:])
+        total = jnp.take(quarters, own, axis=0)
+        for j in range(1, radix):
+            send = jnp.take(quarters, own ^ j, axis=0)
+            total = total + lax.ppermute(send, axis, [(i, i ^ (j * size)) for i in range(count)])
+        blocks = total
     return blocks[0]
 
 

time: 477 us -> 481 us (level)
  waiting for transfers between devices: 50.1 us -> 39.3 us
  local copies, waits for them, and re-layouts: 30.6 us -> 37.2 us
  starting transfers between devices: 218 us -> 224 us
    ppermute x35 -> x49, waiting for transfers between devices: 49.3 us -> 29.3 us  [the longest x28 27.7 us: scatter_rows(): lax.ppermute(send, axis, [(i, i ^ j * size) for i in range(count)])]
    ppermute x35 -> x49, starting transfers between devices: 156 us -> 173 us  [the longest x28 96.1 us: scatter_rows(): lax.ppermute(send, axis, [(i, i ^ j * size) for i in range(count)])]
    ppermute x16, starting transfers between devices: 51.5 us -> 40.3 us  [from_behind(): lax.ppermute(value, axis, [(source, source + steps) for source in range(l...]
    all_gather x3, blocking collectives: 50.6 us -> 61.7 us  [total_over_mesh(): value = jnp.sum(lax.all_gather(value, 'gy', axis=0), axis=0)]
    all_gather x4, blocking collectives: 81.4 us -> 71.2 us  [apply_prec(): line = lax.all_gather(coarse, 'gy', axis=0, tiled=True)]
    ppermute x16, waiting for transfers between devices: 0.88 us -> 10 us  [from_behind(): lax.ppermute(value, axis, [(source, source + steps) for source in range(l...]
    gather x0 -> x9, local copies, waits for them, and re-layouts: none -> 5.14 us  [total_over_mesh(): ordered = jnp.stack(parts)[jnp.arange(radix) ^ own]]
  transfers between devices with their start and end apart: 52 -> 66, of which waited for: 32 -> 18; matrix products, arithmetic and copies ran while one was open for 3% -> 5% of each run, Pallas kernels for 0% -> 0%
where the time goes in v4:
time: 481 us; the launch traced here: 477 us
  starting transfers between devices  224 us (47%)
  blocking collectives  133 us (28%)
  waiting for transfers between devices  39.3 us (8%)
  local copies, waits for them, and re-layouts  37.2 us (8%)
  other arithmetic  28.5 us (6%)
  matrix products  10.1 us (2%)
    ppermute x28, starting transfers between devices, scatter_rows(): lax.ppermute(send, axis, [(i, i ^ j * size) for i in range(count)])  96.1 us
    ppermute x21, starting transfers between devices, total_over_mesh(): lax.ppermute(value, 'gx', [(i, i ^ j * size) for i in range(count)])  77.1 us
    all_gather x4, blocking collectives, apply_prec(): line = lax.all_gather(coarse, 'gy', axis=0, tiled=True)  71.2 us
    all_gather x3, blocking collectives, total_over_mesh(): value = jnp.sum(lax.all_gather(value, 'gy', axis=0), axis=0)  61.7 us
    ppermute x16, starting transfers between devices, from_behind(): lax.ppermute(value, axis, [(source, source + steps) for source in range(l...  40.3 us
    ppermute x28, waiting for transfers between devices, scatter_rows(): lax.ppermute(send, axis, [(i, i ^ j * size) for i in range(count)])  27.7 us
    gather x2, local copies, waits for them, and re-layouts, shards(): coarse_cols = jnp.take(coarse_inverse, coarse_map, axis=1)  17.9 us
    scatter-add x4, other arithmetic, finish_schur(): return result.at[flat_rows].add(-coupled.reshape(-1, coupled.shape[-1]))  14.1 us
  transfers between devices with their start and end apart: 66, of which 18 were waited for; matrix products, arithmetic and copies ran while one was open for 5% of the time, Pallas kernels for 0%

profile of v4, /device:TPU:1, one launch (start us, length us, event | category | flops | bytes accessed | tf_op | source)
XLA Modules:
  0.0 476.6 jit_solution(6498284373217702372)
XLA Ops:
  2.2 2.9 copy.44
  5.1 15.8 %gather_fusion = f32[4096,8]{1,0:T(8,128)} fusion(f32[8,4096]{0,1:T(8,128)} %copy.44, s32[4096]{0:T(1024)S(1)} %fusion.139), kind=kCustom, calls=%fused_computation | custom fusion | bytes 278528 | tf_op jit(solution)/shard_map/jit(_take)/gather | solution.py:90
  23.7 10.5 %all-to-all-start = ((f32[8,32,128]{2,0,1:T(8,128)}), f32[8,32,128]{2,0,1:T(8,128)S(1)}, u32[]{:S(2)}, u32[]{:S(2)}) async-start(f32[8,32,128]{2,0,1:T(8,128)} %broadcast_select_fusion), calls=%async_computation | async-start | bytes 262144 | tf_op jit(solution)/shard_map/all_to_all | solution.py:91
  34.5 24.1 %all_gather.30 = f32[128,128]{1,0:T(8,128)S(1)} all-gather(f32[8,128]{1,0:T(8,128)S(1)} %fusion.137), channel_id=1, replica_groups=mesh['gx'=32,'gy'=16] {'gy'}, dimensions={0}, use_global_device_ids=true | all-gather | bytes 69632 | tf_op jit(solution)/shard_map/all_gather | solution.py:132
  59.6 3.4 collective-permute-start
  63.0 4.3 collective-permute-start.1
  69.4 3.8 collective-permute-done.2
  73.3 4.0 collective-permute-start.3
  77.3 5.2 %collective-permute-start.4 = (f32[2,8,128]{2,1,0:T(8,128)S(1)}, f32[2,8,128]{2,1,0:T(8,128)S(1)}, u32[]{:S(2)}, u32[]{:S(2)}) collective-permute-start(f32[2,8,128]{2,1,0:T(8,128)S(1)} %get-tuple-element.94), channel_id=1, source_target_pairs={{0,64},{16,80},{32,96},{48,112},{64,0},{80,16},{96,32},{112,48},{1... | collective-permute-start | bytes 24584 | tf_op jit(solution)/shard_map/ppermute | solution.py:53
  85.6 3.4 collective-permute-done.5
  89.0 2.5 collective-permute-start.6
  95.2 2.5 collective-permute-start.7
  99.0 5.6 %collective-permute-start.9 = (bf16[128,128]{1,0:T(8,128)(2,1)S(1)}, bf16[128,128]{1,0:T(8,128)(2,1)S(1)}, u32[]{:S(2)}, u32[]{:S(2)}) collective-permute-start(bf16[128,128]{1,0:T(8,128)(2,1)S(1)} %get-tuple-element.77), channel_id=1, source_target_pairs={{0,1},{1,2},{2,3},{3,4},{4,5},{5,6},{6,7},{7,8},{8,9},{9,10},{10,1... | collective-permute-start | bytes 98312 | tf_op jit(solution)/shard_map/ppermute | solution.py:12
  110.0 3.5 scatter_fusion
  113.7 15.1 %all_gather.31 = f32[128,128]{1,0:T(8,128)S(1)} all-gather(f32[8,128]{1,0:T(8,128)S(1)} %convolution_bitcast_fusion.6), channel_id=1, replica_groups=mesh['gx'=32,'gy'=16] {'gy'}, dimensions={0}, use_global_device_ids=true | all-gather | bytes 69632 | tf_op jit(solution)/shard_map/all_gather | solution.py:132
  129.0 4.8 %collective-permute-start.11 = (f32[8,8,128]{2,1,0:T(8,128)S(1)}, f32[8,8,128]{2,1,0:T(8,128)S(1)}, u32[]{:S(2)}, u32[]{:S(2)}) collective-permute-start(f32[8,8,128]{2,1,0:T(8,128)S(1)} %get-tuple-element.73), channel_id=1, source_target_pairs={{0,128},{16,144},{32,160},{48,176},{64,192},{80,208},{96,224},{112... | collective-permute-start | bytes 98312 | tf_op jit(solution)/shard_map/ppermute | solution.py:53
  133.8 4.6 collective-permute-start.12
  140.4 3.9 collective-permute-done.13
  146.2 3.2 collective-permute-start.15
  149.4 6.3 %collective-permute-start.16 = (f32[2,8,128]{2,1,0:T(8,128)S(1)}, f32[2,8,128]{2,1,0:T(8,128)S(1)}, u32[]{:S(2)}, u32[]{:S(2)}) collective-permute-start(f32[2,8,128]{2,1,0:T(8,128)S(1)} %get-tuple-element.90), channel_id=1, source_target_pairs={{0,96},{16,112},{32,64},{48,80},{64,32},{80,48},{96,0},{112,16},{1... | collective-permute-start | bytes 24584 | tf_op jit(solution)/shard_map/ppermute | solution.py:53
  161.9 19.8 %all-gather.3 = f32[16,2,128]{2,1,0:T(2,128)S(1)} all-gather(f32[1,2,128]{2,1,0:T(2,128)S(1)} %maximum_bitcast_fusion), channel_id=2, replica_groups=mesh['gx'=32,'gy'=16] {'gy'}, dimensions={0}, use_global_device_ids=true | all-gather | bytes 17408 | tf_op jit(solution)/shard_map/all_gather | solution.py:25
  183.6 4.6 collective-permute-start.19
  188.2 3.0 collective-permute-start.20
  196.7 6.1 %collective-permute-start.21 = (f32[2,128]{1,0:T(2,128)S(1)}, f32[2,128]{1,0:T(2,128)S(1)}, u32[]{:S(2)}, u32[]{:S(2)}) collective-permute-start(f32[2,128]{1,0:T(2,128)S(1)} %fusion.258), channel_id=1, source_target_pairs={{0,32},{16,48},{32,0},{48,16},{64,96},{80,112},{96,64},{112,80},{1... | collective-permute-start | bytes 3080 | tf_op jit(solution)/shard_map/ppermute | solution.py:33
  202.7 6.0 %collective-permute-start.22 = (f32[2,128]{1,0:T(2,128)S(1)}, f32[2,128]{1,0:T(2,128)S(1)}, u32[]{:S(2)}, u32[]{:S(2)}) collective-permute-start(f32[2,128]{1,0:T(2,128)S(1)} %fusion.258), channel_id=1, source_target_pairs={{0,64},{16,80},{32,96},{48,112},{64,0},{80,16},{96,32},{112,48},{1... | collective-permute-start | bytes 3080 | tf_op jit(solution)/shard_map/ppermute | solution.py:33
  210.7 4.0 collective-permute-start.26
  217.3 3.7 collective-permute-done.27
  229.4 3.7 scatter_fusion.1
  233.2 15.5 %all_gather.34 = f32[128,128]{1,0:T(8,128)S(1)} all-gather(f32[8,128]{1,0:T(8,128)S(1)} %convolution_bitcast_fusion.5), channel_id=1, replica_groups=mesh['gx'=32,'gy'=16] {'gy'}, dimensions={0}, use_global_device_ids=true | all-gather | bytes 69632 | tf_op jit(solution)/shard_map/all_gather | solution.py:132
  249.1 3.8 collective-permute-start.29
  252.8 4.9 %collective-permute-start.30 = (f32[8,8,128]{2,1,0:T(8,128)S(1)}, f32[8,8,128]{2,1,0:T(8,128)S(1)}, u32[]{:S(2)}, u32[]{:S(2)}) collective-permute-start(f32[8,8,128]{2,1,0:T(8,128)S(1)} %get-tuple-element.72), channel_id=1, source_target_pairs={{0,256},{16,272},{32,288},{48,304},{64,320},{80,336},{96,352},{112... | collective-permute-start | bytes 98312 | tf_op jit(solution)/shard_map/ppermute | solution.py:53
  259.7 3.9 collective-permute-done.31
  263.6 2.4 collective-permute-start.32
  266.1 4.9 %collective-permute-start.33 = (f32[2,8,128]{2,1,0:T(8,128)S(1)}, f32[2,8,128]{2,1,0:T(8,128)S(1)}, u32[]{:S(2)}, u32[]{:S(2)}) collective-permute-start(f32[2,8,128]{2,1,0:T(8,128)S(1)} %get-tuple-element.88), channel_id=1, source_target_pairs={{0,64},{16,80},{32,96},{48,112},{64,0},{80,16},{96,32},{112,48},{1... | collective-permute-start | bytes 24584 | tf_op jit(solution)/shard_map/ppermute | solution.py:53
  271.0 4.0 collective-permute-start.34
  275.1 2.5 collective-permute-done.34
  282.4 21.4 %all-gather.4 = f32[16,2,128]{2,1,0:T(2,128)S(1)} all-gather(f32[1,2,128]{2,1,0:T(2,128)S(1)} %maximum_bitcast_fusion.1), channel_id=3, replica_groups=mesh['gx'=32,'gy'=16] {'gy'}, dimensions={0}, use_global_device_ids=true | all-gather | bytes 17408 | tf_op jit(solution)/shard_map/all_gather | solution.py:25
  305.8 4.7 collective-permute-start.37
  310.5 2.9 collective-permute-start.38
  320.2 6.2 %collective-permute-start.39 = (f32[2,128]{1,0:T(2,128)S(1)}, f32[2,128]{1,0:T(2,128)S(1)}, u32[]{:S(2)}, u32[]{:S(2)}) collective-permute-start(f32[2,128]{1,0:T(2,128)S(1)} %fusion.256), channel_id=1, source_target_pairs={{0,32},{16,48},{32,0},{48,16},{64,96},{80,112},{96,64},{112,80},{1... | collective-permute-start | bytes 3080 | tf_op jit(solution)/shard_map/ppermute | solution.py:33
  326.4 3.7 collective-permute-start.40
  330.2 3.4 collective-permute-start.41
  333.6 2.8 collective-permute-start.44
  336.4 3.2 collective-permute-start.45
  340.2 2.7 collective-permute-done.45
  344.2 3.1 collective-permute-start.46
  351.7 3.5 scatter_fusion.2
  355.4 16.6 %all_gather.37 = f32[128,128]{1,0:T(8,128)S(1)} all-gather(f32[8,128]{1,0:T(8,128)S(1)} %convolution_bitcast_fusion.4), channel_id=1, replica_groups=mesh['gx'=32,'gy'=16] {'gy'}, dimensions={0}, use_global_device_ids=true | all-gather | bytes 69632 | tf_op jit(solution)/shard_map/all_gather | solution.py:132
  372.2 3.0 collective-permute-start.47
  375.2 5.8 %collective-permute-start.48 = (f32[8,8,128]{2,1,0:T(8,128)S(1)}, f32[8,8,128]{2,1,0:T(8,128)S(1)}, u32[]{:S(2)}, u32[]{:S(2)}) collective-permute-start(f32[8,8,128]{2,1,0:T(8,128)S(1)} %get-tuple-element.69), channel_id=1, source_target_pairs={{0,256},{16,272},{32,288},{48,304},{64,320},{80,336},{96,352},{112... | collective-permute-start | bytes 98312 | tf_op jit(solution)/shard_map/ppermute | solution.py:53
  382.9 3.9 collective-permute-done.49
  388.8 3.7 collective-permute-start.51
  392.5 5.8 %collective-permute-start.52 = (f32[2,8,128]{2,1,0:T(8,128)S(1)}, f32[2,8,128]{2,1,0:T(8,128)S(1)}, u32[]{:S(2)}, u32[]{:S(2)}) collective-permute-start(f32[2,8,128]{2,1,0:T(8,128)S(1)} %get-tuple-element.84), channel_id=1, source_target_pairs={{0,96},{16,112},{32,64},{48,80},{64,32},{80,48},{96,0},{112,16},{1... | collective-permute-start | bytes 24584 | tf_op jit(solution)/shard_map/ppermute | solution.py:53
  405.3 20.4 %all-gather.5 = f32[16,2,128]{2,1,0:T(2,128)S(1)} all-gather(f32[1,2,128]{2,1,0:T(2,128)S(1)} %maximum_bitcast_fusion.2), channel_id=4, replica_groups=mesh['gx'=32,'gy'=16] {'gy'}, dimensions={0}, use_global_device_ids=true | all-gather | bytes 17408 | tf_op jit(solution)/shard_map/all_gather | solution.py:25
  427.7 5.0 %collective-permute-start.55 = (f32[2,128]{1,0:T(2,128)S(1)}, f32[2,128]{1,0:T(2,128)S(1)}, u32[]{:S(2)}, u32[]{:S(2)}) collective-permute-start(f32[2,128]{1,0:T(2,128)S(1)} %reduce_sum.118), channel_id=1, source_target_pairs={{0,256},{16,272},{32,288},{48,304},{64,320},{80,336},{96,352},{112... | collective-permute-start | bytes 3080 | tf_op jit(solution)/shard_map/ppermute | solution.py:33
  432.7 2.6 collective-permute-start.56
  437.0 3.3 collective-permute-start.60
  442.5 3.7 collective-permute-start.57
  446.3 6.7 %collective-permute-start.58 = (f32[2,128]{1,0:T(2,128)S(1)}, f32[2,128]{1,0:T(2,128)S(1)}, u32[]{:S(2)}, u32[]{:S(2)}) collective-permute-start(f32[2,128]{1,0:T(2,128)S(1)} %fusion.254), channel_id=1, source_target_pairs={{0,64},{16,80},{32,96},{48,112},{64,0},{80,16},{96,32},{112,48},{1... | collective-permute-start | bytes 3080 | tf_op jit(solution)/shard_map/ppermute | solution.py:33
  454.9 2.5 collective-permute-start.62
  457.4 2.9 collective-permute-start.63
  460.9 2.8 collective-permute-done.63
  465.1 3.4 collective-permute-start.64
  472.2 3.5 scatter_fusion.3
  (258 shorter events, 96.7 us)
Async XLA Ops:
  23.7 35.5 %all-to-all-start = ((f32[8,32,128]{2,0,1:T(8,128)}), f32[8,32,128]{2,0,1:T(8,128)S(1)}, u32[]{:S(2)}, u32[]{:S(2)}) async-start(f32[8,32,128]{2,0,1:T(8,128)} %broadcast_select_fusion), calls=%async_computation | async-start | bytes 262144 | tf_op jit(solution)/shard_map/all_to_all | solution.py:91
  59.6 9.8 %collective-permute-start = (f32[8,8,128]{2,1,0:T(8,128)S(1)}, f32[8,8,128]{2,1,0:T(8,128)S(1)}, u32[]{:S(2)}, u32[]{:S(2)}) collective-permute-start(f32[8,8,128]{2,1,0:T(8,128)S(1)} %get-tuple-element.80), channel_id=1, source_target_pairs={{0,128},{16,144},{32,160},{48,176},{64,192},{80,208},{96,224},{112... | collective-permute-start | bytes 98312 | tf_op jit(solution)/shard_map/ppermute | solution.py:53
  63.0 6.4 %collective-permute-start.1 = (f32[8,8,128]{2,1,0:T(8,128)S(1)}, f32[8,8,128]{2,1,0:T(8,128)S(1)}, u32[]{:S(2)}, u32[]{:S(2)}) collective-permute-start(f32[8,8,128]{2,1,0:T(8,128)S(1)} %get-tuple-element.82), channel_id=1, source_target_pairs={{0,256},{16,272},{32,288},{48,304},{64,320},{80,336},{96,352},{112... | collective-permute-start | bytes 98312 | tf_op jit(solution)/shard_map/ppermute | solution.py:53
  67.4 5.9 %collective-permute-start.2 = (f32[8,8,128]{2,1,0:T(8,128)S(1)}, f32[8,8,128]{2,1,0:T(8,128)S(1)}, u32[]{:S(2)}, u32[]{:S(2)}) collective-permute-start(f32[8,8,128]{2,1,0:T(8,128)S(1)} %get-tuple-element.81), channel_id=1, source_target_pairs={{0,384},{16,400},{32,416},{48,432},{64,448},{80,464},{96,480},{112... | collective-permute-start | bytes 98312 | tf_op jit(solution)/shard_map/ppermute | solution.py:53
  73.3 11.5 %collective-permute-start.3 = (f32[2,8,128]{2,1,0:T(8,128)S(1)}, f32[2,8,128]{2,1,0:T(8,128)S(1)}, u32[]{:S(2)}, u32[]{:S(2)}) collective-permute-start(f32[2,8,128]{2,1,0:T(8,128)S(1)} %get-tuple-element.92), channel_id=1, source_target_pairs={{0,32},{16,48},{32,0},{48,16},{64,96},{80,112},{96,64},{112,80},{1... | collective-permute-start | bytes 24584 | tf_op jit(solution)/shard_map/ppermute | solution.py:53
  77.3 8.3 %collective-permute-start.4 = (f32[2,8,128]{2,1,0:T(8,128)S(1)}, f32[2,8,128]{2,1,0:T(8,128)S(1)}, u32[]{:S(2)}, u32[]{:S(2)}) collective-permute-start(f32[2,8,128]{2,1,0:T(8,128)S(1)} %get-tuple-element.94), channel_id=1, source_target_pairs={{0,64},{16,80},{32,96},{48,112},{64,0},{80,16},{96,32},{112,48},{1... | collective-permute-start | bytes 24584 | tf_op jit(solution)/shard_map/ppermute | solution.py:53
  82.5 6.5 %collective-permute-start.5 = (f32[2,8,128]{2,1,0:T(8,128)S(1)}, f32[2,8,128]{2,1,0:T(8,128)S(1)}, u32[]{:S(2)}, u32[]{:S(2)}) collective-permute-start(f32[2,8,128]{2,1,0:T(8,128)S(1)} %get-tuple-element.93), channel_id=1, source_target_pairs={{0,96},{16,112},{32,64},{48,80},{64,32},{80,48},{96,0},{112,16},{1... | collective-permute-start | bytes 24584 | tf_op jit(solution)/shard_map/ppermute | solution.py:53
  89.0 4.4 collective-permute-start.6
  95.2 13.8 %collective-permute-start.7 = (bf16[128,128]{1,0:T(8,128)(2,1)S(1)}, bf16[128,128]{1,0:T(8,128)(2,1)S(1)}, u32[]{:S(2)}, u32[]{:S(2)}) collective-permute-start(bf16[128,128]{1,0:T(8,128)(2,1)S(1)} %get-tuple-element.76), channel_id=1, source_target_pairs={{0,16},{16,32},{32,48},{48,64},{64,80},{80,96},{96,112},{112,128},... | collective-permute-start | bytes 98312 | tf_op jit(solution)/shard_map/ppermute | solution.py:12
  97.7 11.2 %collective-permute-start.8 = (bf16[128,128]{1,0:T(8,128)(2,1)S(1)}, bf16[128,128]{1,0:T(8,128)(2,1)S(1)}, u32[]{:S(2)}, u32[]{:S(2)}) collective-permute-start(bf16[128,128]{1,0:T(8,128)(2,1)S(1)} %get-tuple-element.78), channel_id=1, source_target_pairs={{16,0},{32,16},{48,32},{64,48},{80,64},{96,80},{112,96},{128,112},... | collective-permute-start | bytes 98312 | tf_op jit(solution)/shard_map/ppermute | solution.py:12
  99.0 10.0 %collective-permute-start.9 = (bf16[128,128]{1,0:T(8,128)(2,1)S(1)}, bf16[128,128]{1,0:T(8,128)(2,1)S(1)}, u32[]{:S(2)}, u32[]{:S(2)}) collective-permute-start(bf16[128,128]{1,0:T(8,128)(2,1)S(1)} %get-tuple-element.77), channel_id=1, source_target_pairs={{0,1},{1,2},{2,3},{3,4},{4,5},{5,6},{6,7},{7,8},{8,9},{9,10},{10,1... | collective-permute-start | bytes 98312 | tf_op jit(solution)/shard_map/ppermute | solution.py:12
  104.6 5.2 %collective-permute-start.10 = (bf16[128,128]{1,0:T(8,128)(2,1)S(1)}, bf16[128,128]{1,0:T(8,128)(2,1)S(1)}, u32[]{:S(2)}, u32[]{:S(2)}) collective-permute-start(bf16[128,128]{1,0:T(8,128)(2,1)S(1)} %get-tuple-element.79), channel_id=1, source_target_pairs={{1,0},{2,1},{3,2},{4,3},{5,4},{6,5},{7,6},{8,7},{9,8},{10,9},{11,1... | collective-permute-start | bytes 98312 | tf_op jit(solution)/shard_map/ppermute | solution.py:12
  129.0 11.3 %collective-permute-start.11 = (f32[8,8,128]{2,1,0:T(8,128)S(1)}, f32[8,8,128]{2,1,0:T(8,128)S(1)}, u32[]{:S(2)}, u32[]{:S(2)}) collective-permute-start(f32[8,8,128]{2,1,0:T(8,128)S(1)} %get-tuple-element.73), channel_id=1, source_target_pairs={{0,128},{16,144},{32,160},{48,176},{64,192},{80,208},{96,224},{112... | collective-permute-start | bytes 98312 | tf_op jit(solution)/shard_map/ppermute | solution.py:53
  133.8 6.5 %collective-permute-start.12 = (f32[8,8,128]{2,1,0:T(8,128)S(1)}, f32[8,8,128]{2,1,0:T(8,128)S(1)}, u32[]{:S(2)}, u32[]{:S(2)}) collective-permute-start(f32[8,8,128]{2,1,0:T(8,128)S(1)} %get-tuple-element.75), channel_id=1, source_target_pairs={{0,256},{16,272},{32,288},{48,304},{64,320},{80,336},{96,352},{112... | collective-permute-start | bytes 98312 | tf_op jit(solution)/shard_map/ppermute | solution.py:53
  138.4 5.9 %collective-permute-start.13 = (f32[8,8,128]{2,1,0:T(8,128)S(1)}, f32[8,8,128]{2,1,0:T(8,128)S(1)}, u32[]{:S(2)}, u32[]{:S(2)}) collective-permute-start(f32[8,8,128]{2,1,0:T(8,128)S(1)} %get-tuple-element.74), channel_id=1, source_target_pairs={{0,384},{16,400},{32,416},{48,432},{64,448},{80,464},{96,480},{112... | collective-permute-start | bytes 98312 | tf_op jit(solution)/shard_map/ppermute | solution.py:53
  144.3 12.5 %collective-permute-start.14 = (f32[2,8,128]{2,1,0:T(8,128)S(1)}, f32[2,8,128]{2,1,0:T(8,128)S(1)}, u32[]{:S(2)}, u32[]{:S(2)}) collective-permute-start(f32[2,8,128]{2,1,0:T(8,128)S(1)} %get-tuple-element.89), channel_id=1, source_target_pairs={{0,32},{16,48},{32,0},{48,16},{64,96},{80,112},{96,64},{112,80},{1... | collective-permute-start | bytes 24584 | tf_op jit(solution)/shard_map/ppermute | solution.py:53
  146.2 10.6 %collective-permute-start.15 = (f32[2,8,128]{2,1,0:T(8,128)S(1)}, f32[2,8,128]{2,1,0:T(8,128)S(1)}, u32[]{:S(2)}, u32[]{:S(2)}) collective-permute-start(f32[2,8,128]{2,1,0:T(8,128)S(1)} %get-tuple-element.91), channel_id=1, source_target_pairs={{0,64},{16,80},{32,96},{48,112},{64,0},{80,16},{96,32},{112,48},{1... | collective-permute-start | bytes 24584 | tf_op jit(solution)/shard_map/ppermute | solution.py:53
  149.4 7.6 %collective-permute-start.16 = (f32[2,8,128]{2,1,0:T(8,128)S(1)}, f32[2,8,128]{2,1,0:T(8,128)S(1)}, u32[]{:S(2)}, u32[]{:S(2)}) collective-permute-start(f32[2,8,128]{2,1,0:T(8,128)S(1)} %get-tuple-element.90), channel_id=1, source_target_pairs={{0,96},{16,112},{32,64},{48,80},{64,32},{80,48},{96,0},{112,16},{1... | collective-permute-start | bytes 24584 | tf_op jit(solution)/shard_map/ppermute | solution.py:53
  157.1 4.4 collective-permute-start.17
  181.7 14.3 %collective-permute-start.18 = (f32[2,128]{1,0:T(2,128)S(1)}, f32[2,128]{1,0:T(2,128)S(1)}, u32[]{:S(2)}, u32[]{:S(2)}) collective-permute-start(f32[2,128]{1,0:T(2,128)S(1)} %reduce_sum.110), channel_id=1, source_target_pairs={{0,128},{16,144},{32,160},{48,176},{64,192},{80,208},{96,224},{112... | collective-permute-start | bytes 3080 | tf_op jit(solution)/shard_map/ppermute | solution.py:33
  183.6 12.4 %collective-permute-start.19 = (f32[2,128]{1,0:T(2,128)S(1)}, f32[2,128]{1,0:T(2,128)S(1)}, u32[]{:S(2)}, u32[]{:S(2)}) collective-permute-start(f32[2,128]{1,0:T(2,128)S(1)} %reduce_sum.110), channel_id=1, source_target_pairs={{0,256},{16,272},{32,288},{48,304},{64,320},{80,336},{96,352},{112... | collective-permute-start | bytes 3080 | tf_op jit(solution)/shard_map/ppermute | solution.py:33
  188.2 7.8 %collective-permute-start.20 = (f32[2,128]{1,0:T(2,128)S(1)}, f32[2,128]{1,0:T(2,128)S(1)}, u32[]{:S(2)}, u32[]{:S(2)}) collective-permute-start(f32[2,128]{1,0:T(2,128)S(1)} %reduce_sum.110), channel_id=1, source_target_pairs={{0,384},{16,400},{32,416},{48,432},{64,448},{80,464},{96,480},{112... | collective-permute-start | bytes 3080 | tf_op jit(solution)/shard_map/ppermute | solution.py:33
  193.1 24.2 %collective-permute-start.24 = (f32[2,128,128]{2,1,0:T(8,128)}, f32[2,128,128]{2,1,0:T(8,128)S(1)}, u32[]{:S(2)}, u32[]{:S(2)}) collective-permute-start(f32[2,128,128]{2,1,0:T(8,128)} %get-tuple-element.62), channel_id=1, source_target_pairs={{0,16},{16,32},{32,48},{48,64},{64,80},{80,96},{96,112},{112,128},... | collective-permute-start | bytes 393224 | tf_op jit(solution)/shard_map/ppermute | solution.py:12
  194.7 22.5 %collective-permute-start.25 = (f32[2,128,128]{2,1,0:T(8,128)}, f32[2,128,128]{2,1,0:T(8,128)S(1)}, u32[]{:S(2)}, u32[]{:S(2)}) collective-permute-start(f32[2,128,128]{2,1,0:T(8,128)} %get-tuple-element.63), channel_id=1, source_target_pairs={{16,0},{32,16},{48,32},{64,48},{80,64},{96,80},{112,96},{128,112},... | collective-permute-start | bytes 393224 | tf_op jit(solution)/shard_map/ppermute | solution.py:12
  196.7 14.0 %collective-permute-start.21 = (f32[2,128]{1,0:T(2,128)S(1)}, f32[2,128]{1,0:T(2,128)S(1)}, u32[]{:S(2)}, u32[]{:S(2)}) collective-permute-start(f32[2,128]{1,0:T(2,128)S(1)} %fusion.258), channel_id=1, source_target_pairs={{0,32},{16,48},{32,0},{48,16},{64,96},{80,112},{96,64},{112,80},{1... | collective-permute-start | bytes 3080 | tf_op jit(solution)/shard_map/ppermute | solution.py:33
  202.7 12.0 %collective-permute-start.22 = (f32[2,128]{1,0:T(2,128)S(1)}, f32[2,128]{1,0:T(2,128)S(1)}, u32[]{:S(2)}, u32[]{:S(2)}) collective-permute-start(f32[2,128]{1,0:T(2,128)S(1)} %fusion.258), channel_id=1, source_target_pairs={{0,64},{16,80},{32,96},{48,112},{64,0},{80,16},{96,32},{112,48},{1... | collective-permute-start | bytes 3080 | tf_op jit(solution)/shard_map/ppermute | solution.py:33
  208.8 7.9 %collective-permute-start.23 = (f32[2,128]{1,0:T(2,128)S(1)}, f32[2,128]{1,0:T(2,128)S(1)}, u32[]{:S(2)}, u32[]{:S(2)}) collective-permute-start(f32[2,128]{1,0:T(2,128)S(1)} %fusion.258), channel_id=1, source_target_pairs={{0,96},{16,112},{32,64},{48,80},{64,32},{80,48},{96,0},{112,16},{1... | collective-permute-start | bytes 3080 | tf_op jit(solution)/shard_map/ppermute | solution.py:33
  210.7 6.6 %collective-permute-start.26 = (f32[2,128,128]{2,1,0:T(8,128)}, f32[2,128,128]{2,1,0:T(8,128)S(1)}, u32[]{:S(2)}, u32[]{:S(2)}) collective-permute-start(f32[2,128,128]{2,1,0:T(8,128)} %get-tuple-element.65), channel_id=1, source_target_pairs={{0,1},{1,2},{2,3},{3,4},{4,5},{5,6},{6,7},{7,8},{8,9},{9,10},{10,1... | collective-permute-start | bytes 393224 | tf_op jit(solution)/shard_map/ppermute | solution.py:12
  214.7 6.3 %collective-permute-start.27 = (f32[2,128,128]{2,1,0:T(8,128)S(1)}, f32[2,128,128]{2,1,0:T(8,128)S(1)}, u32[]{:S(2)}, u32[]{:S(2)}) collective-permute-start(f32[2,128,128]{2,1,0:T(8,128)S(1)} %get-tuple-element.64), channel_id=1, source_target_pairs={{1,0},{2,1},{3,2},{4,3},{5,4},{6,5},{7,6},{8,7},{9,8},{10,9},{11,1... | collective-permute-start | bytes 393224 | tf_op jit(solution)/shard_map/ppermute | solution.py:12
  249.1 10.6 %collective-permute-start.29 = (f32[8,8,128]{2,1,0:T(8,128)S(1)}, f32[8,8,128]{2,1,0:T(8,128)S(1)}, u32[]{:S(2)}, u32[]{:S(2)}) collective-permute-start(f32[8,8,128]{2,1,0:T(8,128)S(1)} %get-tuple-element.70), channel_id=1, source_target_pairs={{0,128},{16,144},{32,160},{48,176},{64,192},{80,208},{96,224},{112... | collective-permute-start | bytes 98312 | tf_op jit(solution)/shard_map/ppermute | solution.py:53
  252.8 6.9 %collective-permute-start.30 = (f32[8,8,128]{2,1,0:T(8,128)S(1)}, f32[8,8,128]{2,1,0:T(8,128)S(1)}, u32[]{:S(2)}, u32[]{:S(2)}) collective-permute-start(f32[8,8,128]{2,1,0:T(8,128)S(1)} %get-tuple-element.72), channel_id=1, source_target_pairs={{0,256},{16,272},{32,288},{48,304},{64,320},{80,336},{96,352},{112... | collective-permute-start | bytes 98312 | tf_op jit(solution)/shard_map/ppermute | solution.py:53
  257.7 5.9 %collective-permute-start.31 = (f32[8,8,128]{2,1,0:T(8,128)S(1)}, f32[8,8,128]{2,1,0:T(8,128)S(1)}, u32[]{:S(2)}, u32[]{:S(2)}) collective-permute-start(f32[8,8,128]{2,1,0:T(8,128)S(1)} %get-tuple-element.71), channel_id=1, source_target_pairs={{0,384},{16,400},{32,416},{48,432},{64,448},{80,464},{96,480},{112... | collective-permute-start | bytes 98312 | tf_op jit(solution)/shard_map/ppermute | solution.py:53
  263.6 11.4 %collective-permute-start.32 = (f32[2,8,128]{2,1,0:T(8,128)S(1)}, f32[2,8,128]{2,1,0:T(8,128)S(1)}, u32[]{:S(2)}, u32[]{:S(2)}) collective-permute-start(f32[2,8,128]{2,1,0:T(8,128)S(1)} %get-tuple-element.86), channel_id=1, source_target_pairs={{0,32},{16,48},{32,0},{48,16},{64,96},{80,112},{96,64},{112,80},{1... | collective-permute-start | bytes 24584 | tf_op jit(solution)/shard_map/ppermute | solution.py:53
  266.1 9.0 %collective-permute-start.33 = (f32[2,8,128]{2,1,0:T(8,128)S(1)}, f32[2,8,128]{2,1,0:T(8,128)S(1)}, u32[]{:S(2)}, u32[]{:S(2)}) collective-permute-start(f32[2,8,128]{2,1,0:T(8,128)S(1)} %get-tuple-element.88), channel_id=1, source_target_pairs={{0,64},{16,80},{32,96},{48,112},{64,0},{80,16},{96,32},{112,48},{1... | collective-permute-start | bytes 24584 | tf_op jit(solution)/shard_map/ppermute | solution.py:53
  271.0 6.5 %collective-permute-start.34 = (f32[2,8,128]{2,1,0:T(8,128)S(1)}, f32[2,8,128]{2,1,0:T(8,128)S(1)}, u32[]{:S(2)}, u32[]{:S(2)}) collective-permute-start(f32[2,8,128]{2,1,0:T(8,128)S(1)} %get-tuple-element.87), channel_id=1, source_target_pairs={{0,96},{16,112},{32,64},{48,80},{64,32},{80,48},{96,0},{112,16},{1... | collective-permute-start | bytes 24584 | tf_op jit(solution)/shard_map/ppermute | solution.py:53
  277.6 4.4 collective-permute-start.35
  303.8 15.1 %collective-permute-start.36 = (f32[2,128]{1,0:T(2,128)S(1)}, f32[2,128]{1,0:T(2,128)}, u32[]{:S(2)}, u32[]{:S(2)}) collective-permute-start(f32[2,128]{1,0:T(2,128)S(1)} %reduce_sum.114), channel_id=1, source_target_pairs={{0,128},{16,144},{32,160},{48,176},{64,192},{80,208},{96,224},{112... | collective-permute-start | bytes 3080 | tf_op jit(solution)/shard_map/ppermute | solution.py:33
  305.8 13.2 %collective-permute-start.37 = (f32[2,128]{1,0:T(2,128)S(1)}, f32[2,128]{1,0:T(2,128)}, u32[]{:S(2)}, u32[]{:S(2)}) collective-permute-start(f32[2,128]{1,0:T(2,128)S(1)} %reduce_sum.114), channel_id=1, source_target_pairs={{0,256},{16,272},{32,288},{48,304},{64,320},{80,336},{96,352},{112... | collective-permute-start | bytes 3080 | tf_op jit(solution)/shard_map/ppermute | solution.py:33
  310.5 8.4 %collective-permute-start.38 = (f32[2,128]{1,0:T(2,128)S(1)}, f32[2,128]{1,0:T(2,128)}, u32[]{:S(2)}, u32[]{:S(2)}) collective-permute-start(f32[2,128]{1,0:T(2,128)S(1)} %reduce_sum.114), channel_id=1, source_target_pairs={{0,384},{16,400},{32,416},{48,432},{64,448},{80,464},{96,480},{112... | collective-permute-start | bytes 3080 | tf_op jit(solution)/shard_map/ppermute | solution.py:33
  315.3 24.9 %collective-permute-start.42 = (f32[2,128,128]{2,1,0:T(8,128)}, f32[2,128,128]{2,1,0:T(8,128)S(1)}, u32[]{:S(2)}, u32[]{:S(2)}) collective-permute-start(f32[2,128,128]{2,1,0:T(8,128)} %get-tuple-element.58), channel_id=1, source_target_pairs={{0,16},{16,32},{32,48},{48,64},{64,80},{80,96},{96,112},{112,128},... | collective-permute-start | bytes 393224 | tf_op jit(solution)/shard_map/ppermute | solution.py:12
  317.6 22.6 %collective-permute-start.43 = (f32[2,128,128]{2,1,0:T(8,128)}, f32[2,128,128]{2,1,0:T(8,128)S(1)}, u32[]{:S(2)}, u32[]{:S(2)}) collective-permute-start(f32[2,128,128]{2,1,0:T(8,128)} %get-tuple-element.59), channel_id=1, source_target_pairs={{16,0},{32,16},{48,32},{64,48},{80,64},{96,80},{112,96},{128,112},... | collective-permute-start | bytes 393224 | tf_op jit(solution)/shard_map/ppermute | solution.py:12
  320.2 13.4 %collective-permute-start.39 = (f32[2,128]{1,0:T(2,128)S(1)}, f32[2,128]{1,0:T(2,128)S(1)}, u32[]{:S(2)}, u32[]{:S(2)}) collective-permute-start(f32[2,128]{1,0:T(2,128)S(1)} %fusion.256), channel_id=1, source_target_pairs={{0,32},{16,48},{32,0},{48,16},{64,96},{80,112},{96,64},{112,80},{1... | collective-permute-start | bytes 3080 | tf_op jit(solution)/shard_map/ppermute | solution.py:33
  326.4 10.0 %collective-permute-start.40 = (f32[2,128]{1,0:T(2,128)S(1)}, f32[2,128]{1,0:T(2,128)S(1)}, u32[]{:S(2)}, u32[]{:S(2)}) collective-permute-start(f32[2,128]{1,0:T(2,128)S(1)} %fusion.256), channel_id=1, source_target_pairs={{0,64},{16,80},{32,96},{48,112},{64,0},{80,16},{96,32},{112,48},{1... | collective-permute-start | bytes 3080 | tf_op jit(solution)/shard_map/ppermute | solution.py:33
  330.2 9.4 %collective-permute-start.41 = (f32[2,128]{1,0:T(2,128)S(1)}, f32[2,128]{1,0:T(2,128)S(1)}, u32[]{:S(2)}, u32[]{:S(2)}) collective-permute-start(f32[2,128]{1,0:T(2,128)S(1)} %fusion.256), channel_id=1, source_target_pairs={{0,96},{16,112},{32,64},{48,80},{64,32},{80,48},{96,0},{112,16},{1... | collective-permute-start | bytes 3080 | tf_op jit(solution)/shard_map/ppermute | solution.py:33
  333.6 6.6 %collective-permute-start.44 = (f32[2,128,128]{2,1,0:T(8,128)}, f32[2,128,128]{2,1,0:T(8,128)S(1)}, u32[]{:S(2)}, u32[]{:S(2)}) collective-permute-start(f32[2,128,128]{2,1,0:T(8,128)} %get-tuple-element.61), channel_id=1, source_target_pairs={{0,1},{1,2},{2,3},{3,4},{4,5},{5,6},{6,7},{7,8},{8,9},{9,10},{10,1... | collective-permute-start | bytes 393224 | tf_op jit(solution)/shard_map/ppermute | solution.py:12
  336.4 6.5 %collective-permute-start.45 = (f32[2,128,128]{2,1,0:T(8,128)}, f32[2,128,128]{2,1,0:T(8,128)S(1)}, u32[]{:S(2)}, u32[]{:S(2)}) collective-permute-start(f32[2,128,128]{2,1,0:T(8,128)} %get-tuple-element.60), channel_id=1, source_target_pairs={{1,0},{2,1},{3,2},{4,3},{5,4},{6,5},{7,6},{8,7},{9,8},{10,9},{11,1... | collective-permute-start | bytes 393224 | tf_op jit(solution)/shard_map/ppermute | solution.py:12
  372.2 10.7 %collective-permute-start.47 = (f32[8,8,128]{2,1,0:T(8,128)S(1)}, f32[8,8,128]{2,1,0:T(8,128)S(1)}, u32[]{:S(2)}, u32[]{:S(2)}) collective-permute-start(f32[8,8,128]{2,1,0:T(8,128)S(1)} %get-tuple-element.67), channel_id=1, source_target_pairs={{0,128},{16,144},{32,160},{48,176},{64,192},{80,208},{96,224},{112... | collective-permute-start | bytes 98312 | tf_op jit(solution)/shard_map/ppermute | solution.py:53
  375.2 7.8 %collective-permute-start.48 = (f32[8,8,128]{2,1,0:T(8,128)S(1)}, f32[8,8,128]{2,1,0:T(8,128)S(1)}, u32[]{:S(2)}, u32[]{:S(2)}) collective-permute-start(f32[8,8,128]{2,1,0:T(8,128)S(1)} %get-tuple-element.69), channel_id=1, source_target_pairs={{0,256},{16,272},{32,288},{48,304},{64,320},{80,336},{96,352},{112... | collective-permute-start | bytes 98312 | tf_op jit(solution)/shard_map/ppermute | solution.py:53
  381.0 5.9 %collective-permute-start.49 = (f32[8,8,128]{2,1,0:T(8,128)S(1)}, f32[8,8,128]{2,1,0:T(8,128)S(1)}, u32[]{:S(2)}, u32[]{:S(2)}) collective-permute-start(f32[8,8,128]{2,1,0:T(8,128)S(1)} %get-tuple-element.68), channel_id=1, source_target_pairs={{0,384},{16,400},{32,416},{48,432},{64,448},{80,464},{96,480},{112... | collective-permute-start | bytes 98312 | tf_op jit(solution)/shard_map/ppermute | solution.py:53
  386.9 11.4 %collective-permute-start.50 = (f32[2,8,128]{2,1,0:T(8,128)S(1)}, f32[2,8,128]{2,1,0:T(8,128)S(1)}, u32[]{:S(2)}, u32[]{:S(2)}) collective-permute-start(f32[2,8,128]{2,1,0:T(8,128)S(1)} %get-tuple-element.83), channel_id=1, source_target_pairs={{0,32},{16,48},{32,0},{48,16},{64,96},{80,112},{96,64},{112,80},{1... | collective-permute-start | bytes 24584 | tf_op jit(solution)/shard_map/ppermute | solution.py:53
  388.8 9.5 %collective-permute-start.51 = (f32[2,8,128]{2,1,0:T(8,128)S(1)}, f32[2,8,128]{2,1,0:T(8,128)S(1)}, u32[]{:S(2)}, u32[]{:S(2)}) collective-permute-start(f32[2,8,128]{2,1,0:T(8,128)S(1)} %get-tuple-element.85), channel_id=1, source_target_pairs={{0,64},{16,80},{32,96},{48,112},{64,0},{80,16},{96,32},{112,48},{1... | collective-permute-start | bytes 24584 | tf_op jit(solution)/shard_map/ppermute | solution.py:53
  392.5 7.1 %collective-permute-start.52 = (f32[2,8,128]{2,1,0:T(8,128)S(1)}, f32[2,8,128]{2,1,0:T(8,128)S(1)}, u32[]{:S(2)}, u32[]{:S(2)}) collective-permute-start(f32[2,8,128]{2,1,0:T(8,128)S(1)} %get-tuple-element.84), channel_id=1, source_target_pairs={{0,96},{16,112},{32,64},{48,80},{64,32},{80,48},{96,0},{112,16},{1... | collective-permute-start | bytes 24584 | tf_op jit(solution)/shard_map/ppermute | solution.py:53
  399.6 5.2 %collective-permute-start.53 = (f32[1,8,128]{2,1,0:T(8,128)S(1)}, f32[1,8,128]{2,1,0:T(8,128)S(1)}, u32[]{:S(2)}, u32[]{:S(2)}) collective-permute-start(f32[1,8,128]{2,1,0:T(8,128)S(1)} %fusion.204), channel_id=1, source_target_pairs={{0,16},{16,0},{32,48},{48,32},{64,80},{80,64},{96,112},{112,96},{1... | collective-permute-start | bytes 12296 | tf_op jit(solution)/shard_map/ppermute | solution.py:53
  425.7 16.2 %collective-permute-start.54 = (f32[2,128]{1,0:T(2,128)S(1)}, f32[2,128]{1,0:T(2,128)S(1)}, u32[]{:S(2)}, u32[]{:S(2)}) collective-permute-start(f32[2,128]{1,0:T(2,128)S(1)} %reduce_sum.118), channel_id=1, source_target_pairs={{0,128},{16,144},{32,160},{48,176},{64,192},{80,208},{96,224},{112... | collective-permute-start | bytes 3080 | tf_op jit(solution)/shard_map/ppermute | solution.py:33
  427.7 14.3 %collective-permute-start.55 = (f32[2,128]{1,0:T(2,128)S(1)}, f32[2,128]{1,0:T(2,128)S(1)}, u32[]{:S(2)}, u32[]{:S(2)}) collective-permute-start(f32[2,128]{1,0:T(2,128)S(1)} %reduce_sum.118), channel_id=1, source_target_pairs={{0,256},{16,272},{32,288},{48,304},{64,320},{80,336},{96,352},{112... | collective-permute-start | bytes 3080 | tf_op jit(solution)/shard_map/ppermute | solution.py:33
  432.7 9.2 %collective-permute-start.56 = (f32[2,128]{1,0:T(2,128)S(1)}, f32[2,128]{1,0:T(2,128)S(1)}, u32[]{:S(2)}, u32[]{:S(2)}) collective-permute-start(f32[2,128]{1,0:T(2,128)S(1)} %reduce_sum.118), channel_id=1, source_target_pairs={{0,384},{16,400},{32,416},{48,432},{64,448},{80,464},{96,480},{112... | collective-permute-start | bytes 3080 | tf_op jit(solution)/shard_map/ppermute | solution.py:33
  437.0 23.8 %collective-permute-start.60 = (f32[2,128,128]{2,1,0:T(8,128)}, f32[2,128,128]{2,1,0:T(8,128)S(1)}, u32[]{:S(2)}, u32[]{:S(2)}) collective-permute-start(f32[2,128,128]{2,1,0:T(8,128)} %get-tuple-element.54), channel_id=1, source_target_pairs={{0,16},{16,32},{32,48},{48,64},{64,80},{80,96},{96,112},{112,128},... | collective-permute-start | bytes 393224 | tf_op jit(solution)/shard_map/ppermute | solution.py:12
  440.4 20.5 %collective-permute-start.61 = (f32[2,128,128]{2,1,0:T(8,128)}, f32[2,128,128]{2,1,0:T(8,128)S(1)}, u32[]{:S(2)}, u32[]{:S(2)}) collective-permute-start(f32[2,128,128]{2,1,0:T(8,128)} %get-tuple-element.55), channel_id=1, source_target_pairs={{16,0},{32,16},{48,32},{64,48},{80,64},{96,80},{112,96},{128,112},... | collective-permute-start | bytes 393224 | tf_op jit(solution)/shard_map/ppermute | solution.py:12
  442.5 12.3 %collective-permute-start.57 = (f32[2,128]{1,0:T(2,128)S(1)}, f32[2,128]{1,0:T(2,128)S(1)}, u32[]{:S(2)}, u32[]{:S(2)}) collective-permute-start(f32[2,128]{1,0:T(2,128)S(1)} %fusion.254), channel_id=1, source_target_pairs={{0,32},{16,48},{32,0},{48,16},{64,96},{80,112},{96,64},{112,80},{1... | collective-permute-start | bytes 3080 | tf_op jit(solution)/shard_map/ppermute | solution.py:33
  446.3 11.1 %collective-permute-start.58 = (f32[2,128]{1,0:T(2,128)S(1)}, f32[2,128]{1,0:T(2,128)S(1)}, u32[]{:S(2)}, u32[]{:S(2)}) collective-permute-start(f32[2,128]{1,0:T(2,128)S(1)} %fusion.254), channel_id=1, source_target_pairs={{0,64},{16,80},{32,96},{48,112},{64,0},{80,16},{96,32},{112,48},{1... | collective-permute-start | bytes 3080 | tf_op jit(solution)/shard_map/ppermute | solution.py:33
  452.9 7.3 %collective-permute-start.59 = (f32[2,128]{1,0:T(2,128)S(1)}, f32[2,128]{1,0:T(2,128)S(1)}, u32[]{:S(2)}, u32[]{:S(2)}) collective-permute-start(f32[2,128]{1,0:T(2,128)S(1)} %fusion.254), channel_id=1, source_target_pairs={{0,96},{16,112},{32,64},{48,80},{64,32},{80,48},{96,0},{112,16},{1... | collective-permute-start | bytes 3080 | tf_op jit(solution)/shard_map/ppermute | solution.py:33
  454.9 6.0 %collective-permute-start.62 = (f32[2,128,128]{2,1,0:T(8,128)}, f32[2,128,128]{2,1,0:T(8,128)S(1)}, u32[]{:S(2)}, u32[]{:S(2)}) collective-permute-start(f32[2,128,128]{2,1,0:T(8,128)} %get-tuple-element.57), channel_id=1, source_target_pairs={{0,1},{1,2},{2,3},{3,4},{4,5},{5,6},{6,7},{7,8},{8,9},{9,10},{10,1... | collective-permute-start | bytes 393224 | tf_op jit(solution)/shard_map/ppermute | solution.py:12
  457.4 6.3 %collective-permute-start.63 = (f32[2,128,128]{2,1,0:T(8,128)S(1)}, f32[2,128,128]{2,1,0:T(8,128)S(1)}, u32[]{:S(2)}, u32[]{:S(2)}) collective-permute-start(f32[2,128,128]{2,1,0:T(8,128)S(1)} %get-tuple-element.56), channel_id=1, source_target_pairs={{1,0},{2,1},{3,2},{4,3},{5,4},{6,5},{7,6},{8,7},{9,8},{10,9},{11,1... | collective-permute-start | bytes 393224 | tf_op jit(solution)/shard_map/ppermute | solution.py:12
  465.1 4.4 collective-permute-start.64
  (24 other events, 520.8 us)

commit v5 on v3

--- a/solution.py
+++ b/solution.py
@@ -22,20 +22,6 @@
         value = value + lax.ppermute(value, "gx", [(i, i ^ step) for i in range(count)])
         step *= 2
     return value
-
-
-def scatter_rows(stacked, axis, rows):
-    count = lax.axis_size(axis)
-    index = lax.axis_index(axis)
-    blocks = stacked.reshape(count, rows, stacked.shape[-1])
-    half = count // 2
-    while half >= 1:
-        upper = (index // half) % 2 == 1
-        keep = jnp.where(upper, blocks[half:], blocks[:half])
-        send = jnp.where(upper, blocks[:half], blocks[half:])
-        blocks = keep + lax.ppermute(send, axis, [(i, i ^ half) for i in range(count)])
-        half //= 2
-    return blocks[0]
 
 
 def pass_columns(rows, offset):
@@ -114,7 +100,8 @@
         coarse = jnp.dot(vectors, rounded, preferred_element_type=jnp.float32)
         line = lax.all_gather(coarse, "gy", axis=0, tiled=True)
         partial = jnp.dot(coarse_block, line, precision=lax.Precision.HIGHEST)
-        solved = scatter_rows(partial, "gx", depth)
+        pieces = lax.all_to_all(partial, "gx", 0, 0, tiled=True)
+        solved = jnp.sum(pieces.reshape(count_x, depth, pieces.shape[-1]), axis=0)
         return result + jnp.dot(vectors_wide, solved, precision=lax.Precision.HIGHEST)
 
     solution = jnp.zeros(rhs_wide.shape, jnp.float32)

time: 477 us -> 401 us (0.84)
  starting transfers between devices: 218 us -> 141 us
    ppermute x20 -> x0, starting transfers between devices: 77.9 us -> none  [scatter_rows(): lax.ppermute(send, axis, [(i, i ^ half) for i in range(count)])]
    ppermute x20 -> x0, waiting for transfers between devices: 35.1 us -> none  [scatter_rows(): lax.ppermute(send, axis, [(i, i ^ half) for i in range(count)])]
    all_to_all x0 -> x4, waiting for transfers between devices: none -> 24.7 us  [apply_prec(): pieces = lax.all_to_all(partial, 'gx', 0, 0, tiled=True)]
    all_to_all x0 -> x4, starting transfers between devices: none -> 24.4 us  [apply_prec(): pieces = lax.all_to_all(partial, 'gx', 0, 0, tiled=True)]
    ppermute x15, starting transfers between devices: 77.6 us -> 63.9 us  [total_over_mesh(): lax.ppermute(value, 'gx', [(i, i ^ step) for i in range(count)])]
    ppermute x16, starting transfers between devices: 51.5 us -> 41.8 us  [from_behind(): lax.ppermute(value, axis, [(source, source + steps) for source in range(l...]
    ppermute x15, waiting for transfers between devices: 14.1 us -> 20.9 us  [total_over_mesh(): lax.ppermute(value, 'gx', [(i, i ^ step) for i in range(count)])]
  transfers between devices with their start and end apart: 52 -> 36, of which waited for: 32 -> 15; matrix products, arithmetic and copies ran while one was open for 3% -> 4% of each run, Pallas kernels for 0% -> 0%
where the time goes in v5:
time: 401 us; the launch traced here: 395 us
  starting transfers between devices  141 us (35%)
  blocking collectives  131 us (33%)
  waiting for transfers between devices  46.5 us (12%)
  local copies, waits for them, and re-layouts  31.3 us (8%)
  other arithmetic  28 us (7%)
  matrix products  14.2 us (4%)
    all_gather x4, blocking collectives, apply_prec(): line = lax.all_gather(coarse, 'gy', axis=0, tiled=True)  81.2 us
    ppermute x15, starting transfers between devices, total_over_mesh(): lax.ppermute(value, 'gx', [(i, i ^ step) for i in range(count)])  63.9 us
    all_gather x3, blocking collectives, total_over_mesh(): value = jnp.sum(lax.all_gather(value, 'gy', axis=0), axis=0)  50 us
    ppermute x16, starting transfers between devices, from_behind(): lax.ppermute(value, axis, [(source, source + steps) for source in range(l...  41.8 us
    all_to_all x4, waiting for transfers between devices, apply_prec(): pieces = lax.all_to_all(partial, 'gx', 0, 0, tiled=True)  24.7 us
    all_to_all x4, starting transfers between devices, apply_prec(): pieces = lax.all_to_all(partial, 'gx', 0, 0, tiled=True)  24.4 us
    ppermute x15, waiting for transfers between devices, total_over_mesh(): lax.ppermute(value, 'gx', [(i, i ^ step) for i in range(count)])  20.9 us
    gather x2, local copies, waits for them, and re-layouts, shards(): coarse_cols = jnp.take(coarse_inverse, coarse_map, axis=1)  17.9 us
  transfers between devices with their start and end apart: 36, of which 15 were waited for; matrix products, arithmetic and copies ran while one was open for 4% of the time, Pallas kernels for 0%

profile of v5, /device:TPU:1, one launch (start us, length us, event | category | flops | bytes accessed | tf_op | source)
XLA Modules:
  0.0 395.2 jit_solution(9644150382744015353)
XLA Ops:
  2.2 2.9 copy.67
  5.1 15.8 %gather_fusion = f32[4096,8]{1,0:T(8,128)} fusion(f32[8,4096]{0,1:T(8,128)} %copy.67, s32[4096]{0:T(1024)S(1)} %fusion.143), kind=kCustom, calls=%fused_computation | custom fusion | bytes 278528 | tf_op jit(solution)/shard_map/jit(_take)/gather | solution.py:59
  20.9 2.2 copy.68
  23.7 10.5 %all-to-all-start = ((f32[8,32,128]{2,0,1:T(8,128)}), f32[8,32,128]{2,0,1:T(8,128)S(1)}, u32[]{:S(2)}, u32[]{:S(2)}) async-start(f32[8,32,128]{2,0,1:T(8,128)} %broadcast_select_fusion), calls=%async_computation | async-start | bytes 262144 | tf_op jit(solution)/shard_map/all_to_all | solution.py:60
  34.4 24.1 %all_gather.30 = f32[128,128]{1,0:T(8,128)S(1)} all-gather(f32[8,128]{1,0:T(8,128)S(1)} %fusion.141), channel_id=1, replica_groups=mesh['gx'=32,'gy'=16] {'gy'}, dimensions={0}, use_global_device_ids=true | all-gather | bytes 69632 | tf_op jit(solution)/shard_map/all_gather | solution.py:101
  59.5 9.5 %all-to-all-start.1 = ((f32[32,8,128]{2,1,0:T(8,128)}), f32[32,8,128]{2,1,0:T(8,128)S(1)}, u32[]{:S(2)}, u32[]{:S(2)}) async-start(f32[32,8,128]{2,1,0:T(8,128)} %fusion.121), calls=%async_computation.1 | async-start | bytes 262144 | tf_op jit(solution)/shard_map/all_to_all | solution.py:103
  69.1 9.1 %all-to-all-done.1 = f32[32,8,128]{2,1,0:T(8,128)S(1)} async-done(((f32[32,8,128]{2,1,0:T(8,128)}), f32[32,8,128]{2,1,0:T(8,128)S(1)}, u32[]{:S(2)}, u32[]{:S(2)}) %all-to-all-start.1) | async-done | bytes 131104 | tf_op jit(solution)/shard_map/all_to_all | solution.py:103
  80.6 3.6 collective-permute-start
  85.4 2.5 collective-permute-start.2
  87.9 2.3 collective-permute-start.3
  90.3 2.0 fusion.37
  93.3 3.5 scatter_fusion
  97.0 15.0 %all_gather.31 = f32[128,128]{1,0:T(8,128)S(1)} all-gather(f32[8,128]{1,0:T(8,128)S(1)} %convolution_bitcast_fusion.6), channel_id=1, replica_groups=mesh['gx'=32,'gy'=16] {'gy'}, dimensions={0}, use_global_device_ids=true | all-gather | bytes 69632 | tf_op jit(solution)/shard_map/all_gather | solution.py:101
  112.9 6.4 %all-to-all-start.2 = ((f32[32,8,128]{2,1,0:T(8,128)}), f32[32,8,128]{2,1,0:T(8,128)S(1)}, u32[]{:S(2)}, u32[]{:S(2)}) async-start(f32[32,8,128]{2,1,0:T(8,128)} %fusion.119), calls=%async_computation.2 | async-start | bytes 262144 | tf_op jit(solution)/shard_map/all_to_all | solution.py:103
  120.4 8.1 %all-to-all-done.2 = f32[32,8,128]{2,1,0:T(8,128)S(1)} async-done(((f32[32,8,128]{2,1,0:T(8,128)}), f32[32,8,128]{2,1,0:T(8,128)S(1)}, u32[]{:S(2)}, u32[]{:S(2)}) %all-to-all-start.2) | async-done | bytes 131104 | tf_op jit(solution)/shard_map/all_to_all | solution.py:103
  129.6 1.6 gather_fusion.3
  131.2 1.7 fusion.102
  132.9 3.5 collective-permute-start.8
  137.8 3.7 collective-permute-start.10
  141.5 1.9 collective-permute-start.11
  143.4 17.3 %all-gather.3 = f32[16,2,128]{2,1,0:T(2,128)S(1)} all-gather(f32[1,2,128]{2,1,0:T(2,128)S(1)} %maximum_bitcast_fusion), channel_id=2, replica_groups=mesh['gx'=32,'gy'=16] {'gy'}, dimensions={0}, use_global_device_ids=true | all-gather | bytes 17408 | tf_op jit(solution)/shard_map/all_gather | solution.py:16
  160.8 4.3 %collective-permute-start.4 = (f32[2,128]{1,0:T(2,128)S(1)}, f32[2,128]{1,0:T(2,128)S(1)}, u32[]{:S(2)}, u32[]{:S(2)}) collective-permute-start(f32[2,128]{1,0:T(2,128)S(1)} %reduce_sum.148), channel_id=1, source_target_pairs={{0,16},{16,0},{32,48},{48,32},{64,80},{80,64},{96,112},{112,96},{1... | collective-permute-start | bytes 3080 | tf_op jit(solution)/shard_map/ppermute | solution.py:22
  166.0 3.4 collective-permute-start.5
  169.4 1.8 collective-permute-done.5
  171.2 4.7 %collective-permute-start.6 = (f32[2,128]{1,0:T(2,128)S(1)}, f32[2,128]{1,0:T(2,128)S(1)}, u32[]{:S(2)}, u32[]{:S(2)}) collective-permute-start(f32[2,128]{1,0:T(2,128)S(1)} %add.175), channel_id=1, source_target_pairs={{0,64},{16,80},{32,96},{48,112},{64,0},{80,16},{96,32},{112,48},{1... | collective-permute-start | bytes 3080 | tf_op jit(solution)/shard_map/ppermute | solution.py:22
  175.9 3.5 collective-permute-done.6
  179.4 4.9 %collective-permute-start.7 = (f32[2,128]{1,0:T(2,128)S(1)}, f32[2,128]{1,0:T(2,128)S(1)}, u32[]{:S(2)}, u32[]{:S(2)}) collective-permute-start(f32[2,128]{1,0:T(2,128)S(1)} %add.176), channel_id=1, source_target_pairs={{0,128},{16,144},{32,160},{48,176},{64,192},{80,208},{96,224},{112... | collective-permute-start | bytes 3080 | tf_op jit(solution)/shard_map/ppermute | solution.py:22
  185.6 3.9 collective-permute-start.12
  189.6 2.0 collective-permute-done.12
  193.1 4.1 %scatter_fusion.1 = f32[896,128]{1,0:T(8,128)S(1)} fusion(f32[896,128]{1,0:T(8,128)S(1)} %fusion.40, s32[512]{0:T(512)S(1)} %bitcast.376, f32[512,128]{1,0:T(8,128)} %bitcast.351), kind=kCustom, calls=%fused_computation.9 | custom fusion | flops 65536 | bytes 788480 | tf_op jit(solution)/shard_map/scatter-add | solution.py:81
  197.4 20.6 %all_gather.34 = f32[128,128]{1,0:T(8,128)S(1)} all-gather(f32[8,128]{1,0:T(8,128)S(1)} %convolution_bitcast_fusion.5), channel_id=1, replica_groups=mesh['gx'=32,'gy'=16] {'gy'}, dimensions={0}, use_global_device_ids=true | all-gather | bytes 69632 | tf_op jit(solution)/shard_map/all_gather | solution.py:101
  218.9 4.2 %all-to-all-start.3 = ((f32[32,8,128]{2,1,0:T(8,128)}), f32[32,8,128]{2,1,0:T(8,128)S(1)}, u32[]{:S(2)}, u32[]{:S(2)}) async-start(f32[32,8,128]{2,1,0:T(8,128)} %fusion.117), calls=%async_computation.3 | async-start | bytes 262144 | tf_op jit(solution)/shard_map/all_to_all | solution.py:103
  223.2 1.6 gather_fusion.4
  224.8 7.5 %all-to-all-done.3 = f32[32,8,128]{2,1,0:T(8,128)S(1)} async-done(((f32[32,8,128]{2,1,0:T(8,128)}), f32[32,8,128]{2,1,0:T(8,128)S(1)}, u32[]{:S(2)}, u32[]{:S(2)}) %all-to-all-start.3) | async-done | bytes 131104 | tf_op jit(solution)/shard_map/all_to_all | solution.py:103
  233.4 1.6 gather_fusion.5
  235.0 1.7 fusion.96
  236.8 3.5 collective-permute-start.17
  241.6 3.9 collective-permute-start.19
  245.6 1.9 collective-permute-start.20
  247.5 16.2 %all-gather.4 = f32[16,2,128]{2,1,0:T(2,128)S(1)} all-gather(f32[1,2,128]{2,1,0:T(2,128)S(1)} %maximum_bitcast_fusion.1), channel_id=3, replica_groups=mesh['gx'=32,'gy'=16] {'gy'}, dimensions={0}, use_global_device_ids=true | all-gather | bytes 17408 | tf_op jit(solution)/shard_map/all_gather | solution.py:16
  263.8 4.3 %collective-permute-start.13 = (f32[2,128]{1,0:T(2,128)S(1)}, f32[2,128]{1,0:T(2,128)S(1)}, u32[]{:S(2)}, u32[]{:S(2)}) collective-permute-start(f32[2,128]{1,0:T(2,128)S(1)} %reduce_sum.153), channel_id=1, source_target_pairs={{0,16},{16,0},{32,48},{48,32},{64,80},{80,64},{96,112},{112,96},{1... | collective-permute-start | bytes 3080 | tf_op jit(solution)/shard_map/ppermute | solution.py:22
  269.0 3.4 collective-permute-start.14
  272.4 1.8 collective-permute-done.14
  274.2 4.7 %collective-permute-start.15 = (f32[2,128]{1,0:T(2,128)S(1)}, f32[2,128]{1,0:T(2,128)S(1)}, u32[]{:S(2)}, u32[]{:S(2)}) collective-permute-start(f32[2,128]{1,0:T(2,128)S(1)} %add.187), channel_id=1, source_target_pairs={{0,64},{16,80},{32,96},{48,112},{64,0},{80,16},{96,32},{112,48},{1... | collective-permute-start | bytes 3080 | tf_op jit(solution)/shard_map/ppermute | solution.py:22
  278.9 3.5 collective-permute-done.15
  282.4 4.9 %collective-permute-start.16 = (f32[2,128]{1,0:T(2,128)S(1)}, f32[2,128]{1,0:T(2,128)S(1)}, u32[]{:S(2)}, u32[]{:S(2)}) collective-permute-start(f32[2,128]{1,0:T(2,128)S(1)} %add.188), channel_id=1, source_target_pairs={{0,128},{16,144},{32,160},{48,176},{64,192},{80,208},{96,224},{112... | collective-permute-start | bytes 3080 | tf_op jit(solution)/shard_map/ppermute | solution.py:22
  288.6 3.8 collective-permute-start.21
  292.5 2.1 collective-permute-done.21
  296.6 3.5 scatter_fusion.2
  300.2 21.5 %all_gather.37 = f32[128,128]{1,0:T(8,128)S(1)} all-gather(f32[8,128]{1,0:T(8,128)S(1)} %convolution_bitcast_fusion.4), channel_id=1, replica_groups=mesh['gx'=32,'gy'=16] {'gy'}, dimensions={0}, use_global_device_ids=true | all-gather | bytes 69632 | tf_op jit(solution)/shard_map/all_gather | solution.py:101
  322.7 4.2 %all-to-all-start.4 = ((f32[32,8,128]{2,1,0:T(8,128)}), f32[32,8,128]{2,1,0:T(8,128)S(1)}, u32[]{:S(2)}, u32[]{:S(2)}) async-start(f32[32,8,128]{2,1,0:T(8,128)} %fusion.115), calls=%async_computation.4 | async-start | bytes 262144 | tf_op jit(solution)/shard_map/all_to_all | solution.py:103
  328.0 1.6 gather_fusion.7
  329.6 1.7 fusion.90
  332.6 1.9 collective-permute-start.28
  334.6 3.0 collective-permute-start.29
  337.6 4.6 %collective-permute-start.26 = (f32[2,128,128]{2,1,0:T(8,128)}, f32[2,128,128]{2,1,0:T(8,128)}, u32[]{:S(2)}, u32[]{:S(2)}) collective-permute-start(f32[2,128,128]{2,1,0:T(8,128)} %get-tuple-element.18), channel_id=1, source_target_pairs={{0,16},{16,32},{32,48},{48,64},{64,80},{80,96},{96,112},{112,128},... | collective-permute-start | bytes 393224 | tf_op jit(solution)/shard_map/ppermute | solution.py:12
  343.4 16.5 %all-gather.5 = f32[16,2,128]{2,1,0:T(2,128)S(1)} all-gather(f32[1,2,128]{2,1,0:T(2,128)S(1)} %maximum_bitcast_fusion.2), channel_id=4, replica_groups=mesh['gx'=32,'gy'=16] {'gy'}, dimensions={0}, use_global_device_ids=true | all-gather | bytes 17408 | tf_op jit(solution)/shard_map/all_gather | solution.py:16
  359.9 2.9 collective-permute-start.22
  364.3 4.6 %collective-permute-start.23 = (f32[2,128]{1,0:T(2,128)S(1)}, f32[2,128]{1,0:T(2,128)S(1)}, u32[]{:S(2)}, u32[]{:S(2)}) collective-permute-start(f32[2,128]{1,0:T(2,128)S(1)} %add.199), channel_id=1, source_target_pairs={{0,32},{16,48},{32,0},{48,16},{64,96},{80,112},{96,64},{112,80},{1... | collective-permute-start | bytes 3080 | tf_op jit(solution)/shard_map/ppermute | solution.py:22
  369.9 6.3 %collective-permute-start.24 = (f32[2,128]{1,0:T(2,128)S(1)}, f32[2,128]{1,0:T(2,128)S(1)}, u32[]{:S(2)}, u32[]{:S(2)}) collective-permute-start(f32[2,128]{1,0:T(2,128)S(1)} %add.200), channel_id=1, source_target_pairs={{0,64},{16,80},{32,96},{48,112},{64,0},{80,16},{96,32},{112,48},{1... | collective-permute-start | bytes 3080 | tf_op jit(solution)/shard_map/ppermute | solution.py:22
  376.2 1.9 collective-permute-done.24
  378.1 3.1 collective-permute-start.25
  383.2 4.8 %collective-permute-start.30 = (f32[2,128]{1,0:T(2,128)S(1)}, f32[2,128]{1,0:T(2,128)S(1)}, u32[]{:S(2)}, u32[]{:S(2)}) collective-permute-start(f32[2,128]{1,0:T(2,128)S(1)} %add_add_fusion), channel_id=1, source_target_pairs={{0,256},{16,272},{32,288},{48,304},{64,320},{80,336},{96,352},{112... | collective-permute-start | bytes 3080 | tf_op jit(solution)/shard_map/ppermute | solution.py:22
  390.8 3.5 scatter_fusion.3
  (142 shorter events, 34.8 us)
Async XLA Ops:
  0.6 77.9 %copy-start = (bf16[1,1,896,896]{3,2,1,0:T(8,128)(2,1)S(1)}, bf16[1,1,896,896]{3,2,1,0:T(8,128)(2,1)}, u32[]{:S(2)}) copy-start(bf16[1,1,896,896]{3,2,1,0:T(8,128)(2,1)} %param.13) | copy-start | bytes 4816900
  20.8 13.4 %copy-start.8 = (bf16[1,1,896,128]{3,2,1,0:T(8,128)(2,1)S(1)}, bf16[1,1,896,128]{3,2,1,0:T(8,128)(2,1)}, u32[]{:S(2)}) copy-start(bf16[1,1,896,128]{3,2,1,0:T(8,128)(2,1)} %param.10) | copy-start | bytes 688132
  20.8 13.4 %copy-start.14 = (bf16[1,1,8,896]{3,2,1,0:T(8,128)(2,1)S(1)}, bf16[1,1,8,896]{3,2,1,0:T(8,128)(2,1)}, u32[]{:S(2)}) copy-start(bf16[1,1,8,896]{3,2,1,0:T(8,128)(2,1)} %param.17) | copy-start | bytes 43012
  20.8 37.7 %copy-start.15 = (s32[1,1,4,128]{3,2,1,0:T(4,128)S(1)}, s32[1,1,4,128]{3,2,1,0:T(4,128)}, u32[]{:S(2)}) copy-start(s32[1,1,4,128]{3,2,1,0:T(4,128)} %param.16) | copy-start | bytes 6148
  20.8 48.1 %copy-start.16 = (f32[1,1,896]{2,1,0:T(1,128)S(1)}, f32[1,1,896]{2,1,0:T(1,128)}, u32[]{:S(2)}) copy-start(f32[1,1,896]{2,1,0:T(1,128)} %param.14) | copy-start | bytes 10756
  20.8 48.2 %copy-start.17 = (f32[1,1,896]{2,1,0:T(1,128)S(1)}, f32[1,1,896]{2,1,0:T(1,128)}, u32[]{:S(2)}) copy-start(f32[1,1,896]{2,1,0:T(1,128)} %param.12) | copy-start | bytes 10756
  23.7 34.8 %all-to-all-start = ((f32[8,32,128]{2,0,1:T(8,128)}), f32[8,32,128]{2,0,1:T(8,128)S(1)}, u32[]{:S(2)}, u32[]{:S(2)}) async-start(f32[8,32,128]{2,0,1:T(8,128)} %broadcast_select_fusion), calls=%async_computation | async-start | bytes 262144 | tf_op jit(solution)/shard_map/all_to_all | solution.py:60
  58.5 159.5 %copy-start.6 = (f32[8,32,128]{2,0,1:T(8,128)}, f32[8,32,128]{2,0,1:T(8,128)S(1)}, u32[]{:S(2)}) copy-start(f32[8,32,128]{2,0,1:T(8,128)S(1)} %all-to-all-done) | copy-start | bytes 393220
  59.5 18.7 %all-to-all-start.1 = ((f32[32,8,128]{2,1,0:T(8,128)}), f32[32,8,128]{2,1,0:T(8,128)S(1)}, u32[]{:S(2)}, u32[]{:S(2)}) async-start(f32[32,8,128]{2,1,0:T(8,128)} %fusion.121), calls=%async_computation.1 | async-start | bytes 262144 | tf_op jit(solution)/shard_map/all_to_all | solution.py:103
  79.2 14.0 %copy-start.10 = (bf16[1,1,4,128,128]{4,3,2,1,0:T(8,128)(2,1)S(1)}, bf16[1,1,4,128,128]{4,3,2,1,0:T(8,128)(2,1)}, u32[]{:S(2)}) copy-start(bf16[1,1,4,128,128]{4,3,2,1,0:T(8,128)(2,1)} %param.15) | copy-start | bytes 393220
  80.6 11.7 %collective-permute-start = (bf16[128,128]{1,0:T(8,128)(2,1)S(1)}, bf16[128,128]{1,0:T(8,128)(2,1)S(1)}, u32[]{:S(2)}, u32[]{:S(2)}) collective-permute-start(bf16[128,128]{1,0:T(8,128)(2,1)S(1)} %get-tuple-element.31), channel_id=1, source_target_pairs={{0,16},{16,32},{32,48},{48,64},{64,80},{80,96},{96,112},{112,128},... | collective-permute-start | bytes 98312 | tf_op jit(solution)/shard_map/ppermute | solution.py:12
  84.1 8.2 %collective-permute-start.1 = (bf16[128,128]{1,0:T(8,128)(2,1)S(1)}, bf16[128,128]{1,0:T(8,128)(2,1)S(1)}, u32[]{:S(2)}, u32[]{:S(2)}) collective-permute-start(bf16[128,128]{1,0:T(8,128)(2,1)S(1)} %get-tuple-element.33), channel_id=1, source_target_pairs={{16,0},{32,16},{48,32},{64,48},{80,64},{96,80},{112,96},{128,112},... | collective-permute-start | bytes 98312 | tf_op jit(solution)/shard_map/ppermute | solution.py:12
  85.4 6.9 %collective-permute-start.2 = (bf16[128,128]{1,0:T(8,128)(2,1)S(1)}, bf16[128,128]{1,0:T(8,128)(2,1)S(1)}, u32[]{:S(2)}, u32[]{:S(2)}) collective-permute-start(bf16[128,128]{1,0:T(8,128)(2,1)S(1)} %get-tuple-element.32), channel_id=1, source_target_pairs={{0,1},{1,2},{2,3},{3,4},{4,5},{5,6},{6,7},{7,8},{8,9},{9,10},{10,1... | collective-permute-start | bytes 98312 | tf_op jit(solution)/shard_map/ppermute | solution.py:12
  87.9 5.2 %collective-permute-start.3 = (bf16[128,128]{1,0:T(8,128)(2,1)S(1)}, bf16[128,128]{1,0:T(8,128)(2,1)S(1)}, u32[]{:S(2)}, u32[]{:S(2)}) collective-permute-start(bf16[128,128]{1,0:T(8,128)(2,1)S(1)} %get-tuple-element.34), channel_id=1, source_target_pairs={{1,0},{2,1},{3,2},{4,3},{5,4},{6,5},{7,6},{8,7},{9,8},{10,9},{11,1... | collective-permute-start | bytes 98312 | tf_op jit(solution)/shard_map/ppermute | solution.py:12
  112.9 15.6 %all-to-all-start.2 = ((f32[32,8,128]{2,1,0:T(8,128)}), f32[32,8,128]{2,1,0:T(8,128)S(1)}, u32[]{:S(2)}, u32[]{:S(2)}) async-start(f32[32,8,128]{2,1,0:T(8,128)} %fusion.119), calls=%async_computation.2 | async-start | bytes 262144 | tf_op jit(solution)/shard_map/all_to_all | solution.py:103
  132.9 51.4 %collective-permute-start.8 = (f32[2,128,128]{2,1,0:T(8,128)}, f32[2,128,128]{2,1,0:T(8,128)S(1)}, u32[]{:S(2)}, u32[]{:S(2)}) collective-permute-start(f32[2,128,128]{2,1,0:T(8,128)} %get-tuple-element.26), channel_id=1, source_target_pairs={{0,16},{16,32},{32,48},{48,64},{64,80},{80,96},{96,112},{112,128},... | collective-permute-start | bytes 393224 | tf_op jit(solution)/shard_map/ppermute | solution.py:12
  136.5 47.8 %collective-permute-start.9 = (f32[2,128,128]{2,1,0:T(8,128)}, f32[2,128,128]{2,1,0:T(8,128)S(1)}, u32[]{:S(2)}, u32[]{:S(2)}) collective-permute-start(f32[2,128,128]{2,1,0:T(8,128)} %get-tuple-element.27), channel_id=1, source_target_pairs={{16,0},{32,16},{48,32},{64,48},{80,64},{96,80},{112,96},{128,112},... | collective-permute-start | bytes 393224 | tf_op jit(solution)/shard_map/ppermute | solution.py:12
  137.8 46.5 %collective-permute-start.10 = (f32[2,128,128]{2,1,0:T(8,128)}, f32[2,128,128]{2,1,0:T(8,128)S(1)}, u32[]{:S(2)}, u32[]{:S(2)}) collective-permute-start(f32[2,128,128]{2,1,0:T(8,128)} %get-tuple-element.29), channel_id=1, source_target_pairs={{0,1},{1,2},{2,3},{3,4},{4,5},{5,6},{6,7},{7,8},{8,9},{9,10},{10,1... | collective-permute-start | bytes 393224 | tf_op jit(solution)/shard_map/ppermute | solution.py:12
  141.5 42.8 %collective-permute-start.11 = (f32[2,128,128]{2,1,0:T(8,128)}, f32[2,128,128]{2,1,0:T(8,128)S(1)}, u32[]{:S(2)}, u32[]{:S(2)}) collective-permute-start(f32[2,128,128]{2,1,0:T(8,128)} %get-tuple-element.28), channel_id=1, source_target_pairs={{1,0},{2,1},{3,2},{4,3},{5,4},{6,5},{7,6},{8,7},{9,8},{10,9},{11,1... | collective-permute-start | bytes 393224 | tf_op jit(solution)/shard_map/ppermute | solution.py:12
  160.8 5.2 %collective-permute-start.4 = (f32[2,128]{1,0:T(2,128)S(1)}, f32[2,128]{1,0:T(2,128)S(1)}, u32[]{:S(2)}, u32[]{:S(2)}) collective-permute-start(f32[2,128]{1,0:T(2,128)S(1)} %reduce_sum.148), channel_id=1, source_target_pairs={{0,16},{16,0},{32,48},{48,32},{64,80},{80,64},{96,112},{112,96},{1... | collective-permute-start | bytes 3080 | tf_op jit(solution)/shard_map/ppermute | solution.py:22
  166.0 5.2 %collective-permute-start.5 = (f32[2,128]{1,0:T(2,128)S(1)}, f32[2,128]{1,0:T(2,128)S(1)}, u32[]{:S(2)}, u32[]{:S(2)}) collective-permute-start(f32[2,128]{1,0:T(2,128)S(1)} %add.174), channel_id=1, source_target_pairs={{0,32},{16,48},{32,0},{48,16},{64,96},{80,112},{96,64},{112,80},{1... | collective-permute-start | bytes 3080 | tf_op jit(solution)/shard_map/ppermute | solution.py:22
  171.2 8.2 %collective-permute-start.6 = (f32[2,128]{1,0:T(2,128)S(1)}, f32[2,128]{1,0:T(2,128)S(1)}, u32[]{:S(2)}, u32[]{:S(2)}) collective-permute-start(f32[2,128]{1,0:T(2,128)S(1)} %add.175), channel_id=1, source_target_pairs={{0,64},{16,80},{32,96},{48,112},{64,0},{80,16},{96,32},{112,48},{1... | collective-permute-start | bytes 3080 | tf_op jit(solution)/shard_map/ppermute | solution.py:22
  179.4 6.2 %collective-permute-start.7 = (f32[2,128]{1,0:T(2,128)S(1)}, f32[2,128]{1,0:T(2,128)S(1)}, u32[]{:S(2)}, u32[]{:S(2)}) collective-permute-start(f32[2,128]{1,0:T(2,128)S(1)} %add.176), channel_id=1, source_target_pairs={{0,128},{16,144},{32,160},{48,176},{64,192},{80,208},{96,224},{112... | collective-permute-start | bytes 3080 | tf_op jit(solution)/shard_map/ppermute | solution.py:22
  185.6 6.9 %copy-start.1 = (bf16[1,1,896,896]{3,2,1,0:T(8,128)(2,1)S(1)}, bf16[1,1,896,896]{3,2,1,0:T(8,128)(2,1)}, u32[]{:S(2)}) copy-start(bf16[1,1,896,896]{3,2,1,0:T(8,128)(2,1)} %param.11) | copy-start | bytes 4816900
  185.6 5.9 %collective-permute-start.12 = (f32[2,128]{1,0:T(2,128)S(1)}, f32[2,128]{1,0:T(2,128)S(1)}, u32[]{:S(2)}, u32[]{:S(2)}) collective-permute-start(f32[2,128]{1,0:T(2,128)S(1)} %add_add_fusion.2), channel_id=1, source_target_pairs={{0,256},{16,272},{32,288},{48,304},{64,320},{80,336},{96,352},{112... | collective-permute-start | bytes 3080 | tf_op jit(solution)/shard_map/ppermute | solution.py:22
  218.9 13.4 %all-to-all-start.3 = ((f32[32,8,128]{2,1,0:T(8,128)}), f32[32,8,128]{2,1,0:T(8,128)S(1)}, u32[]{:S(2)}, u32[]{:S(2)}) async-start(f32[32,8,128]{2,1,0:T(8,128)} %fusion.117), calls=%async_computation.3 | async-start | bytes 262144 | tf_op jit(solution)/shard_map/all_to_all | solution.py:103
  233.4 3.4 copy-start.4
  233.4 1.7 copy-start.13
  236.8 50.5 %collective-permute-start.17 = (f32[2,128,128]{2,1,0:T(8,128)}, f32[2,128,128]{2,1,0:T(8,128)S(1)}, u32[]{:S(2)}, u32[]{:S(2)}) collective-permute-start(f32[2,128,128]{2,1,0:T(8,128)} %get-tuple-element.22), channel_id=1, source_target_pairs={{0,16},{16,32},{32,48},{48,64},{64,80},{80,96},{96,112},{112,128},... | collective-permute-start | bytes 393224 | tf_op jit(solution)/shard_map/ppermute | solution.py:12
  240.3 47.0 %collective-permute-start.18 = (f32[2,128,128]{2,1,0:T(8,128)}, f32[2,128,128]{2,1,0:T(8,128)S(1)}, u32[]{:S(2)}, u32[]{:S(2)}) collective-permute-start(f32[2,128,128]{2,1,0:T(8,128)} %get-tuple-element.23), channel_id=1, source_target_pairs={{16,0},{32,16},{48,32},{64,48},{80,64},{96,80},{112,96},{128,112},... | collective-permute-start | bytes 393224 | tf_op jit(solution)/shard_map/ppermute | solution.py:12
  241.6 45.7 %collective-permute-start.19 = (f32[2,128,128]{2,1,0:T(8,128)}, f32[2,128,128]{2,1,0:T(8,128)S(1)}, u32[]{:S(2)}, u32[]{:S(2)}) collective-permute-start(f32[2,128,128]{2,1,0:T(8,128)} %get-tuple-element.25), channel_id=1, source_target_pairs={{0,1},{1,2},{2,3},{3,4},{4,5},{5,6},{6,7},{7,8},{8,9},{9,10},{10,1... | collective-permute-start | bytes 393224 | tf_op jit(solution)/shard_map/ppermute | solution.py:12
  245.6 41.7 %collective-permute-start.20 = (f32[2,128,128]{2,1,0:T(8,128)}, f32[2,128,128]{2,1,0:T(8,128)S(1)}, u32[]{:S(2)}, u32[]{:S(2)}) collective-permute-start(f32[2,128,128]{2,1,0:T(8,128)} %get-tuple-element.24), channel_id=1, source_target_pairs={{1,0},{2,1},{3,2},{4,3},{5,4},{6,5},{7,6},{8,7},{9,8},{10,9},{11,1... | collective-permute-start | bytes 393224 | tf_op jit(solution)/shard_map/ppermute | solution.py:12
  263.8 5.2 %collective-permute-start.13 = (f32[2,128]{1,0:T(2,128)S(1)}, f32[2,128]{1,0:T(2,128)S(1)}, u32[]{:S(2)}, u32[]{:S(2)}) collective-permute-start(f32[2,128]{1,0:T(2,128)S(1)} %reduce_sum.153), channel_id=1, source_target_pairs={{0,16},{16,0},{32,48},{48,32},{64,80},{80,64},{96,112},{112,96},{1... | collective-permute-start | bytes 3080 | tf_op jit(solution)/shard_map/ppermute | solution.py:22
  269.0 5.2 %collective-permute-start.14 = (f32[2,128]{1,0:T(2,128)S(1)}, f32[2,128]{1,0:T(2,128)S(1)}, u32[]{:S(2)}, u32[]{:S(2)}) collective-permute-start(f32[2,128]{1,0:T(2,128)S(1)} %add.186), channel_id=1, source_target_pairs={{0,32},{16,48},{32,0},{48,16},{64,96},{80,112},{96,64},{112,80},{1... | collective-permute-start | bytes 3080 | tf_op jit(solution)/shard_map/ppermute | solution.py:22
  274.2 8.2 %collective-permute-start.15 = (f32[2,128]{1,0:T(2,128)S(1)}, f32[2,128]{1,0:T(2,128)S(1)}, u32[]{:S(2)}, u32[]{:S(2)}) collective-permute-start(f32[2,128]{1,0:T(2,128)S(1)} %add.187), channel_id=1, source_target_pairs={{0,64},{16,80},{32,96},{48,112},{64,0},{80,16},{96,32},{112,48},{1... | collective-permute-start | bytes 3080 | tf_op jit(solution)/shard_map/ppermute | solution.py:22
  282.4 6.2 %collective-permute-start.16 = (f32[2,128]{1,0:T(2,128)S(1)}, f32[2,128]{1,0:T(2,128)S(1)}, u32[]{:S(2)}, u32[]{:S(2)}) collective-permute-start(f32[2,128]{1,0:T(2,128)S(1)} %add.188), channel_id=1, source_target_pairs={{0,128},{16,144},{32,160},{48,176},{64,192},{80,208},{96,224},{112... | collective-permute-start | bytes 3080 | tf_op jit(solution)/shard_map/ppermute | solution.py:22
  288.6 6.9 %copy-start.5 = (f32[896,128]{1,0:T(8,128)S(1)}, f32[896,128]{1,0:T(8,128)}, u32[]{:S(2)}) copy-start(f32[896,128]{1,0:T(8,128)} %copy-done.4) | copy-start | bytes 1376260
  288.6 5.9 %collective-permute-start.21 = (f32[2,128]{1,0:T(2,128)S(1)}, f32[2,128]{1,0:T(2,128)S(1)}, u32[]{:S(2)}, u32[]{:S(2)}) collective-permute-start(f32[2,128]{1,0:T(2,128)S(1)} %add_add_fusion.1), channel_id=1, source_target_pairs={{0,256},{16,272},{32,288},{48,304},{64,320},{80,336},{96,352},{112... | collective-permute-start | bytes 3080 | tf_op jit(solution)/shard_map/ppermute | solution.py:22
  292.5 3.1 copy-start.2
  295.6 1.0 copy-start.12
  296.5 25.2 %copy-start.7 = (f32[8,32,128]{2,0,1:T(8,128)S(1)}, f32[8,32,128]{2,0,1:T(8,128)}, u32[]{:S(2)}) copy-start(f32[8,32,128]{2,0,1:T(8,128)} %copy-done.6) | copy-start | bytes 393220
  322.7 19.6 %all-to-all-start.4 = ((f32[32,8,128]{2,1,0:T(8,128)}), f32[32,8,128]{2,1,0:T(8,128)S(1)}, u32[]{:S(2)}, u32[]{:S(2)}) async-start(f32[32,8,128]{2,1,0:T(8,128)} %fusion.115), calls=%async_computation.4 | async-start | bytes 262144 | tf_op jit(solution)/shard_map/all_to_all | solution.py:103
  331.4 49.8 %collective-permute-start.27 = (f32[2,128,128]{2,1,0:T(8,128)}, f32[2,128,128]{2,1,0:T(8,128)}, u32[]{:S(2)}, u32[]{:S(2)}) collective-permute-start(f32[2,128,128]{2,1,0:T(8,128)} %get-tuple-element.19), channel_id=1, source_target_pairs={{16,0},{32,16},{48,32},{64,48},{80,64},{96,80},{112,96},{128,112},... | collective-permute-start | bytes 393224 | tf_op jit(solution)/shard_map/ppermute | solution.py:12
  332.6 48.6 %collective-permute-start.28 = (f32[2,128,128]{2,1,0:T(8,128)}, f32[2,128,128]{2,1,0:T(8,128)}, u32[]{:S(2)}, u32[]{:S(2)}) collective-permute-start(f32[2,128,128]{2,1,0:T(8,128)} %get-tuple-element.21), channel_id=1, source_target_pairs={{0,1},{1,2},{2,3},{3,4},{4,5},{5,6},{6,7},{7,8},{8,9},{9,10},{10,1... | collective-permute-start | bytes 393224 | tf_op jit(solution)/shard_map/ppermute | solution.py:12
  334.6 46.6 %collective-permute-start.29 = (f32[2,128,128]{2,1,0:T(8,128)}, f32[2,128,128]{2,1,0:T(8,128)}, u32[]{:S(2)}, u32[]{:S(2)}) collective-permute-start(f32[2,128,128]{2,1,0:T(8,128)} %get-tuple-element.20), channel_id=1, source_target_pairs={{1,0},{2,1},{3,2},{4,3},{5,4},{6,5},{7,6},{8,7},{9,8},{10,9},{11,1... | collective-permute-start | bytes 393224 | tf_op jit(solution)/shard_map/ppermute | solution.py:12
  337.6 43.6 %collective-permute-start.26 = (f32[2,128,128]{2,1,0:T(8,128)}, f32[2,128,128]{2,1,0:T(8,128)}, u32[]{:S(2)}, u32[]{:S(2)}) collective-permute-start(f32[2,128,128]{2,1,0:T(8,128)} %get-tuple-element.18), channel_id=1, source_target_pairs={{0,16},{16,32},{32,48},{48,64},{64,80},{80,96},{96,112},{112,128},... | collective-permute-start | bytes 393224 | tf_op jit(solution)/shard_map/ppermute | solution.py:12
  359.9 30.2 %copy-start.11 = (bf16[1,1,4,128,128]{4,3,2,1,0:T(8,128)(2,1)S(1)}, bf16[1,1,4,128,128]{4,3,2,1,0:T(8,128)(2,1)}, u32[]{:S(2)}) copy-start(bf16[1,1,4,128,128]{4,3,2,1,0:T(8,128)(2,1)} %param.15) | copy-start | bytes 393220
  359.9 4.4 %collective-permute-start.22 = (f32[2,128]{1,0:T(2,128)S(1)}, f32[2,128]{1,0:T(2,128)S(1)}, u32[]{:S(2)}, u32[]{:S(2)}) collective-permute-start(f32[2,128]{1,0:T(2,128)S(1)} %reduce_sum.158), channel_id=1, source_target_pairs={{0,16},{16,0},{32,48},{48,32},{64,80},{80,64},{96,112},{112,96},{1... | collective-permute-start | bytes 3080 | tf_op jit(solution)/shard_map/ppermute | solution.py:22
  364.3 5.6 %collective-permute-start.23 = (f32[2,128]{1,0:T(2,128)S(1)}, f32[2,128]{1,0:T(2,128)S(1)}, u32[]{:S(2)}, u32[]{:S(2)}) collective-permute-start(f32[2,128]{1,0:T(2,128)S(1)} %add.199), channel_id=1, source_target_pairs={{0,32},{16,48},{32,0},{48,16},{64,96},{80,112},{96,64},{112,80},{1... | collective-permute-start | bytes 3080 | tf_op jit(solution)/shard_map/ppermute | solution.py:22
  369.9 8.2 %collective-permute-start.24 = (f32[2,128]{1,0:T(2,128)S(1)}, f32[2,128]{1,0:T(2,128)S(1)}, u32[]{:S(2)}, u32[]{:S(2)}) collective-permute-start(f32[2,128]{1,0:T(2,128)S(1)} %add.200), channel_id=1, source_target_pairs={{0,64},{16,80},{32,96},{48,112},{64,0},{80,16},{96,32},{112,48},{1... | collective-permute-start | bytes 3080 | tf_op jit(solution)/shard_map/ppermute | solution.py:22
  378.1 5.1 %collective-permute-start.25 = (f32[2,128]{1,0:T(2,128)S(1)}, f32[2,128]{1,0:T(2,128)S(1)}, u32[]{:S(2)}, u32[]{:S(2)}) collective-permute-start(f32[2,128]{1,0:T(2,128)S(1)} %add.201), channel_id=1, source_target_pairs={{0,128},{16,144},{32,160},{48,176},{64,192},{80,208},{96,224},{112... | collective-permute-start | bytes 3080 | tf_op jit(solution)/shard_map/ppermute | solution.py:22
  383.2 7.0 %copy-start.3 = (bf16[1,1,896,896]{3,2,1,0:T(8,128)(2,1)S(1)}, bf16[1,1,896,896]{3,2,1,0:T(8,128)(2,1)}, u32[]{:S(2)}) copy-start(bf16[1,1,896,896]{3,2,1,0:T(8,128)(2,1)} %param.11) | copy-start | bytes 4816900
  383.2 5.9 %collective-permute-start.30 = (f32[2,128]{1,0:T(2,128)S(1)}, f32[2,128]{1,0:T(2,128)S(1)}, u32[]{:S(2)}, u32[]{:S(2)}) collective-permute-start(f32[2,128]{1,0:T(2,128)S(1)} %add_add_fusion), channel_id=1, source_target_pairs={{0,256},{16,272},{32,288},{48,304},{64,320},{80,336},{96,352},{112... | collective-permute-start | bytes 3080 | tf_op jit(solution)/shard_map/ppermute | solution.py:22
  390.8 3.5 copy-start.9

commit v6 on v5

--- a/solution.py
+++ b/solution.py
@@ -12,15 +12,18 @@
     return lax.ppermute(value, axis, [(source, source + steps) for source in range(leading, last)])
 
 
+def gather_rows(value, axis):
+    count = lax.axis_size(axis)
+    copies = jnp.broadcast_to(value[None], (count,) + value.shape)
+    return lax.all_to_all(copies.reshape((-1,) + value.shape[1:]), axis, 0, 0, tiled=True)
+
+
 def total_over_mesh(value, tie):
-    value = jnp.sum(lax.all_gather(value, "gy", axis=0), axis=0)
-    count = lax.axis_size("gx")
-    step = 1
-    while step < count:
-        if step == count // 2:
+    for axis in ("gy", "gx"):
+        if axis == "gx":
             value = value + 0.0 * tie
-        value = value + lax.ppermute(value, "gx", [(i, i ^ step) for i in range(count)])
-        step *= 2
+        count = lax.axis_size(axis)
+        value = jnp.sum(gather_rows(value, axis).reshape((count,) + value.shape), axis=0)
     return value
 
 
@@ -98,7 +101,7 @@
             trace_mat, rounded, preferred_element_type=jnp.float32
         )
         coarse = jnp.dot(vectors, rounded, preferred_element_type=jnp.float32)
-        line = lax.all_gather(coarse, "gy", axis=0, tiled=True)
+        line = gather_rows(coarse, "gy")
         partial = jnp.dot(coarse_block, line, precision=lax.Precision.HIGHEST)
         pieces = lax.all_to_all(partial, "gx", 0, 0, tiled=True)
         solved = jnp.sum(pieces.reshape(count_x, depth, pieces.shape[-1]), axis=0)

time: 401 us -> 325 us (0.81); the launches traced: 395 us -> 323 us
  blocking collectives: 131 us -> 63.1 us
  starting transfers between devices: 141 us -> 110 us
  waiting for transfers between devices: 46.5 us -> 62.9 us
    all_gather x7 -> x0, blocking collectives: 131 us -> none  [the longest x4 81.2 us: apply_prec(): line = lax.all_gather(coarse, 'gy', axis=0, tiled=True)]
    ppermute x15 -> x0, starting transfers between devices: 63.9 us -> none  [total_over_mesh(): lax.ppermute(value, 'gx', [(i, i ^ step) for i in range(count)])]
    all_to_all x0 -> x5, blocking collectives: none -> 63.1 us  [gather_rows(): lax.all_to_all(copies.reshape((-1,) + value.shape[1:]), axis, 0, 0, tiled...]
    all_to_all x0 -> x5, starting transfers between devices: none -> 38.2 us  [gather_rows(): lax.all_to_all(copies.reshape((-1,) + value.shape[1:]), axis, 0, 0, tiled...]
    all_to_all x0 -> x5, waiting for transfers between devices: none -> 27.8 us  [gather_rows(): lax.all_to_all(copies.reshape((-1,) + value.shape[1:]), axis, 0, 0, tiled...]
    ppermute x15 -> x0, waiting for transfers between devices: 20.9 us -> none  [total_over_mesh(): lax.ppermute(value, 'gx', [(i, i ^ step) for i in range(count)])]
    all_to_all x1, waiting for transfers between devices: 0.01 us -> 9.13 us  [shards(): lax.all_to_all(coarse_cols.reshape(depth, count_x, count_y * depth), 'gx'...]
    all_to_all x4, starting transfers between devices: 24.4 us -> 18.6 us  [apply_prec(): pieces = lax.all_to_all(partial, 'gx', 0, 0, tiled=True)]
  transfers between devices with their start and end apart: 36 -> 26, of which waited for: 15 -> 9; matrix products, arithmetic and copies ran while one was open for 4% -> 12% of each run, Pallas kernels for 0% -> 0%
where the time goes in v6:
time: 325 us; the launch traced here: 323 us
  starting transfers between devices  110 us (34%)
  blocking collectives  63.1 us (19%)
  waiting for transfers between devices  62.9 us (19%)
  local copies, waits for them, and re-layouts  34.3 us (11%)
  other arithmetic  31.6 us (10%)
  matrix products  17.4 us (5%)
  between operations  3.38 us (1%)
    all_to_all x5, blocking collectives, gather_rows(): lax.all_to_all(copies.reshape((-1,) + value.shape[1:]), axis, 0, 0, tiled...  63.1 us
    ppermute x16, starting transfers between devices, from_behind(): lax.ppermute(value, axis, [(source, source + steps) for source in range(l...  43.9 us
    all_to_all x5, starting transfers between devices, gather_rows(): lax.all_to_all(copies.reshape((-1,) + value.shape[1:]), axis, 0, 0, tiled...  38.2 us
    all_to_all x5, waiting for transfers between devices, gather_rows(): lax.all_to_all(copies.reshape((-1,) + value.shape[1:]), axis, 0, 0, tiled...  27.8 us
    all_to_all x4, waiting for transfers between devices, apply_prec(): pieces = lax.all_to_all(partial, 'gx', 0, 0, tiled=True)  24.7 us
    all_to_all x4, starting transfers between devices, apply_prec(): pieces = lax.all_to_all(partial, 'gx', 0, 0, tiled=True)  18.6 us
    gather x2, local copies, waits for them, and re-layouts, shards(): coarse_cols = jnp.take(coarse_inverse, coarse_map, axis=1)  17.9 us
    scatter-add x4, other arithmetic, finish_schur(): return result.at[flat_rows].add(-coupled.reshape(-1, coupled.shape[-1]))  14.5 us
  transfers between devices with their start and end apart: 26, of which 9 were waited for; matrix products, arithmetic and copies ran while one was open for 12% of the time, Pallas kernels for 0%

profile of v6, /device:TPU:1, one launch (start us, length us, event | category | flops | bytes accessed | tf_op | source)
XLA Modules:
  0.0 323.2 jit_solution(4670399440162674395)
XLA Ops:
  0.6 1.2 fusion.141
  2.5 11.8 %all-to-all-start.1 = ((f32[16,8,128]{2,1,0:T(8,128)}), f32[16,8,128]{2,1,0:T(8,128)S(1)}, u32[]{:S(2)}, u32[]{:S(2)}) async-start(f32[16,8,128]{2,1,0:T(8,128)} %broadcast_in_dim.42), calls=%async_computation.1 | async-start | bytes 131072 | tf_op jit(solution)/shard_map/all_to_all | solution.py:18
  15.8 2.9 copy.95
  18.7 15.7 %gather_fusion = f32[4096,8]{1,0:T(8,128)} fusion(f32[8,4096]{0,1:T(8,128)} %copy.95, s32[4096]{0:T(1024)S(1)} %fusion.143), kind=kCustom, calls=%fused_computation | custom fusion | bytes 278528 | tf_op jit(solution)/shard_map/jit(_take)/gather | solution.py:62
  34.4 2.2 copy.96
  37.2 9.7 %all-to-all-start = ((f32[8,32,128]{2,0,1:T(8,128)}), f32[8,32,128]{2,0,1:T(8,128)S(1)}, u32[]{:S(2)}, u32[]{:S(2)}) async-start(f32[8,32,128]{2,0,1:T(8,128)} %broadcast_select_fusion), calls=%async_computation | async-start | bytes 262144 | tf_op jit(solution)/shard_map/all_to_all | solution.py:63
  47.0 9.1 %all-to-all-done = f32[8,32,128]{2,0,1:T(8,128)S(1)} async-done(((f32[8,32,128]{2,0,1:T(8,128)}), f32[8,32,128]{2,0,1:T(8,128)S(1)}, u32[]{:S(2)}, u32[]{:S(2)}) %all-to-all-start) | async-done | bytes 131104 | tf_op jit(solution)/shard_map/all_to_all | solution.py:63
  57.0 4.5 %all-to-all-start.2 = ((f32[32,8,128]{2,1,0:T(8,128)}), f32[32,8,128]{2,1,0:T(8,128)S(1)}, u32[]{:S(2)}, u32[]{:S(2)}) async-start(f32[32,8,128]{2,1,0:T(8,128)} %fusion.121), calls=%async_computation.2 | async-start | bytes 262144 | tf_op jit(solution)/shard_map/all_to_all | solution.py:106
  61.6 9.1 %all-to-all-done.2 = f32[32,8,128]{2,1,0:T(8,128)S(1)} async-done(((f32[32,8,128]{2,1,0:T(8,128)}), f32[32,8,128]{2,1,0:T(8,128)S(1)}, u32[]{:S(2)}, u32[]{:S(2)}) %all-to-all-start.2) | async-done | bytes 131104 | tf_op jit(solution)/shard_map/all_to_all | solution.py:106
  71.8 1.3 gather_fusion.1
  73.1 3.1 collective-permute-start
  76.2 1.3 collective-permute-start.1
  77.5 5.9 %collective-permute-start.2 = (bf16[128,128]{1,0:T(8,128)(2,1)S(1)}, bf16[128,128]{1,0:T(8,128)(2,1)S(1)}, u32[]{:S(2)}, u32[]{:S(2)}) collective-permute-start(bf16[128,128]{1,0:T(8,128)(2,1)S(1)} %get-tuple-element.32), channel_id=1, source_target_pairs={{0,1},{1,2},{2,3},{3,4},{4,5},{5,6},{6,7},{7,8},{8,9},{9,10},{10,1... | collective-permute-start | bytes 98312 | tf_op jit(solution)/shard_map/ppermute | solution.py:12
  83.4 1.9 collective-permute-start.3
  85.3 2.0 fusion.37
  87.3 1.3 collective-permute-done.3
  88.8 3.5 %scatter_fusion = f32[896,128]{1,0:T(8,128)S(1)} fusion(f32[896,128]{1,0:T(8,128)S(1)} %fusion.37, s32[512]{0:T(512)S(1)} %bitcast.377, f32[512,128]{1,0:T(8,128)S(1)} %bitcast.376), kind=kCustom, calls=%fused_computation.8 | custom fusion | flops 65536 | bytes 788480 | tf_op jit(solution)/shard_map/scatter-add | solution.py:84
  92.5 14.9 %all_to_all.111 = f32[16,8,128]{2,1,0:T(8,128)S(1)} all-to-all(f32[16,8,128]{2,1,0:T(8,128)S(1)} %broadcast_in_dim.43), channel_id=1, replica_groups=mesh['gx'=32,'gy'=16] {'gy'}, dimensions={0} | all-to-all | bytes 131072 | tf_op jit(solution)/shard_map/all_to_all | solution.py:18
  108.3 6.4 %all-to-all-start.4 = ((f32[32,8,128]{2,1,0:T(8,128)}), f32[32,8,128]{2,1,0:T(8,128)S(1)}, u32[]{:S(2)}, u32[]{:S(2)}) async-start(f32[32,8,128]{2,1,0:T(8,128)} %fusion.119), calls=%async_computation.4 | async-start | bytes 262144 | tf_op jit(solution)/shard_map/all_to_all | solution.py:106
  114.6 1.0 gather_fusion.2
  115.7 8.1 %all-to-all-done.4 = f32[32,8,128]{2,1,0:T(8,128)S(1)} async-done(((f32[32,8,128]{2,1,0:T(8,128)}), f32[32,8,128]{2,1,0:T(8,128)S(1)}, u32[]{:S(2)}, u32[]{:S(2)}) %all-to-all-start.4) | async-done | bytes 131104 | tf_op jit(solution)/shard_map/all_to_all | solution.py:106
  124.8 1.6 gather_fusion.3
  126.5 1.7 fusion.102
  128.2 3.6 %collective-permute-start.4 = (f32[2,128,128]{2,1,0:T(8,128)}, f32[2,128,128]{2,1,0:T(8,128)S(1)}, u32[]{:S(2)}, u32[]{:S(2)}) collective-permute-start(f32[2,128,128]{2,1,0:T(8,128)} %get-tuple-element.26), channel_id=1, source_target_pairs={{0,16},{16,32},{32,48},{48,64},{64,80},{80,96},{96,112},{112,128},... | collective-permute-start | bytes 393224 | tf_op jit(solution)/shard_map/ppermute | solution.py:12
  131.8 1.3 collective-permute-start.5
  133.1 3.6 %collective-permute-start.6 = (f32[2,128,128]{2,1,0:T(8,128)}, f32[2,128,128]{2,1,0:T(8,128)S(1)}, u32[]{:S(2)}, u32[]{:S(2)}) collective-permute-start(f32[2,128,128]{2,1,0:T(8,128)} %get-tuple-element.29), channel_id=1, source_target_pairs={{0,1},{1,2},{2,3},{3,4},{4,5},{5,6},{6,7},{7,8},{8,9},{9,10},{10,1... | collective-permute-start | bytes 393224 | tf_op jit(solution)/shard_map/ppermute | solution.py:12
  136.7 1.9 collective-permute-start.7
  138.7 12.1 %all_to_all.112 = f32[16,2,128]{2,1,0:T(2,128)S(1)} all-to-all(f32[16,2,128]{2,1,0:T(2,128)S(1)} %broadcast_in_dim.44), channel_id=1, replica_groups=mesh['gx'=32,'gy'=16] {'gy'}, dimensions={0} | all-to-all | bytes 32768 | tf_op jit(solution)/shard_map/all_to_all | solution.py:18
  152.8 6.2 %all-to-all-start.6 = ((f32[32,2,128]{2,1,0:T(2,128)}), f32[32,2,128]{2,1,0:T(2,128)S(1)}, u32[]{:S(2)}, u32[]{:S(2)}) async-start(f32[32,2,128]{2,1,0:T(2,128)} %broadcast_in_dim.45), calls=%async_computation.6 | async-start | bytes 65536 | tf_op jit(solution)/shard_map/all_to_all | solution.py:18
  159.9 7.9 %all-to-all-done.6 = f32[32,2,128]{2,1,0:T(2,128)S(1)} async-done(((f32[32,2,128]{2,1,0:T(2,128)}), f32[32,2,128]{2,1,0:T(2,128)S(1)}, u32[]{:S(2)}, u32[]{:S(2)}) %all-to-all-start.6) | async-done | bytes 32800 | tf_op jit(solution)/shard_map/all_to_all | solution.py:18
  167.9 2.0 convolution_negate_fusion.2
  170.5 4.1 %scatter_fusion.1 = f32[896,128]{1,0:T(8,128)S(1)} fusion(f32[896,128]{1,0:T(8,128)S(1)} %fusion.40, s32[512]{0:T(512)S(1)} %bitcast.378, f32[512,128]{1,0:T(8,128)} %bitcast.353), kind=kCustom, calls=%fused_computation.9 | custom fusion | flops 65536 | bytes 788480 | tf_op jit(solution)/shard_map/scatter-add | solution.py:84
  174.8 12.0 %all_to_all.113 = f32[16,8,128]{2,1,0:T(8,128)S(1)} all-to-all(f32[16,8,128]{2,1,0:T(8,128)S(1)} %broadcast_in_dim.46), channel_id=1, replica_groups=mesh['gx'=32,'gy'=16] {'gy'}, dimensions={0} | all-to-all | bytes 131072 | tf_op jit(solution)/shard_map/all_to_all | solution.py:18
  187.7 3.9 %all-to-all-start.8 = ((f32[32,8,128]{2,1,0:T(8,128)}), f32[32,8,128]{2,1,0:T(8,128)S(1)}, u32[]{:S(2)}, u32[]{:S(2)}) async-start(f32[32,8,128]{2,1,0:T(8,128)} %fusion.117), calls=%async_computation.8 | async-start | bytes 262144 | tf_op jit(solution)/shard_map/all_to_all | solution.py:106
  191.6 1.6 gather_fusion.4
  193.2 7.5 %all-to-all-done.8 = f32[32,8,128]{2,1,0:T(8,128)S(1)} async-done(((f32[32,8,128]{2,1,0:T(8,128)}), f32[32,8,128]{2,1,0:T(8,128)S(1)}, u32[]{:S(2)}, u32[]{:S(2)}) %all-to-all-start.8) | async-done | bytes 131104 | tf_op jit(solution)/shard_map/all_to_all | solution.py:106
  201.8 1.6 gather_fusion.5
  203.5 1.7 fusion.96
  205.2 3.7 %collective-permute-start.8 = (f32[2,128,128]{2,1,0:T(8,128)}, f32[2,128,128]{2,1,0:T(8,128)S(1)}, u32[]{:S(2)}, u32[]{:S(2)}) collective-permute-start(f32[2,128,128]{2,1,0:T(8,128)} %get-tuple-element.22), channel_id=1, source_target_pairs={{0,16},{16,32},{32,48},{48,64},{64,80},{80,96},{96,112},{112,128},... | collective-permute-start | bytes 393224 | tf_op jit(solution)/shard_map/ppermute | solution.py:12
  208.9 1.3 collective-permute-start.9
  210.2 3.6 %collective-permute-start.10 = (f32[2,128,128]{2,1,0:T(8,128)}, f32[2,128,128]{2,1,0:T(8,128)S(1)}, u32[]{:S(2)}, u32[]{:S(2)}) collective-permute-start(f32[2,128,128]{2,1,0:T(8,128)} %get-tuple-element.25), channel_id=1, source_target_pairs={{0,1},{1,2},{2,3},{3,4},{4,5},{5,6},{6,7},{7,8},{8,9},{9,10},{10,1... | collective-permute-start | bytes 393224 | tf_op jit(solution)/shard_map/ppermute | solution.py:12
  213.8 1.9 collective-permute-start.11
  215.7 12.1 %all_to_all.114 = f32[16,2,128]{2,1,0:T(2,128)S(1)} all-to-all(f32[16,2,128]{2,1,0:T(2,128)S(1)} %broadcast_in_dim.47), channel_id=1, replica_groups=mesh['gx'=32,'gy'=16] {'gy'}, dimensions={0} | all-to-all | bytes 32768 | tf_op jit(solution)/shard_map/all_to_all | solution.py:18
  229.9 6.4 %all-to-all-start.10 = ((f32[32,2,128]{2,1,0:T(2,128)}), f32[32,2,128]{2,1,0:T(2,128)S(1)}, u32[]{:S(2)}, u32[]{:S(2)}) async-start(f32[32,2,128]{2,1,0:T(2,128)} %broadcast_in_dim.48), calls=%async_computation.10 | async-start | bytes 65536 | tf_op jit(solution)/shard_map/all_to_all | solution.py:18
  237.3 7.8 %all-to-all-done.10 = f32[32,2,128]{2,1,0:T(2,128)S(1)} async-done(((f32[32,2,128]{2,1,0:T(2,128)}), f32[32,2,128]{2,1,0:T(2,128)S(1)}, u32[]{:S(2)}, u32[]{:S(2)}) %all-to-all-start.10) | async-done | bytes 32800 | tf_op jit(solution)/shard_map/all_to_all | solution.py:18
  246.0 1.1 fusion.147
  248.1 3.5 %scatter_fusion.2 = f32[896,128]{1,0:T(8,128)S(1)} fusion(f32[896,128]{1,0:T(8,128)S(1)} %fusion.43, s32[512]{0:T(512)S(1)} %bitcast.379, f32[512,128]{1,0:T(8,128)S(1)} %bitcast.351), kind=kCustom, calls=%fused_computation.10 | custom fusion | flops 65536 | bytes 788480 | tf_op jit(solution)/shard_map/scatter-add | solution.py:84
  251.8 12.0 %all_to_all.115 = f32[16,8,128]{2,1,0:T(8,128)S(1)} all-to-all(f32[16,8,128]{2,1,0:T(8,128)S(1)} %broadcast_in_dim.49), channel_id=1, replica_groups=mesh['gx'=32,'gy'=16] {'gy'}, dimensions={0} | all-to-all | bytes 131072 | tf_op jit(solution)/shard_map/all_to_all | solution.py:18
  264.7 3.9 %all-to-all-start.12 = ((f32[32,8,128]{2,1,0:T(8,128)}), f32[32,8,128]{2,1,0:T(8,128)S(1)}, u32[]{:S(2)}, u32[]{:S(2)}) async-start(f32[32,8,128]{2,1,0:T(8,128)} %fusion.115), calls=%async_computation.12 | async-start | bytes 262144 | tf_op jit(solution)/shard_map/all_to_all | solution.py:106
  268.6 1.0 gather_fusion.6
  269.6 1.6 gather_fusion.7
  271.3 1.7 fusion.90
  273.0 1.3 collective-permute-start.13
  274.3 2.3 collective-permute-start.14
  276.6 2.6 collective-permute-start.15
  279.2 4.7 %collective-permute-start.12 = (f32[2,128,128]{2,1,0:T(8,128)}, f32[2,128,128]{2,1,0:T(8,128)}, u32[]{:S(2)}, u32[]{:S(2)}) collective-permute-start(f32[2,128,128]{2,1,0:T(8,128)} %get-tuple-element.18), channel_id=1, source_target_pairs={{0,16},{16,32},{32,48},{48,64},{64,80},{80,96},{96,112},{112,128},... | collective-permute-start | bytes 393224 | tf_op jit(solution)/shard_map/ppermute | solution.py:12
  285.6 4.9 %all-to-all-start.13 = ((f32[16,2,128]{2,1,0:T(2,128)}), f32[16,2,128]{2,1,0:T(2,128)S(1)}, u32[]{:S(2)}, u32[]{:S(2)}) async-start(f32[16,2,128]{2,1,0:T(2,128)} %broadcast_in_dim.50), calls=%async_computation.13 | async-start | bytes 32768 | tf_op jit(solution)/shard_map/all_to_all | solution.py:18
  290.6 1.3 maximum_reduce_fusion
  292.6 5.3 %all-to-all-done.13 = f32[16,2,128]{2,1,0:T(2,128)S(1)} async-done(((f32[16,2,128]{2,1,0:T(2,128)}), f32[16,2,128]{2,1,0:T(2,128)S(1)}, u32[]{:S(2)}, u32[]{:S(2)}) %all-to-all-start.13) | async-done | bytes 16416 | tf_op jit(solution)/shard_map/all_to_all | solution.py:18
  298.5 8.9 %all-to-all-start.14 = ((f32[32,2,128]{2,1,0:T(2,128)}), f32[32,2,128]{2,1,0:T(2,128)S(1)}, u32[]{:S(2)}, u32[]{:S(2)}) async-start(f32[32,2,128]{2,1,0:T(2,128)} %broadcast_in_dim.51), calls=%async_computation.14 | async-start | bytes 65536 | tf_op jit(solution)/shard_map/all_to_all | solution.py:18
  307.4 1.9 pad_maximum_fusion.2
  309.3 6.8 %all-to-all-done.14 = f32[32,2,128]{2,1,0:T(2,128)S(1)} async-done(((f32[32,2,128]{2,1,0:T(2,128)}), f32[32,2,128]{2,1,0:T(2,128)S(1)}, u32[]{:S(2)}, u32[]{:S(2)}) %all-to-all-start.14) | async-done | bytes 32800 | tf_op jit(solution)/shard_map/all_to_all | solution.py:18
  317.0 1.2 convolution_negate_fusion
  318.9 3.5 %scatter_fusion.3 = f32[896,128]{1,0:T(8,128)S(1)} fusion(f32[896,128]{1,0:T(8,128)S(1)} %fusion.46, s32[512]{0:T(512)S(1)} %bitcast.380, f32[512,128]{1,0:T(8,128)S(1)} %bitcast.352), kind=kCustom, calls=%fused_computation.11 | custom fusion | flops 65536 | bytes 788480 | tf_op jit(solution)/shard_map/scatter-add | solution.py:84
  (123 shorter events, 22.1 us)
Async XLA Ops:
  0.6 70.5 %copy-start = (bf16[1,1,896,896]{3,2,1,0:T(8,128)(2,1)S(1)}, bf16[1,1,896,896]{3,2,1,0:T(8,128)(2,1)}, u32[]{:S(2)}) copy-start(bf16[1,1,896,896]{3,2,1,0:T(8,128)(2,1)} %param.13) | copy-start | bytes 4816900
  2.5 34.7 %all-to-all-start.1 = ((f32[16,8,128]{2,1,0:T(8,128)}), f32[16,8,128]{2,1,0:T(8,128)S(1)}, u32[]{:S(2)}, u32[]{:S(2)}) async-start(f32[16,8,128]{2,1,0:T(8,128)} %broadcast_in_dim.42), calls=%async_computation.1 | async-start | bytes 131072 | tf_op jit(solution)/shard_map/all_to_all | solution.py:18
  34.3 12.6 %copy-start.16 = (s32[1,1,4,128]{3,2,1,0:T(4,128)S(1)}, s32[1,1,4,128]{3,2,1,0:T(4,128)}, u32[]{:S(2)}) copy-start(s32[1,1,4,128]{3,2,1,0:T(4,128)} %param.16) | copy-start | bytes 6148
  34.3 27.2 %copy-start.17 = (f32[1,1,896]{2,1,0:T(1,128)S(1)}, f32[1,1,896]{2,1,0:T(1,128)}, u32[]{:S(2)}) copy-start(f32[1,1,896]{2,1,0:T(1,128)} %param.14) | copy-start | bytes 10756
  34.3 27.2 %copy-start.18 = (f32[1,1,896]{2,1,0:T(1,128)S(1)}, f32[1,1,896]{2,1,0:T(1,128)}, u32[]{:S(2)}) copy-start(f32[1,1,896]{2,1,0:T(1,128)} %param.12) | copy-start | bytes 10756
  34.3 36.4 %copy-start.13 = (bf16[1,1,8,896]{3,2,1,0:T(8,128)(2,1)S(1)}, bf16[1,1,8,896]{3,2,1,0:T(8,128)(2,1)}, u32[]{:S(2)}) copy-start(bf16[1,1,8,896]{3,2,1,0:T(8,128)(2,1)} %param.17) | copy-start | bytes 43012
  34.3 36.8 %copy-start.7 = (bf16[1,1,896,128]{3,2,1,0:T(8,128)(2,1)S(1)}, bf16[1,1,896,128]{3,2,1,0:T(8,128)(2,1)}, u32[]{:S(2)}) copy-start(bf16[1,1,896,128]{3,2,1,0:T(8,128)(2,1)} %param.10) | copy-start | bytes 688132
  37.2 18.9 %all-to-all-start = ((f32[8,32,128]{2,0,1:T(8,128)}), f32[8,32,128]{2,0,1:T(8,128)S(1)}, u32[]{:S(2)}, u32[]{:S(2)}) async-start(f32[8,32,128]{2,0,1:T(8,128)} %broadcast_select_fusion), calls=%async_computation | async-start | bytes 262144 | tf_op jit(solution)/shard_map/all_to_all | solution.py:63
  56.1 130.7 %copy-start.5 = (f32[8,32,128]{2,0,1:T(8,128)}, f32[8,32,128]{2,0,1:T(8,128)S(1)}, u32[]{:S(2)}) copy-start(f32[8,32,128]{2,0,1:T(8,128)S(1)} %all-to-all-done) | copy-start | bytes 393220
  57.0 13.7 %all-to-all-start.2 = ((f32[32,8,128]{2,1,0:T(8,128)}), f32[32,8,128]{2,1,0:T(8,128)S(1)}, u32[]{:S(2)}, u32[]{:S(2)}) async-start(f32[32,8,128]{2,1,0:T(8,128)} %fusion.121), calls=%async_computation.2 | async-start | bytes 262144 | tf_op jit(solution)/shard_map/all_to_all | solution.py:106
  71.8 16.8 %copy-start.9 = (bf16[1,1,4,128,128]{4,3,2,1,0:T(8,128)(2,1)S(1)}, bf16[1,1,4,128,128]{4,3,2,1,0:T(8,128)(2,1)}, u32[]{:S(2)}) copy-start(bf16[1,1,4,128,128]{4,3,2,1,0:T(8,128)(2,1)} %param.15) | copy-start | bytes 393220
  73.1 14.2 %collective-permute-start = (bf16[128,128]{1,0:T(8,128)(2,1)S(1)}, bf16[128,128]{1,0:T(8,128)(2,1)S(1)}, u32[]{:S(2)}, u32[]{:S(2)}) collective-permute-start(bf16[128,128]{1,0:T(8,128)(2,1)S(1)} %get-tuple-element.31), channel_id=1, source_target_pairs={{0,16},{16,32},{32,48},{48,64},{64,80},{80,96},{96,112},{112,128},... | collective-permute-start | bytes 98312 | tf_op jit(solution)/shard_map/ppermute | solution.py:12
  76.2 11.1 %collective-permute-start.1 = (bf16[128,128]{1,0:T(8,128)(2,1)S(1)}, bf16[128,128]{1,0:T(8,128)(2,1)S(1)}, u32[]{:S(2)}, u32[]{:S(2)}) collective-permute-start(bf16[128,128]{1,0:T(8,128)(2,1)S(1)} %get-tuple-element.33), channel_id=1, source_target_pairs={{16,0},{32,16},{48,32},{64,48},{80,64},{96,80},{112,96},{128,112},... | collective-permute-start | bytes 98312 | tf_op jit(solution)/shard_map/ppermute | solution.py:12
  77.5 9.8 %collective-permute-start.2 = (bf16[128,128]{1,0:T(8,128)(2,1)S(1)}, bf16[128,128]{1,0:T(8,128)(2,1)S(1)}, u32[]{:S(2)}, u32[]{:S(2)}) collective-permute-start(bf16[128,128]{1,0:T(8,128)(2,1)S(1)} %get-tuple-element.32), channel_id=1, source_target_pairs={{0,1},{1,2},{2,3},{3,4},{4,5},{5,6},{6,7},{7,8},{8,9},{9,10},{10,1... | collective-permute-start | bytes 98312 | tf_op jit(solution)/shard_map/ppermute | solution.py:12
  83.4 5.2 %collective-permute-start.3 = (bf16[128,128]{1,0:T(8,128)(2,1)S(1)}, bf16[128,128]{1,0:T(8,128)(2,1)S(1)}, u32[]{:S(2)}, u32[]{:S(2)}) collective-permute-start(bf16[128,128]{1,0:T(8,128)(2,1)S(1)} %get-tuple-element.34), channel_id=1, source_target_pairs={{1,0},{2,1},{3,2},{4,3},{5,4},{6,5},{7,6},{8,7},{9,8},{10,9},{11,1... | collective-permute-start | bytes 98312 | tf_op jit(solution)/shard_map/ppermute | solution.py:12
  108.3 15.5 %all-to-all-start.4 = ((f32[32,8,128]{2,1,0:T(8,128)}), f32[32,8,128]{2,1,0:T(8,128)S(1)}, u32[]{:S(2)}, u32[]{:S(2)}) async-start(f32[32,8,128]{2,1,0:T(8,128)} %fusion.119), calls=%async_computation.4 | async-start | bytes 262144 | tf_op jit(solution)/shard_map/all_to_all | solution.py:106
  128.2 22.6 %collective-permute-start.4 = (f32[2,128,128]{2,1,0:T(8,128)}, f32[2,128,128]{2,1,0:T(8,128)S(1)}, u32[]{:S(2)}, u32[]{:S(2)}) collective-permute-start(f32[2,128,128]{2,1,0:T(8,128)} %get-tuple-element.26), channel_id=1, source_target_pairs={{0,16},{16,32},{32,48},{48,64},{64,80},{80,96},{96,112},{112,128},... | collective-permute-start | bytes 393224 | tf_op jit(solution)/shard_map/ppermute | solution.py:12
  131.8 19.1 %collective-permute-start.5 = (f32[2,128,128]{2,1,0:T(8,128)}, f32[2,128,128]{2,1,0:T(8,128)S(1)}, u32[]{:S(2)}, u32[]{:S(2)}) collective-permute-start(f32[2,128,128]{2,1,0:T(8,128)} %get-tuple-element.27), channel_id=1, source_target_pairs={{16,0},{32,16},{48,32},{64,48},{80,64},{96,80},{112,96},{128,112},... | collective-permute-start | bytes 393224 | tf_op jit(solution)/shard_map/ppermute | solution.py:12
  133.1 17.8 %collective-permute-start.6 = (f32[2,128,128]{2,1,0:T(8,128)}, f32[2,128,128]{2,1,0:T(8,128)S(1)}, u32[]{:S(2)}, u32[]{:S(2)}) collective-permute-start(f32[2,128,128]{2,1,0:T(8,128)} %get-tuple-element.29), channel_id=1, source_target_pairs={{0,1},{1,2},{2,3},{3,4},{4,5},{5,6},{6,7},{7,8},{8,9},{9,10},{10,1... | collective-permute-start | bytes 393224 | tf_op jit(solution)/shard_map/ppermute | solution.py:12
  136.7 14.1 %collective-permute-start.7 = (f32[2,128,128]{2,1,0:T(8,128)}, f32[2,128,128]{2,1,0:T(8,128)S(1)}, u32[]{:S(2)}, u32[]{:S(2)}) collective-permute-start(f32[2,128,128]{2,1,0:T(8,128)} %get-tuple-element.28), channel_id=1, source_target_pairs={{1,0},{2,1},{3,2},{4,3},{5,4},{6,5},{7,6},{8,7},{9,8},{10,9},{11,1... | collective-permute-start | bytes 393224 | tf_op jit(solution)/shard_map/ppermute | solution.py:12
  152.8 15.0 %all-to-all-start.6 = ((f32[32,2,128]{2,1,0:T(2,128)}), f32[32,2,128]{2,1,0:T(2,128)S(1)}, u32[]{:S(2)}, u32[]{:S(2)}) async-start(f32[32,2,128]{2,1,0:T(2,128)} %broadcast_in_dim.45), calls=%async_computation.6 | async-start | bytes 65536 | tf_op jit(solution)/shard_map/all_to_all | solution.py:18
  167.8 2.1 copy-start.1
  187.7 13.0 %all-to-all-start.8 = ((f32[32,8,128]{2,1,0:T(8,128)}), f32[32,8,128]{2,1,0:T(8,128)S(1)}, u32[]{:S(2)}, u32[]{:S(2)}) async-start(f32[32,8,128]{2,1,0:T(8,128)} %fusion.117), calls=%async_computation.8 | async-start | bytes 262144 | tf_op jit(solution)/shard_map/all_to_all | solution.py:106
  201.8 3.4 %copy-start.4 = (f32[896,128]{1,0:T(8,128)}, f32[896,128]{1,0:T(8,128)S(1)}, u32[]{:S(2)}) copy-start(f32[896,128]{1,0:T(8,128)S(1)} %get-tuple-element.38) | copy-start | bytes 1376260
  201.8 1.7 copy-start.12
  205.2 22.6 %collective-permute-start.8 = (f32[2,128,128]{2,1,0:T(8,128)}, f32[2,128,128]{2,1,0:T(8,128)S(1)}, u32[]{:S(2)}, u32[]{:S(2)}) collective-permute-start(f32[2,128,128]{2,1,0:T(8,128)} %get-tuple-element.22), channel_id=1, source_target_pairs={{0,16},{16,32},{32,48},{48,64},{64,80},{80,96},{96,112},{112,128},... | collective-permute-start | bytes 393224 | tf_op jit(solution)/shard_map/ppermute | solution.py:12
  208.9 18.9 %collective-permute-start.9 = (f32[2,128,128]{2,1,0:T(8,128)}, f32[2,128,128]{2,1,0:T(8,128)S(1)}, u32[]{:S(2)}, u32[]{:S(2)}) collective-permute-start(f32[2,128,128]{2,1,0:T(8,128)} %get-tuple-element.23), channel_id=1, source_target_pairs={{16,0},{32,16},{48,32},{64,48},{80,64},{96,80},{112,96},{128,112},... | collective-permute-start | bytes 393224 | tf_op jit(solution)/shard_map/ppermute | solution.py:12
  210.2 17.7 %collective-permute-start.10 = (f32[2,128,128]{2,1,0:T(8,128)}, f32[2,128,128]{2,1,0:T(8,128)S(1)}, u32[]{:S(2)}, u32[]{:S(2)}) collective-permute-start(f32[2,128,128]{2,1,0:T(8,128)} %get-tuple-element.25), channel_id=1, source_target_pairs={{0,1},{1,2},{2,3},{3,4},{4,5},{5,6},{6,7},{7,8},{8,9},{9,10},{10,1... | collective-permute-start | bytes 393224 | tf_op jit(solution)/shard_map/ppermute | solution.py:12
  213.8 14.1 %collective-permute-start.11 = (f32[2,128,128]{2,1,0:T(8,128)}, f32[2,128,128]{2,1,0:T(8,128)S(1)}, u32[]{:S(2)}, u32[]{:S(2)}) collective-permute-start(f32[2,128,128]{2,1,0:T(8,128)} %get-tuple-element.24), channel_id=1, source_target_pairs={{1,0},{2,1},{3,2},{4,3},{5,4},{6,5},{7,6},{8,7},{9,8},{10,9},{11,1... | collective-permute-start | bytes 393224 | tf_op jit(solution)/shard_map/ppermute | solution.py:12
  227.9 2.0 copy-start.14
  227.9 2.0 copy-start.15
  229.9 15.2 %all-to-all-start.10 = ((f32[32,2,128]{2,1,0:T(2,128)}), f32[32,2,128]{2,1,0:T(2,128)S(1)}, u32[]{:S(2)}, u32[]{:S(2)}) async-start(f32[32,2,128]{2,1,0:T(2,128)} %broadcast_in_dim.48), calls=%async_computation.10 | async-start | bytes 65536 | tf_op jit(solution)/shard_map/all_to_all | solution.py:18
  245.1 2.0 copy-start.2
  247.1 1.0 copy-start.11
  248.1 15.7 %copy-start.6 = (f32[8,32,128]{2,0,1:T(8,128)S(1)}, f32[8,32,128]{2,0,1:T(8,128)}, u32[]{:S(2)}) copy-start(f32[8,32,128]{2,0,1:T(8,128)} %copy-done.5) | copy-start | bytes 393220
  264.7 19.2 %all-to-all-start.12 = ((f32[32,8,128]{2,1,0:T(8,128)}), f32[32,8,128]{2,1,0:T(8,128)S(1)}, u32[]{:S(2)}, u32[]{:S(2)}) async-start(f32[32,8,128]{2,1,0:T(8,128)} %fusion.115), calls=%async_computation.12 | async-start | bytes 262144 | tf_op jit(solution)/shard_map/all_to_all | solution.py:106
  273.0 17.5 %collective-permute-start.13 = (f32[2,128,128]{2,1,0:T(8,128)}, f32[2,128,128]{2,1,0:T(8,128)}, u32[]{:S(2)}, u32[]{:S(2)}) collective-permute-start(f32[2,128,128]{2,1,0:T(8,128)} %get-tuple-element.19), channel_id=1, source_target_pairs={{16,0},{32,16},{48,32},{64,48},{80,64},{96,80},{112,96},{128,112},... | collective-permute-start | bytes 393224 | tf_op jit(solution)/shard_map/ppermute | solution.py:12
  274.3 16.3 %collective-permute-start.14 = (f32[2,128,128]{2,1,0:T(8,128)}, f32[2,128,128]{2,1,0:T(8,128)}, u32[]{:S(2)}, u32[]{:S(2)}) collective-permute-start(f32[2,128,128]{2,1,0:T(8,128)} %get-tuple-element.21), channel_id=1, source_target_pairs={{0,1},{1,2},{2,3},{3,4},{4,5},{5,6},{6,7},{7,8},{8,9},{9,10},{10,1... | collective-permute-start | bytes 393224 | tf_op jit(solution)/shard_map/ppermute | solution.py:12
  276.6 13.9 %collective-permute-start.15 = (f32[2,128,128]{2,1,0:T(8,128)}, f32[2,128,128]{2,1,0:T(8,128)}, u32[]{:S(2)}, u32[]{:S(2)}) collective-permute-start(f32[2,128,128]{2,1,0:T(8,128)} %get-tuple-element.20), channel_id=1, source_target_pairs={{1,0},{2,1},{3,2},{4,3},{5,4},{6,5},{7,6},{8,7},{9,8},{10,9},{11,1... | collective-permute-start | bytes 393224 | tf_op jit(solution)/shard_map/ppermute | solution.py:12
  279.2 11.3 %collective-permute-start.12 = (f32[2,128,128]{2,1,0:T(8,128)}, f32[2,128,128]{2,1,0:T(8,128)}, u32[]{:S(2)}, u32[]{:S(2)}) collective-permute-start(f32[2,128,128]{2,1,0:T(8,128)} %get-tuple-element.18), channel_id=1, source_target_pairs={{0,16},{16,32},{32,48},{48,64},{64,80},{80,96},{96,112},{112,128},... | collective-permute-start | bytes 393224 | tf_op jit(solution)/shard_map/ppermute | solution.py:12
  285.6 12.3 %all-to-all-start.13 = ((f32[16,2,128]{2,1,0:T(2,128)}), f32[16,2,128]{2,1,0:T(2,128)S(1)}, u32[]{:S(2)}, u32[]{:S(2)}) async-start(f32[16,2,128]{2,1,0:T(2,128)} %broadcast_in_dim.50), calls=%async_computation.13 | async-start | bytes 32768 | tf_op jit(solution)/shard_map/all_to_all | solution.py:18
  290.6 26.5 %copy-start.10 = (bf16[1,1,4,128,128]{4,3,2,1,0:T(8,128)(2,1)S(1)}, bf16[1,1,4,128,128]{4,3,2,1,0:T(8,128)(2,1)}, u32[]{:S(2)}) copy-start(bf16[1,1,4,128,128]{4,3,2,1,0:T(8,128)(2,1)} %param.15) | copy-start | bytes 393220
  298.5 17.6 %all-to-all-start.14 = ((f32[32,2,128]{2,1,0:T(2,128)}), f32[32,2,128]{2,1,0:T(2,128)S(1)}, u32[]{:S(2)}, u32[]{:S(2)}) async-start(f32[32,2,128]{2,1,0:T(2,128)} %broadcast_in_dim.51), calls=%async_computation.14 | async-start | bytes 65536 | tf_op jit(solution)/shard_map/all_to_all | solution.py:18
  316.2 2.1 copy-start.3
  318.9 3.5 %copy-start.8 = (bf16[1,1,896,128]{3,2,1,0:T(8,128)(2,1)S(1)}, bf16[1,1,896,128]{3,2,1,0:T(8,128)(2,1)}, u32[]{:S(2)}) copy-start(bf16[1,1,896,128]{3,2,1,0:T(8,128)(2,1)} %param.10) | copy-start | bytes 688132

commit v7 on v6

--- a/solution.py
+++ b/solution.py
@@ -18,13 +18,9 @@
     return lax.all_to_all(copies.reshape((-1,) + value.shape[1:]), axis, 0, 0, tiled=True)
 
 
-def total_over_mesh(value, tie):
-    for axis in ("gy", "gx"):
-        if axis == "gx":
-            value = value + 0.0 * tie
-        count = lax.axis_size(axis)
-        value = jnp.sum(gather_rows(value, axis).reshape((count,) + value.shape), axis=0)
-    return value
+def total_over_axis(value, axis):
+    count = lax.axis_size(axis)
+    return jnp.sum(gather_rows(value, axis).reshape((count,) + value.shape), axis=0)
 
 
 def pass_columns(rows, offset):
@@ -87,8 +83,9 @@
         rounded = lax.optimization_barrier(field.astype(jnp.bfloat16))
         return finish_schur(rounded, exchange(rounded[rows_lists]))
 
-    def send_early(base, step):
-        return exchange(jnp.stack([base[rows_lists], step[rows_lists]], axis=1))
+    def send_early(base, step, after):
+        rows = jnp.stack([base[rows_lists], step[rows_lists]], axis=1)
+        return exchange(rows + 0.0 * after)
 
     def apply_schur_late(field, pair, coef):
         rounded = lax.optimization_barrier(field.astype(jnp.bfloat16))
@@ -112,14 +109,15 @@
     image = apply_schur(direction)
     for iteration in range(ITERS):
         mapped = apply_prec(image)
+        line_total = total_over_axis(
+            jnp.stack([jnp.sum(mapped * direction, axis=0), jnp.sum(mapped * mapped, axis=0)]), "gy"
+        )
+        after = line_total[0, 0]
         if iteration + 1 < ITERS:
-            pair = send_early(direction, mapped)
+            pair = send_early(direction, mapped, after)
         else:
-            pair = send_early(solution, direction)
-        numer, denom = total_over_mesh(
-            jnp.stack([jnp.sum(mapped * direction, axis=0), jnp.sum(mapped * mapped, axis=0)]),
-            jnp.sum(pair[:, 0, 0, 0]),
-        )
+            pair = send_early(solution, direction, after)
+        numer, denom = total_over_axis(line_total, "gx")
         alpha = numer / denom
         solution = solution + alpha * direction
         direction = direction + (-alpha) * mapped

time: 325 us -> 326 us (level)
  blocking collectives: 63.1 us -> 104 us
  starting transfers between devices: 110 us -> 89.8 us
  waiting for transfers between devices: 62.9 us -> 44 us
  other arithmetic: 31.6 us -> 24.3 us
  local copies, waits for them, and re-layouts: 34.3 us -> 40.4 us
    all_to_all x0 -> x3, blocking collectives: none -> 55.2 us  [apply_prec(): pieces = lax.all_to_all(partial, 'gx', 0, 0, tiled=True)]
    all_to_all x4 -> x1, waiting for transfers between devices: 24.7 us -> 9.06 us  [apply_prec(): pieces = lax.all_to_all(partial, 'gx', 0, 0, tiled=True)]
    all_to_all x5 -> x4, blocking collectives: 63.1 us -> 48.8 us  [gather_rows(): lax.all_to_all(copies.reshape((-1,) + value.shape[1:]), axis, 0, 0, tiled...]
    all_to_all x4 -> x1, starting transfers between devices: 18.6 us -> 4.51 us  [apply_prec(): pieces = lax.all_to_all(partial, 'gx', 0, 0, tiled=True)]
    all_to_all x5 -> x6, waiting for transfers between devices: 27.8 us -> 15.9 us  [gather_rows(): lax.all_to_all(copies.reshape((-1,) + value.shape[1:]), axis, 0, 0, tiled...]
    ppermute x16, waiting for transfers between devices: 1.3 us -> 9.88 us  [from_behind(): lax.ppermute(value, axis, [(source, source + steps) for source in range(l...]
    squeeze x3 -> x0, other arithmetic: 5.17 us -> none  [exchange(): sent_rows[1]]
    all_to_all x5 -> x6, starting transfers between devices: 38.2 us -> 34.3 us  [gather_rows(): lax.all_to_all(copies.reshape((-1,) + value.shape[1:]), axis, 0, 0, tiled...]
  transfers between devices with their start and end apart: 26 -> 24, of which waited for: 9 -> 9; matrix products, arithmetic and copies ran while one was open for 12% -> 11% of each run, Pallas kernels for 0% -> 0%
where the time goes in v7:
time: 326 us; the launch traced here: 322 us
  blocking collectives  104 us (32%)
  starting transfers between devices  89.8 us (28%)
  waiting for transfers between devices  44 us (13%)
  local copies, waits for them, and re-layouts  40.4 us (12%)
  other arithmetic  24.3 us (7%)
  matrix products  16 us (5%)
    all_to_all x3, blocking collectives, apply_prec(): pieces = lax.all_to_all(partial, 'gx', 0, 0, tiled=True)  55.2 us
    all_to_all x4, blocking collectives, gather_rows(): lax.all_to_all(copies.reshape((-1,) + value.shape[1:]), axis, 0, 0, tiled...  48.8 us
    ppermute x16, starting transfers between devices, from_behind(): lax.ppermute(value, axis, [(source, source + steps) for source in range(l...  41.3 us
    all_to_all x6, starting transfers between devices, gather_rows(): lax.all_to_all(copies.reshape((-1,) + value.shape[1:]), axis, 0, 0, tiled...  34.3 us
    gather x2, local copies, waits for them, and re-layouts, shards(): coarse_cols = jnp.take(coarse_inverse, coarse_map, axis=1)  17.9 us
    all_to_all x6, waiting for transfers between devices, gather_rows(): lax.all_to_all(copies.reshape((-1,) + value.shape[1:]), axis, 0, 0, tiled...  15.9 us
    scatter-add x4, other arithmetic, finish_schur(): return result.at[flat_rows].add(-coupled.reshape(-1, coupled.shape[-1]))  15.3 us
    ppermute x16, waiting for transfers between devices, from_behind(): lax.ppermute(value, axis, [(source, source + steps) for source in range(l...  9.88 us
  transfers between devices with their start and end apart: 24, of which 9 were waited for; matrix products, arithmetic and copies ran while one was open for 11% of the time, Pallas kernels for 0%

profile of v7, /device:TPU:1, one launch (start us, length us, event | category | flops | bytes accessed | tf_op | source)
XLA Modules:
  0.0 321.8 jit_solution(11841094125030827425)
XLA Ops:
  0.6 1.2 fusion.120
  2.5 11.8 %all-to-all-start.1 = ((f32[16,8,128]{2,1,0:T(8,128)}), f32[16,8,128]{2,1,0:T(8,128)S(1)}, u32[]{:S(2)}, u32[]{:S(2)}) async-start(f32[16,8,128]{2,1,0:T(8,128)} %broadcast_in_dim.42), calls=%async_computation.1 | async-start | bytes 131072 | tf_op jit(solution)/shard_map/all_to_all | solution.py:18
  15.8 2.9 copy.95
  18.7 15.7 %gather_fusion = f32[4096,8]{1,0:T(8,128)} fusion(f32[8,4096]{0,1:T(8,128)} %copy.95, s32[4096]{0:T(1024)S(1)} %fusion.122), kind=kCustom, calls=%fused_computation | custom fusion | bytes 278528 | tf_op jit(solution)/shard_map/jit(_take)/gather | solution.py:58
  34.4 2.2 copy.96
  37.2 9.7 %all-to-all-start = ((f32[8,32,128]{2,0,1:T(8,128)}), f32[8,32,128]{2,0,1:T(8,128)S(1)}, u32[]{:S(2)}, u32[]{:S(2)}) async-start(f32[8,32,128]{2,0,1:T(8,128)} %broadcast_select_fusion), calls=%async_computation | async-start | bytes 262144 | tf_op jit(solution)/shard_map/all_to_all | solution.py:59
  47.0 9.1 %all-to-all-done = f32[8,32,128]{2,0,1:T(8,128)S(1)} async-done(((f32[8,32,128]{2,0,1:T(8,128)}), f32[8,32,128]{2,0,1:T(8,128)S(1)}, u32[]{:S(2)}, u32[]{:S(2)}) %all-to-all-start) | async-done | bytes 131104 | tf_op jit(solution)/shard_map/all_to_all | solution.py:59
  57.0 4.5 %all-to-all-start.2 = ((f32[32,8,128]{2,1,0:T(8,128)}), f32[32,8,128]{2,1,0:T(8,128)S(1)}, u32[]{:S(2)}, u32[]{:S(2)}) async-start(f32[32,8,128]{2,1,0:T(8,128)} %fusion.100), calls=%async_computation.2 | async-start | bytes 262144 | tf_op jit(solution)/shard_map/all_to_all | solution.py:103
  61.6 9.1 %all-to-all-done.2 = f32[32,8,128]{2,1,0:T(8,128)S(1)} async-done(((f32[32,8,128]{2,1,0:T(8,128)}), f32[32,8,128]{2,1,0:T(8,128)S(1)}, u32[]{:S(2)}, u32[]{:S(2)}) %all-to-all-start.2) | async-done | bytes 131104 | tf_op jit(solution)/shard_map/all_to_all | solution.py:103
  71.8 1.3 gather_fusion.1
  73.1 3.1 collective-permute-start
  76.2 1.3 collective-permute-start.1
  77.5 5.9 %collective-permute-start.2 = (bf16[128,128]{1,0:T(8,128)(2,1)S(1)}, bf16[128,128]{1,0:T(8,128)(2,1)S(1)}, u32[]{:S(2)}, u32[]{:S(2)}) collective-permute-start(bf16[128,128]{1,0:T(8,128)(2,1)S(1)} %get-tuple-element.31), channel_id=1, source_target_pairs={{0,1},{1,2},{2,3},{3,4},{4,5},{5,6},{6,7},{7,8},{8,9},{9,10},{10,1... | collective-permute-start | bytes 98312 | tf_op jit(solution)/shard_map/ppermute | solution.py:12
  83.4 1.9 collective-permute-start.3
  85.3 2.0 fusion.37
  87.3 1.3 collective-permute-done.3
  88.8 3.5 %scatter_fusion = f32[896,128]{1,0:T(8,128)S(1)} fusion(f32[896,128]{1,0:T(8,128)S(1)} %fusion.37, s32[512]{0:T(512)S(1)} %bitcast.368, f32[512,128]{1,0:T(8,128)S(1)} %bitcast.363), kind=kCustom, calls=%fused_computation.8 | custom fusion | flops 65536 | bytes 788480 | tf_op jit(solution)/shard_map/scatter-add | solution.py:80
  92.5 14.9 %all_to_all.111 = f32[16,8,128]{2,1,0:T(8,128)S(1)} all-to-all(f32[16,8,128]{2,1,0:T(8,128)S(1)} %broadcast_in_dim.43), channel_id=1, replica_groups=mesh['gx'=32,'gy'=16] {'gy'}, dimensions={0} | all-to-all | bytes 131072 | tf_op jit(solution)/shard_map/all_to_all | solution.py:18
  107.6 15.3 %all_to_all.112 = f32[32,8,128]{2,1,0:T(8,128)S(1)} all-to-all(f32[32,8,128]{2,1,0:T(8,128)S(1)} %fusion.98), channel_id=1, replica_groups=mesh['gx'=32,'gy'=16] {'gx'}, dimensions={0} | all-to-all | bytes 262144 | tf_op jit(solution)/shard_map/all_to_all | solution.py:103
  124.6 5.4 %all-to-all-start.5 = ((f32[16,2,128]{2,1,0:T(2,128)}), f32[16,2,128]{2,1,0:T(2,128)S(1)}, u32[]{:S(2)}, u32[]{:S(2)}) async-start(f32[16,2,128]{2,1,0:T(2,128)} %broadcast_in_dim.44), calls=%async_computation.5 | async-start | bytes 32768 | tf_op jit(solution)/shard_map/all_to_all | solution.py:18
  130.0 1.0 gather_fusion.2
  131.0 1.0 gather_fusion.3
  132.1 5.3 %all-to-all-done.5 = f32[16,2,128]{2,1,0:T(2,128)S(1)} async-done(((f32[16,2,128]{2,1,0:T(2,128)}), f32[16,2,128]{2,1,0:T(2,128)S(1)}, u32[]{:S(2)}, u32[]{:S(2)}) %all-to-all-start.5) | async-done | bytes 16416 | tf_op jit(solution)/shard_map/all_to_all | solution.py:18
  138.6 3.8 %all-to-all-start.6 = ((f32[32,2,128]{2,1,0:T(2,128)}), f32[32,2,128]{2,1,0:T(2,128)S(1)}, u32[]{:S(2)}, u32[]{:S(2)}) async-start(f32[32,2,128]{2,1,0:T(2,128)} %broadcast_in_dim.45), calls=%async_computation.6 | async-start | bytes 65536 | tf_op jit(solution)/shard_map/all_to_all | solution.py:18
  143.8 3.7 %collective-permute-start.4 = (f32[2,128,128]{2,1,0:T(8,128)}, f32[2,128,128]{2,1,0:T(8,128)}, u32[]{:S(2)}, u32[]{:S(2)}) collective-permute-start(f32[2,128,128]{2,1,0:T(8,128)} %get-tuple-element.26), channel_id=1, source_target_pairs={{0,16},{16,32},{32,48},{48,64},{64,80},{80,96},{96,112},{112,128},... | collective-permute-start | bytes 393224 | tf_op jit(solution)/shard_map/ppermute | solution.py:12
  147.5 1.3 collective-permute-start.5
  148.8 3.0 collective-permute-start.6
  151.8 2.0 collective-permute-start.7
  153.9 1.3 copy-done.1
  155.9 2.3 collective-permute-done.7
  158.2 1.1 pad_maximum_fusion
  160.2 4.0 %scatter_fusion.1 = f32[896,128]{1,0:T(8,128)S(1)} fusion(f32[896,128]{1,0:T(8,128)S(1)} %fusion.40, s32[512]{0:T(512)S(1)} %bitcast.369, f32[512,128]{1,0:T(8,128)} %bitcast.354), kind=kCustom, calls=%fused_computation.9 | custom fusion | flops 65536 | bytes 788480 | tf_op jit(solution)/shard_map/scatter-add | solution.py:80
  164.5 10.9 %all_to_all.113 = f32[16,8,128]{2,1,0:T(8,128)S(1)} all-to-all(f32[16,8,128]{2,1,0:T(8,128)S(1)} %broadcast_in_dim.46), channel_id=1, replica_groups=mesh['gx'=32,'gy'=16] {'gy'}, dimensions={0} | all-to-all | bytes 131072 | tf_op jit(solution)/shard_map/all_to_all | solution.py:18
  175.6 20.0 %all_to_all.114 = f32[32,8,128]{2,1,0:T(8,128)S(1)} all-to-all(f32[32,8,128]{2,1,0:T(8,128)S(1)} %fusion.96), channel_id=1, replica_groups=mesh['gx'=32,'gy'=16] {'gx'}, dimensions={0} | all-to-all | bytes 262144 | tf_op jit(solution)/shard_map/all_to_all | solution.py:103
  197.3 5.4 %all-to-all-start.9 = ((f32[16,2,128]{2,1,0:T(2,128)}), f32[16,2,128]{2,1,0:T(2,128)S(1)}, u32[]{:S(2)}, u32[]{:S(2)}) async-start(f32[16,2,128]{2,1,0:T(2,128)} %broadcast_in_dim.47), calls=%async_computation.9 | async-start | bytes 32768 | tf_op jit(solution)/shard_map/all_to_all | solution.py:18
  202.7 1.0 gather_fusion.4
  203.7 1.6 gather_fusion.5
  205.4 4.7 %all-to-all-done.9 = f32[16,2,128]{2,1,0:T(2,128)S(1)} async-done(((f32[16,2,128]{2,1,0:T(2,128)}), f32[16,2,128]{2,1,0:T(2,128)S(1)}, u32[]{:S(2)}, u32[]{:S(2)}) %all-to-all-start.9) | async-done | bytes 16416 | tf_op jit(solution)/shard_map/all_to_all | solution.py:18
  211.9 3.8 %all-to-all-start.10 = ((f32[32,2,128]{2,1,0:T(2,128)}), f32[32,2,128]{2,1,0:T(2,128)S(1)}, u32[]{:S(2)}, u32[]{:S(2)}) async-start(f32[32,2,128]{2,1,0:T(2,128)} %broadcast_in_dim.48), calls=%async_computation.10 | async-start | bytes 65536 | tf_op jit(solution)/shard_map/all_to_all | solution.py:18
  217.5 3.7 %collective-permute-start.8 = (f32[2,128,128]{2,1,0:T(8,128)}, f32[2,128,128]{2,1,0:T(8,128)}, u32[]{:S(2)}, u32[]{:S(2)}) collective-permute-start(f32[2,128,128]{2,1,0:T(8,128)} %get-tuple-element.22), channel_id=1, source_target_pairs={{0,16},{16,32},{32,48},{48,64},{64,80},{80,96},{96,112},{112,128},... | collective-permute-start | bytes 393224 | tf_op jit(solution)/shard_map/ppermute | solution.py:12
  221.2 1.3 collective-permute-start.9
  222.5 3.0 collective-permute-start.10
  225.5 1.9 collective-permute-start.11
  227.6 1.3 copy-done.2
  229.5 2.6 collective-permute-done.11
  232.1 1.1 pad_maximum_fusion.1
  234.1 3.9 %scatter_fusion.2 = f32[896,128]{1,0:T(8,128)S(1)} fusion(f32[896,128]{1,0:T(8,128)S(1)} %fusion.43, s32[512]{0:T(512)S(1)} %bitcast.370, f32[512,128]{1,0:T(8,128)} %bitcast.355), kind=kCustom, calls=%fused_computation.10 | custom fusion | flops 65536 | bytes 788480 | tf_op jit(solution)/shard_map/scatter-add | solution.py:80
  238.9 11.1 %all_to_all.115 = f32[16,8,128]{2,1,0:T(8,128)S(1)} all-to-all(f32[16,8,128]{2,1,0:T(8,128)S(1)} %broadcast_in_dim.49), channel_id=1, replica_groups=mesh['gx'=32,'gy'=16] {'gy'}, dimensions={0} | all-to-all | bytes 131072 | tf_op jit(solution)/shard_map/all_to_all | solution.py:18
  250.0 1.2 fusion.94
  251.2 19.9 %all_to_all.116 = f32[32,8,128]{2,1,0:T(8,128)S(1)} all-to-all(f32[32,8,128]{2,1,0:T(8,128)S(1)} %fusion.94), channel_id=1, replica_groups=mesh['gx'=32,'gy'=16] {'gx'}, dimensions={0} | all-to-all | bytes 262144 | tf_op jit(solution)/shard_map/all_to_all | solution.py:103
  271.6 1.7 multiply_reduce_fusion.1
  273.3 11.9 %all_to_all.117 = f32[16,2,128]{2,1,0:T(2,128)S(1)} all-to-all(f32[16,2,128]{2,1,0:T(2,128)S(1)} %broadcast_in_dim.50), channel_id=1, replica_groups=mesh['gx'=32,'gy'=16] {'gy'}, dimensions={0} | all-to-all | bytes 32768 | tf_op jit(solution)/shard_map/all_to_all | solution.py:18
  285.8 4.1 %all-to-all-start.14 = ((f32[32,2,128]{2,1,0:T(2,128)}), f32[32,2,128]{2,1,0:T(2,128)S(1)}, u32[]{:S(2)}, u32[]{:S(2)}) async-start(f32[32,2,128]{2,1,0:T(2,128)} %broadcast_in_dim.51), calls=%async_computation.14 | async-start | bytes 65536 | tf_op jit(solution)/shard_map/all_to_all | solution.py:18
  289.9 1.6 gather_fusion.7
  292.6 5.8 %all-to-all-done.14 = f32[32,2,128]{2,1,0:T(2,128)S(1)} async-done(((f32[32,2,128]{2,1,0:T(2,128)}), f32[32,2,128]{2,1,0:T(2,128)S(1)}, u32[]{:S(2)}, u32[]{:S(2)}) %all-to-all-start.14) | async-done | bytes 32800 | tf_op jit(solution)/shard_map/all_to_all | solution.py:18
  299.3 1.6 gather_fusion.6
  301.0 1.1 maximum_add_fusion.2
  302.1 2.3 collective-permute-start.12
  304.4 1.3 collective-permute-start.13
  305.7 3.9 %collective-permute-start.14 = (f32[2,128,128]{2,1,0:T(8,128)S(1)}, f32[2,128,128]{2,1,0:T(8,128)S(1)}, u32[]{:S(2)}, u32[]{:S(2)}) collective-permute-start(f32[2,128,128]{2,1,0:T(8,128)S(1)} %get-tuple-element.20), channel_id=1, source_target_pairs={{0,1},{1,2},{2,3},{3,4},{4,5},{5,6},{6,7},{7,8},{8,9},{9,10},{10,1... | collective-permute-start | bytes 393224 | tf_op jit(solution)/shard_map/ppermute | solution.py:12
  309.6 1.9 collective-permute-start.15
  312.2 3.7 %collective-permute-done.15 = f32[2,128,128]{2,1,0:T(8,128)S(1)} collective-permute-done((f32[2,128,128]{2,1,0:T(8,128)S(1)}, f32[2,128,128]{2,1,0:T(8,128)S(1)}, u32[]{:S(2)}, u32[]{:S(2)}) %collective-permute-start.15) | collective-permute-done | bytes 131104 | tf_op jit(solution)/shard_map/ppermute | solution.py:12
  316.9 3.9 %scatter_fusion.3 = f32[896,128]{1,0:T(8,128)S(1)} fusion(f32[896,128]{1,0:T(8,128)S(1)} %fusion.46, s32[512]{0:T(512)S(1)} %bitcast.371, f32[512,128]{1,0:T(8,128)} %bitcast.356), kind=kCustom, calls=%fused_computation.11 | custom fusion | flops 65536 | bytes 788480 | tf_op jit(solution)/shard_map/scatter-add | solution.py:80
  320.8 1.0 subtract_bitcast_fusion
  (119 shorter events, 22.3 us)
Async XLA Ops:
  0.6 70.5 %copy-start = (bf16[1,1,896,896]{3,2,1,0:T(8,128)(2,1)S(1)}, bf16[1,1,896,896]{3,2,1,0:T(8,128)(2,1)}, u32[]{:S(2)}) copy-start(bf16[1,1,896,896]{3,2,1,0:T(8,128)(2,1)} %param.13) | copy-start | bytes 4816900
  2.5 34.7 %all-to-all-start.1 = ((f32[16,8,128]{2,1,0:T(8,128)}), f32[16,8,128]{2,1,0:T(8,128)S(1)}, u32[]{:S(2)}, u32[]{:S(2)}) async-start(f32[16,8,128]{2,1,0:T(8,128)} %broadcast_in_dim.42), calls=%async_computation.1 | async-start | bytes 131072 | tf_op jit(solution)/shard_map/all_to_all | solution.py:18
  34.3 12.6 %copy-start.15 = (s32[1,1,4,128]{3,2,1,0:T(4,128)S(1)}, s32[1,1,4,128]{3,2,1,0:T(4,128)}, u32[]{:S(2)}) copy-start(s32[1,1,4,128]{3,2,1,0:T(4,128)} %param.16) | copy-start | bytes 6148
  34.3 27.2 %copy-start.16 = (f32[1,1,896]{2,1,0:T(1,128)S(1)}, f32[1,1,896]{2,1,0:T(1,128)}, u32[]{:S(2)}) copy-start(f32[1,1,896]{2,1,0:T(1,128)} %param.14) | copy-start | bytes 10756
  34.3 27.2 %copy-start.17 = (f32[1,1,896]{2,1,0:T(1,128)S(1)}, f32[1,1,896]{2,1,0:T(1,128)}, u32[]{:S(2)}) copy-start(f32[1,1,896]{2,1,0:T(1,128)} %param.12) | copy-start | bytes 10756
  34.3 36.4 %copy-start.14 = (bf16[1,1,8,896]{3,2,1,0:T(8,128)(2,1)S(1)}, bf16[1,1,8,896]{3,2,1,0:T(8,128)(2,1)}, u32[]{:S(2)}) copy-start(bf16[1,1,8,896]{3,2,1,0:T(8,128)(2,1)} %param.17) | copy-start | bytes 43012
  34.3 36.8 %copy-start.5 = (bf16[1,1,896,128]{3,2,1,0:T(8,128)(2,1)S(1)}, bf16[1,1,896,128]{3,2,1,0:T(8,128)(2,1)}, u32[]{:S(2)}) copy-start(bf16[1,1,896,128]{3,2,1,0:T(8,128)(2,1)} %param.10) | copy-start | bytes 688132
  37.2 18.9 %all-to-all-start = ((f32[8,32,128]{2,0,1:T(8,128)}), f32[8,32,128]{2,0,1:T(8,128)S(1)}, u32[]{:S(2)}, u32[]{:S(2)}) async-start(f32[8,32,128]{2,0,1:T(8,128)} %broadcast_select_fusion), calls=%async_computation | async-start | bytes 262144 | tf_op jit(solution)/shard_map/all_to_all | solution.py:59
  56.1 119.2 %copy-start.4 = (f32[8,32,128]{2,0,1:T(8,128)}, f32[8,32,128]{2,0,1:T(8,128)S(1)}, u32[]{:S(2)}) copy-start(f32[8,32,128]{2,0,1:T(8,128)S(1)} %all-to-all-done) | copy-start | bytes 393220
  57.0 13.7 %all-to-all-start.2 = ((f32[32,8,128]{2,1,0:T(8,128)}), f32[32,8,128]{2,1,0:T(8,128)S(1)}, u32[]{:S(2)}, u32[]{:S(2)}) async-start(f32[32,8,128]{2,1,0:T(8,128)} %fusion.100), calls=%async_computation.2 | async-start | bytes 262144 | tf_op jit(solution)/shard_map/all_to_all | solution.py:103
  71.8 16.8 %copy-start.8 = (bf16[1,1,4,128,128]{4,3,2,1,0:T(8,128)(2,1)S(1)}, bf16[1,1,4,128,128]{4,3,2,1,0:T(8,128)(2,1)}, u32[]{:S(2)}) copy-start(bf16[1,1,4,128,128]{4,3,2,1,0:T(8,128)(2,1)} %param.15) | copy-start | bytes 393220
  73.1 14.2 %collective-permute-start = (bf16[128,128]{1,0:T(8,128)(2,1)S(1)}, bf16[128,128]{1,0:T(8,128)(2,1)S(1)}, u32[]{:S(2)}, u32[]{:S(2)}) collective-permute-start(bf16[128,128]{1,0:T(8,128)(2,1)S(1)} %get-tuple-element.30), channel_id=1, source_target_pairs={{0,16},{16,32},{32,48},{48,64},{64,80},{80,96},{96,112},{112,128},... | collective-permute-start | bytes 98312 | tf_op jit(solution)/shard_map/ppermute | solution.py:12
  76.2 11.1 %collective-permute-start.1 = (bf16[128,128]{1,0:T(8,128)(2,1)S(1)}, bf16[128,128]{1,0:T(8,128)(2,1)S(1)}, u32[]{:S(2)}, u32[]{:S(2)}) collective-permute-start(bf16[128,128]{1,0:T(8,128)(2,1)S(1)} %get-tuple-element.32), channel_id=1, source_target_pairs={{16,0},{32,16},{48,32},{64,48},{80,64},{96,80},{112,96},{128,112},... | collective-permute-start | bytes 98312 | tf_op jit(solution)/shard_map/ppermute | solution.py:12
  77.5 9.8 %collective-permute-start.2 = (bf16[128,128]{1,0:T(8,128)(2,1)S(1)}, bf16[128,128]{1,0:T(8,128)(2,1)S(1)}, u32[]{:S(2)}, u32[]{:S(2)}) collective-permute-start(bf16[128,128]{1,0:T(8,128)(2,1)S(1)} %get-tuple-element.31), channel_id=1, source_target_pairs={{0,1},{1,2},{2,3},{3,4},{4,5},{5,6},{6,7},{7,8},{8,9},{9,10},{10,1... | collective-permute-start | bytes 98312 | tf_op jit(solution)/shard_map/ppermute | solution.py:12
  83.4 5.2 %collective-permute-start.3 = (bf16[128,128]{1,0:T(8,128)(2,1)S(1)}, bf16[128,128]{1,0:T(8,128)(2,1)S(1)}, u32[]{:S(2)}, u32[]{:S(2)}) collective-permute-start(bf16[128,128]{1,0:T(8,128)(2,1)S(1)} %get-tuple-element.33), channel_id=1, source_target_pairs={{1,0},{2,1},{3,2},{4,3},{5,4},{6,5},{7,6},{8,7},{9,8},{10,9},{11,1... | collective-permute-start | bytes 98312 | tf_op jit(solution)/shard_map/ppermute | solution.py:12
  124.6 12.8 %all-to-all-start.5 = ((f32[16,2,128]{2,1,0:T(2,128)}), f32[16,2,128]{2,1,0:T(2,128)S(1)}, u32[]{:S(2)}, u32[]{:S(2)}) async-start(f32[16,2,128]{2,1,0:T(2,128)} %broadcast_in_dim.44), calls=%async_computation.5 | async-start | bytes 32768 | tf_op jit(solution)/shard_map/all_to_all | solution.py:18
  138.6 15.2 %all-to-all-start.6 = ((f32[32,2,128]{2,1,0:T(2,128)}), f32[32,2,128]{2,1,0:T(2,128)S(1)}, u32[]{:S(2)}, u32[]{:S(2)}) async-start(f32[32,2,128]{2,1,0:T(2,128)} %broadcast_in_dim.45), calls=%async_computation.6 | async-start | bytes 65536 | tf_op jit(solution)/shard_map/all_to_all | solution.py:18
  143.8 12.0 %collective-permute-start.4 = (f32[2,128,128]{2,1,0:T(8,128)}, f32[2,128,128]{2,1,0:T(8,128)}, u32[]{:S(2)}, u32[]{:S(2)}) collective-permute-start(f32[2,128,128]{2,1,0:T(8,128)} %get-tuple-element.26), channel_id=1, source_target_pairs={{0,16},{16,32},{32,48},{48,64},{64,80},{80,96},{96,112},{112,128},... | collective-permute-start | bytes 393224 | tf_op jit(solution)/shard_map/ppermute | solution.py:12
  147.5 8.3 %collective-permute-start.5 = (f32[2,128,128]{2,1,0:T(8,128)}, f32[2,128,128]{2,1,0:T(8,128)}, u32[]{:S(2)}, u32[]{:S(2)}) collective-permute-start(f32[2,128,128]{2,1,0:T(8,128)} %get-tuple-element.29), channel_id=1, source_target_pairs={{16,0},{32,16},{48,32},{64,48},{80,64},{96,80},{112,96},{128,112},... | collective-permute-start | bytes 393224 | tf_op jit(solution)/shard_map/ppermute | solution.py:12
  148.8 7.1 %collective-permute-start.6 = (f32[2,128,128]{2,1,0:T(8,128)}, f32[2,128,128]{2,1,0:T(8,128)}, u32[]{:S(2)}, u32[]{:S(2)}) collective-permute-start(f32[2,128,128]{2,1,0:T(8,128)} %get-tuple-element.28), channel_id=1, source_target_pairs={{0,1},{1,2},{2,3},{3,4},{4,5},{5,6},{6,7},{7,8},{8,9},{9,10},{10,1... | collective-permute-start | bytes 393224 | tf_op jit(solution)/shard_map/ppermute | solution.py:12
  151.8 6.4 %collective-permute-start.7 = (f32[2,128,128]{2,1,0:T(8,128)S(1)}, f32[2,128,128]{2,1,0:T(8,128)}, u32[]{:S(2)}, u32[]{:S(2)}) collective-permute-start(f32[2,128,128]{2,1,0:T(8,128)S(1)} %get-tuple-element.27), channel_id=1, source_target_pairs={{1,0},{2,1},{3,2},{4,3},{5,4},{6,5},{7,6},{8,7},{9,8},{10,9},{11,1... | collective-permute-start | bytes 393224 | tf_op jit(solution)/shard_map/ppermute | solution.py:12
  153.8 1.4 copy-start.1
  155.2 4.1 %copy-start.9 = (bf16[1,1,4,128,128]{4,3,2,1,0:T(8,128)(2,1)S(1)}, bf16[1,1,4,128,128]{4,3,2,1,0:T(8,128)(2,1)}, u32[]{:S(2)}) copy-start(bf16[1,1,4,128,128]{4,3,2,1,0:T(8,128)(2,1)} %param.15) | copy-start | bytes 393220
  197.3 12.8 %all-to-all-start.9 = ((f32[16,2,128]{2,1,0:T(2,128)}), f32[16,2,128]{2,1,0:T(2,128)S(1)}, u32[]{:S(2)}, u32[]{:S(2)}) async-start(f32[16,2,128]{2,1,0:T(2,128)} %broadcast_in_dim.47), calls=%async_computation.9 | async-start | bytes 32768 | tf_op jit(solution)/shard_map/all_to_all | solution.py:18
  211.9 15.6 %all-to-all-start.10 = ((f32[32,2,128]{2,1,0:T(2,128)}), f32[32,2,128]{2,1,0:T(2,128)S(1)}, u32[]{:S(2)}, u32[]{:S(2)}) async-start(f32[32,2,128]{2,1,0:T(2,128)} %broadcast_in_dim.48), calls=%async_computation.10 | async-start | bytes 65536 | tf_op jit(solution)/shard_map/all_to_all | solution.py:18
  217.5 12.0 %collective-permute-start.8 = (f32[2,128,128]{2,1,0:T(8,128)}, f32[2,128,128]{2,1,0:T(8,128)}, u32[]{:S(2)}, u32[]{:S(2)}) collective-permute-start(f32[2,128,128]{2,1,0:T(8,128)} %get-tuple-element.22), channel_id=1, source_target_pairs={{0,16},{16,32},{32,48},{48,64},{64,80},{80,96},{96,112},{112,128},... | collective-permute-start | bytes 393224 | tf_op jit(solution)/shard_map/ppermute | solution.py:12
  221.2 8.3 %collective-permute-start.9 = (f32[2,128,128]{2,1,0:T(8,128)}, f32[2,128,128]{2,1,0:T(8,128)}, u32[]{:S(2)}, u32[]{:S(2)}) collective-permute-start(f32[2,128,128]{2,1,0:T(8,128)} %get-tuple-element.25), channel_id=1, source_target_pairs={{16,0},{32,16},{48,32},{64,48},{80,64},{96,80},{112,96},{128,112},... | collective-permute-start | bytes 393224 | tf_op jit(solution)/shard_map/ppermute | solution.py:12
  222.5 7.1 %collective-permute-start.10 = (f32[2,128,128]{2,1,0:T(8,128)}, f32[2,128,128]{2,1,0:T(8,128)}, u32[]{:S(2)}, u32[]{:S(2)}) collective-permute-start(f32[2,128,128]{2,1,0:T(8,128)} %get-tuple-element.24), channel_id=1, source_target_pairs={{0,1},{1,2},{2,3},{3,4},{4,5},{5,6},{6,7},{7,8},{8,9},{9,10},{10,1... | collective-permute-start | bytes 393224 | tf_op jit(solution)/shard_map/ppermute | solution.py:12
  225.5 6.6 %collective-permute-start.11 = (f32[2,128,128]{2,1,0:T(8,128)}, f32[2,128,128]{2,1,0:T(8,128)}, u32[]{:S(2)}, u32[]{:S(2)}) collective-permute-start(f32[2,128,128]{2,1,0:T(8,128)} %get-tuple-element.23), channel_id=1, source_target_pairs={{1,0},{2,1},{3,2},{4,3},{5,4},{6,5},{7,6},{8,7},{9,8},{10,9},{11,1... | collective-permute-start | bytes 393224 | tf_op jit(solution)/shard_map/ppermute | solution.py:12
  227.5 1.4 copy-start.2
  228.9 4.3 %copy-start.10 = (bf16[1,1,4,128,128]{4,3,2,1,0:T(8,128)(2,1)S(1)}, bf16[1,1,4,128,128]{4,3,2,1,0:T(8,128)(2,1)}, u32[]{:S(2)}) copy-start(bf16[1,1,4,128,128]{4,3,2,1,0:T(8,128)(2,1)} %param.15) | copy-start | bytes 393220
  238.0 0.7 copy-start.7
  285.8 12.6 %all-to-all-start.14 = ((f32[32,2,128]{2,1,0:T(2,128)}), f32[32,2,128]{2,1,0:T(2,128)S(1)}, u32[]{:S(2)}, u32[]{:S(2)}) async-start(f32[32,2,128]{2,1,0:T(2,128)} %broadcast_in_dim.51), calls=%async_computation.14 | async-start | bytes 65536 | tf_op jit(solution)/shard_map/all_to_all | solution.py:18
  299.3 1.6 copy-start.12
  300.9 10.6 %copy-start.3 = (bf16[1,1,896,896]{3,2,1,0:T(8,128)(2,1)S(1)}, bf16[1,1,896,896]{3,2,1,0:T(8,128)(2,1)}, u32[]{:S(2)}) copy-start(bf16[1,1,896,896]{3,2,1,0:T(8,128)(2,1)} %param.11) | copy-start | bytes 4816900
  300.9 10.6 %copy-start.13 = (bf16[896,128]{1,0:T(8,128)(2,1)S(1)}, bf16[896,128]{1,0:T(8,128)(2,1)}, u32[]{:S(2)}) copy-start(bf16[896,128]{1,0:T(8,128)(2,1)} %get-tuple-element.8) | copy-start | bytes 688132
  302.1 10.1 %collective-permute-start.12 = (f32[2,128,128]{2,1,0:T(8,128)S(1)}, f32[2,128,128]{2,1,0:T(8,128)S(1)}, u32[]{:S(2)}, u32[]{:S(2)}) collective-permute-start(f32[2,128,128]{2,1,0:T(8,128)S(1)} %get-tuple-element.18), channel_id=1, source_target_pairs={{0,16},{16,32},{32,48},{48,64},{64,80},{80,96},{96,112},{112,128},... | collective-permute-start | bytes 393224 | tf_op jit(solution)/shard_map/ppermute | solution.py:12
  304.4 7.8 %collective-permute-start.13 = (f32[2,128,128]{2,1,0:T(8,128)S(1)}, f32[2,128,128]{2,1,0:T(8,128)S(1)}, u32[]{:S(2)}, u32[]{:S(2)}) collective-permute-start(f32[2,128,128]{2,1,0:T(8,128)S(1)} %get-tuple-element.21), channel_id=1, source_target_pairs={{16,0},{32,16},{48,32},{64,48},{80,64},{96,80},{112,96},{128,112},... | collective-permute-start | bytes 393224 | tf_op jit(solution)/shard_map/ppermute | solution.py:12
  305.7 6.5 %collective-permute-start.14 = (f32[2,128,128]{2,1,0:T(8,128)S(1)}, f32[2,128,128]{2,1,0:T(8,128)S(1)}, u32[]{:S(2)}, u32[]{:S(2)}) collective-permute-start(f32[2,128,128]{2,1,0:T(8,128)S(1)} %get-tuple-element.20), channel_id=1, source_target_pairs={{0,1},{1,2},{2,3},{3,4},{4,5},{5,6},{6,7},{7,8},{8,9},{9,10},{10,1... | collective-permute-start | bytes 393224 | tf_op jit(solution)/shard_map/ppermute | solution.py:12
  309.6 6.3 %collective-permute-start.15 = (f32[2,128,128]{2,1,0:T(8,128)S(1)}, f32[2,128,128]{2,1,0:T(8,128)S(1)}, u32[]{:S(2)}, u32[]{:S(2)}) collective-permute-start(f32[2,128,128]{2,1,0:T(8,128)S(1)} %get-tuple-element.19), channel_id=1, source_target_pairs={{1,0},{2,1},{3,2},{4,3},{5,4},{6,5},{7,6},{8,7},{9,8},{10,9},{11,1... | collective-permute-start | bytes 393224 | tf_op jit(solution)/shard_map/ppermute | solution.py:12
  311.6 4.4 %copy-start.11 = (bf16[1,1,4,128,128]{4,3,2,1,0:T(8,128)(2,1)S(1)}, bf16[1,1,4,128,128]{4,3,2,1,0:T(8,128)(2,1)}, u32[]{:S(2)}) copy-start(bf16[1,1,4,128,128]{4,3,2,1,0:T(8,128)(2,1)} %param.15) | copy-start | bytes 393220
  316.9 3.9 %copy-start.6 = (bf16[1,1,896,128]{3,2,1,0:T(8,128)(2,1)S(1)}, bf16[1,1,896,128]{3,2,1,0:T(8,128)(2,1)}, u32[]{:S(2)}) copy-start(bf16[1,1,896,128]{3,2,1,0:T(8,128)(2,1)} %param.10) | copy-start | bytes 688132

commit v8 on v6

--- a/solution.py
+++ b/solution.py
@@ -54,7 +54,12 @@
     trace_scale = trace_diag[0, 0][:, None]
     coupling_blocks = couplings[0, 0]
     rows_lists = margin_rows[0, 0]
-    flat_rows = rows_lists.reshape(-1)
+    sides, width = coupling_blocks.shape[0], coupling_blocks.shape[-1]
+    placed_couplings = (
+        jnp.zeros((schur_mat.shape[0], sides * width), coupling_blocks.dtype)
+        .at[rows_lists[:, :, None], (jnp.arange(sides)[:, None, None] * width + jnp.arange(width))]
+        .set(coupling_blocks)
+    )
     vectors = deflation[0, 0]
     vectors_wide = vectors.astype(jnp.float32).T
     count_x, count_y = lax.axis_size("gx"), lax.axis_size("gy")
@@ -78,10 +83,10 @@
         result = schur_scale * rounded.astype(jnp.float32) + jnp.dot(
             schur_mat, rounded, preferred_element_type=jnp.float32
         )
-        coupled = jnp.einsum(
-            "dab,dbs->das", coupling_blocks, received, preferred_element_type=jnp.float32
+        coupled = jnp.dot(
+            placed_couplings, received.reshape(-1, received.shape[-1]), preferred_element_type=jnp.float32
         )
-        return result.at[flat_rows].add(-coupled.reshape(-1, coupled.shape[-1]))
+        return result - coupled
 
     def apply_schur(field):
         rounded = lax.optimization_barrier(field.astype(jnp.bfloat16))

time: 325 us -> 767 us (2.36)
  local copies, waits for them, and re-layouts: 34.3 us -> 493 us
  other arithmetic: 31.6 us -> 18.3 us
  waiting for transfers between devices: 62.9 us -> 50.9 us
    unnamed x39 -> x64, local copies, waits for them, and re-layouts: 3.3 us -> 456 us
    scatter-add x4 -> x0, other arithmetic: 14.5 us -> none  [finish_schur(): return result.at[flat_rows].add(-coupled.reshape(-1, coupled.shape[-1]))]
    all_to_all x1, waiting for transfers between devices: 9.13 us -> 0.01 us  [shards(): lax.all_to_all(coarse_cols.reshape(depth, count_x, count_y * depth), 'gx'...]
  transfers between devices with their start and end apart: 26 -> 26, of which waited for: 9 -> 7; matrix products, arithmetic and copies ran while one was open for 12% -> 64% of each run, Pallas kernels for 0% -> 0%
where the time goes in v8:
time: 767 us; the launch traced here: 764 us
  local copies, waits for them, and re-layouts  493 us (64%)
  starting transfers between devices  115 us (15%)
  blocking collectives  60.4 us (8%)
  waiting for transfers between devices  50.9 us (7%)
  matrix products  23.2 us (3%)
  other arithmetic  18.3 us (2%)
    unnamed x64, local copies, waits for them, and re-layouts  456 us
    all_to_all x5, blocking collectives, gather_rows(): lax.all_to_all(copies.reshape((-1,) + value.shape[1:]), axis, 0, 0, tiled...  60.4 us
    ppermute x16, starting transfers between devices, from_behind(): lax.ppermute(value, axis, [(source, source + steps) for source in range(l...  46.7 us
    all_to_all x5, starting transfers between devices, gather_rows(): lax.all_to_all(copies.reshape((-1,) + value.shape[1:]), axis, 0, 0, tiled...  33.7 us
    all_to_all x5, waiting for transfers between devices, gather_rows(): lax.all_to_all(copies.reshape((-1,) + value.shape[1:]), axis, 0, 0, tiled...  26.9 us
    all_to_all x4, starting transfers between devices, apply_prec(): pieces = lax.all_to_all(partial, 'gx', 0, 0, tiled=True)  25 us
    all_to_all x4, waiting for transfers between devices, apply_prec(): pieces = lax.all_to_all(partial, 'gx', 0, 0, tiled=True)  24 us
    gather x2, local copies, waits for them, and re-layouts, shards(): coarse_cols = jnp.take(coarse_inverse, coarse_map, axis=1)  17.9 us
  transfers between devices with their start and end apart: 26, of which 7 were waited for; matrix products, arithmetic and copies ran while one was open for 64% of the time, Pallas kernels for 0%

profile of v8, /device:TPU:1, one launch (start us, length us, event | category | flops | bytes accessed | tf_op | source)
XLA Modules:
  0.0 764.4 jit_solution(16109511515207688700)
XLA Ops:
  2.5 11.8 %all-to-all-start.1 = ((f32[16,8,128]{2,1,0:T(8,128)}), f32[16,8,128]{2,1,0:T(8,128)S(1)}, u32[]{:S(2)}, u32[]{:S(2)}) async-start(f32[16,8,128]{2,1,0:T(8,128)} %broadcast_in_dim.48), calls=%async_computation.1 | async-start | bytes 131072 | tf_op jit(solution)/shard_map/all_to_all | solution.py:18
  15.8 2.8 copy.77
  18.6 15.8 %gather_fusion = f32[4096,8]{1,0:T(8,128)} fusion(f32[8,4096]{0,1:T(8,128)} %copy.77, s32[4096]{0:T(1024)S(1)} %fusion.153), kind=kCustom, calls=%fused_computation | custom fusion | bytes 278528 | tf_op jit(solution)/shard_map/jit(_take)/gather | solution.py:67
  34.4 2.2 copy.78
  37.7 9.8 %all-to-all-start = ((f32[8,32,128]{2,0,1:T(8,128)}), f32[8,32,128]{2,0,1:T(8,128)}, u32[]{:S(2)}, u32[]{:S(2)}) async-start(f32[8,32,128]{2,0,1:T(8,128)} %broadcast_select_fusion.1), calls=%async_computation | async-start | bytes 262144 | tf_op jit(solution)/shard_map/all_to_all | solution.py:68
  47.8 448.8 %scatter_custom_fusion = bf16[458752]{0:T(1024)(128)(2,1)S(1)} fusion(s32[65536]{0:T(1024)S(1)} %bitcast.362, bf16[65536]{0:T(1024)(128)(2,1)} %bitcast.375, bf16[]{:T(256)} %constant.14.clone.1), kind=kCustom, calls=%fused_computation.88 | custom fusion | bytes 918016
  497.2 2.0 fusion.138
  499.2 9.2 %all-to-all-start.2 = ((f32[32,8,128]{2,1,0:T(8,128)}), f32[32,8,128]{2,1,0:T(8,128)S(1)}, u32[]{:S(2)}, u32[]{:S(2)}) async-start(f32[32,8,128]{2,1,0:T(8,128)} %fusion.138), calls=%async_computation.2 | async-start | bytes 262144 | tf_op jit(solution)/shard_map/all_to_all | solution.py:111
  508.4 9.2 %all-to-all-done.2 = f32[32,8,128]{2,1,0:T(8,128)S(1)} async-done(((f32[32,8,128]{2,1,0:T(8,128)}), f32[32,8,128]{2,1,0:T(8,128)S(1)}, u32[]{:S(2)}, u32[]{:S(2)}) %all-to-all-start.2) | async-done | bytes 131104 | tf_op jit(solution)/shard_map/all_to_all | solution.py:111
  518.0 1.6 fusion.162
  519.7 1.3 gather_fusion.1
  521.0 3.9 collective-permute-start.3
  524.9 3.5 collective-permute-start.2
  528.4 1.3 collective-permute-start.1
  529.7 4.0 collective-permute-start
  533.7 2.0 fusion.37
  537.0 14.2 %all_to_all.111 = f32[16,8,128]{2,1,0:T(8,128)S(1)} all-to-all(f32[16,8,128]{2,1,0:T(8,128)S(1)} %broadcast_in_dim.52), channel_id=1, replica_groups=mesh['gx'=32,'gy'=16] {'gy'}, dimensions={0} | all-to-all | bytes 131072 | tf_op jit(solution)/shard_map/all_to_all | solution.py:18
  551.3 1.8 fusion.136
  553.1 7.2 all-to-all-start.4
  560.3 1.6 gather_fusion.2
  562.0 7.3 all-to-all-done.4
  569.7 1.7 multiply_reduce_fusion.5
  571.4 1.6 gather_fusion.3
  573.1 1.9 fusion.126
  575.0 4.0 collective-permute-start.7
  579.0 2.0 collective-permute-start.6
  581.0 1.3 collective-permute-start.5
  582.3 4.0 collective-permute-start.4
  586.3 10.8 %all_to_all.112 = f32[16,2,128]{2,1,0:T(2,128)S(1)} all-to-all(f32[16,2,128]{2,1,0:T(2,128)S(1)} %broadcast_in_dim.53), channel_id=1, replica_groups=mesh['gx'=32,'gy'=16] {'gy'}, dimensions={0} | all-to-all | bytes 32768 | tf_op jit(solution)/shard_map/all_to_all | solution.py:18
  600.9 4.9 all-to-all-start.6
  606.6 7.9 %all-to-all-done.6 = f32[32,2,128]{2,1,0:T(2,128)S(1)} async-done(((f32[32,2,128]{2,1,0:T(2,128)}), f32[32,2,128]{2,1,0:T(2,128)S(1)}, u32[]{:S(2)}, u32[]{:S(2)}) %all-to-all-start.6) | async-done | bytes 32800 | tf_op jit(solution)/shard_map/all_to_all | solution.py:18
  614.7 1.2 fusion.157
  617.8 12.0 %all_to_all.113 = f32[16,8,128]{2,1,0:T(8,128)S(1)} all-to-all(f32[16,8,128]{2,1,0:T(8,128)S(1)} %broadcast_in_dim.55), channel_id=1, replica_groups=mesh['gx'=32,'gy'=16] {'gy'}, dimensions={0} | all-to-all | bytes 131072 | tf_op jit(solution)/shard_map/all_to_all | solution.py:18
  629.8 1.8 fusion.134
  631.7 4.7 all-to-all-start.8
  636.4 1.6 gather_fusion.4
  638.0 7.5 all-to-all-done.8
  646.9 2.4 multiply_reduce_fusion.3
  649.3 2.6 gather_fusion.5
  651.9 1.9 fusion.120
  653.8 3.9 collective-permute-start.11
  657.8 2.1 collective-permute-start.10
  659.8 1.3 collective-permute-start.9
  661.1 4.6 collective-permute-start.8
  665.8 11.3 %all_to_all.114 = f32[16,2,128]{2,1,0:T(2,128)S(1)} all-to-all(f32[16,2,128]{2,1,0:T(2,128)S(1)} %broadcast_in_dim.56), channel_id=1, replica_groups=mesh['gx'=32,'gy'=16] {'gy'}, dimensions={0} | all-to-all | bytes 32768 | tf_op jit(solution)/shard_map/all_to_all | solution.py:18
  677.2 1.3 maximum_reduce_fusion.1
  678.5 1.9 pad_maximum_fusion.1
  681.8 4.3 all-to-all-start.10
  686.0 1.9 fusion.159
  687.9 6.9 all-to-all-done.10
  696.5 1.3 copy-done.2
  698.6 12.0 %all_to_all.115 = f32[16,8,128]{2,1,0:T(8,128)S(1)} all-to-all(f32[16,8,128]{2,1,0:T(8,128)S(1)} %broadcast_in_dim.58), channel_id=1, replica_groups=mesh['gx'=32,'gy'=16] {'gy'}, dimensions={0} | all-to-all | bytes 131072 | tf_op jit(solution)/shard_map/all_to_all | solution.py:18
  710.6 1.8 fusion.132
  712.4 3.9 all-to-all-start.12
  719.1 2.0 collective-permute-start.15
  721.2 3.5 collective-permute-start.14
  724.7 1.3 collective-permute-start.13
  726.0 4.0 collective-permute-start.12
  731.7 3.5 all-to-all-start.13
  737.4 5.2 all-to-all-done.13
  743.2 9.2 %all-to-all-start.14 = ((f32[32,2,128]{2,1,0:T(2,128)}), f32[32,2,128]{2,1,0:T(2,128)S(1)}, u32[]{:S(2)}, u32[]{:S(2)}) async-start(f32[32,2,128]{2,1,0:T(2,128)} %broadcast_in_dim.60), calls=%async_computation.14 | async-start | bytes 65536 | tf_op jit(solution)/shard_map/all_to_all | solution.py:18
  752.5 1.9 fusion.158
  754.4 6.8 all-to-all-done.14
  763.0 1.4 fusion.85
  (155 shorter events, 26.1 us)
Async XLA Ops:
  0.6 517.4 %copy-start = (bf16[1,1,896,896]{3,2,1,0:T(8,128)(2,1)S(1)}, bf16[1,1,896,896]{3,2,1,0:T(8,128)(2,1)}, u32[]{:S(2)}) copy-start(bf16[1,1,896,896]{3,2,1,0:T(8,128)(2,1)} %param.13) | copy-start | bytes 4816900
  2.5 35.2 %all-to-all-start.1 = ((f32[16,8,128]{2,1,0:T(8,128)}), f32[16,8,128]{2,1,0:T(8,128)S(1)}, u32[]{:S(2)}, u32[]{:S(2)}) async-start(f32[16,8,128]{2,1,0:T(8,128)} %broadcast_in_dim.48), calls=%async_computation.1 | async-start | bytes 131072 | tf_op jit(solution)/shard_map/all_to_all | solution.py:18
  18.6 18.0 %copy-start.26 = (s32[1,1,4,128]{3,2,1,0:T(4,128)S(1)}, s32[1,1,4,128]{3,2,1,0:T(4,128)}, u32[]{:S(2)}) copy-start(s32[1,1,4,128]{3,2,1,0:T(4,128)} %param.16) | copy-start | bytes 6148
  34.4 3.1 copy-start.30
  34.4 13.1 %copy-start.29 = (s32[2]{0:T(128)S(1)}, s32[2]{0:T(128)}, u32[]{:S(2)}) copy-start(s32[2]{0:T(128)} %constant.39) | copy-start | bytes 28
  36.6 11.1 %copy-start.27 = (f32[1,1,896]{2,1,0:T(1,128)S(1)}, f32[1,1,896]{2,1,0:T(1,128)}, u32[]{:S(2)}) copy-start(f32[1,1,896]{2,1,0:T(1,128)} %param.14) | copy-start | bytes 10756
  36.6 11.1 %copy-start.28 = (f32[1,1,896]{2,1,0:T(1,128)S(1)}, f32[1,1,896]{2,1,0:T(1,128)}, u32[]{:S(2)}) copy-start(f32[1,1,896]{2,1,0:T(1,128)} %param.12) | copy-start | bytes 10756
  37.7 459.5 %all-to-all-start = ((f32[8,32,128]{2,0,1:T(8,128)}), f32[8,32,128]{2,0,1:T(8,128)}, u32[]{:S(2)}, u32[]{:S(2)}) async-start(f32[8,32,128]{2,0,1:T(8,128)} %broadcast_select_fusion.1), calls=%async_computation | async-start | bytes 262144 | tf_op jit(solution)/shard_map/all_to_all | solution.py:68
  47.7 522.0 %copy-start.22 = (f32[896]{0:T(1024)}, f32[896]{0:T(1024)S(1)}, u32[]{:S(2)}) copy-start(f32[896]{0:T(1024)S(1)} %reduce.15) | copy-start | bytes 10756
  47.7 485.9 %copy-start.20 = (f32[896]{0:T(1024)}, f32[896]{0:T(1024)S(1)}, u32[]{:S(2)}) copy-start(f32[896]{0:T(1024)S(1)} %reduce.16) | copy-start | bytes 10756
  47.8 469.8 %copy-start.15 = (bf16[1,1,8,896]{3,2,1,0:T(8,128)(2,1)S(1)}, bf16[1,1,8,896]{3,2,1,0:T(8,128)(2,1)}, u32[]{:S(2)}) copy-start(bf16[1,1,8,896]{3,2,1,0:T(8,128)(2,1)} %param.17) | copy-start | bytes 43012
  497.2 198.8 %copy-start.4 = (bf16[896,512]{1,0:T(8,128)(2,1)}, bf16[896,512]{1,0:T(8,128)(2,1)S(1)}, u32[]{:S(2)}) copy-start(bf16[896,512]{1,0:T(8,128)(2,1)S(1)} %reshape.232) | copy-start | bytes 2752516
  499.2 18.4 %all-to-all-start.2 = ((f32[32,8,128]{2,1,0:T(8,128)}), f32[32,8,128]{2,1,0:T(8,128)S(1)}, u32[]{:S(2)}, u32[]{:S(2)}) async-start(f32[32,8,128]{2,1,0:T(8,128)} %fusion.138), calls=%async_computation.2 | async-start | bytes 262144 | tf_op jit(solution)/shard_map/all_to_all | solution.py:111
  508.3 63.1 %copy-start.24 = (s32[1024]{0:T(1024)}, s32[1024]{0:T(1024)S(1)}, u32[]{:S(2)}) copy-start(s32[1024]{0:T(1024)S(1)} %pad_clamp_fusion) | copy-start | bytes 12292
  521.0 14.6 %collective-permute-start.3 = (bf16[128,128]{1,0:T(8,128)(2,1)S(1)}, bf16[128,128]{1,0:T(8,128)(2,1)S(1)}, u32[]{:S(2)}, u32[]{:S(2)}) collective-permute-start(bf16[128,128]{1,0:T(8,128)(2,1)S(1)} %get-tuple-element.40), channel_id=1, source_target_pairs={{1,0},{2,1},{3,2},{4,3},{5,4},{6,5},{7,6},{8,7},{9,8},{10,9},{11,1... | collective-permute-start | bytes 98312 | tf_op jit(solution)/shard_map/ppermute | solution.py:12
  524.9 10.8 %collective-permute-start.2 = (bf16[128,128]{1,0:T(8,128)(2,1)S(1)}, bf16[128,128]{1,0:T(8,128)(2,1)S(1)}, u32[]{:S(2)}, u32[]{:S(2)}) collective-permute-start(bf16[128,128]{1,0:T(8,128)(2,1)S(1)} %get-tuple-element.38), channel_id=1, source_target_pairs={{0,1},{1,2},{2,3},{3,4},{4,5},{5,6},{6,7},{7,8},{8,9},{9,10},{10,1... | collective-permute-start | bytes 98312 | tf_op jit(solution)/shard_map/ppermute | solution.py:12
  528.4 7.3 collective-permute-start.1
  529.7 6.1 collective-permute-start
  536.2 0.7 copy-start.10
  553.1 16.2 %all-to-all-start.4 = ((f32[32,8,128]{2,1,0:T(8,128)}), f32[32,8,128]{2,1,0:T(8,128)S(1)}, u32[]{:S(2)}, u32[]{:S(2)}) async-start(f32[32,8,128]{2,1,0:T(8,128)} %fusion.136), calls=%async_computation.4 | async-start | bytes 262144 | tf_op jit(solution)/shard_map/all_to_all | solution.py:111
  571.4 3.5 copy-start.7
  575.0 22.2 %collective-permute-start.7 = (f32[2,128,128]{2,1,0:T(8,128)}, f32[2,128,128]{2,1,0:T(8,128)S(1)}, u32[]{:S(2)}, u32[]{:S(2)}) collective-permute-start(f32[2,128,128]{2,1,0:T(8,128)} %get-tuple-element.34), channel_id=1, source_target_pairs={{1,0},{2,1},{3,2},{4,3},{5,4},{6,5},{7,6},{8,7},{9,8},{10,9},{11,1... | collective-permute-start | bytes 393224 | tf_op jit(solution)/shard_map/ppermute | solution.py:12
  579.0 18.2 %collective-permute-start.6 = (f32[2,128,128]{2,1,0:T(8,128)}, f32[2,128,128]{2,1,0:T(8,128)S(1)}, u32[]{:S(2)}, u32[]{:S(2)}) collective-permute-start(f32[2,128,128]{2,1,0:T(8,128)} %get-tuple-element.35), channel_id=1, source_target_pairs={{0,1},{1,2},{2,3},{3,4},{4,5},{5,6},{6,7},{7,8},{8,9},{9,10},{10,1... | collective-permute-start | bytes 393224 | tf_op jit(solution)/shard_map/ppermute | solution.py:12
  581.0 16.2 %collective-permute-start.5 = (f32[2,128,128]{2,1,0:T(8,128)}, f32[2,128,128]{2,1,0:T(8,128)S(1)}, u32[]{:S(2)}, u32[]{:S(2)}) collective-permute-start(f32[2,128,128]{2,1,0:T(8,128)} %get-tuple-element.33), channel_id=1, source_target_pairs={{16,0},{32,16},{48,32},{64,48},{80,64},{96,80},{112,96},{128,112},... | collective-permute-start | bytes 393224 | tf_op jit(solution)/shard_map/ppermute | solution.py:12
  582.3 14.9 %collective-permute-start.4 = (f32[2,128,128]{2,1,0:T(8,128)}, f32[2,128,128]{2,1,0:T(8,128)S(1)}, u32[]{:S(2)}, u32[]{:S(2)}) collective-permute-start(f32[2,128,128]{2,1,0:T(8,128)} %get-tuple-element.32), channel_id=1, source_target_pairs={{0,16},{16,32},{32,48},{48,64},{64,80},{80,96},{96,112},{112,128},... | collective-permute-start | bytes 393224 | tf_op jit(solution)/shard_map/ppermute | solution.py:12
  597.1 0.7 copy-start.16
  597.1 0.7 copy-start.17
  597.2 0.7 copy-start.18
  597.2 0.7 copy-start.19
  600.9 13.6 %all-to-all-start.6 = ((f32[32,2,128]{2,1,0:T(2,128)}), f32[32,2,128]{2,1,0:T(2,128)S(1)}, u32[]{:S(2)}, u32[]{:S(2)}) async-start(f32[32,2,128]{2,1,0:T(2,128)} %broadcast_in_dim.54), calls=%async_computation.6 | async-start | bytes 65536 | tf_op jit(solution)/shard_map/all_to_all | solution.py:18
  614.6 1.3 copy-start.11
  614.6 1.3 copy-start.12
  614.6 1.7 copy-start.1
  614.6 1.7 copy-start.21
  616.4 20.0 %copy-start.25 = (s32[1024]{0:T(1024)S(1)}, s32[1024]{0:T(1024)}, u32[]{:S(2)}) copy-start(s32[1024]{0:T(1024)} %copy-done.24) | copy-start | bytes 12292
  617.0 0.7 copy-start.9
  631.7 15.2 %copy-start.23 = (f32[896]{0:T(1024)S(1)}, f32[896]{0:T(1024)}, u32[]{:S(2)}) copy-start(f32[896]{0:T(1024)} %copy-done.22) | copy-start | bytes 10756
  631.7 13.8 %all-to-all-start.8 = ((f32[32,8,128]{2,1,0:T(8,128)}), f32[32,8,128]{2,1,0:T(8,128)}, u32[]{:S(2)}, u32[]{:S(2)}) async-start(f32[32,8,128]{2,1,0:T(8,128)} %fusion.134), calls=%async_computation.8 | async-start | bytes 262144 | tf_op jit(solution)/shard_map/all_to_all | solution.py:111
  653.8 23.4 %collective-permute-start.11 = (f32[2,128,128]{2,1,0:T(8,128)}, f32[2,128,128]{2,1,0:T(8,128)}, u32[]{:S(2)}, u32[]{:S(2)}) collective-permute-start(f32[2,128,128]{2,1,0:T(8,128)} %get-tuple-element.28), channel_id=1, source_target_pairs={{1,0},{2,1},{3,2},{4,3},{5,4},{6,5},{7,6},{8,7},{9,8},{10,9},{11,1... | collective-permute-start | bytes 393224 | tf_op jit(solution)/shard_map/ppermute | solution.py:12
  657.8 19.4 %collective-permute-start.10 = (f32[2,128,128]{2,1,0:T(8,128)}, f32[2,128,128]{2,1,0:T(8,128)}, u32[]{:S(2)}, u32[]{:S(2)}) collective-permute-start(f32[2,128,128]{2,1,0:T(8,128)} %get-tuple-element.29), channel_id=1, source_target_pairs={{0,1},{1,2},{2,3},{3,4},{4,5},{5,6},{6,7},{7,8},{8,9},{9,10},{10,1... | collective-permute-start | bytes 393224 | tf_op jit(solution)/shard_map/ppermute | solution.py:12
  659.8 17.4 %collective-permute-start.9 = (f32[2,128,128]{2,1,0:T(8,128)}, f32[2,128,128]{2,1,0:T(8,128)}, u32[]{:S(2)}, u32[]{:S(2)}) collective-permute-start(f32[2,128,128]{2,1,0:T(8,128)} %get-tuple-element.27), channel_id=1, source_target_pairs={{16,0},{32,16},{48,32},{64,48},{80,64},{96,80},{112,96},{128,112},... | collective-permute-start | bytes 393224 | tf_op jit(solution)/shard_map/ppermute | solution.py:12
  661.1 16.1 %collective-permute-start.8 = (f32[2,128,128]{2,1,0:T(8,128)}, f32[2,128,128]{2,1,0:T(8,128)}, u32[]{:S(2)}, u32[]{:S(2)}) collective-permute-start(f32[2,128,128]{2,1,0:T(8,128)} %get-tuple-element.26), channel_id=1, source_target_pairs={{0,16},{16,32},{32,48},{48,64},{64,80},{80,96},{96,112},{112,128},... | collective-permute-start | bytes 393224 | tf_op jit(solution)/shard_map/ppermute | solution.py:12
  681.8 13.0 %all-to-all-start.10 = ((f32[32,2,128]{2,1,0:T(2,128)}), f32[32,2,128]{2,1,0:T(2,128)S(1)}, u32[]{:S(2)}, u32[]{:S(2)}) async-start(f32[32,2,128]{2,1,0:T(2,128)} %broadcast_in_dim.57), calls=%async_computation.10 | async-start | bytes 65536 | tf_op jit(solution)/shard_map/all_to_all | solution.py:18
  694.8 1.6 copy-start.6
  696.4 1.4 copy-start.2
  712.4 17.6 %all-to-all-start.12 = ((f32[32,8,128]{2,1,0:T(8,128)}), f32[32,8,128]{2,1,0:T(8,128)S(1)}, u32[]{:S(2)}, u32[]{:S(2)}) async-start(f32[32,8,128]{2,1,0:T(8,128)} %fusion.132), calls=%async_computation.12 | async-start | bytes 262144 | tf_op jit(solution)/shard_map/all_to_all | solution.py:111
  719.1 16.1 %collective-permute-start.15 = (f32[2,128,128]{2,1,0:T(8,128)}, f32[2,128,128]{2,1,0:T(8,128)S(1)}, u32[]{:S(2)}, u32[]{:S(2)}) collective-permute-start(f32[2,128,128]{2,1,0:T(8,128)} %get-tuple-element.22), channel_id=1, source_target_pairs={{1,0},{2,1},{3,2},{4,3},{5,4},{6,5},{7,6},{8,7},{9,8},{10,9},{11,1... | collective-permute-start | bytes 393224 | tf_op jit(solution)/shard_map/ppermute | solution.py:12
  721.2 14.1 %collective-permute-start.14 = (f32[2,128,128]{2,1,0:T(8,128)}, f32[2,128,128]{2,1,0:T(8,128)S(1)}, u32[]{:S(2)}, u32[]{:S(2)}) collective-permute-start(f32[2,128,128]{2,1,0:T(8,128)} %get-tuple-element.23), channel_id=1, source_target_pairs={{0,1},{1,2},{2,3},{3,4},{4,5},{5,6},{6,7},{7,8},{8,9},{9,10},{10,1... | collective-permute-start | bytes 393224 | tf_op jit(solution)/shard_map/ppermute | solution.py:12
  724.7 10.6 %collective-permute-start.13 = (f32[2,128,128]{2,1,0:T(8,128)}, f32[2,128,128]{2,1,0:T(8,128)S(1)}, u32[]{:S(2)}, u32[]{:S(2)}) collective-permute-start(f32[2,128,128]{2,1,0:T(8,128)} %get-tuple-element.21), channel_id=1, source_target_pairs={{16,0},{32,16},{48,32},{64,48},{80,64},{96,80},{112,96},{128,112},... | collective-permute-start | bytes 393224 | tf_op jit(solution)/shard_map/ppermute | solution.py:12
  726.0 9.3 %collective-permute-start.12 = (f32[2,128,128]{2,1,0:T(8,128)}, f32[2,128,128]{2,1,0:T(8,128)S(1)}, u32[]{:S(2)}, u32[]{:S(2)}) collective-permute-start(f32[2,128,128]{2,1,0:T(8,128)} %get-tuple-element.20), channel_id=1, source_target_pairs={{0,16},{16,32},{32,48},{48,64},{64,80},{80,96},{96,112},{112,128},... | collective-permute-start | bytes 393224 | tf_op jit(solution)/shard_map/ppermute | solution.py:12
  731.7 10.9 %all-to-all-start.13 = ((f32[16,2,128]{2,1,0:T(2,128)}), f32[16,2,128]{2,1,0:T(2,128)S(1)}, u32[]{:S(2)}, u32[]{:S(2)}) async-start(f32[16,2,128]{2,1,0:T(2,128)} %broadcast_in_dim.59), calls=%async_computation.13 | async-start | bytes 32768 | tf_op jit(solution)/shard_map/all_to_all | solution.py:18
  743.2 18.0 %all-to-all-start.14 = ((f32[32,2,128]{2,1,0:T(2,128)}), f32[32,2,128]{2,1,0:T(2,128)S(1)}, u32[]{:S(2)}, u32[]{:S(2)}) async-start(f32[32,2,128]{2,1,0:T(2,128)} %broadcast_in_dim.60), calls=%async_computation.14 | async-start | bytes 65536 | tf_op jit(solution)/shard_map/all_to_all | solution.py:18
  752.5 10.0 %copy-start.5 = (bf16[896,512]{1,0:T(8,128)(2,1)S(1)}, bf16[896,512]{1,0:T(8,128)(2,1)}, u32[]{:S(2)}) copy-start(bf16[896,512]{1,0:T(8,128)(2,1)} %copy-done.4) | copy-start | bytes 2752516
  761.3 1.0 copy-start.13
  761.3 1.1 copy-start.14
  761.3 1.7 copy-start.3
  761.3 1.7 copy-start.8

commit v9 on v8

--- a/solution.py
+++ b/solution.py
@@ -55,10 +55,13 @@
     coupling_blocks = couplings[0, 0]
     rows_lists = margin_rows[0, 0]
     sides, width = coupling_blocks.shape[0], coupling_blocks.shape[-1]
+    selectors = (
+        rows_lists[:, None, :] == jnp.arange(schur_mat.shape[0], dtype=rows_lists.dtype)[None, :, None]
+    ).astype(coupling_blocks.dtype)
     placed_couplings = (
-        jnp.zeros((schur_mat.shape[0], sides * width), coupling_blocks.dtype)
-        .at[rows_lists[:, :, None], (jnp.arange(sides)[:, None, None] * width + jnp.arange(width))]
-        .set(coupling_blocks)
+        jnp.einsum("dra,dab->rdb", selectors, coupling_blocks, preferred_element_type=jnp.float32)
+        .astype(coupling_blocks.dtype)
+        .reshape(schur_mat.shape[0], sides * width)
     )
     vectors = deflation[0, 0]
     vectors_wide = vectors.astype(jnp.float32).T

time: 767 us -> 320 us (0.42)
  local copies, waits for them, and re-layouts: 493 us -> 37.7 us
  waiting for transfers between devices: 50.9 us -> 62.1 us
    unnamed x64 -> x59, local copies, waits for them, and re-layouts: 456 us -> 5.63 us
    all_to_all x1, waiting for transfers between devices: 0.01 us -> 9.13 us  [shards(): lax.all_to_all(coarse_cols.reshape(depth, count_x, count_y * depth), 'gx'...]
  transfers between devices with their start and end apart: 26 -> 26, of which waited for: 7 -> 9; matrix products, arithmetic and copies ran while one was open for 64% -> 12% of each run, Pallas kernels for 0% -> 0%
where the time goes in v9:
time: 320 us; the launch traced here: 318 us
  starting transfers between devices  113 us (35%)
  blocking collectives  63.1 us (20%)
  waiting for transfers between devices  62.1 us (19%)
  local copies, waits for them, and re-layouts  37.7 us (12%)
  matrix products  22.2 us (7%)
  other arithmetic  16.8 us (5%)
  between operations  3.4 us (1%)
    all_to_all x5, blocking collectives, gather_rows(): lax.all_to_all(copies.reshape((-1,) + value.shape[1:]), axis, 0, 0, tiled...  63.1 us
    ppermute x16, starting transfers between devices, from_behind(): lax.ppermute(value, axis, [(source, source + steps) for source in range(l...  42.5 us
    all_to_all x5, starting transfers between devices, gather_rows(): lax.all_to_all(copies.reshape((-1,) + value.shape[1:]), axis, 0, 0, tiled...  40.9 us
    all_to_all x5, waiting for transfers between devices, gather_rows(): lax.all_to_all(copies.reshape((-1,) + value.shape[1:]), axis, 0, 0, tiled...  28.3 us
    all_to_all x4, waiting for transfers between devices, apply_prec(): pieces = lax.all_to_all(partial, 'gx', 0, 0, tiled=True)  23.3 us
    all_to_all x4, starting transfers between devices, apply_prec(): pieces = lax.all_to_all(partial, 'gx', 0, 0, tiled=True)  19.6 us
    gather x2, local copies, waits for them, and re-layouts, shards(): coarse_cols = jnp.take(coarse_inverse, coarse_map, axis=1)  17.9 us
    all_to_all x1, starting transfers between devices, shards(): lax.all_to_all(coarse_cols.reshape(depth, count_x, count_y * depth), 'gx'...  9.7 us
  transfers between devices with their start and end apart: 26, of which 9 were waited for; matrix products, arithmetic and copies ran while one was open for 12% of the time, Pallas kernels for 0%

profile of v9, /device:TPU:1, one launch (start us, length us, event | category | flops | bytes accessed | tf_op | source)
XLA Modules:
  0.0 317.9 jit_solution(17552022898723685129)
XLA Ops:
  0.6 1.2 fusion.165
  2.5 11.8 %all-to-all-start.1 = ((f32[16,8,128]{2,1,0:T(8,128)}), f32[16,8,128]{2,1,0:T(8,128)S(1)}, u32[]{:S(2)}, u32[]{:S(2)}) async-start(f32[16,8,128]{2,1,0:T(8,128)} %broadcast_in_dim.42), calls=%async_computation.1 | async-start | bytes 131072 | tf_op jit(solution)/shard_map/all_to_all | solution.py:18
  15.8 2.8 copy.95
  18.6 15.7 %gather_fusion = f32[4096,8]{1,0:T(8,128)} fusion(f32[8,4096]{0,1:T(8,128)} %copy.95, s32[4096]{0:T(1024)S(1)} %fusion.167), kind=kCustom, calls=%fused_computation | custom fusion | bytes 278528 | tf_op jit(solution)/shard_map/jit(_take)/gather | solution.py:70
  34.3 2.2 copy.96
  37.2 9.7 %all-to-all-start = ((f32[8,32,128]{2,0,1:T(8,128)}), f32[8,32,128]{2,0,1:T(8,128)S(1)}, u32[]{:S(2)}, u32[]{:S(2)}) async-start(f32[8,32,128]{2,0,1:T(8,128)} %broadcast_select_fusion), calls=%async_computation | async-start | bytes 262144 | tf_op jit(solution)/shard_map/all_to_all | solution.py:71
  47.0 9.1 %all-to-all-done = f32[8,32,128]{2,0,1:T(8,128)S(1)} async-done(((f32[8,32,128]{2,0,1:T(8,128)}), f32[8,32,128]{2,0,1:T(8,128)S(1)}, u32[]{:S(2)}, u32[]{:S(2)}) %all-to-all-start) | async-done | bytes 131104 | tf_op jit(solution)/shard_map/all_to_all | solution.py:71
  57.0 4.5 %all-to-all-start.2 = ((f32[32,8,128]{2,1,0:T(8,128)}), f32[32,8,128]{2,1,0:T(8,128)S(1)}, u32[]{:S(2)}, u32[]{:S(2)}) async-start(f32[32,8,128]{2,1,0:T(8,128)} %fusion.148), calls=%async_computation.2 | async-start | bytes 262144 | tf_op jit(solution)/shard_map/all_to_all | solution.py:114
  62.1 8.6 %all-to-all-done.2 = f32[32,8,128]{2,1,0:T(8,128)S(1)} async-done(((f32[32,8,128]{2,1,0:T(8,128)}), f32[32,8,128]{2,1,0:T(8,128)S(1)}, u32[]{:S(2)}, u32[]{:S(2)}) %all-to-all-start.2) | async-done | bytes 131104 | tf_op jit(solution)/shard_map/all_to_all | solution.py:114
  71.2 1.6 fusion.174
  72.8 1.3 gather_fusion.1
  74.2 3.0 collective-permute-start
  77.2 1.3 collective-permute-start.1
  78.5 5.9 %collective-permute-start.2 = (bf16[128,128]{1,0:T(8,128)(2,1)S(1)}, bf16[128,128]{1,0:T(8,128)(2,1)S(1)}, u32[]{:S(2)}, u32[]{:S(2)}) collective-permute-start(bf16[128,128]{1,0:T(8,128)(2,1)S(1)} %get-tuple-element.32), channel_id=1, source_target_pairs={{0,1},{1,2},{2,3},{3,4},{4,5},{5,6},{6,7},{7,8},{8,9},{9,10},{10,1... | collective-permute-start | bytes 98312 | tf_op jit(solution)/shard_map/ppermute | solution.py:12
  84.4 1.9 collective-permute-start.3
  86.3 2.0 fusion.40
  88.4 1.3 collective-permute-done.3
  90.9 14.9 %all_to_all.111 = f32[16,8,128]{2,1,0:T(8,128)S(1)} all-to-all(f32[16,8,128]{2,1,0:T(8,128)S(1)} %broadcast_in_dim.43), channel_id=1, replica_groups=mesh['gx'=32,'gy'=16] {'gy'}, dimensions={0} | all-to-all | bytes 131072 | tf_op jit(solution)/shard_map/all_to_all | solution.py:18
  106.7 6.4 %all-to-all-start.4 = ((f32[32,8,128]{2,1,0:T(8,128)}), f32[32,8,128]{2,1,0:T(8,128)S(1)}, u32[]{:S(2)}, u32[]{:S(2)}) async-start(f32[32,8,128]{2,1,0:T(8,128)} %fusion.146), calls=%async_computation.4 | async-start | bytes 262144 | tf_op jit(solution)/shard_map/all_to_all | solution.py:114
  113.1 1.6 gather_fusion.2
  114.7 7.5 %all-to-all-done.4 = f32[32,8,128]{2,1,0:T(8,128)S(1)} async-done(((f32[32,8,128]{2,1,0:T(8,128)}), f32[32,8,128]{2,1,0:T(8,128)S(1)}, u32[]{:S(2)}, u32[]{:S(2)}) %all-to-all-start.4) | async-done | bytes 131104 | tf_op jit(solution)/shard_map/all_to_all | solution.py:114
  122.7 1.7 multiply_reduce_fusion.5
  124.4 1.6 gather_fusion.3
  126.0 1.9 fusion.129
  127.9 3.6 %collective-permute-start.4 = (f32[2,128,128]{2,1,0:T(8,128)}, f32[2,128,128]{2,1,0:T(8,128)S(1)}, u32[]{:S(2)}, u32[]{:S(2)}) collective-permute-start(f32[2,128,128]{2,1,0:T(8,128)} %get-tuple-element.26), channel_id=1, source_target_pairs={{0,16},{16,32},{32,48},{48,64},{64,80},{80,96},{96,112},{112,128},... | collective-permute-start | bytes 393224 | tf_op jit(solution)/shard_map/ppermute | solution.py:12
  131.4 1.3 collective-permute-start.5
  132.7 3.6 %collective-permute-start.6 = (f32[2,128,128]{2,1,0:T(8,128)}, f32[2,128,128]{2,1,0:T(8,128)S(1)}, u32[]{:S(2)}, u32[]{:S(2)}) collective-permute-start(f32[2,128,128]{2,1,0:T(8,128)} %get-tuple-element.29), channel_id=1, source_target_pairs={{0,1},{1,2},{2,3},{3,4},{4,5},{5,6},{6,7},{7,8},{8,9},{9,10},{10,1... | collective-permute-start | bytes 393224 | tf_op jit(solution)/shard_map/ppermute | solution.py:12
  136.4 1.9 collective-permute-start.7
  138.3 12.1 %all_to_all.112 = f32[16,2,128]{2,1,0:T(2,128)S(1)} all-to-all(f32[16,2,128]{2,1,0:T(2,128)S(1)} %broadcast_in_dim.44), channel_id=1, replica_groups=mesh['gx'=32,'gy'=16] {'gy'}, dimensions={0} | all-to-all | bytes 32768 | tf_op jit(solution)/shard_map/all_to_all | solution.py:18
  152.4 6.3 %all-to-all-start.6 = ((f32[32,2,128]{2,1,0:T(2,128)}), f32[32,2,128]{2,1,0:T(2,128)S(1)}, u32[]{:S(2)}, u32[]{:S(2)}) async-start(f32[32,2,128]{2,1,0:T(2,128)} %broadcast_in_dim.45), calls=%async_computation.6 | async-start | bytes 65536 | tf_op jit(solution)/shard_map/all_to_all | solution.py:18
  159.5 7.9 %all-to-all-done.6 = f32[32,2,128]{2,1,0:T(2,128)S(1)} async-done(((f32[32,2,128]{2,1,0:T(2,128)}), f32[32,2,128]{2,1,0:T(2,128)S(1)}, u32[]{:S(2)}, u32[]{:S(2)}) %all-to-all-start.6) | async-done | bytes 32800 | tf_op jit(solution)/shard_map/all_to_all | solution.py:18
  167.5 1.2 fusion.172
  170.7 12.0 %all_to_all.113 = f32[16,8,128]{2,1,0:T(8,128)S(1)} all-to-all(f32[16,8,128]{2,1,0:T(8,128)S(1)} %broadcast_in_dim.46), channel_id=1, replica_groups=mesh['gx'=32,'gy'=16] {'gy'}, dimensions={0} | all-to-all | bytes 131072 | tf_op jit(solution)/shard_map/all_to_all | solution.py:18
  183.6 4.9 %all-to-all-start.8 = ((f32[32,8,128]{2,1,0:T(8,128)}), f32[32,8,128]{2,1,0:T(8,128)}, u32[]{:S(2)}, u32[]{:S(2)}) async-start(f32[32,8,128]{2,1,0:T(8,128)} %fusion.144), calls=%async_computation.8 | async-start | bytes 262144 | tf_op jit(solution)/shard_map/all_to_all | solution.py:114
  188.5 1.6 gather_fusion.4
  190.2 7.3 %all-to-all-done.8 = f32[32,8,128]{2,1,0:T(8,128)} async-done(((f32[32,8,128]{2,1,0:T(8,128)}), f32[32,8,128]{2,1,0:T(8,128)}, u32[]{:S(2)}, u32[]{:S(2)}) %all-to-all-start.8) | async-done | bytes 131104 | tf_op jit(solution)/shard_map/all_to_all | solution.py:114
  198.8 2.4 multiply_reduce_fusion.3
  201.2 2.6 gather_fusion.5
  203.9 1.9 fusion.123
  205.8 4.3 %collective-permute-start.8 = (f32[2,128,128]{2,1,0:T(8,128)}, f32[2,128,128]{2,1,0:T(8,128)}, u32[]{:S(2)}, u32[]{:S(2)}) collective-permute-start(f32[2,128,128]{2,1,0:T(8,128)} %get-tuple-element.22), channel_id=1, source_target_pairs={{0,16},{16,32},{32,48},{48,64},{64,80},{80,96},{96,112},{112,128},... | collective-permute-start | bytes 393224 | tf_op jit(solution)/shard_map/ppermute | solution.py:12
  210.1 1.3 collective-permute-start.9
  211.4 3.6 %collective-permute-start.10 = (f32[2,128,128]{2,1,0:T(8,128)}, f32[2,128,128]{2,1,0:T(8,128)}, u32[]{:S(2)}, u32[]{:S(2)}) collective-permute-start(f32[2,128,128]{2,1,0:T(8,128)} %get-tuple-element.25), channel_id=1, source_target_pairs={{0,1},{1,2},{2,3},{3,4},{4,5},{5,6},{6,7},{7,8},{8,9},{9,10},{10,1... | collective-permute-start | bytes 393224 | tf_op jit(solution)/shard_map/ppermute | solution.py:12
  215.0 1.9 collective-permute-start.11
  216.9 12.1 %all_to_all.114 = f32[16,2,128]{2,1,0:T(2,128)S(1)} all-to-all(f32[16,2,128]{2,1,0:T(2,128)S(1)} %broadcast_in_dim.47), channel_id=1, replica_groups=mesh['gx'=32,'gy'=16] {'gy'}, dimensions={0} | all-to-all | bytes 32768 | tf_op jit(solution)/shard_map/all_to_all | solution.py:18
  229.1 1.3 maximum_reduce_fusion.1
  231.7 5.8 %all-to-all-start.10 = ((f32[32,2,128]{2,1,0:T(2,128)}), f32[32,2,128]{2,1,0:T(2,128)S(1)}, u32[]{:S(2)}, u32[]{:S(2)}) async-start(f32[32,2,128]{2,1,0:T(2,128)} %broadcast_in_dim.48), calls=%async_computation.10 | async-start | bytes 65536 | tf_op jit(solution)/shard_map/all_to_all | solution.py:18
  237.5 2.0 pad_maximum_fusion.1
  239.4 6.8 %all-to-all-done.10 = f32[32,2,128]{2,1,0:T(2,128)S(1)} async-done(((f32[32,2,128]{2,1,0:T(2,128)}), f32[32,2,128]{2,1,0:T(2,128)S(1)}, u32[]{:S(2)}, u32[]{:S(2)}) %all-to-all-start.10) | async-done | bytes 32800 | tf_op jit(solution)/shard_map/all_to_all | solution.py:18
  246.3 1.5 convolution_bitcast_fusion.2
  247.9 1.3 copy-done.2
  250.0 12.0 %all_to_all.115 = f32[16,8,128]{2,1,0:T(8,128)S(1)} all-to-all(f32[16,8,128]{2,1,0:T(8,128)S(1)} %broadcast_in_dim.49), channel_id=1, replica_groups=mesh['gx'=32,'gy'=16] {'gy'}, dimensions={0} | all-to-all | bytes 131072 | tf_op jit(solution)/shard_map/all_to_all | solution.py:18
  262.9 3.9 %all-to-all-start.12 = ((f32[32,8,128]{2,1,0:T(8,128)}), f32[32,8,128]{2,1,0:T(8,128)S(1)}, u32[]{:S(2)}, u32[]{:S(2)}) async-start(f32[32,8,128]{2,1,0:T(8,128)} %fusion.142), calls=%async_computation.12 | async-start | bytes 262144 | tf_op jit(solution)/shard_map/all_to_all | solution.py:114
  267.8 1.0 gather_fusion.7
  269.6 2.3 collective-permute-start.14
  272.0 2.0 collective-permute-start.15
  274.0 3.2 %collective-permute-start.12 = (f32[2,128,128]{2,1,0:T(8,128)}, f32[2,128,128]{2,1,0:T(8,128)S(1)}, u32[]{:S(2)}, u32[]{:S(2)}) collective-permute-start(f32[2,128,128]{2,1,0:T(8,128)} %get-tuple-element.18), channel_id=1, source_target_pairs={{0,16},{16,32},{32,48},{48,64},{64,80},{80,96},{96,112},{112,128},... | collective-permute-start | bytes 393224 | tf_op jit(solution)/shard_map/ppermute | solution.py:12
  277.2 1.3 collective-permute-start.13
  280.2 5.4 %all-to-all-start.13 = ((f32[16,2,128]{2,1,0:T(2,128)}), f32[16,2,128]{2,1,0:T(2,128)S(1)}, u32[]{:S(2)}, u32[]{:S(2)}) async-start(f32[16,2,128]{2,1,0:T(2,128)} %broadcast_in_dim.50), calls=%async_computation.13 | async-start | bytes 32768 | tf_op jit(solution)/shard_map/all_to_all | solution.py:18
  286.9 6.0 %all-to-all-done.13 = f32[16,2,128]{2,1,0:T(2,128)S(1)} async-done(((f32[16,2,128]{2,1,0:T(2,128)}), f32[16,2,128]{2,1,0:T(2,128)S(1)}, u32[]{:S(2)}, u32[]{:S(2)}) %all-to-all-start.13) | async-done | bytes 16416 | tf_op jit(solution)/shard_map/all_to_all | solution.py:18
  293.5 11.7 %all-to-all-start.14 = ((f32[32,2,128]{2,1,0:T(2,128)}), f32[32,2,128]{2,1,0:T(2,128)S(1)}, u32[]{:S(2)}, u32[]{:S(2)}) async-start(f32[32,2,128]{2,1,0:T(2,128)} %broadcast_in_dim.51), calls=%async_computation.14 | async-start | bytes 65536 | tf_op jit(solution)/shard_map/all_to_all | solution.py:18
  305.2 1.1 pad_maximum_fusion.2
  306.4 7.6 %all-to-all-done.14 = f32[32,2,128]{2,1,0:T(2,128)S(1)} async-done(((f32[32,2,128]{2,1,0:T(2,128)}), f32[32,2,128]{2,1,0:T(2,128)S(1)}, u32[]{:S(2)}, u32[]{:S(2)}) %all-to-all-start.14) | async-done | bytes 32800 | tf_op jit(solution)/shard_map/all_to_all | solution.py:18
  314.9 1.6 convolution_bitcast_fusion
  316.5 1.4 fusion.88
  (135 shorter events, 21.9 us)
Async XLA Ops:
  0.6 70.5 %copy-start = (bf16[1,1,896,896]{3,2,1,0:T(8,128)(2,1)S(1)}, bf16[1,1,896,896]{3,2,1,0:T(8,128)(2,1)}, u32[]{:S(2)}) copy-start(bf16[1,1,896,896]{3,2,1,0:T(8,128)(2,1)} %param.13) | copy-start | bytes 4816900
  2.5 34.7 %all-to-all-start.1 = ((f32[16,8,128]{2,1,0:T(8,128)}), f32[16,8,128]{2,1,0:T(8,128)S(1)}, u32[]{:S(2)}, u32[]{:S(2)}) async-start(f32[16,8,128]{2,1,0:T(8,128)} %broadcast_in_dim.42), calls=%async_computation.1 | async-start | bytes 131072 | tf_op jit(solution)/shard_map/all_to_all | solution.py:18
  34.3 12.6 %copy-start.26 = (s32[1,1,4,128]{3,2,1,0:T(4,128)S(1)}, s32[1,1,4,128]{3,2,1,0:T(4,128)}, u32[]{:S(2)}) copy-start(s32[1,1,4,128]{3,2,1,0:T(4,128)} %param.16) | copy-start | bytes 6148
  34.3 27.2 %copy-start.27 = (f32[1,1,896]{2,1,0:T(1,128)S(1)}, f32[1,1,896]{2,1,0:T(1,128)}, u32[]{:S(2)}) copy-start(f32[1,1,896]{2,1,0:T(1,128)} %param.14) | copy-start | bytes 10756
  34.3 27.3 %copy-start.28 = (f32[1,1,896]{2,1,0:T(1,128)S(1)}, f32[1,1,896]{2,1,0:T(1,128)}, u32[]{:S(2)}) copy-start(f32[1,1,896]{2,1,0:T(1,128)} %param.12) | copy-start | bytes 10756
  34.3 27.3 %copy-start.19 = (bf16[1,1,4,128,128]{4,3,2,1,0:T(8,128)(2,1)S(1)}, bf16[1,1,4,128,128]{4,3,2,1,0:T(8,128)(2,1)}, u32[]{:S(2)}) copy-start(bf16[1,1,4,128,128]{4,3,2,1,0:T(8,128)(2,1)} %param.15) | copy-start | bytes 393220
  36.6 34.2 %copy-start.14 = (bf16[1,1,8,896]{3,2,1,0:T(8,128)(2,1)S(1)}, bf16[1,1,8,896]{3,2,1,0:T(8,128)(2,1)}, u32[]{:S(2)}) copy-start(bf16[1,1,8,896]{3,2,1,0:T(8,128)(2,1)} %param.17) | copy-start | bytes 43012
  37.2 18.9 %all-to-all-start = ((f32[8,32,128]{2,0,1:T(8,128)}), f32[8,32,128]{2,0,1:T(8,128)S(1)}, u32[]{:S(2)}, u32[]{:S(2)}) async-start(f32[8,32,128]{2,0,1:T(8,128)} %broadcast_select_fusion), calls=%async_computation | async-start | bytes 262144 | tf_op jit(solution)/shard_map/all_to_all | solution.py:71
  56.1 49.7 %copy-start.7 = (f32[8,32,128]{2,0,1:T(8,128)}, f32[8,32,128]{2,0,1:T(8,128)S(1)}, u32[]{:S(2)}) copy-start(f32[8,32,128]{2,0,1:T(8,128)S(1)} %all-to-all-done) | copy-start | bytes 393220
  57.0 13.7 %all-to-all-start.2 = ((f32[32,8,128]{2,1,0:T(8,128)}), f32[32,8,128]{2,1,0:T(8,128)S(1)}, u32[]{:S(2)}, u32[]{:S(2)}) async-start(f32[32,8,128]{2,1,0:T(8,128)} %fusion.148), calls=%async_computation.2 | async-start | bytes 262144 | tf_op jit(solution)/shard_map/all_to_all | solution.py:114
  61.6 62.8 %copy-start.24 = (s32[1024]{0:T(1024)}, s32[1024]{0:T(1024)S(1)}, u32[]{:S(2)}) copy-start(s32[1024]{0:T(1024)S(1)} %pad_clamp_fusion) | copy-start | bytes 12292
  61.6 61.1 %copy-start.22 = (f32[896]{0:T(1024)}, f32[896]{0:T(1024)S(1)}, u32[]{:S(2)}) copy-start(f32[896]{0:T(1024)S(1)} %reduce.13) | copy-start | bytes 10756
  61.6 24.7 %copy-start.20 = (f32[896]{0:T(1024)}, f32[896]{0:T(1024)S(1)}, u32[]{:S(2)}) copy-start(f32[896]{0:T(1024)S(1)} %reduce.14) | copy-start | bytes 10756
  62.1 184.2 %copy-start.4 = (bf16[896,4,128]{2,0,1:T(8,128)(2,1)}, bf16[896,4,128]{2,0,1:T(8,128)(2,1)S(1)}, u32[]{:S(2)}) copy-start(bf16[896,4,128]{2,0,1:T(8,128)(2,1)S(1)} %fusion.18) | copy-start | bytes 2752516
  74.2 14.2 %collective-permute-start = (bf16[128,128]{1,0:T(8,128)(2,1)S(1)}, bf16[128,128]{1,0:T(8,128)(2,1)S(1)}, u32[]{:S(2)}, u32[]{:S(2)}) collective-permute-start(bf16[128,128]{1,0:T(8,128)(2,1)S(1)} %get-tuple-element.31), channel_id=1, source_target_pairs={{0,16},{16,32},{32,48},{48,64},{64,80},{80,96},{96,112},{112,128},... | collective-permute-start | bytes 98312 | tf_op jit(solution)/shard_map/ppermute | solution.py:12
  77.2 11.2 %collective-permute-start.1 = (bf16[128,128]{1,0:T(8,128)(2,1)S(1)}, bf16[128,128]{1,0:T(8,128)(2,1)S(1)}, u32[]{:S(2)}, u32[]{:S(2)}) collective-permute-start(bf16[128,128]{1,0:T(8,128)(2,1)S(1)} %get-tuple-element.33), channel_id=1, source_target_pairs={{16,0},{32,16},{48,32},{64,48},{80,64},{96,80},{112,96},{128,112},... | collective-permute-start | bytes 98312 | tf_op jit(solution)/shard_map/ppermute | solution.py:12
  78.5 9.9 %collective-permute-start.2 = (bf16[128,128]{1,0:T(8,128)(2,1)S(1)}, bf16[128,128]{1,0:T(8,128)(2,1)S(1)}, u32[]{:S(2)}, u32[]{:S(2)}) collective-permute-start(bf16[128,128]{1,0:T(8,128)(2,1)S(1)} %get-tuple-element.32), channel_id=1, source_target_pairs={{0,1},{1,2},{2,3},{3,4},{4,5},{5,6},{6,7},{7,8},{8,9},{9,10},{10,1... | collective-permute-start | bytes 98312 | tf_op jit(solution)/shard_map/ppermute | solution.py:12
  84.4 5.2 %collective-permute-start.3 = (bf16[128,128]{1,0:T(8,128)(2,1)S(1)}, bf16[128,128]{1,0:T(8,128)(2,1)S(1)}, u32[]{:S(2)}, u32[]{:S(2)}) collective-permute-start(bf16[128,128]{1,0:T(8,128)(2,1)S(1)} %get-tuple-element.34), channel_id=1, source_target_pairs={{1,0},{2,1},{3,2},{4,3},{5,4},{6,5},{7,6},{8,7},{9,8},{10,9},{11,1... | collective-permute-start | bytes 98312 | tf_op jit(solution)/shard_map/ppermute | solution.py:12
  90.0 0.7 copy-start.12
  106.7 15.5 %all-to-all-start.4 = ((f32[32,8,128]{2,1,0:T(8,128)}), f32[32,8,128]{2,1,0:T(8,128)S(1)}, u32[]{:S(2)}, u32[]{:S(2)}) async-start(f32[32,8,128]{2,1,0:T(8,128)} %fusion.146), calls=%async_computation.4 | async-start | bytes 262144 | tf_op jit(solution)/shard_map/all_to_all | solution.py:114
  124.3 3.6 %copy-start.6 = (f32[896,128]{1,0:T(8,128)}, f32[896,128]{1,0:T(8,128)S(1)}, u32[]{:S(2)}) copy-start(f32[896,128]{1,0:T(8,128)S(1)} %get-tuple-element.37) | copy-start | bytes 1376260
  127.9 22.6 %collective-permute-start.4 = (f32[2,128,128]{2,1,0:T(8,128)}, f32[2,128,128]{2,1,0:T(8,128)S(1)}, u32[]{:S(2)}, u32[]{:S(2)}) collective-permute-start(f32[2,128,128]{2,1,0:T(8,128)} %get-tuple-element.26), channel_id=1, source_target_pairs={{0,16},{16,32},{32,48},{48,64},{64,80},{80,96},{96,112},{112,128},... | collective-permute-start | bytes 393224 | tf_op jit(solution)/shard_map/ppermute | solution.py:12
  131.4 19.1 %collective-permute-start.5 = (f32[2,128,128]{2,1,0:T(8,128)}, f32[2,128,128]{2,1,0:T(8,128)S(1)}, u32[]{:S(2)}, u32[]{:S(2)}) collective-permute-start(f32[2,128,128]{2,1,0:T(8,128)} %get-tuple-element.27), channel_id=1, source_target_pairs={{16,0},{32,16},{48,32},{64,48},{80,64},{96,80},{112,96},{128,112},... | collective-permute-start | bytes 393224 | tf_op jit(solution)/shard_map/ppermute | solution.py:12
  132.7 17.8 %collective-permute-start.6 = (f32[2,128,128]{2,1,0:T(8,128)}, f32[2,128,128]{2,1,0:T(8,128)S(1)}, u32[]{:S(2)}, u32[]{:S(2)}) collective-permute-start(f32[2,128,128]{2,1,0:T(8,128)} %get-tuple-element.29), channel_id=1, source_target_pairs={{0,1},{1,2},{2,3},{3,4},{4,5},{5,6},{6,7},{7,8},{8,9},{9,10},{10,1... | collective-permute-start | bytes 393224 | tf_op jit(solution)/shard_map/ppermute | solution.py:12
  136.4 14.1 %collective-permute-start.7 = (f32[2,128,128]{2,1,0:T(8,128)}, f32[2,128,128]{2,1,0:T(8,128)S(1)}, u32[]{:S(2)}, u32[]{:S(2)}) collective-permute-start(f32[2,128,128]{2,1,0:T(8,128)} %get-tuple-element.28), channel_id=1, source_target_pairs={{1,0},{2,1},{3,2},{4,3},{5,4},{6,5},{7,6},{8,7},{9,8},{10,9},{11,1... | collective-permute-start | bytes 393224 | tf_op jit(solution)/shard_map/ppermute | solution.py:12
  152.4 15.0 %all-to-all-start.6 = ((f32[32,2,128]{2,1,0:T(2,128)}), f32[32,2,128]{2,1,0:T(2,128)S(1)}, u32[]{:S(2)}, u32[]{:S(2)}) async-start(f32[32,2,128]{2,1,0:T(2,128)} %broadcast_in_dim.45), calls=%async_computation.6 | async-start | bytes 65536 | tf_op jit(solution)/shard_map/all_to_all | solution.py:18
  167.5 1.3 copy-start.13
  167.5 1.7 copy-start.1
  167.5 1.7 copy-start.21
  169.2 13.5 %copy-start.8 = (f32[8,32,128]{2,0,1:T(8,128)S(1)}, f32[8,32,128]{2,0,1:T(8,128)}, u32[]{:S(2)}) copy-start(f32[8,32,128]{2,0,1:T(8,128)} %copy-done.7) | copy-start | bytes 393220
  169.2 19.3 %copy-start.25 = (s32[1024]{0:T(1024)S(1)}, s32[1024]{0:T(1024)}, u32[]{:S(2)}) copy-start(s32[1024]{0:T(1024)} %copy-done.24) | copy-start | bytes 12292
  169.8 0.7 copy-start.11
  183.6 15.2 %copy-start.23 = (f32[896]{0:T(1024)S(1)}, f32[896]{0:T(1024)}, u32[]{:S(2)}) copy-start(f32[896]{0:T(1024)} %copy-done.22) | copy-start | bytes 10756
  183.6 13.8 %all-to-all-start.8 = ((f32[32,8,128]{2,1,0:T(8,128)}), f32[32,8,128]{2,1,0:T(8,128)}, u32[]{:S(2)}, u32[]{:S(2)}) async-start(f32[32,8,128]{2,1,0:T(8,128)} %fusion.144), calls=%async_computation.8 | async-start | bytes 262144 | tf_op jit(solution)/shard_map/all_to_all | solution.py:114
  205.8 23.3 %collective-permute-start.8 = (f32[2,128,128]{2,1,0:T(8,128)}, f32[2,128,128]{2,1,0:T(8,128)}, u32[]{:S(2)}, u32[]{:S(2)}) collective-permute-start(f32[2,128,128]{2,1,0:T(8,128)} %get-tuple-element.22), channel_id=1, source_target_pairs={{0,16},{16,32},{32,48},{48,64},{64,80},{80,96},{96,112},{112,128},... | collective-permute-start | bytes 393224 | tf_op jit(solution)/shard_map/ppermute | solution.py:12
  210.1 18.9 %collective-permute-start.9 = (f32[2,128,128]{2,1,0:T(8,128)}, f32[2,128,128]{2,1,0:T(8,128)}, u32[]{:S(2)}, u32[]{:S(2)}) collective-permute-start(f32[2,128,128]{2,1,0:T(8,128)} %get-tuple-element.23), channel_id=1, source_target_pairs={{16,0},{32,16},{48,32},{64,48},{80,64},{96,80},{112,96},{128,112},... | collective-permute-start | bytes 393224 | tf_op jit(solution)/shard_map/ppermute | solution.py:12
  211.4 17.7 %collective-permute-start.10 = (f32[2,128,128]{2,1,0:T(8,128)}, f32[2,128,128]{2,1,0:T(8,128)}, u32[]{:S(2)}, u32[]{:S(2)}) collective-permute-start(f32[2,128,128]{2,1,0:T(8,128)} %get-tuple-element.25), channel_id=1, source_target_pairs={{0,1},{1,2},{2,3},{3,4},{4,5},{5,6},{6,7},{7,8},{8,9},{9,10},{10,1... | collective-permute-start | bytes 393224 | tf_op jit(solution)/shard_map/ppermute | solution.py:12
  215.0 14.1 %collective-permute-start.11 = (f32[2,128,128]{2,1,0:T(8,128)}, f32[2,128,128]{2,1,0:T(8,128)}, u32[]{:S(2)}, u32[]{:S(2)}) collective-permute-start(f32[2,128,128]{2,1,0:T(8,128)} %get-tuple-element.24), channel_id=1, source_target_pairs={{1,0},{2,1},{3,2},{4,3},{5,4},{6,5},{7,6},{8,7},{9,8},{10,9},{11,1... | collective-permute-start | bytes 393224 | tf_op jit(solution)/shard_map/ppermute | solution.py:12
  231.7 14.5 %all-to-all-start.10 = ((f32[32,2,128]{2,1,0:T(2,128)}), f32[32,2,128]{2,1,0:T(2,128)S(1)}, u32[]{:S(2)}, u32[]{:S(2)}) async-start(f32[32,2,128]{2,1,0:T(2,128)} %broadcast_in_dim.48), calls=%async_computation.10 | async-start | bytes 65536 | tf_op jit(solution)/shard_map/all_to_all | solution.py:18
  246.3 1.5 copy-start.5
  247.8 1.4 copy-start.2
  247.9 14.0 %copy-start.9 = (f32[8,32,128]{2,0,1:T(8,128)S(1)}, f32[8,32,128]{2,0,1:T(8,128)}, u32[]{:S(2)}) copy-start(f32[8,32,128]{2,0,1:T(8,128)} %copy-done.7) | copy-start | bytes 393220
  262.9 15.6 %all-to-all-start.12 = ((f32[32,8,128]{2,1,0:T(8,128)}), f32[32,8,128]{2,1,0:T(8,128)S(1)}, u32[]{:S(2)}, u32[]{:S(2)}) async-start(f32[32,8,128]{2,1,0:T(8,128)} %fusion.142), calls=%async_computation.12 | async-start | bytes 262144 | tf_op jit(solution)/shard_map/all_to_all | solution.py:114
  269.6 15.9 %collective-permute-start.14 = (f32[2,128,128]{2,1,0:T(8,128)}, f32[2,128,128]{2,1,0:T(8,128)S(1)}, u32[]{:S(2)}, u32[]{:S(2)}) collective-permute-start(f32[2,128,128]{2,1,0:T(8,128)} %get-tuple-element.21), channel_id=1, source_target_pairs={{0,1},{1,2},{2,3},{3,4},{4,5},{5,6},{6,7},{7,8},{8,9},{9,10},{10,1... | collective-permute-start | bytes 393224 | tf_op jit(solution)/shard_map/ppermute | solution.py:12
  272.0 13.6 %collective-permute-start.15 = (f32[2,128,128]{2,1,0:T(8,128)}, f32[2,128,128]{2,1,0:T(8,128)S(1)}, u32[]{:S(2)}, u32[]{:S(2)}) collective-permute-start(f32[2,128,128]{2,1,0:T(8,128)} %get-tuple-element.20), channel_id=1, source_target_pairs={{1,0},{2,1},{3,2},{4,3},{5,4},{6,5},{7,6},{8,7},{9,8},{10,9},{11,1... | collective-permute-start | bytes 393224 | tf_op jit(solution)/shard_map/ppermute | solution.py:12
  274.0 11.6 %collective-permute-start.12 = (f32[2,128,128]{2,1,0:T(8,128)}, f32[2,128,128]{2,1,0:T(8,128)S(1)}, u32[]{:S(2)}, u32[]{:S(2)}) collective-permute-start(f32[2,128,128]{2,1,0:T(8,128)} %get-tuple-element.18), channel_id=1, source_target_pairs={{0,16},{16,32},{32,48},{48,64},{64,80},{80,96},{96,112},{112,128},... | collective-permute-start | bytes 393224 | tf_op jit(solution)/shard_map/ppermute | solution.py:12
  277.2 8.4 %collective-permute-start.13 = (f32[2,128,128]{2,1,0:T(8,128)}, f32[2,128,128]{2,1,0:T(8,128)S(1)}, u32[]{:S(2)}, u32[]{:S(2)}) collective-permute-start(f32[2,128,128]{2,1,0:T(8,128)} %get-tuple-element.19), channel_id=1, source_target_pairs={{16,0},{32,16},{48,32},{64,48},{80,64},{96,80},{112,96},{128,112},... | collective-permute-start | bytes 393224 | tf_op jit(solution)/shard_map/ppermute | solution.py:12
  280.2 12.7 %all-to-all-start.13 = ((f32[16,2,128]{2,1,0:T(2,128)}), f32[16,2,128]{2,1,0:T(2,128)S(1)}, u32[]{:S(2)}, u32[]{:S(2)}) async-start(f32[16,2,128]{2,1,0:T(2,128)} %broadcast_in_dim.50), calls=%async_computation.13 | async-start | bytes 32768 | tf_op jit(solution)/shard_map/all_to_all | solution.py:18
  285.6 8.0 %copy-start.15 = (f32[2,128,128]{2,1,0:T(8,128)}, f32[2,128,128]{2,1,0:T(8,128)S(1)}, u32[]{:S(2)}) copy-start(f32[2,128,128]{2,1,0:T(8,128)S(1)} %collective-permute-done.14) | copy-start | bytes 393220
  285.6 8.0 %copy-start.16 = (f32[2,128,128]{2,1,0:T(8,128)}, f32[2,128,128]{2,1,0:T(8,128)S(1)}, u32[]{:S(2)}) copy-start(f32[2,128,128]{2,1,0:T(8,128)S(1)} %collective-permute-done.15) | copy-start | bytes 393220
  285.6 7.9 %copy-start.17 = (f32[2,128,128]{2,1,0:T(8,128)}, f32[2,128,128]{2,1,0:T(8,128)S(1)}, u32[]{:S(2)}) copy-start(f32[2,128,128]{2,1,0:T(8,128)S(1)} %collective-permute-done.12) | copy-start | bytes 393220
  285.6 7.9 %copy-start.18 = (f32[2,128,128]{2,1,0:T(8,128)}, f32[2,128,128]{2,1,0:T(8,128)S(1)}, u32[]{:S(2)}) copy-start(f32[2,128,128]{2,1,0:T(8,128)S(1)} %collective-permute-done.13) | copy-start | bytes 393220
  293.5 20.5 %all-to-all-start.14 = ((f32[32,2,128]{2,1,0:T(2,128)}), f32[32,2,128]{2,1,0:T(2,128)S(1)}, u32[]{:S(2)}, u32[]{:S(2)}) async-start(f32[32,2,128]{2,1,0:T(2,128)} %broadcast_in_dim.51), calls=%async_computation.14 | async-start | bytes 65536 | tf_op jit(solution)/shard_map/all_to_all | solution.py:18
  314.1 2.4 copy-start.3
  314.1 2.4 copy-start.10

commit v10 on v9

--- a/solution.py
+++ b/solution.py
@@ -63,6 +63,7 @@
         .astype(coupling_blocks.dtype)
         .reshape(schur_mat.shape[0], sides * width)
     )
+    schur_with_couplings = jnp.concatenate([schur_mat, -placed_couplings], axis=1)
     vectors = deflation[0, 0]
     vectors_wide = vectors.astype(jnp.float32).T
     count_x, count_y = lax.axis_size("gx"), lax.axis_size("gy")
@@ -83,13 +84,10 @@
         )
 
     def finish_schur(rounded, received):
-        result = schur_scale * rounded.astype(jnp.float32) + jnp.dot(
-            schur_mat, rounded, preferred_element_type=jnp.float32
+        stacked = jnp.concatenate([rounded, received.reshape(-1, received.shape[-1])], axis=0)
+        return schur_scale * rounded.astype(jnp.float32) + jnp.dot(
+            schur_with_couplings, stacked, preferred_element_type=jnp.float32
         )
-        coupled = jnp.dot(
-            placed_couplings, received.reshape(-1, received.shape[-1]), preferred_element_type=jnp.float32
-        )
-        return result - coupled
 
     def apply_schur(field):
         rounded = lax.optimization_barrier(field.astype(jnp.bfloat16))

time: 320 us -> 309 us (0.966)
  starting transfers between devices: 113 us -> 108 us
  blocking collectives: 63.1 us -> 59.7 us
    all_to_all x5, starting transfers between devices: 40.9 us -> 33.9 us  [gather_rows(): lax.all_to_all(copies.reshape((-1,) + value.shape[1:]), axis, 0, 0, tiled...]
    ppermute x16, starting transfers between devices: 42.5 us -> 47.2 us  [from_behind(): lax.ppermute(value, axis, [(source, source + steps) for source in range(l...]
    slice x0 -> x3, local copies, waits for them, and re-layouts: none -> 3.68 us  [apply_schur_late(): received = (pair[:, 0] + coef * pair[:, 1]).astype(jnp.bfloat16)]
    gather x6, local copies, waits for them, and re-layouts: 9.66 us -> 6.23 us  [send_early(): return exchange(jnp.stack([base[rows_lists], step[rows_lists]], axis=1))]
    all_to_all x5, blocking collectives: 63.1 us -> 59.7 us  [gather_rows(): lax.all_to_all(copies.reshape((-1,) + value.shape[1:]), axis, 0, 0, tiled...]
    dot_general x8 -> x4, matrix products: 8.4 us -> 8.63 us  [finish_schur(): jnp.dot(schur_with_couplings, stacked, preferred_element_type=jnp.float32)]
  transfers between devices with their start and end apart: 26 -> 26, of which waited for: 9 -> 8; matrix products, arithmetic and copies ran while one was open for 12% -> 14% of each run, Pallas kernels for 0% -> 0%
where the time goes in v10:
time: 309 us; the launch traced here: 307 us
  starting transfers between devices  108 us (35%)
  waiting for transfers between devices  60.4 us (20%)
  blocking collectives  59.7 us (19%)
  local copies, waits for them, and re-layouts  39.3 us (13%)
  matrix products  21.6 us (7%)
  other arithmetic  15.1 us (5%)
  between operations  3.26 us (1%)
    all_to_all x5, blocking collectives, gather_rows(): lax.all_to_all(copies.reshape((-1,) + value.shape[1:]), axis, 0, 0, tiled...  59.7 us
    ppermute x16, starting transfers between devices, from_behind(): lax.ppermute(value, axis, [(source, source + steps) for source in range(l...  47.2 us
    all_to_all x5, starting transfers between devices, gather_rows(): lax.all_to_all(copies.reshape((-1,) + value.shape[1:]), axis, 0, 0, tiled...  33.9 us
    all_to_all x5, waiting for transfers between devices, gather_rows(): lax.all_to_all(copies.reshape((-1,) + value.shape[1:]), axis, 0, 0, tiled...  26.1 us
    all_to_all x4, waiting for transfers between devices, apply_prec(): pieces = lax.all_to_all(partial, 'gx', 0, 0, tiled=True)  25.1 us
    gather x2, local copies, waits for them, and re-layouts, shards(): coarse_cols = jnp.take(coarse_inverse, coarse_map, axis=1)  17.9 us
    all_to_all x4, starting transfers between devices, apply_prec(): pieces = lax.all_to_all(partial, 'gx', 0, 0, tiled=True)  17.3 us
    all_to_all x1, starting transfers between devices, shards(): lax.all_to_all(coarse_cols.reshape(depth, count_x, count_y * depth), 'gx'...  9.69 us
  transfers between devices with their start and end apart: 26, of which 8 were waited for; matrix products, arithmetic and copies ran while one was open for 14% of the time, Pallas kernels for 0%

profile of v10, /device:TPU:1, one launch (start us, length us, event | category | flops | bytes accessed | tf_op | source)
XLA Modules:
  0.0 307.5 jit_solution(5997054683908092051)
XLA Ops:
  0.6 1.2 fusion.111
  2.5 11.8 %all-to-all-start.1 = ((f32[16,8,128]{2,1,0:T(8,128)}), f32[16,8,128]{2,1,0:T(8,128)S(1)}, u32[]{:S(2)}, u32[]{:S(2)}) async-start(f32[16,8,128]{2,1,0:T(8,128)} %broadcast_in_dim.42), calls=%async_computation.1 | async-start | bytes 131072 | tf_op jit(solution)/shard_map/all_to_all | solution.py:18
  15.8 2.9 copy.89
  18.6 15.7 %gather_fusion = f32[4096,8]{1,0:T(8,128)} fusion(f32[8,4096]{0,1:T(8,128)} %copy.89, s32[4096]{0:T(1024)S(1)} %fusion.113), kind=kCustom, calls=%fused_computation | custom fusion | bytes 278528 | tf_op jit(solution)/shard_map/jit(_take)/gather | solution.py:71
  34.4 2.2 copy.90
  37.3 9.7 %all-to-all-start = ((f32[8,32,128]{2,0,1:T(8,128)}), f32[8,32,128]{2,0,1:T(8,128)S(1)}, u32[]{:S(2)}, u32[]{:S(2)}) async-start(f32[8,32,128]{2,0,1:T(8,128)} %broadcast_select_fusion), calls=%async_computation | async-start | bytes 262144 | tf_op jit(solution)/shard_map/all_to_all | solution.py:72
  47.0 9.1 %all-to-all-done = f32[8,32,128]{2,0,1:T(8,128)S(1)} async-done(((f32[8,32,128]{2,0,1:T(8,128)}), f32[8,32,128]{2,0,1:T(8,128)S(1)}, u32[]{:S(2)}, u32[]{:S(2)}) %all-to-all-start) | async-done | bytes 131104 | tf_op jit(solution)/shard_map/all_to_all | solution.py:72
  57.0 4.5 %all-to-all-start.2 = ((f32[32,8,128]{2,1,0:T(8,128)}), f32[32,8,128]{2,1,0:T(8,128)S(1)}, u32[]{:S(2)}, u32[]{:S(2)}) async-start(f32[32,8,128]{2,1,0:T(8,128)} %fusion.97), calls=%async_computation.2 | async-start | bytes 262144 | tf_op jit(solution)/shard_map/all_to_all | solution.py:112
  61.6 9.1 %all-to-all-done.2 = f32[32,8,128]{2,1,0:T(8,128)S(1)} async-done(((f32[32,8,128]{2,1,0:T(8,128)}), f32[32,8,128]{2,1,0:T(8,128)S(1)}, u32[]{:S(2)}, u32[]{:S(2)}) %all-to-all-start.2) | async-done | bytes 131104 | tf_op jit(solution)/shard_map/all_to_all | solution.py:112
  71.8 1.3 gather_fusion.1
  73.1 4.6 %collective-permute-start.3 = (bf16[128,128]{1,0:T(8,128)(2,1)S(1)}, bf16[128,128]{1,0:T(8,128)(2,1)S(1)}, u32[]{:S(2)}, u32[]{:S(2)}) collective-permute-start(bf16[128,128]{1,0:T(8,128)(2,1)S(1)} %get-tuple-element.40), channel_id=1, source_target_pairs={{1,0},{2,1},{3,2},{4,3},{5,4},{6,5},{7,6},{8,7},{9,8},{10,9},{11,1... | collective-permute-start | bytes 98312 | tf_op jit(solution)/shard_map/ppermute | solution.py:12
  77.8 3.2 %collective-permute-start.2 = (bf16[128,128]{1,0:T(8,128)(2,1)S(1)}, bf16[128,128]{1,0:T(8,128)(2,1)S(1)}, u32[]{:S(2)}, u32[]{:S(2)}) collective-permute-start(bf16[128,128]{1,0:T(8,128)(2,1)S(1)} %get-tuple-element.38), channel_id=1, source_target_pairs={{0,1},{1,2},{2,3},{3,4},{4,5},{5,6},{6,7},{7,8},{8,9},{9,10},{10,1... | collective-permute-start | bytes 98312 | tf_op jit(solution)/shard_map/ppermute | solution.py:12
  81.0 1.3 collective-permute-start.1
  82.3 4.0 %collective-permute-start = (bf16[128,128]{1,0:T(8,128)(2,1)S(1)}, bf16[128,128]{1,0:T(8,128)(2,1)S(1)}, u32[]{:S(2)}, u32[]{:S(2)}) collective-permute-start(bf16[128,128]{1,0:T(8,128)(2,1)S(1)} %get-tuple-element.37), channel_id=1, source_target_pairs={{0,16},{16,32},{32,48},{48,64},{64,80},{80,96},{96,112},{112,128},... | collective-permute-start | bytes 98312 | tf_op jit(solution)/shard_map/ppermute | solution.py:12
  86.3 2.5 fusion.10
  88.8 2.3 copy.93
  91.1 2.5 fusion.46
  93.8 14.2 %all_to_all.111 = f32[16,8,128]{2,1,0:T(8,128)S(1)} all-to-all(f32[16,8,128]{2,1,0:T(8,128)S(1)} %broadcast_in_dim.43), channel_id=1, replica_groups=mesh['gx'=32,'gy'=16] {'gy'}, dimensions={0} | all-to-all | bytes 131072 | tf_op jit(solution)/shard_map/all_to_all | solution.py:18
  109.0 4.9 %all-to-all-start.4 = ((f32[32,8,128]{2,1,0:T(8,128)}), f32[32,8,128]{2,1,0:T(8,128)S(1)}, u32[]{:S(2)}, u32[]{:S(2)}) async-start(f32[32,8,128]{2,1,0:T(8,128)} %fusion.95), calls=%async_computation.4 | async-start | bytes 262144 | tf_op jit(solution)/shard_map/all_to_all | solution.py:112
  113.8 1.0 gather_fusion.2
  114.9 8.1 %all-to-all-done.4 = f32[32,8,128]{2,1,0:T(8,128)S(1)} async-done(((f32[32,8,128]{2,1,0:T(8,128)}), f32[32,8,128]{2,1,0:T(8,128)S(1)}, u32[]{:S(2)}, u32[]{:S(2)}) %all-to-all-start.4) | async-done | bytes 131104 | tf_op jit(solution)/shard_map/all_to_all | solution.py:112
  124.1 1.0 gather_fusion.3
  125.8 4.0 %collective-permute-start.7 = (f32[2,128,128]{2,1,0:T(8,128)}, f32[2,128,128]{2,1,0:T(8,128)S(1)}, u32[]{:S(2)}, u32[]{:S(2)}) collective-permute-start(f32[2,128,128]{2,1,0:T(8,128)} %get-tuple-element.34), channel_id=1, source_target_pairs={{1,0},{2,1},{3,2},{4,3},{5,4},{6,5},{7,6},{8,7},{9,8},{10,9},{11,1... | collective-permute-start | bytes 393224 | tf_op jit(solution)/shard_map/ppermute | solution.py:12
  129.8 2.0 collective-permute-start.6
  131.9 1.3 collective-permute-start.5
  133.2 4.0 %collective-permute-start.4 = (f32[2,128,128]{2,1,0:T(8,128)S(1)}, f32[2,128,128]{2,1,0:T(8,128)S(1)}, u32[]{:S(2)}, u32[]{:S(2)}) collective-permute-start(f32[2,128,128]{2,1,0:T(8,128)S(1)} %get-tuple-element.32), channel_id=1, source_target_pairs={{0,16},{16,32},{32,48},{48,64},{64,80},{80,96},{96,112},{112,128},... | collective-permute-start | bytes 393224 | tf_op jit(solution)/shard_map/ppermute | solution.py:12
  137.2 10.8 %all_to_all.112 = f32[16,2,128]{2,1,0:T(2,128)S(1)} all-to-all(f32[16,2,128]{2,1,0:T(2,128)S(1)} %broadcast_in_dim.44), channel_id=1, replica_groups=mesh['gx'=32,'gy'=16] {'gy'}, dimensions={0} | all-to-all | bytes 32768 | tf_op jit(solution)/shard_map/all_to_all | solution.py:18
  150.8 4.8 %all-to-all-start.6 = ((f32[32,2,128]{2,1,0:T(2,128)}), f32[32,2,128]{2,1,0:T(2,128)S(1)}, u32[]{:S(2)}, u32[]{:S(2)}) async-start(f32[32,2,128]{2,1,0:T(2,128)} %broadcast_in_dim.45), calls=%async_computation.6 | async-start | bytes 65536 | tf_op jit(solution)/shard_map/all_to_all | solution.py:18
  155.6 1.8 fusion.124
  157.4 7.0 %all-to-all-done.6 = f32[32,2,128]{2,1,0:T(2,128)S(1)} async-done(((f32[32,2,128]{2,1,0:T(2,128)}), f32[32,2,128]{2,1,0:T(2,128)S(1)}, u32[]{:S(2)}, u32[]{:S(2)}) %all-to-all-start.6) | async-done | bytes 32800 | tf_op jit(solution)/shard_map/all_to_all | solution.py:18
  165.0 1.0 fusion.67
  166.0 2.3 fusion.47
  168.4 12.0 %all_to_all.113 = f32[16,8,128]{2,1,0:T(8,128)S(1)} all-to-all(f32[16,8,128]{2,1,0:T(8,128)S(1)} %broadcast_in_dim.46), channel_id=1, replica_groups=mesh['gx'=32,'gy'=16] {'gy'}, dimensions={0} | all-to-all | bytes 131072 | tf_op jit(solution)/shard_map/all_to_all | solution.py:18
  181.3 4.0 %all-to-all-start.8 = ((f32[32,8,128]{2,1,0:T(8,128)}), f32[32,8,128]{2,1,0:T(8,128)S(1)}, u32[]{:S(2)}, u32[]{:S(2)}) async-start(f32[32,8,128]{2,1,0:T(8,128)} %fusion.93), calls=%async_computation.8 | async-start | bytes 262144 | tf_op jit(solution)/shard_map/all_to_all | solution.py:112
  185.4 1.0 gather_fusion.4
  186.4 7.9 %all-to-all-done.8 = f32[32,8,128]{2,1,0:T(8,128)S(1)} async-done(((f32[32,8,128]{2,1,0:T(8,128)}), f32[32,8,128]{2,1,0:T(8,128)S(1)}, u32[]{:S(2)}, u32[]{:S(2)}) %all-to-all-start.8) | async-done | bytes 131104 | tf_op jit(solution)/shard_map/all_to_all | solution.py:112
  195.4 1.0 gather_fusion.5
  197.3 3.9 %collective-permute-start.11 = (f32[2,128,128]{2,1,0:T(8,128)}, f32[2,128,128]{2,1,0:T(8,128)S(1)}, u32[]{:S(2)}, u32[]{:S(2)}) collective-permute-start(f32[2,128,128]{2,1,0:T(8,128)} %get-tuple-element.28), channel_id=1, source_target_pairs={{1,0},{2,1},{3,2},{4,3},{5,4},{6,5},{7,6},{8,7},{9,8},{10,9},{11,1... | collective-permute-start | bytes 393224 | tf_op jit(solution)/shard_map/ppermute | solution.py:12
  201.2 2.1 collective-permute-start.10
  203.3 1.3 collective-permute-start.9
  204.6 4.0 %collective-permute-start.8 = (f32[2,128,128]{2,1,0:T(8,128)}, f32[2,128,128]{2,1,0:T(8,128)S(1)}, u32[]{:S(2)}, u32[]{:S(2)}) collective-permute-start(f32[2,128,128]{2,1,0:T(8,128)} %get-tuple-element.26), channel_id=1, source_target_pairs={{0,16},{16,32},{32,48},{48,64},{64,80},{80,96},{96,112},{112,128},... | collective-permute-start | bytes 393224 | tf_op jit(solution)/shard_map/ppermute | solution.py:12
  208.6 10.7 %all_to_all.114 = f32[16,2,128]{2,1,0:T(2,128)S(1)} all-to-all(f32[16,2,128]{2,1,0:T(2,128)S(1)} %broadcast_in_dim.47), channel_id=1, replica_groups=mesh['gx'=32,'gy'=16] {'gy'}, dimensions={0} | all-to-all | bytes 32768 | tf_op jit(solution)/shard_map/all_to_all | solution.py:18
  220.8 1.1 pad_maximum_fusion.2
  223.2 5.1 %all-to-all-start.10 = ((f32[32,2,128]{2,1,0:T(2,128)}), f32[32,2,128]{2,1,0:T(2,128)S(1)}, u32[]{:S(2)}, u32[]{:S(2)}) async-start(f32[32,2,128]{2,1,0:T(2,128)} %broadcast_in_dim.48), calls=%async_computation.10 | async-start | bytes 65536 | tf_op jit(solution)/shard_map/all_to_all | solution.py:18
  229.2 7.9 %all-to-all-done.10 = f32[32,2,128]{2,1,0:T(2,128)S(1)} async-done(((f32[32,2,128]{2,1,0:T(2,128)}), f32[32,2,128]{2,1,0:T(2,128)S(1)}, u32[]{:S(2)}, u32[]{:S(2)}) %all-to-all-start.10) | async-done | bytes 32800 | tf_op jit(solution)/shard_map/all_to_all | solution.py:18
  237.2 1.3 fusion.120
  240.2 12.0 %all_to_all.115 = f32[16,8,128]{2,1,0:T(8,128)S(1)} all-to-all(f32[16,8,128]{2,1,0:T(8,128)S(1)} %broadcast_in_dim.49), channel_id=1, replica_groups=mesh['gx'=32,'gy'=16] {'gy'}, dimensions={0} | all-to-all | bytes 131072 | tf_op jit(solution)/shard_map/all_to_all | solution.py:18
  252.2 0.9 fusion.91
  253.1 3.9 %all-to-all-start.12 = ((f32[32,8,128]{2,1,0:T(8,128)}), f32[32,8,128]{2,1,0:T(8,128)S(1)}, u32[]{:S(2)}, u32[]{:S(2)}) async-start(f32[32,8,128]{2,1,0:T(8,128)} %fusion.91), calls=%async_computation.12 | async-start | bytes 262144 | tf_op jit(solution)/shard_map/all_to_all | solution.py:112
  257.0 1.0 gather_fusion.6
  258.0 1.0 gather_fusion.7
  259.9 2.0 collective-permute-start.15
  262.0 3.5 %collective-permute-start.14 = (f32[2,128,128]{2,1,0:T(8,128)}, f32[2,128,128]{2,1,0:T(8,128)S(1)}, u32[]{:S(2)}, u32[]{:S(2)}) collective-permute-start(f32[2,128,128]{2,1,0:T(8,128)} %get-tuple-element.23), channel_id=1, source_target_pairs={{0,1},{1,2},{2,3},{3,4},{4,5},{5,6},{6,7},{7,8},{8,9},{9,10},{10,1... | collective-permute-start | bytes 393224 | tf_op jit(solution)/shard_map/ppermute | solution.py:12
  265.5 1.3 collective-permute-start.13
  266.8 4.7 %collective-permute-start.12 = (f32[2,128,128]{2,1,0:T(8,128)}, f32[2,128,128]{2,1,0:T(8,128)}, u32[]{:S(2)}, u32[]{:S(2)}) collective-permute-start(f32[2,128,128]{2,1,0:T(8,128)} %get-tuple-element.20), channel_id=1, source_target_pairs={{0,16},{16,32},{32,48},{48,64},{64,80},{80,96},{96,112},{112,128},... | collective-permute-start | bytes 393224 | tf_op jit(solution)/shard_map/ppermute | solution.py:12
  271.9 1.7 multiply_reduce_fusion.1
  274.2 3.5 %all-to-all-start.13 = ((f32[16,2,128]{2,1,0:T(2,128)}), f32[16,2,128]{2,1,0:T(2,128)S(1)}, u32[]{:S(2)}, u32[]{:S(2)}) async-start(f32[16,2,128]{2,1,0:T(2,128)} %broadcast_in_dim.50), calls=%async_computation.13 | async-start | bytes 32768 | tf_op jit(solution)/shard_map/all_to_all | solution.py:18
  277.8 1.8 pad_maximum_fusion.3
  279.6 1.3 maximum_reduce_fusion
  281.5 3.5 %all-to-all-done.13 = f32[16,2,128]{2,1,0:T(2,128)S(1)} async-done(((f32[16,2,128]{2,1,0:T(2,128)}), f32[16,2,128]{2,1,0:T(2,128)S(1)}, u32[]{:S(2)}, u32[]{:S(2)}) %all-to-all-start.13) | async-done | bytes 16416 | tf_op jit(solution)/shard_map/all_to_all | solution.py:18
  285.7 8.6 %all-to-all-start.14 = ((f32[32,2,128]{2,1,0:T(2,128)}), f32[32,2,128]{2,1,0:T(2,128)S(1)}, u32[]{:S(2)}, u32[]{:S(2)}) async-start(f32[32,2,128]{2,1,0:T(2,128)} %broadcast_in_dim.51), calls=%async_computation.14 | async-start | bytes 65536 | tf_op jit(solution)/shard_map/all_to_all | solution.py:18
  294.3 1.1 fusion.122
  295.4 7.7 %all-to-all-done.14 = f32[32,2,128]{2,1,0:T(2,128)S(1)} async-done(((f32[32,2,128]{2,1,0:T(2,128)}), f32[32,2,128]{2,1,0:T(2,128)S(1)}, u32[]{:S(2)}, u32[]{:S(2)}) %all-to-all-start.14) | async-done | bytes 32800 | tf_op jit(solution)/shard_map/all_to_all | solution.py:18
  304.5 3.0 fusion.45
  (121 shorter events, 22.0 us)
Async XLA Ops:
  0.6 70.5 %copy-start = (bf16[1,1,896,896]{3,2,1,0:T(8,128)(2,1)S(1)}, bf16[1,1,896,896]{3,2,1,0:T(8,128)(2,1)}, u32[]{:S(2)}) copy-start(bf16[1,1,896,896]{3,2,1,0:T(8,128)(2,1)} %param.13) | copy-start | bytes 4816900
  2.5 34.7 %all-to-all-start.1 = ((f32[16,8,128]{2,1,0:T(8,128)}), f32[16,8,128]{2,1,0:T(8,128)S(1)}, u32[]{:S(2)}, u32[]{:S(2)}) async-start(f32[16,8,128]{2,1,0:T(8,128)} %broadcast_in_dim.42), calls=%async_computation.1 | async-start | bytes 131072 | tf_op jit(solution)/shard_map/all_to_all | solution.py:18
  18.6 28.3 %copy-start.16 = (f32[1,1,896]{2,1,0:T(1,128)S(1)}, f32[1,1,896]{2,1,0:T(1,128)}, u32[]{:S(2)}) copy-start(f32[1,1,896]{2,1,0:T(1,128)} %param.14) | copy-start | bytes 10756
  18.6 42.9 %copy-start.18 = (s32[1,1,4,128]{3,2,1,0:T(4,128)S(1)}, s32[1,1,4,128]{3,2,1,0:T(4,128)}, u32[]{:S(2)}) copy-start(s32[1,1,4,128]{3,2,1,0:T(4,128)} %param.16) | copy-start | bytes 6148
  18.6 52.1 %copy-start.11 = (bf16[1,1,8,896]{3,2,1,0:T(8,128)(2,1)S(1)}, bf16[1,1,8,896]{3,2,1,0:T(8,128)(2,1)}, u32[]{:S(2)}) copy-start(bf16[1,1,8,896]{3,2,1,0:T(8,128)(2,1)} %param.17) | copy-start | bytes 43012
  34.4 36.8 %copy-start.6 = (bf16[1,1,896,128]{3,2,1,0:T(8,128)(2,1)S(1)}, bf16[1,1,896,128]{3,2,1,0:T(8,128)(2,1)}, u32[]{:S(2)}) copy-start(bf16[1,1,896,128]{3,2,1,0:T(8,128)(2,1)} %param.10) | copy-start | bytes 688132
  37.3 18.9 %all-to-all-start = ((f32[8,32,128]{2,0,1:T(8,128)}), f32[8,32,128]{2,0,1:T(8,128)S(1)}, u32[]{:S(2)}, u32[]{:S(2)}) async-start(f32[8,32,128]{2,0,1:T(8,128)} %broadcast_select_fusion), calls=%async_computation | async-start | bytes 262144 | tf_op jit(solution)/shard_map/all_to_all | solution.py:72
  56.1 124.3 %copy-start.2 = (f32[8,32,128]{2,0,1:T(8,128)}, f32[8,32,128]{2,0,1:T(8,128)S(1)}, u32[]{:S(2)}) copy-start(f32[8,32,128]{2,0,1:T(8,128)S(1)} %all-to-all-done) | copy-start | bytes 393220
  57.0 13.7 %all-to-all-start.2 = ((f32[32,8,128]{2,1,0:T(8,128)}), f32[32,8,128]{2,1,0:T(8,128)S(1)}, u32[]{:S(2)}, u32[]{:S(2)}) async-start(f32[32,8,128]{2,1,0:T(8,128)} %fusion.97), calls=%async_computation.2 | async-start | bytes 262144 | tf_op jit(solution)/shard_map/all_to_all | solution.py:112
  71.8 17.0 %copy-start.17 = (f32[1,1,896]{2,1,0:T(1,128)S(1)}, f32[1,1,896]{2,1,0:T(1,128)}, u32[]{:S(2)}) copy-start(f32[1,1,896]{2,1,0:T(1,128)} %param.12) | copy-start | bytes 10756
  73.1 17.9 %collective-permute-start.3 = (bf16[128,128]{1,0:T(8,128)(2,1)S(1)}, bf16[128,128]{1,0:T(8,128)(2,1)S(1)}, u32[]{:S(2)}, u32[]{:S(2)}) collective-permute-start(bf16[128,128]{1,0:T(8,128)(2,1)S(1)} %get-tuple-element.40), channel_id=1, source_target_pairs={{1,0},{2,1},{3,2},{4,3},{5,4},{6,5},{7,6},{8,7},{9,8},{10,9},{11,1... | collective-permute-start | bytes 98312 | tf_op jit(solution)/shard_map/ppermute | solution.py:12
  77.8 13.3 %collective-permute-start.2 = (bf16[128,128]{1,0:T(8,128)(2,1)S(1)}, bf16[128,128]{1,0:T(8,128)(2,1)S(1)}, u32[]{:S(2)}, u32[]{:S(2)}) collective-permute-start(bf16[128,128]{1,0:T(8,128)(2,1)S(1)} %get-tuple-element.38), channel_id=1, source_target_pairs={{0,1},{1,2},{2,3},{3,4},{4,5},{5,6},{6,7},{7,8},{8,9},{9,10},{10,1... | collective-permute-start | bytes 98312 | tf_op jit(solution)/shard_map/ppermute | solution.py:12
  81.0 10.1 %collective-permute-start.1 = (bf16[128,128]{1,0:T(8,128)(2,1)S(1)}, bf16[128,128]{1,0:T(8,128)(2,1)S(1)}, u32[]{:S(2)}, u32[]{:S(2)}) collective-permute-start(bf16[128,128]{1,0:T(8,128)(2,1)S(1)} %get-tuple-element.39), channel_id=1, source_target_pairs={{16,0},{32,16},{48,32},{64,48},{80,64},{96,80},{112,96},{128,112},... | collective-permute-start | bytes 98312 | tf_op jit(solution)/shard_map/ppermute | solution.py:12
  82.3 8.8 %collective-permute-start = (bf16[128,128]{1,0:T(8,128)(2,1)S(1)}, bf16[128,128]{1,0:T(8,128)(2,1)S(1)}, u32[]{:S(2)}, u32[]{:S(2)}) collective-permute-start(bf16[128,128]{1,0:T(8,128)(2,1)S(1)} %get-tuple-element.37), channel_id=1, source_target_pairs={{0,16},{16,32},{32,48},{48,64},{64,80},{80,96},{96,112},{112,128},... | collective-permute-start | bytes 98312 | tf_op jit(solution)/shard_map/ppermute | solution.py:12
  109.0 14.0 %all-to-all-start.4 = ((f32[32,8,128]{2,1,0:T(8,128)}), f32[32,8,128]{2,1,0:T(8,128)S(1)}, u32[]{:S(2)}, u32[]{:S(2)}) async-start(f32[32,8,128]{2,1,0:T(8,128)} %fusion.95), calls=%async_computation.4 | async-start | bytes 262144 | tf_op jit(solution)/shard_map/all_to_all | solution.py:112
  125.8 22.2 %collective-permute-start.7 = (f32[2,128,128]{2,1,0:T(8,128)}, f32[2,128,128]{2,1,0:T(8,128)S(1)}, u32[]{:S(2)}, u32[]{:S(2)}) collective-permute-start(f32[2,128,128]{2,1,0:T(8,128)} %get-tuple-element.34), channel_id=1, source_target_pairs={{1,0},{2,1},{3,2},{4,3},{5,4},{6,5},{7,6},{8,7},{9,8},{10,9},{11,1... | collective-permute-start | bytes 393224 | tf_op jit(solution)/shard_map/ppermute | solution.py:12
  129.8 18.2 %collective-permute-start.6 = (f32[2,128,128]{2,1,0:T(8,128)}, f32[2,128,128]{2,1,0:T(8,128)S(1)}, u32[]{:S(2)}, u32[]{:S(2)}) collective-permute-start(f32[2,128,128]{2,1,0:T(8,128)} %get-tuple-element.35), channel_id=1, source_target_pairs={{0,1},{1,2},{2,3},{3,4},{4,5},{5,6},{6,7},{7,8},{8,9},{9,10},{10,1... | collective-permute-start | bytes 393224 | tf_op jit(solution)/shard_map/ppermute | solution.py:12
  131.9 16.1 %collective-permute-start.5 = (f32[2,128,128]{2,1,0:T(8,128)}, f32[2,128,128]{2,1,0:T(8,128)S(1)}, u32[]{:S(2)}, u32[]{:S(2)}) collective-permute-start(f32[2,128,128]{2,1,0:T(8,128)} %get-tuple-element.33), channel_id=1, source_target_pairs={{16,0},{32,16},{48,32},{64,48},{80,64},{96,80},{112,96},{128,112},... | collective-permute-start | bytes 393224 | tf_op jit(solution)/shard_map/ppermute | solution.py:12
  133.2 14.8 %collective-permute-start.4 = (f32[2,128,128]{2,1,0:T(8,128)S(1)}, f32[2,128,128]{2,1,0:T(8,128)S(1)}, u32[]{:S(2)}, u32[]{:S(2)}) collective-permute-start(f32[2,128,128]{2,1,0:T(8,128)S(1)} %get-tuple-element.32), channel_id=1, source_target_pairs={{0,16},{16,32},{32,48},{48,64},{64,80},{80,96},{96,112},{112,128},... | collective-permute-start | bytes 393224 | tf_op jit(solution)/shard_map/ppermute | solution.py:12
  150.8 13.6 %all-to-all-start.6 = ((f32[32,2,128]{2,1,0:T(2,128)}), f32[32,2,128]{2,1,0:T(2,128)S(1)}, u32[]{:S(2)}, u32[]{:S(2)}) async-start(f32[32,2,128]{2,1,0:T(2,128)} %broadcast_in_dim.45), calls=%async_computation.6 | async-start | bytes 65536 | tf_op jit(solution)/shard_map/all_to_all | solution.py:18
  164.4 1.6 copy-start.8
  181.3 13.0 %all-to-all-start.8 = ((f32[32,8,128]{2,1,0:T(8,128)}), f32[32,8,128]{2,1,0:T(8,128)S(1)}, u32[]{:S(2)}, u32[]{:S(2)}) async-start(f32[32,8,128]{2,1,0:T(8,128)} %fusion.93), calls=%async_computation.8 | async-start | bytes 262144 | tf_op jit(solution)/shard_map/all_to_all | solution.py:112
  195.4 26.5 %copy-start.1 = (f32[896,128]{1,0:T(8,128)}, f32[896,128]{1,0:T(8,128)S(1)}, u32[]{:S(2)}) copy-start(f32[896,128]{1,0:T(8,128)S(1)} %get-tuple-element.44) | copy-start | bytes 1376260
  197.3 22.1 %collective-permute-start.11 = (f32[2,128,128]{2,1,0:T(8,128)}, f32[2,128,128]{2,1,0:T(8,128)S(1)}, u32[]{:S(2)}, u32[]{:S(2)}) collective-permute-start(f32[2,128,128]{2,1,0:T(8,128)} %get-tuple-element.28), channel_id=1, source_target_pairs={{1,0},{2,1},{3,2},{4,3},{5,4},{6,5},{7,6},{8,7},{9,8},{10,9},{11,1... | collective-permute-start | bytes 393224 | tf_op jit(solution)/shard_map/ppermute | solution.py:12
  201.2 18.2 %collective-permute-start.10 = (f32[2,128,128]{2,1,0:T(8,128)}, f32[2,128,128]{2,1,0:T(8,128)S(1)}, u32[]{:S(2)}, u32[]{:S(2)}) collective-permute-start(f32[2,128,128]{2,1,0:T(8,128)} %get-tuple-element.29), channel_id=1, source_target_pairs={{0,1},{1,2},{2,3},{3,4},{4,5},{5,6},{6,7},{7,8},{8,9},{9,10},{10,1... | collective-permute-start | bytes 393224 | tf_op jit(solution)/shard_map/ppermute | solution.py:12
  203.3 16.1 %collective-permute-start.9 = (f32[2,128,128]{2,1,0:T(8,128)}, f32[2,128,128]{2,1,0:T(8,128)S(1)}, u32[]{:S(2)}, u32[]{:S(2)}) collective-permute-start(f32[2,128,128]{2,1,0:T(8,128)} %get-tuple-element.27), channel_id=1, source_target_pairs={{16,0},{32,16},{48,32},{64,48},{80,64},{96,80},{112,96},{128,112},... | collective-permute-start | bytes 393224 | tf_op jit(solution)/shard_map/ppermute | solution.py:12
  204.6 14.8 %collective-permute-start.8 = (f32[2,128,128]{2,1,0:T(8,128)}, f32[2,128,128]{2,1,0:T(8,128)S(1)}, u32[]{:S(2)}, u32[]{:S(2)}) collective-permute-start(f32[2,128,128]{2,1,0:T(8,128)} %get-tuple-element.26), channel_id=1, source_target_pairs={{0,16},{16,32},{32,48},{48,64},{64,80},{80,96},{96,112},{112,128},... | collective-permute-start | bytes 393224 | tf_op jit(solution)/shard_map/ppermute | solution.py:12
  219.4 0.6 copy-start.12
  219.4 0.7 copy-start.13
  219.4 0.7 copy-start.14
  219.4 0.7 copy-start.15
  223.2 13.9 %all-to-all-start.10 = ((f32[32,2,128]{2,1,0:T(2,128)}), f32[32,2,128]{2,1,0:T(2,128)S(1)}, u32[]{:S(2)}, u32[]{:S(2)}) async-start(f32[32,2,128]{2,1,0:T(2,128)} %broadcast_in_dim.48), calls=%async_computation.10 | async-start | bytes 65536 | tf_op jit(solution)/shard_map/all_to_all | solution.py:18
  237.2 1.3 copy-start.4
  237.2 1.3 copy-start.5
  237.2 1.5 copy-start.9
  237.2 2.0 copy-start.19
  239.2 13.0 %copy-start.3 = (f32[8,32,128]{2,0,1:T(8,128)S(1)}, f32[8,32,128]{2,0,1:T(8,128)}, u32[]{:S(2)}) copy-start(f32[8,32,128]{2,0,1:T(8,128)} %copy-done.2) | copy-start | bytes 393220
  240.0 17.0 %copy-start.7 = (bf16[896,128]{1,0:T(8,128)(2,1)}, bf16[896,128]{1,0:T(8,128)(2,1)S(1)}, u32[]{:S(2)}) copy-start(bf16[896,128]{1,0:T(8,128)(2,1)S(1)} %fusion.48) | copy-start | bytes 688132
  253.1 18.3 %all-to-all-start.12 = ((f32[32,8,128]{2,1,0:T(8,128)}), f32[32,8,128]{2,1,0:T(8,128)S(1)}, u32[]{:S(2)}, u32[]{:S(2)}) async-start(f32[32,8,128]{2,1,0:T(8,128)} %fusion.91), calls=%async_computation.12 | async-start | bytes 262144 | tf_op jit(solution)/shard_map/all_to_all | solution.py:112
  259.9 17.8 %collective-permute-start.15 = (f32[2,128,128]{2,1,0:T(8,128)}, f32[2,128,128]{2,1,0:T(8,128)S(1)}, u32[]{:S(2)}, u32[]{:S(2)}) collective-permute-start(f32[2,128,128]{2,1,0:T(8,128)} %get-tuple-element.22), channel_id=1, source_target_pairs={{1,0},{2,1},{3,2},{4,3},{5,4},{6,5},{7,6},{8,7},{9,8},{10,9},{11,1... | collective-permute-start | bytes 393224 | tf_op jit(solution)/shard_map/ppermute | solution.py:12
  262.0 15.7 %collective-permute-start.14 = (f32[2,128,128]{2,1,0:T(8,128)}, f32[2,128,128]{2,1,0:T(8,128)S(1)}, u32[]{:S(2)}, u32[]{:S(2)}) collective-permute-start(f32[2,128,128]{2,1,0:T(8,128)} %get-tuple-element.23), channel_id=1, source_target_pairs={{0,1},{1,2},{2,3},{3,4},{4,5},{5,6},{6,7},{7,8},{8,9},{9,10},{10,1... | collective-permute-start | bytes 393224 | tf_op jit(solution)/shard_map/ppermute | solution.py:12
  265.5 12.2 %collective-permute-start.13 = (f32[2,128,128]{2,1,0:T(8,128)}, f32[2,128,128]{2,1,0:T(8,128)}, u32[]{:S(2)}, u32[]{:S(2)}) collective-permute-start(f32[2,128,128]{2,1,0:T(8,128)} %get-tuple-element.21), channel_id=1, source_target_pairs={{16,0},{32,16},{48,32},{64,48},{80,64},{96,80},{112,96},{128,112},... | collective-permute-start | bytes 393224 | tf_op jit(solution)/shard_map/ppermute | solution.py:12
  266.8 11.0 %collective-permute-start.12 = (f32[2,128,128]{2,1,0:T(8,128)}, f32[2,128,128]{2,1,0:T(8,128)}, u32[]{:S(2)}, u32[]{:S(2)}) collective-permute-start(f32[2,128,128]{2,1,0:T(8,128)} %get-tuple-element.20), channel_id=1, source_target_pairs={{0,16},{16,32},{32,48},{48,64},{64,80},{80,96},{96,112},{112,128},... | collective-permute-start | bytes 393224 | tf_op jit(solution)/shard_map/ppermute | solution.py:12
  274.2 10.9 %all-to-all-start.13 = ((f32[16,2,128]{2,1,0:T(2,128)}), f32[16,2,128]{2,1,0:T(2,128)S(1)}, u32[]{:S(2)}, u32[]{:S(2)}) async-start(f32[16,2,128]{2,1,0:T(2,128)} %broadcast_in_dim.50), calls=%async_computation.13 | async-start | bytes 32768 | tf_op jit(solution)/shard_map/all_to_all | solution.py:18
  285.7 17.4 %all-to-all-start.14 = ((f32[32,2,128]{2,1,0:T(2,128)}), f32[32,2,128]{2,1,0:T(2,128)S(1)}, u32[]{:S(2)}, u32[]{:S(2)}) async-start(f32[32,2,128]{2,1,0:T(2,128)} %broadcast_in_dim.51), calls=%async_computation.14 | async-start | bytes 65536 | tf_op jit(solution)/shard_map/all_to_all | solution.py:18
  303.1 1.3 copy-start.10

commit v11 on v10

--- a/solution.py
+++ b/solution.py
@@ -66,6 +66,7 @@
     schur_with_couplings = jnp.concatenate([schur_mat, -placed_couplings], axis=1)
     vectors = deflation[0, 0]
     vectors_wide = vectors.astype(jnp.float32).T
+    trace_with_vectors = jnp.concatenate([vectors, trace_mat], axis=0)
     count_x, count_y = lax.axis_size("gx"), lax.axis_size("gy")
     depth = vectors.shape[0]
     coarse_cols = jnp.take(coarse_inverse, coarse_map, axis=1)
@@ -103,10 +104,9 @@
 
     def apply_prec(field):
         rounded = lax.optimization_barrier(field.astype(jnp.bfloat16))
-        result = trace_scale * rounded.astype(jnp.float32) + jnp.dot(
-            trace_mat, rounded, preferred_element_type=jnp.float32
-        )
-        coarse = jnp.dot(vectors, rounded, preferred_element_type=jnp.float32)
+        both = jnp.dot(trace_with_vectors, rounded, preferred_element_type=jnp.float32)
+        coarse = both[: vectors.shape[0]]
+        result = trace_scale * rounded.astype(jnp.float32) + both[vectors.shape[0] :]
         line = gather_rows(coarse, "gy")
         partial = jnp.dot(coarse_block, line, precision=lax.Precision.HIGHEST)
         pieces = lax.all_to_all(partial, "gx", 0, 0, tiled=True)

time: 309 us -> 297 us (0.961)
  other arithmetic: 15.1 us -> 4.99 us
  local copies, waits for them, and re-layouts: 39.3 us -> 31.5 us
  waiting for transfers between devices: 60.4 us -> 66.6 us
    all_to_all x5, waiting for transfers between devices: 26.1 us -> 32.1 us  [gather_rows(): lax.all_to_all(copies.reshape((-1,) + value.shape[1:]), axis, 0, 0, tiled...]
    another operation x4, other arithmetic: 3.81 us -> 0.13 us  [exchange(): jnp.stack([pass_columns(sent_rows[1], 1), pass_columns(sent_rows[0], -1),...]
    slice x3, local copies, waits for them, and re-layouts: 3.68 us -> 0.11 us  [apply_schur_late(): received = (pair[:, 0] + coef * pair[:, 1]).astype(jnp.bfloat16)]
  transfers between devices with their start and end apart: 26 -> 26, of which waited for: 8 -> 8; matrix products, arithmetic and copies ran while one was open for 14% -> 9% of each run, Pallas kernels for 0% -> 0%
where the time goes in v11:
time: 297 us; the launch traced here: 296 us
  starting transfers between devices  110 us (37%)
  waiting for transfers between devices  66.6 us (22%)
  blocking collectives  60 us (20%)
  local copies, waits for them, and re-layouts  31.5 us (11%)
  matrix products  18.6 us (6%)
  other arithmetic  4.99 us (2%)
  between operations  3.48 us (1%)
    all_to_all x5, blocking collectives, gather_rows(): lax.all_to_all(copies.reshape((-1,) + value.shape[1:]), axis, 0, 0, tiled...  60 us
    ppermute x16, starting transfers between devices, from_behind(): lax.ppermute(value, axis, [(source, source + steps) for source in range(l...  46.7 us
    all_to_all x5, starting transfers between devices, gather_rows(): lax.all_to_all(copies.reshape((-1,) + value.shape[1:]), axis, 0, 0, tiled...  34.5 us
    all_to_all x5, waiting for transfers between devices, gather_rows(): lax.all_to_all(copies.reshape((-1,) + value.shape[1:]), axis, 0, 0, tiled...  32.1 us
    all_to_all x4, waiting for transfers between devices, apply_prec(): pieces = lax.all_to_all(partial, 'gx', 0, 0, tiled=True)  25.3 us
    all_to_all x4, starting transfers between devices, apply_prec(): pieces = lax.all_to_all(partial, 'gx', 0, 0, tiled=True)  19.5 us
    gather x2, local copies, waits for them, and re-layouts, shards(): coarse_cols = jnp.take(coarse_inverse, coarse_map, axis=1)  16.3 us
    all_to_all x1, starting transfers between devices, shards(): lax.all_to_all(coarse_cols.reshape(depth, count_x, count_y * depth), 'gx'...  9.69 us
  transfers between devices with their start and end apart: 26, of which 8 were waited for; matrix products, arithmetic and copies ran while one was open for 9% of the time, Pallas kernels for 0%

profile of v11, /device:TPU:1, one launch (start us, length us, event | category | flops | bytes accessed | tf_op | source)
XLA Modules:
  0.0 295.7 jit_solution(11966493947462342048)
XLA Ops:
  0.7 2.1 fusion.81
  3.4 11.8 %all-to-all-start.1 = ((f32[16,8,128]{2,1,0:T(8,128)}), f32[16,8,128]{2,1,0:T(8,128)S(1)}, u32[]{:S(2)}, u32[]{:S(2)}) async-start(f32[16,8,128]{2,1,0:T(8,128)} %broadcast_in_dim.42), calls=%async_computation.1 | async-start | bytes 131072 | tf_op jit(solution)/shard_map/all_to_all | solution.py:18
  16.0 14.1 %gather_fusion = f32[4096,8]{1,0:T(8,128)} fusion(f32[8,4096]{0,1:T(8,128)S(1)} %copy.80, s32[4096]{0:T(1024)S(1)} %fusion.67), kind=kCustom, calls=%fused_computation | custom fusion | bytes 278528 | tf_op jit(solution)/shard_map/jit(_take)/gather | solution.py:72
  30.1 2.2 copy.81
  32.2 0.7 broadcast_select_fusion
  32.9 9.7 %all-to-all-start = ((f32[8,32,128]{2,0,1:T(8,128)}), f32[8,32,128]{2,0,1:T(8,128)S(1)}, u32[]{:S(2)}, u32[]{:S(2)}) async-start(f32[8,32,128]{2,0,1:T(8,128)} %broadcast_select_fusion), calls=%async_computation | async-start | bytes 262144 | tf_op jit(solution)/shard_map/all_to_all | solution.py:73
  42.7 9.1 %all-to-all-done = f32[8,32,128]{2,0,1:T(8,128)S(1)} async-done(((f32[8,32,128]{2,0,1:T(8,128)}), f32[8,32,128]{2,0,1:T(8,128)S(1)}, u32[]{:S(2)}, u32[]{:S(2)}) %all-to-all-start) | async-done | bytes 131104 | tf_op jit(solution)/shard_map/all_to_all | solution.py:73
  51.8 0.9 fusion.60
  52.7 4.5 %all-to-all-start.2 = ((f32[32,8,128]{2,1,0:T(8,128)}), f32[32,8,128]{2,1,0:T(8,128)S(1)}, u32[]{:S(2)}, u32[]{:S(2)}) async-start(f32[32,8,128]{2,1,0:T(8,128)} %fusion.60), calls=%async_computation.2 | async-start | bytes 262144 | tf_op jit(solution)/shard_map/all_to_all | solution.py:112
  57.3 9.1 %all-to-all-done.2 = f32[32,8,128]{2,1,0:T(8,128)S(1)} async-done(((f32[32,8,128]{2,1,0:T(8,128)}), f32[32,8,128]{2,1,0:T(8,128)S(1)}, u32[]{:S(2)}, u32[]{:S(2)}) %all-to-all-start.2) | async-done | bytes 131104 | tf_op jit(solution)/shard_map/all_to_all | solution.py:112
  66.9 1.3 gather_fusion.1
  68.3 4.6 %collective-permute-start.3 = (bf16[128,128]{1,0:T(8,128)(2,1)S(1)}, bf16[128,128]{1,0:T(8,128)(2,1)S(1)}, u32[]{:S(2)}, u32[]{:S(2)}) collective-permute-start(bf16[128,128]{1,0:T(8,128)(2,1)S(1)} %get-tuple-element.40), channel_id=1, source_target_pairs={{1,0},{2,1},{3,2},{4,3},{5,4},{6,5},{7,6},{8,7},{9,8},{10,9},{11,1... | collective-permute-start | bytes 98312 | tf_op jit(solution)/shard_map/ppermute | solution.py:12
  72.9 3.2 %collective-permute-start.2 = (bf16[128,128]{1,0:T(8,128)(2,1)S(1)}, bf16[128,128]{1,0:T(8,128)(2,1)S(1)}, u32[]{:S(2)}, u32[]{:S(2)}) collective-permute-start(bf16[128,128]{1,0:T(8,128)(2,1)S(1)} %get-tuple-element.38), channel_id=1, source_target_pairs={{0,1},{1,2},{2,3},{3,4},{4,5},{5,6},{6,7},{7,8},{8,9},{9,10},{10,1... | collective-permute-start | bytes 98312 | tf_op jit(solution)/shard_map/ppermute | solution.py:12
  76.1 1.3 collective-permute-start.1
  77.4 4.0 %collective-permute-start = (bf16[128,128]{1,0:T(8,128)(2,1)S(1)}, bf16[128,128]{1,0:T(8,128)(2,1)S(1)}, u32[]{:S(2)}, u32[]{:S(2)}) collective-permute-start(bf16[128,128]{1,0:T(8,128)(2,1)S(1)} %get-tuple-element.37), channel_id=1, source_target_pairs={{0,16},{16,32},{32,48},{48,64},{64,80},{80,96},{96,112},{112,128},... | collective-permute-start | bytes 98312 | tf_op jit(solution)/shard_map/ppermute | solution.py:12
  82.7 2.5 fusion.9
  85.2 0.7 fusion.80
  85.9 14.4 %all_to_all.111 = f32[16,8,128]{2,1,0:T(8,128)S(1)} all-to-all(f32[16,8,128]{2,1,0:T(8,128)S(1)} %broadcast_in_dim.43), channel_id=1, replica_groups=mesh['gx'=32,'gy'=16] {'gy'}, dimensions={0} | all-to-all | bytes 131072 | tf_op jit(solution)/shard_map/all_to_all | solution.py:18
  100.3 0.9 fusion.58
  101.3 7.3 %all-to-all-start.4 = ((f32[32,8,128]{2,1,0:T(8,128)}), f32[32,8,128]{2,1,0:T(8,128)S(1)}, u32[]{:S(2)}, u32[]{:S(2)}) async-start(f32[32,8,128]{2,1,0:T(8,128)} %fusion.58), calls=%async_computation.4 | async-start | bytes 262144 | tf_op jit(solution)/shard_map/all_to_all | solution.py:112
  108.5 1.0 gather_fusion.2
  109.6 8.1 %all-to-all-done.4 = f32[32,8,128]{2,1,0:T(8,128)S(1)} async-done(((f32[32,8,128]{2,1,0:T(8,128)}), f32[32,8,128]{2,1,0:T(8,128)S(1)}, u32[]{:S(2)}, u32[]{:S(2)}) %all-to-all-start.4) | async-done | bytes 131104 | tf_op jit(solution)/shard_map/all_to_all | solution.py:112
  118.2 1.0 gather_fusion.3
  119.3 4.0 %collective-permute-start.7 = (f32[2,128,128]{2,1,0:T(8,128)S(1)}, f32[2,128,128]{2,1,0:T(8,128)S(1)}, u32[]{:S(2)}, u32[]{:S(2)}) collective-permute-start(f32[2,128,128]{2,1,0:T(8,128)S(1)} %get-tuple-element.34), channel_id=1, source_target_pairs={{1,0},{2,1},{3,2},{4,3},{5,4},{6,5},{7,6},{8,7},{9,8},{10,9},{11,1... | collective-permute-start | bytes 393224 | tf_op jit(solution)/shard_map/ppermute | solution.py:12
  123.3 2.0 collective-permute-start.6
  125.3 1.3 collective-permute-start.5
  126.6 4.0 %collective-permute-start.4 = (f32[2,128,128]{2,1,0:T(8,128)S(1)}, f32[2,128,128]{2,1,0:T(8,128)S(1)}, u32[]{:S(2)}, u32[]{:S(2)}) collective-permute-start(f32[2,128,128]{2,1,0:T(8,128)S(1)} %get-tuple-element.32), channel_id=1, source_target_pairs={{0,16},{16,32},{32,48},{48,64},{64,80},{80,96},{96,112},{112,128},... | collective-permute-start | bytes 393224 | tf_op jit(solution)/shard_map/ppermute | solution.py:12
  130.7 10.8 %all_to_all.112 = f32[16,2,128]{2,1,0:T(2,128)S(1)} all-to-all(f32[16,2,128]{2,1,0:T(2,128)S(1)} %broadcast_in_dim.44), channel_id=1, replica_groups=mesh['gx'=32,'gy'=16] {'gy'}, dimensions={0} | all-to-all | bytes 32768 | tf_op jit(solution)/shard_map/all_to_all | solution.py:18
  143.4 4.8 %all-to-all-start.6 = ((f32[32,2,128]{2,1,0:T(2,128)}), f32[32,2,128]{2,1,0:T(2,128)S(1)}, u32[]{:S(2)}, u32[]{:S(2)}) async-start(f32[32,2,128]{2,1,0:T(2,128)} %broadcast_in_dim.45), calls=%async_computation.6 | async-start | bytes 65536 | tf_op jit(solution)/shard_map/all_to_all | solution.py:18
  148.3 8.7 %all-to-all-done.6 = f32[32,2,128]{2,1,0:T(2,128)S(1)} async-done(((f32[32,2,128]{2,1,0:T(2,128)}), f32[32,2,128]{2,1,0:T(2,128)S(1)}, u32[]{:S(2)}, u32[]{:S(2)}) %all-to-all-start.6) | async-done | bytes 32800 | tf_op jit(solution)/shard_map/all_to_all | solution.py:18
  157.2 1.3 copy-done.13
  158.5 2.1 fusion.10
  161.3 12.0 %all_to_all.113 = f32[16,8,128]{2,1,0:T(8,128)S(1)} all-to-all(f32[16,8,128]{2,1,0:T(8,128)S(1)} %broadcast_in_dim.46), channel_id=1, replica_groups=mesh['gx'=32,'gy'=16] {'gy'}, dimensions={0} | all-to-all | bytes 131072 | tf_op jit(solution)/shard_map/all_to_all | solution.py:18
  173.3 0.9 fusion.56
  174.2 3.9 %all-to-all-start.8 = ((f32[32,8,128]{2,1,0:T(8,128)}), f32[32,8,128]{2,1,0:T(8,128)S(1)}, u32[]{:S(2)}, u32[]{:S(2)}) async-start(f32[32,8,128]{2,1,0:T(8,128)} %fusion.56), calls=%async_computation.8 | async-start | bytes 262144 | tf_op jit(solution)/shard_map/all_to_all | solution.py:112
  178.1 1.0 gather_fusion.4
  179.2 8.1 %all-to-all-done.8 = f32[32,8,128]{2,1,0:T(8,128)S(1)} async-done(((f32[32,8,128]{2,1,0:T(8,128)}), f32[32,8,128]{2,1,0:T(8,128)S(1)}, u32[]{:S(2)}, u32[]{:S(2)}) %all-to-all-start.8) | async-done | bytes 131104 | tf_op jit(solution)/shard_map/all_to_all | solution.py:112
  187.8 1.0 gather_fusion.5
  188.9 4.0 %collective-permute-start.11 = (f32[2,128,128]{2,1,0:T(8,128)S(1)}, f32[2,128,128]{2,1,0:T(8,128)S(1)}, u32[]{:S(2)}, u32[]{:S(2)}) collective-permute-start(f32[2,128,128]{2,1,0:T(8,128)S(1)} %get-tuple-element.28), channel_id=1, source_target_pairs={{1,0},{2,1},{3,2},{4,3},{5,4},{6,5},{7,6},{8,7},{9,8},{10,9},{11,1... | collective-permute-start | bytes 393224 | tf_op jit(solution)/shard_map/ppermute | solution.py:12
  192.8 2.2 collective-permute-start.10
  195.1 1.3 collective-permute-start.9
  196.4 4.0 %collective-permute-start.8 = (f32[2,128,128]{2,1,0:T(8,128)S(1)}, f32[2,128,128]{2,1,0:T(8,128)S(1)}, u32[]{:S(2)}, u32[]{:S(2)}) collective-permute-start(f32[2,128,128]{2,1,0:T(8,128)S(1)} %get-tuple-element.26), channel_id=1, source_target_pairs={{0,16},{16,32},{32,48},{48,64},{64,80},{80,96},{96,112},{112,128},... | collective-permute-start | bytes 393224 | tf_op jit(solution)/shard_map/ppermute | solution.py:12
  200.4 10.7 %all_to_all.114 = f32[16,2,128]{2,1,0:T(2,128)S(1)} all-to-all(f32[16,2,128]{2,1,0:T(2,128)S(1)} %broadcast_in_dim.47), channel_id=1, replica_groups=mesh['gx'=32,'gy'=16] {'gy'}, dimensions={0} | all-to-all | bytes 32768 | tf_op jit(solution)/shard_map/all_to_all | solution.py:18
  213.1 5.1 %all-to-all-start.10 = ((f32[32,2,128]{2,1,0:T(2,128)}), f32[32,2,128]{2,1,0:T(2,128)S(1)}, u32[]{:S(2)}, u32[]{:S(2)}) async-start(f32[32,2,128]{2,1,0:T(2,128)} %broadcast_in_dim.48), calls=%async_computation.10 | async-start | bytes 65536 | tf_op jit(solution)/shard_map/all_to_all | solution.py:18
  218.3 8.7 %all-to-all-done.10 = f32[32,2,128]{2,1,0:T(2,128)S(1)} async-done(((f32[32,2,128]{2,1,0:T(2,128)}), f32[32,2,128]{2,1,0:T(2,128)S(1)}, u32[]{:S(2)}, u32[]{:S(2)}) %all-to-all-start.10) | async-done | bytes 32800 | tf_op jit(solution)/shard_map/all_to_all | solution.py:18
  227.2 1.2 copy-done.14
  228.5 2.1 fusion.11
  231.3 12.0 %all_to_all.115 = f32[16,8,128]{2,1,0:T(8,128)S(1)} all-to-all(f32[16,8,128]{2,1,0:T(8,128)S(1)} %broadcast_in_dim.49), channel_id=1, replica_groups=mesh['gx'=32,'gy'=16] {'gy'}, dimensions={0} | all-to-all | bytes 131072 | tf_op jit(solution)/shard_map/all_to_all | solution.py:18
  243.3 0.9 fusion.54
  244.3 3.9 %all-to-all-start.12 = ((f32[32,8,128]{2,1,0:T(8,128)}), f32[32,8,128]{2,1,0:T(8,128)S(1)}, u32[]{:S(2)}, u32[]{:S(2)}) async-start(f32[32,8,128]{2,1,0:T(8,128)} %fusion.54), calls=%async_computation.12 | async-start | bytes 262144 | tf_op jit(solution)/shard_map/all_to_all | solution.py:112
  248.1 1.0 gather_fusion.6
  249.2 1.0 gather_fusion.7
  250.2 0.7 fusion.36
  250.9 2.0 collective-permute-start.15
  253.0 3.5 %collective-permute-start.14 = (f32[2,128,128]{2,1,0:T(8,128)S(1)}, f32[2,128,128]{2,1,0:T(8,128)S(1)}, u32[]{:S(2)}, u32[]{:S(2)}) collective-permute-start(f32[2,128,128]{2,1,0:T(8,128)S(1)} %get-tuple-element.23), channel_id=1, source_target_pairs={{0,1},{1,2},{2,3},{3,4},{4,5},{5,6},{6,7},{7,8},{8,9},{9,10},{10,1... | collective-permute-start | bytes 393224 | tf_op jit(solution)/shard_map/ppermute | solution.py:12
  256.5 1.3 collective-permute-start.13
  257.8 4.0 %collective-permute-start.12 = (f32[2,128,128]{2,1,0:T(8,128)S(1)}, f32[2,128,128]{2,1,0:T(8,128)S(1)}, u32[]{:S(2)}, u32[]{:S(2)}) collective-permute-start(f32[2,128,128]{2,1,0:T(8,128)S(1)} %get-tuple-element.20), channel_id=1, source_target_pairs={{0,16},{16,32},{32,48},{48,64},{64,80},{80,96},{96,112},{112,128},... | collective-permute-start | bytes 393224 | tf_op jit(solution)/shard_map/ppermute | solution.py:12
  262.9 3.5 %all-to-all-start.13 = ((f32[16,2,128]{2,1,0:T(2,128)}), f32[16,2,128]{2,1,0:T(2,128)S(1)}, u32[]{:S(2)}, u32[]{:S(2)}) async-start(f32[16,2,128]{2,1,0:T(2,128)} %broadcast_in_dim.50), calls=%async_computation.13 | async-start | bytes 32768 | tf_op jit(solution)/shard_map/all_to_all | solution.py:18
  267.8 6.0 %all-to-all-done.13 = f32[16,2,128]{2,1,0:T(2,128)S(1)} async-done(((f32[16,2,128]{2,1,0:T(2,128)}), f32[16,2,128]{2,1,0:T(2,128)S(1)}, u32[]{:S(2)}, u32[]{:S(2)}) %all-to-all-start.13) | async-done | bytes 16416 | tf_op jit(solution)/shard_map/all_to_all | solution.py:18
  274.4 9.2 %all-to-all-start.14 = ((f32[32,2,128]{2,1,0:T(2,128)}), f32[32,2,128]{2,1,0:T(2,128)S(1)}, u32[]{:S(2)}, u32[]{:S(2)}) async-start(f32[32,2,128]{2,1,0:T(2,128)} %broadcast_in_dim.51), calls=%async_computation.14 | async-start | bytes 65536 | tf_op jit(solution)/shard_map/all_to_all | solution.py:18
  283.7 8.7 %all-to-all-done.14 = f32[32,2,128]{2,1,0:T(2,128)S(1)} async-done(((f32[32,2,128]{2,1,0:T(2,128)}), f32[32,2,128]{2,1,0:T(2,128)S(1)}, u32[]{:S(2)}, u32[]{:S(2)}) %all-to-all-start.14) | async-done | bytes 32800 | tf_op jit(solution)/shard_map/all_to_all | solution.py:18
  292.5 0.8 fusion.31
  293.4 0.7 copy-done.15
  294.1 1.6 fusion.4
  (113 shorter events, 11.1 us)
Async XLA Ops:
  0.6 80.8 %copy-start = (bf16[1,1,4,128,128]{4,3,2,1,0:T(8,128)(2,1)S(1)}, bf16[1,1,4,128,128]{4,3,2,1,0:T(8,128)(2,1)}, u32[]{:S(2)}) copy-start(bf16[1,1,4,128,128]{4,3,2,1,0:T(8,128)(2,1)} %param.15) | copy-start | bytes 393220
  0.6 14.6 %copy-start.6 = (s32[4096]{0:T(1024)S(1)}, s32[4096]{0:T(1024)}, u32[]{:S(2)}) copy-start(s32[4096]{0:T(1024)} %param.19) | copy-start | bytes 49156
  0.7 14.7 %copy-start.5 = (f32[8,4096]{1,0:T(8,128)S(1)}, f32[8,4096]{1,0:T(8,128)}, u32[]{:S(2)}) copy-start(f32[8,4096]{1,0:T(8,128)} %param.18) | copy-start | bytes 393220
  3.4 29.5 %all-to-all-start.1 = ((f32[16,8,128]{2,1,0:T(8,128)}), f32[16,8,128]{2,1,0:T(8,128)S(1)}, u32[]{:S(2)}, u32[]{:S(2)}) async-start(f32[16,8,128]{2,1,0:T(8,128)} %broadcast_in_dim.42), calls=%async_computation.1 | async-start | bytes 131072 | tf_op jit(solution)/shard_map/all_to_all | solution.py:18
  15.9 26.7 %copy-start.7 = (f32[1,1,896]{2,1,0:T(1,128)S(1)}, f32[1,1,896]{2,1,0:T(1,128)}, u32[]{:S(2)}) copy-start(f32[1,1,896]{2,1,0:T(1,128)} %param.14) | copy-start | bytes 10756
  15.9 41.3 %copy-start.9 = (s32[1,1,4,128]{3,2,1,0:T(4,128)S(1)}, s32[1,1,4,128]{3,2,1,0:T(4,128)}, u32[]{:S(2)}) copy-start(s32[1,1,4,128]{3,2,1,0:T(4,128)} %param.16) | copy-start | bytes 6148
  16.0 50.5 %copy-start.3 = (bf16[1,1,8,896]{3,2,1,0:T(8,128)(2,1)S(1)}, bf16[1,1,8,896]{3,2,1,0:T(8,128)(2,1)}, u32[]{:S(2)}) copy-start(bf16[1,1,8,896]{3,2,1,0:T(8,128)(2,1)} %param.17) | copy-start | bytes 43012
  16.0 50.5 %copy-start.4 = (bf16[1,1,896,128]{3,2,1,0:T(8,128)(2,1)S(1)}, bf16[1,1,896,128]{3,2,1,0:T(8,128)(2,1)}, u32[]{:S(2)}) copy-start(bf16[1,1,896,128]{3,2,1,0:T(8,128)(2,1)} %param.10) | copy-start | bytes 688132
  32.9 18.9 %all-to-all-start = ((f32[8,32,128]{2,0,1:T(8,128)}), f32[8,32,128]{2,0,1:T(8,128)S(1)}, u32[]{:S(2)}, u32[]{:S(2)}) async-start(f32[8,32,128]{2,0,1:T(8,128)} %broadcast_select_fusion), calls=%async_computation | async-start | bytes 262144 | tf_op jit(solution)/shard_map/all_to_all | solution.py:73
  52.7 13.7 %all-to-all-start.2 = ((f32[32,8,128]{2,1,0:T(8,128)}), f32[32,8,128]{2,1,0:T(8,128)S(1)}, u32[]{:S(2)}, u32[]{:S(2)}) async-start(f32[32,8,128]{2,1,0:T(8,128)} %fusion.60), calls=%async_computation.2 | async-start | bytes 262144 | tf_op jit(solution)/shard_map/all_to_all | solution.py:112
  66.4 15.6 %copy-start.8 = (f32[1,1,896]{2,1,0:T(1,128)S(1)}, f32[1,1,896]{2,1,0:T(1,128)}, u32[]{:S(2)}) copy-start(f32[1,1,896]{2,1,0:T(1,128)} %param.12) | copy-start | bytes 10756
  68.3 14.3 %collective-permute-start.3 = (bf16[128,128]{1,0:T(8,128)(2,1)S(1)}, bf16[128,128]{1,0:T(8,128)(2,1)S(1)}, u32[]{:S(2)}, u32[]{:S(2)}) collective-permute-start(bf16[128,128]{1,0:T(8,128)(2,1)S(1)} %get-tuple-element.40), channel_id=1, source_target_pairs={{1,0},{2,1},{3,2},{4,3},{5,4},{6,5},{7,6},{8,7},{9,8},{10,9},{11,1... | collective-permute-start | bytes 98312 | tf_op jit(solution)/shard_map/ppermute | solution.py:12
  72.9 9.7 %collective-permute-start.2 = (bf16[128,128]{1,0:T(8,128)(2,1)S(1)}, bf16[128,128]{1,0:T(8,128)(2,1)S(1)}, u32[]{:S(2)}, u32[]{:S(2)}) collective-permute-start(bf16[128,128]{1,0:T(8,128)(2,1)S(1)} %get-tuple-element.38), channel_id=1, source_target_pairs={{0,1},{1,2},{2,3},{3,4},{4,5},{5,6},{6,7},{7,8},{8,9},{9,10},{10,1... | collective-permute-start | bytes 98312 | tf_op jit(solution)/shard_map/ppermute | solution.py:12
  76.1 6.5 %collective-permute-start.1 = (bf16[128,128]{1,0:T(8,128)(2,1)S(1)}, bf16[128,128]{1,0:T(8,128)(2,1)S(1)}, u32[]{:S(2)}, u32[]{:S(2)}) collective-permute-start(bf16[128,128]{1,0:T(8,128)(2,1)S(1)} %get-tuple-element.39), channel_id=1, source_target_pairs={{16,0},{32,16},{48,32},{64,48},{80,64},{96,80},{112,96},{128,112},... | collective-permute-start | bytes 98312 | tf_op jit(solution)/shard_map/ppermute | solution.py:12
  77.4 5.2 %collective-permute-start = (bf16[128,128]{1,0:T(8,128)(2,1)S(1)}, bf16[128,128]{1,0:T(8,128)(2,1)S(1)}, u32[]{:S(2)}, u32[]{:S(2)}) collective-permute-start(bf16[128,128]{1,0:T(8,128)(2,1)S(1)} %get-tuple-element.37), channel_id=1, source_target_pairs={{0,16},{16,32},{32,48},{48,64},{64,80},{80,96},{96,112},{112,128},... | collective-permute-start | bytes 98312 | tf_op jit(solution)/shard_map/ppermute | solution.py:12
  82.6 2.6 copy-start.1
  82.6 2.6 copy-start.10
  101.3 16.4 %all-to-all-start.4 = ((f32[32,8,128]{2,1,0:T(8,128)}), f32[32,8,128]{2,1,0:T(8,128)S(1)}, u32[]{:S(2)}, u32[]{:S(2)}) async-start(f32[32,8,128]{2,1,0:T(8,128)} %fusion.58), calls=%async_computation.4 | async-start | bytes 262144 | tf_op jit(solution)/shard_map/all_to_all | solution.py:112
  119.3 22.2 %collective-permute-start.7 = (f32[2,128,128]{2,1,0:T(8,128)S(1)}, f32[2,128,128]{2,1,0:T(8,128)S(1)}, u32[]{:S(2)}, u32[]{:S(2)}) collective-permute-start(f32[2,128,128]{2,1,0:T(8,128)S(1)} %get-tuple-element.34), channel_id=1, source_target_pairs={{1,0},{2,1},{3,2},{4,3},{5,4},{6,5},{7,6},{8,7},{9,8},{10,9},{11,1... | collective-permute-start | bytes 393224 | tf_op jit(solution)/shard_map/ppermute | solution.py:12
  123.3 18.2 %collective-permute-start.6 = (f32[2,128,128]{2,1,0:T(8,128)S(1)}, f32[2,128,128]{2,1,0:T(8,128)S(1)}, u32[]{:S(2)}, u32[]{:S(2)}) collective-permute-start(f32[2,128,128]{2,1,0:T(8,128)S(1)} %get-tuple-element.35), channel_id=1, source_target_pairs={{0,1},{1,2},{2,3},{3,4},{4,5},{5,6},{6,7},{7,8},{8,9},{9,10},{10,1... | collective-permute-start | bytes 393224 | tf_op jit(solution)/shard_map/ppermute | solution.py:12
  125.3 16.1 %collective-permute-start.5 = (f32[2,128,128]{2,1,0:T(8,128)S(1)}, f32[2,128,128]{2,1,0:T(8,128)S(1)}, u32[]{:S(2)}, u32[]{:S(2)}) collective-permute-start(f32[2,128,128]{2,1,0:T(8,128)S(1)} %get-tuple-element.33), channel_id=1, source_target_pairs={{16,0},{32,16},{48,32},{64,48},{80,64},{96,80},{112,96},{128,112},... | collective-permute-start | bytes 393224 | tf_op jit(solution)/shard_map/ppermute | solution.py:12
  126.6 14.8 %collective-permute-start.4 = (f32[2,128,128]{2,1,0:T(8,128)S(1)}, f32[2,128,128]{2,1,0:T(8,128)S(1)}, u32[]{:S(2)}, u32[]{:S(2)}) collective-permute-start(f32[2,128,128]{2,1,0:T(8,128)S(1)} %get-tuple-element.32), channel_id=1, source_target_pairs={{0,16},{16,32},{32,48},{48,64},{64,80},{80,96},{96,112},{112,128},... | collective-permute-start | bytes 393224 | tf_op jit(solution)/shard_map/ppermute | solution.py:12
  143.4 13.6 %all-to-all-start.6 = ((f32[32,2,128]{2,1,0:T(2,128)}), f32[32,2,128]{2,1,0:T(2,128)S(1)}, u32[]{:S(2)}, u32[]{:S(2)}) async-start(f32[32,2,128]{2,1,0:T(2,128)} %broadcast_in_dim.45), calls=%async_computation.6 | async-start | bytes 65536 | tf_op jit(solution)/shard_map/all_to_all | solution.py:18
  157.1 1.4 copy-start.13
  158.5 2.1 copy-start.11
  174.2 13.0 %all-to-all-start.8 = ((f32[32,8,128]{2,1,0:T(8,128)}), f32[32,8,128]{2,1,0:T(8,128)S(1)}, u32[]{:S(2)}, u32[]{:S(2)}) async-start(f32[32,8,128]{2,1,0:T(8,128)} %fusion.56), calls=%async_computation.8 | async-start | bytes 262144 | tf_op jit(solution)/shard_map/all_to_all | solution.py:112
  188.9 22.3 %collective-permute-start.11 = (f32[2,128,128]{2,1,0:T(8,128)S(1)}, f32[2,128,128]{2,1,0:T(8,128)S(1)}, u32[]{:S(2)}, u32[]{:S(2)}) collective-permute-start(f32[2,128,128]{2,1,0:T(8,128)S(1)} %get-tuple-element.28), channel_id=1, source_target_pairs={{1,0},{2,1},{3,2},{4,3},{5,4},{6,5},{7,6},{8,7},{9,8},{10,9},{11,1... | collective-permute-start | bytes 393224 | tf_op jit(solution)/shard_map/ppermute | solution.py:12
  192.8 18.3 %collective-permute-start.10 = (f32[2,128,128]{2,1,0:T(8,128)S(1)}, f32[2,128,128]{2,1,0:T(8,128)S(1)}, u32[]{:S(2)}, u32[]{:S(2)}) collective-permute-start(f32[2,128,128]{2,1,0:T(8,128)S(1)} %get-tuple-element.29), channel_id=1, source_target_pairs={{0,1},{1,2},{2,3},{3,4},{4,5},{5,6},{6,7},{7,8},{8,9},{9,10},{10,1... | collective-permute-start | bytes 393224 | tf_op jit(solution)/shard_map/ppermute | solution.py:12
  195.1 16.1 %collective-permute-start.9 = (f32[2,128,128]{2,1,0:T(8,128)S(1)}, f32[2,128,128]{2,1,0:T(8,128)S(1)}, u32[]{:S(2)}, u32[]{:S(2)}) collective-permute-start(f32[2,128,128]{2,1,0:T(8,128)S(1)} %get-tuple-element.27), channel_id=1, source_target_pairs={{16,0},{32,16},{48,32},{64,48},{80,64},{96,80},{112,96},{128,112},... | collective-permute-start | bytes 393224 | tf_op jit(solution)/shard_map/ppermute | solution.py:12
  196.4 14.8 %collective-permute-start.8 = (f32[2,128,128]{2,1,0:T(8,128)S(1)}, f32[2,128,128]{2,1,0:T(8,128)S(1)}, u32[]{:S(2)}, u32[]{:S(2)}) collective-permute-start(f32[2,128,128]{2,1,0:T(8,128)S(1)} %get-tuple-element.26), channel_id=1, source_target_pairs={{0,16},{16,32},{32,48},{48,64},{64,80},{80,96},{96,112},{112,128},... | collective-permute-start | bytes 393224 | tf_op jit(solution)/shard_map/ppermute | solution.py:12
  213.1 13.9 %all-to-all-start.10 = ((f32[32,2,128]{2,1,0:T(2,128)}), f32[32,2,128]{2,1,0:T(2,128)S(1)}, u32[]{:S(2)}, u32[]{:S(2)}) async-start(f32[32,2,128]{2,1,0:T(2,128)} %broadcast_in_dim.48), calls=%async_computation.10 | async-start | bytes 65536 | tf_op jit(solution)/shard_map/all_to_all | solution.py:18
  227.1 1.4 copy-start.14
  228.5 2.1 copy-start.12
  244.3 17.5 %all-to-all-start.12 = ((f32[32,8,128]{2,1,0:T(8,128)}), f32[32,8,128]{2,1,0:T(8,128)S(1)}, u32[]{:S(2)}, u32[]{:S(2)}) async-start(f32[32,8,128]{2,1,0:T(8,128)} %fusion.54), calls=%async_computation.12 | async-start | bytes 262144 | tf_op jit(solution)/shard_map/all_to_all | solution.py:112
  250.9 15.5 %collective-permute-start.15 = (f32[2,128,128]{2,1,0:T(8,128)}, f32[2,128,128]{2,1,0:T(8,128)S(1)}, u32[]{:S(2)}, u32[]{:S(2)}) collective-permute-start(f32[2,128,128]{2,1,0:T(8,128)} %get-tuple-element.22), channel_id=1, source_target_pairs={{1,0},{2,1},{3,2},{4,3},{5,4},{6,5},{7,6},{8,7},{9,8},{10,9},{11,1... | collective-permute-start | bytes 393224 | tf_op jit(solution)/shard_map/ppermute | solution.py:12
  253.0 13.5 %collective-permute-start.14 = (f32[2,128,128]{2,1,0:T(8,128)S(1)}, f32[2,128,128]{2,1,0:T(8,128)S(1)}, u32[]{:S(2)}, u32[]{:S(2)}) collective-permute-start(f32[2,128,128]{2,1,0:T(8,128)S(1)} %get-tuple-element.23), channel_id=1, source_target_pairs={{0,1},{1,2},{2,3},{3,4},{4,5},{5,6},{6,7},{7,8},{8,9},{9,10},{10,1... | collective-permute-start | bytes 393224 | tf_op jit(solution)/shard_map/ppermute | solution.py:12
  256.5 10.0 %collective-permute-start.13 = (f32[2,128,128]{2,1,0:T(8,128)S(1)}, f32[2,128,128]{2,1,0:T(8,128)S(1)}, u32[]{:S(2)}, u32[]{:S(2)}) collective-permute-start(f32[2,128,128]{2,1,0:T(8,128)S(1)} %get-tuple-element.21), channel_id=1, source_target_pairs={{16,0},{32,16},{48,32},{64,48},{80,64},{96,80},{112,96},{128,112},... | collective-permute-start | bytes 393224 | tf_op jit(solution)/shard_map/ppermute | solution.py:12
  257.8 8.7 %collective-permute-start.12 = (f32[2,128,128]{2,1,0:T(8,128)S(1)}, f32[2,128,128]{2,1,0:T(8,128)S(1)}, u32[]{:S(2)}, u32[]{:S(2)}) collective-permute-start(f32[2,128,128]{2,1,0:T(8,128)S(1)} %get-tuple-element.20), channel_id=1, source_target_pairs={{0,16},{16,32},{32,48},{48,64},{64,80},{80,96},{96,112},{112,128},... | collective-permute-start | bytes 393224 | tf_op jit(solution)/shard_map/ppermute | solution.py:12
  262.9 10.9 %all-to-all-start.13 = ((f32[16,2,128]{2,1,0:T(2,128)}), f32[16,2,128]{2,1,0:T(2,128)S(1)}, u32[]{:S(2)}, u32[]{:S(2)}) async-start(f32[16,2,128]{2,1,0:T(2,128)} %broadcast_in_dim.50), calls=%async_computation.13 | async-start | bytes 32768 | tf_op jit(solution)/shard_map/all_to_all | solution.py:18
  266.5 26.8 %copy-start.2 = (bf16[896,512]{1,0:T(8,128)(2,1)S(1)}, bf16[896,512]{1,0:T(8,128)(2,1)}, u32[]{:S(2)}) copy-start(bf16[896,512]{1,0:T(8,128)(2,1)} %copy-done.1) | copy-start | bytes 2752516
  274.4 18.0 %all-to-all-start.14 = ((f32[32,2,128]{2,1,0:T(2,128)}), f32[32,2,128]{2,1,0:T(2,128)S(1)}, u32[]{:S(2)}, u32[]{:S(2)}) async-start(f32[32,2,128]{2,1,0:T(2,128)} %broadcast_in_dim.51), calls=%async_computation.14 | async-start | bytes 65536 | tf_op jit(solution)/shard_map/all_to_all | solution.py:18
  292.5 1.6 copy-start.15

commit v12 on v11

--- a/solution.py
+++ b/solution.py
@@ -108,10 +108,10 @@
         coarse = both[: vectors.shape[0]]
         result = trace_scale * rounded.astype(jnp.float32) + both[vectors.shape[0] :]
         line = gather_rows(coarse, "gy")
-        partial = jnp.dot(coarse_block, line, precision=lax.Precision.HIGHEST)
+        partial = jnp.dot(coarse_block, line, precision=lax.Precision.HIGH)
         pieces = lax.all_to_all(partial, "gx", 0, 0, tiled=True)
         solved = jnp.sum(pieces.reshape(count_x, depth, pieces.shape[-1]), axis=0)
-        return result + jnp.dot(vectors_wide, solved, precision=lax.Precision.HIGHEST)
+        return result + jnp.dot(vectors_wide, solved, precision=lax.Precision.HIGH)
 
     solution = jnp.zeros(rhs_wide.shape, jnp.float32)
     direction = apply_prec(rhs_wide)

time: 297 us -> 297 us (level)
  no operation moved by 1% of the time
where the time goes in v12:
time: 297 us; the launch traced here: 295 us
  starting transfers between devices  110 us (37%)
  waiting for transfers between devices  66.6 us (22%)
  blocking collectives  59.9 us (20%)
  local copies, waits for them, and re-layouts  31.5 us (11%)
  matrix products  18.1 us (6%)
  other arithmetic  4.99 us (2%)
  between operations  3.48 us (1%)
    all_to_all x5, blocking collectives, gather_rows(): lax.all_to_all(copies.reshape((-1,) + value.shape[1:]), axis, 0, 0, tiled...  59.9 us
    ppermute x16, starting transfers between devices, from_behind(): lax.ppermute(value, axis, [(source, source + steps) for source in range(l...  46.6 us
    all_to_all x5, starting transfers between devices, gather_rows(): lax.all_to_all(copies.reshape((-1,) + value.shape[1:]), axis, 0, 0, tiled...  34.5 us
    all_to_all x5, waiting for transfers between devices, gather_rows(): lax.all_to_all(copies.reshape((-1,) + value.shape[1:]), axis, 0, 0, tiled...  32.1 us
    all_to_all x4, waiting for transfers between devices, apply_prec(): pieces = lax.all_to_all(partial, 'gx', 0, 0, tiled=True)  25.3 us
    all_to_all x4, starting transfers between devices, apply_prec(): pieces = lax.all_to_all(partial, 'gx', 0, 0, tiled=True)  19.5 us
    gather x2, local copies, waits for them, and re-layouts, shards(): coarse_cols = jnp.take(coarse_inverse, coarse_map, axis=1)  16.3 us
    all_to_all x1, starting transfers between devices, shards(): lax.all_to_all(coarse_cols.reshape(depth, count_x, count_y * depth), 'gx'...  9.69 us
  transfers between devices with their start and end apart: 26, of which 8 were waited for; matrix products, arithmetic and copies ran while one was open for 9% of the time, Pallas kernels for 0%

profile of v12, /device:TPU:1, one launch (start us, length us, event | category | flops | bytes accessed | tf_op | source)
XLA Modules:
  0.0 295.0 jit_solution(1990099982153562167)
XLA Ops:
  0.7 2.1 fusion.81
  3.4 11.8 %all-to-all-start.1 = ((f32[16,8,128]{2,1,0:T(8,128)}), f32[16,8,128]{2,1,0:T(8,128)S(1)}, u32[]{:S(2)}, u32[]{:S(2)}) async-start(f32[16,8,128]{2,1,0:T(8,128)} %broadcast_in_dim.42), calls=%async_computation.1 | async-start | bytes 131072 | tf_op jit(solution)/shard_map/all_to_all | solution.py:18
  16.0 14.1 %gather_fusion = f32[4096,8]{1,0:T(8,128)} fusion(f32[8,4096]{0,1:T(8,128)S(1)} %copy.80, s32[4096]{0:T(1024)S(1)} %fusion.67), kind=kCustom, calls=%fused_computation | custom fusion | bytes 278528 | tf_op jit(solution)/shard_map/jit(_take)/gather | solution.py:72
  30.1 2.2 copy.81
  32.2 0.7 broadcast_select_fusion
  32.9 9.7 %all-to-all-start = ((f32[8,32,128]{2,0,1:T(8,128)}), f32[8,32,128]{2,0,1:T(8,128)S(1)}, u32[]{:S(2)}, u32[]{:S(2)}) async-start(f32[8,32,128]{2,0,1:T(8,128)} %broadcast_select_fusion), calls=%async_computation | async-start | bytes 262144 | tf_op jit(solution)/shard_map/all_to_all | solution.py:73
  42.7 9.1 %all-to-all-done = f32[8,32,128]{2,0,1:T(8,128)S(1)} async-done(((f32[8,32,128]{2,0,1:T(8,128)}), f32[8,32,128]{2,0,1:T(8,128)S(1)}, u32[]{:S(2)}, u32[]{:S(2)}) %all-to-all-start) | async-done | bytes 131104 | tf_op jit(solution)/shard_map/all_to_all | solution.py:73
  51.8 0.9 fusion.60
  52.7 4.5 %all-to-all-start.2 = ((f32[32,8,128]{2,1,0:T(8,128)}), f32[32,8,128]{2,1,0:T(8,128)S(1)}, u32[]{:S(2)}, u32[]{:S(2)}) async-start(f32[32,8,128]{2,1,0:T(8,128)} %fusion.60), calls=%async_computation.2 | async-start | bytes 262144 | tf_op jit(solution)/shard_map/all_to_all | solution.py:112
  57.2 9.1 %all-to-all-done.2 = f32[32,8,128]{2,1,0:T(8,128)S(1)} async-done(((f32[32,8,128]{2,1,0:T(8,128)}), f32[32,8,128]{2,1,0:T(8,128)S(1)}, u32[]{:S(2)}, u32[]{:S(2)}) %all-to-all-start.2) | async-done | bytes 131104 | tf_op jit(solution)/shard_map/all_to_all | solution.py:112
  66.8 1.3 gather_fusion.1
  68.1 4.6 %collective-permute-start.3 = (bf16[128,128]{1,0:T(8,128)(2,1)S(1)}, bf16[128,128]{1,0:T(8,128)(2,1)S(1)}, u32[]{:S(2)}, u32[]{:S(2)}) collective-permute-start(bf16[128,128]{1,0:T(8,128)(2,1)S(1)} %get-tuple-element.40), channel_id=1, source_target_pairs={{1,0},{2,1},{3,2},{4,3},{5,4},{6,5},{7,6},{8,7},{9,8},{10,9},{11,1... | collective-permute-start | bytes 98312 | tf_op jit(solution)/shard_map/ppermute | solution.py:12
  72.8 3.2 %collective-permute-start.2 = (bf16[128,128]{1,0:T(8,128)(2,1)S(1)}, bf16[128,128]{1,0:T(8,128)(2,1)S(1)}, u32[]{:S(2)}, u32[]{:S(2)}) collective-permute-start(bf16[128,128]{1,0:T(8,128)(2,1)S(1)} %get-tuple-element.38), channel_id=1, source_target_pairs={{0,1},{1,2},{2,3},{3,4},{4,5},{5,6},{6,7},{7,8},{8,9},{9,10},{10,1... | collective-permute-start | bytes 98312 | tf_op jit(solution)/shard_map/ppermute | solution.py:12
  76.0 1.3 collective-permute-start.1
  77.3 4.0 %collective-permute-start = (bf16[128,128]{1,0:T(8,128)(2,1)S(1)}, bf16[128,128]{1,0:T(8,128)(2,1)S(1)}, u32[]{:S(2)}, u32[]{:S(2)}) collective-permute-start(bf16[128,128]{1,0:T(8,128)(2,1)S(1)} %get-tuple-element.37), channel_id=1, source_target_pairs={{0,16},{16,32},{32,48},{48,64},{64,80},{80,96},{96,112},{112,128},... | collective-permute-start | bytes 98312 | tf_op jit(solution)/shard_map/ppermute | solution.py:12
  82.6 2.5 fusion.9
  85.1 0.6 fusion.80
  85.8 14.4 %all_to_all.111 = f32[16,8,128]{2,1,0:T(8,128)S(1)} all-to-all(f32[16,8,128]{2,1,0:T(8,128)S(1)} %broadcast_in_dim.43), channel_id=1, replica_groups=mesh['gx'=32,'gy'=16] {'gy'}, dimensions={0} | all-to-all | bytes 131072 | tf_op jit(solution)/shard_map/all_to_all | solution.py:18
  100.2 0.9 fusion.58
  101.1 7.3 %all-to-all-start.4 = ((f32[32,8,128]{2,1,0:T(8,128)}), f32[32,8,128]{2,1,0:T(8,128)S(1)}, u32[]{:S(2)}, u32[]{:S(2)}) async-start(f32[32,8,128]{2,1,0:T(8,128)} %fusion.58), calls=%async_computation.4 | async-start | bytes 262144 | tf_op jit(solution)/shard_map/all_to_all | solution.py:112
  108.4 1.0 gather_fusion.2
  109.4 8.1 %all-to-all-done.4 = f32[32,8,128]{2,1,0:T(8,128)S(1)} async-done(((f32[32,8,128]{2,1,0:T(8,128)}), f32[32,8,128]{2,1,0:T(8,128)S(1)}, u32[]{:S(2)}, u32[]{:S(2)}) %all-to-all-start.4) | async-done | bytes 131104 | tf_op jit(solution)/shard_map/all_to_all | solution.py:112
  118.0 1.0 gather_fusion.3
  119.1 4.0 %collective-permute-start.7 = (f32[2,128,128]{2,1,0:T(8,128)S(1)}, f32[2,128,128]{2,1,0:T(8,128)S(1)}, u32[]{:S(2)}, u32[]{:S(2)}) collective-permute-start(f32[2,128,128]{2,1,0:T(8,128)S(1)} %get-tuple-element.34), channel_id=1, source_target_pairs={{1,0},{2,1},{3,2},{4,3},{5,4},{6,5},{7,6},{8,7},{9,8},{10,9},{11,1... | collective-permute-start | bytes 393224 | tf_op jit(solution)/shard_map/ppermute | solution.py:12
  123.1 2.0 collective-permute-start.6
  125.1 1.3 collective-permute-start.5
  126.4 4.0 %collective-permute-start.4 = (f32[2,128,128]{2,1,0:T(8,128)S(1)}, f32[2,128,128]{2,1,0:T(8,128)S(1)}, u32[]{:S(2)}, u32[]{:S(2)}) collective-permute-start(f32[2,128,128]{2,1,0:T(8,128)S(1)} %get-tuple-element.32), channel_id=1, source_target_pairs={{0,16},{16,32},{32,48},{48,64},{64,80},{80,96},{96,112},{112,128},... | collective-permute-start | bytes 393224 | tf_op jit(solution)/shard_map/ppermute | solution.py:12
  130.4 10.8 %all_to_all.112 = f32[16,2,128]{2,1,0:T(2,128)S(1)} all-to-all(f32[16,2,128]{2,1,0:T(2,128)S(1)} %broadcast_in_dim.44), channel_id=1, replica_groups=mesh['gx'=32,'gy'=16] {'gy'}, dimensions={0} | all-to-all | bytes 32768 | tf_op jit(solution)/shard_map/all_to_all | solution.py:18
  143.2 4.8 %all-to-all-start.6 = ((f32[32,2,128]{2,1,0:T(2,128)}), f32[32,2,128]{2,1,0:T(2,128)S(1)}, u32[]{:S(2)}, u32[]{:S(2)}) async-start(f32[32,2,128]{2,1,0:T(2,128)} %broadcast_in_dim.45), calls=%async_computation.6 | async-start | bytes 65536 | tf_op jit(solution)/shard_map/all_to_all | solution.py:18
  148.1 8.7 %all-to-all-done.6 = f32[32,2,128]{2,1,0:T(2,128)S(1)} async-done(((f32[32,2,128]{2,1,0:T(2,128)}), f32[32,2,128]{2,1,0:T(2,128)S(1)}, u32[]{:S(2)}, u32[]{:S(2)}) %all-to-all-start.6) | async-done | bytes 32800 | tf_op jit(solution)/shard_map/all_to_all | solution.py:18
  157.0 1.3 copy-done.13
  158.3 2.1 fusion.10
  161.1 12.0 %all_to_all.113 = f32[16,8,128]{2,1,0:T(8,128)S(1)} all-to-all(f32[16,8,128]{2,1,0:T(8,128)S(1)} %broadcast_in_dim.46), channel_id=1, replica_groups=mesh['gx'=32,'gy'=16] {'gy'}, dimensions={0} | all-to-all | bytes 131072 | tf_op jit(solution)/shard_map/all_to_all | solution.py:18
  173.1 0.9 fusion.56
  174.0 3.9 %all-to-all-start.8 = ((f32[32,8,128]{2,1,0:T(8,128)}), f32[32,8,128]{2,1,0:T(8,128)S(1)}, u32[]{:S(2)}, u32[]{:S(2)}) async-start(f32[32,8,128]{2,1,0:T(8,128)} %fusion.56), calls=%async_computation.8 | async-start | bytes 262144 | tf_op jit(solution)/shard_map/all_to_all | solution.py:112
  177.8 1.0 gather_fusion.4
  178.9 8.1 %all-to-all-done.8 = f32[32,8,128]{2,1,0:T(8,128)S(1)} async-done(((f32[32,8,128]{2,1,0:T(8,128)}), f32[32,8,128]{2,1,0:T(8,128)S(1)}, u32[]{:S(2)}, u32[]{:S(2)}) %all-to-all-start.8) | async-done | bytes 131104 | tf_op jit(solution)/shard_map/all_to_all | solution.py:112
  187.4 1.0 gather_fusion.5
  188.5 4.0 %collective-permute-start.11 = (f32[2,128,128]{2,1,0:T(8,128)S(1)}, f32[2,128,128]{2,1,0:T(8,128)S(1)}, u32[]{:S(2)}, u32[]{:S(2)}) collective-permute-start(f32[2,128,128]{2,1,0:T(8,128)S(1)} %get-tuple-element.28), channel_id=1, source_target_pairs={{1,0},{2,1},{3,2},{4,3},{5,4},{6,5},{7,6},{8,7},{9,8},{10,9},{11,1... | collective-permute-start | bytes 393224 | tf_op jit(solution)/shard_map/ppermute | solution.py:12
  192.5 2.1 collective-permute-start.10
  194.5 1.3 collective-permute-start.9
  195.8 4.0 %collective-permute-start.8 = (f32[2,128,128]{2,1,0:T(8,128)S(1)}, f32[2,128,128]{2,1,0:T(8,128)S(1)}, u32[]{:S(2)}, u32[]{:S(2)}) collective-permute-start(f32[2,128,128]{2,1,0:T(8,128)S(1)} %get-tuple-element.26), channel_id=1, source_target_pairs={{0,16},{16,32},{32,48},{48,64},{64,80},{80,96},{96,112},{112,128},... | collective-permute-start | bytes 393224 | tf_op jit(solution)/shard_map/ppermute | solution.py:12
  199.9 10.7 %all_to_all.114 = f32[16,2,128]{2,1,0:T(2,128)S(1)} all-to-all(f32[16,2,128]{2,1,0:T(2,128)S(1)} %broadcast_in_dim.47), channel_id=1, replica_groups=mesh['gx'=32,'gy'=16] {'gy'}, dimensions={0} | all-to-all | bytes 32768 | tf_op jit(solution)/shard_map/all_to_all | solution.py:18
  212.6 5.1 %all-to-all-start.10 = ((f32[32,2,128]{2,1,0:T(2,128)}), f32[32,2,128]{2,1,0:T(2,128)S(1)}, u32[]{:S(2)}, u32[]{:S(2)}) async-start(f32[32,2,128]{2,1,0:T(2,128)} %broadcast_in_dim.48), calls=%async_computation.10 | async-start | bytes 65536 | tf_op jit(solution)/shard_map/all_to_all | solution.py:18
  217.8 8.7 %all-to-all-done.10 = f32[32,2,128]{2,1,0:T(2,128)S(1)} async-done(((f32[32,2,128]{2,1,0:T(2,128)}), f32[32,2,128]{2,1,0:T(2,128)S(1)}, u32[]{:S(2)}, u32[]{:S(2)}) %all-to-all-start.10) | async-done | bytes 32800 | tf_op jit(solution)/shard_map/all_to_all | solution.py:18
  226.7 1.2 copy-done.14
  228.0 2.1 fusion.11
  230.8 12.0 %all_to_all.115 = f32[16,8,128]{2,1,0:T(8,128)S(1)} all-to-all(f32[16,8,128]{2,1,0:T(8,128)S(1)} %broadcast_in_dim.49), channel_id=1, replica_groups=mesh['gx'=32,'gy'=16] {'gy'}, dimensions={0} | all-to-all | bytes 131072 | tf_op jit(solution)/shard_map/all_to_all | solution.py:18
  242.8 0.9 fusion.54
  243.7 3.9 %all-to-all-start.12 = ((f32[32,8,128]{2,1,0:T(8,128)}), f32[32,8,128]{2,1,0:T(8,128)S(1)}, u32[]{:S(2)}, u32[]{:S(2)}) async-start(f32[32,8,128]{2,1,0:T(8,128)} %fusion.54), calls=%async_computation.12 | async-start | bytes 262144 | tf_op jit(solution)/shard_map/all_to_all | solution.py:112
  247.5 1.0 gather_fusion.6
  248.6 1.0 gather_fusion.7
  249.6 0.7 fusion.36
  250.3 2.0 collective-permute-start.15
  252.4 3.5 %collective-permute-start.14 = (f32[2,128,128]{2,1,0:T(8,128)S(1)}, f32[2,128,128]{2,1,0:T(8,128)S(1)}, u32[]{:S(2)}, u32[]{:S(2)}) collective-permute-start(f32[2,128,128]{2,1,0:T(8,128)S(1)} %get-tuple-element.23), channel_id=1, source_target_pairs={{0,1},{1,2},{2,3},{3,4},{4,5},{5,6},{6,7},{7,8},{8,9},{9,10},{10,1... | collective-permute-start | bytes 393224 | tf_op jit(solution)/shard_map/ppermute | solution.py:12
  255.9 1.3 collective-permute-start.13
  257.2 4.0 %collective-permute-start.12 = (f32[2,128,128]{2,1,0:T(8,128)S(1)}, f32[2,128,128]{2,1,0:T(8,128)S(1)}, u32[]{:S(2)}, u32[]{:S(2)}) collective-permute-start(f32[2,128,128]{2,1,0:T(8,128)S(1)} %get-tuple-element.20), channel_id=1, source_target_pairs={{0,16},{16,32},{32,48},{48,64},{64,80},{80,96},{96,112},{112,128},... | collective-permute-start | bytes 393224 | tf_op jit(solution)/shard_map/ppermute | solution.py:12
  262.3 3.5 %all-to-all-start.13 = ((f32[16,2,128]{2,1,0:T(2,128)}), f32[16,2,128]{2,1,0:T(2,128)S(1)}, u32[]{:S(2)}, u32[]{:S(2)}) async-start(f32[16,2,128]{2,1,0:T(2,128)} %broadcast_in_dim.50), calls=%async_computation.13 | async-start | bytes 32768 | tf_op jit(solution)/shard_map/all_to_all | solution.py:18
  267.1 6.0 %all-to-all-done.13 = f32[16,2,128]{2,1,0:T(2,128)S(1)} async-done(((f32[16,2,128]{2,1,0:T(2,128)}), f32[16,2,128]{2,1,0:T(2,128)S(1)}, u32[]{:S(2)}, u32[]{:S(2)}) %all-to-all-start.13) | async-done | bytes 16416 | tf_op jit(solution)/shard_map/all_to_all | solution.py:18
  273.8 9.2 %all-to-all-start.14 = ((f32[32,2,128]{2,1,0:T(2,128)}), f32[32,2,128]{2,1,0:T(2,128)S(1)}, u32[]{:S(2)}, u32[]{:S(2)}) async-start(f32[32,2,128]{2,1,0:T(2,128)} %broadcast_in_dim.51), calls=%async_computation.14 | async-start | bytes 65536 | tf_op jit(solution)/shard_map/all_to_all | solution.py:18
  283.1 8.7 %all-to-all-done.14 = f32[32,2,128]{2,1,0:T(2,128)S(1)} async-done(((f32[32,2,128]{2,1,0:T(2,128)}), f32[32,2,128]{2,1,0:T(2,128)S(1)}, u32[]{:S(2)}, u32[]{:S(2)}) %all-to-all-start.14) | async-done | bytes 32800 | tf_op jit(solution)/shard_map/all_to_all | solution.py:18
  291.8 0.8 fusion.31
  292.7 0.7 copy-done.15
  293.4 1.6 fusion.4
  (113 shorter events, 10.9 us)
Async XLA Ops:
  0.6 80.7 %copy-start = (bf16[1,1,4,128,128]{4,3,2,1,0:T(8,128)(2,1)S(1)}, bf16[1,1,4,128,128]{4,3,2,1,0:T(8,128)(2,1)}, u32[]{:S(2)}) copy-start(bf16[1,1,4,128,128]{4,3,2,1,0:T(8,128)(2,1)} %param.15) | copy-start | bytes 393220
  0.6 14.6 %copy-start.6 = (s32[4096]{0:T(1024)S(1)}, s32[4096]{0:T(1024)}, u32[]{:S(2)}) copy-start(s32[4096]{0:T(1024)} %param.19) | copy-start | bytes 49156
  0.7 14.7 %copy-start.5 = (f32[8,4096]{1,0:T(8,128)S(1)}, f32[8,4096]{1,0:T(8,128)}, u32[]{:S(2)}) copy-start(f32[8,4096]{1,0:T(8,128)} %param.18) | copy-start | bytes 393220
  3.4 29.5 %all-to-all-start.1 = ((f32[16,8,128]{2,1,0:T(8,128)}), f32[16,8,128]{2,1,0:T(8,128)S(1)}, u32[]{:S(2)}, u32[]{:S(2)}) async-start(f32[16,8,128]{2,1,0:T(8,128)} %broadcast_in_dim.42), calls=%async_computation.1 | async-start | bytes 131072 | tf_op jit(solution)/shard_map/all_to_all | solution.py:18
  15.9 26.7 %copy-start.7 = (f32[1,1,896]{2,1,0:T(1,128)S(1)}, f32[1,1,896]{2,1,0:T(1,128)}, u32[]{:S(2)}) copy-start(f32[1,1,896]{2,1,0:T(1,128)} %param.14) | copy-start | bytes 10756
  15.9 41.2 %copy-start.9 = (s32[1,1,4,128]{3,2,1,0:T(4,128)S(1)}, s32[1,1,4,128]{3,2,1,0:T(4,128)}, u32[]{:S(2)}) copy-start(s32[1,1,4,128]{3,2,1,0:T(4,128)} %param.16) | copy-start | bytes 6148
  16.0 50.4 %copy-start.3 = (bf16[1,1,8,896]{3,2,1,0:T(8,128)(2,1)S(1)}, bf16[1,1,8,896]{3,2,1,0:T(8,128)(2,1)}, u32[]{:S(2)}) copy-start(bf16[1,1,8,896]{3,2,1,0:T(8,128)(2,1)} %param.17) | copy-start | bytes 43012
  16.0 50.4 %copy-start.4 = (bf16[1,1,896,128]{3,2,1,0:T(8,128)(2,1)S(1)}, bf16[1,1,896,128]{3,2,1,0:T(8,128)(2,1)}, u32[]{:S(2)}) copy-start(bf16[1,1,896,128]{3,2,1,0:T(8,128)(2,1)} %param.10) | copy-start | bytes 688132
  32.9 18.9 %all-to-all-start = ((f32[8,32,128]{2,0,1:T(8,128)}), f32[8,32,128]{2,0,1:T(8,128)S(1)}, u32[]{:S(2)}, u32[]{:S(2)}) async-start(f32[8,32,128]{2,0,1:T(8,128)} %broadcast_select_fusion), calls=%async_computation | async-start | bytes 262144 | tf_op jit(solution)/shard_map/all_to_all | solution.py:73
  52.7 13.7 %all-to-all-start.2 = ((f32[32,8,128]{2,1,0:T(8,128)}), f32[32,8,128]{2,1,0:T(8,128)S(1)}, u32[]{:S(2)}, u32[]{:S(2)}) async-start(f32[32,8,128]{2,1,0:T(8,128)} %fusion.60), calls=%async_computation.2 | async-start | bytes 262144 | tf_op jit(solution)/shard_map/all_to_all | solution.py:112
  66.4 15.5 %copy-start.8 = (f32[1,1,896]{2,1,0:T(1,128)S(1)}, f32[1,1,896]{2,1,0:T(1,128)}, u32[]{:S(2)}) copy-start(f32[1,1,896]{2,1,0:T(1,128)} %param.12) | copy-start | bytes 10756
  68.1 14.3 %collective-permute-start.3 = (bf16[128,128]{1,0:T(8,128)(2,1)S(1)}, bf16[128,128]{1,0:T(8,128)(2,1)S(1)}, u32[]{:S(2)}, u32[]{:S(2)}) collective-permute-start(bf16[128,128]{1,0:T(8,128)(2,1)S(1)} %get-tuple-element.40), channel_id=1, source_target_pairs={{1,0},{2,1},{3,2},{4,3},{5,4},{6,5},{7,6},{8,7},{9,8},{10,9},{11,1... | collective-permute-start | bytes 98312 | tf_op jit(solution)/shard_map/ppermute | solution.py:12
  72.8 9.7 %collective-permute-start.2 = (bf16[128,128]{1,0:T(8,128)(2,1)S(1)}, bf16[128,128]{1,0:T(8,128)(2,1)S(1)}, u32[]{:S(2)}, u32[]{:S(2)}) collective-permute-start(bf16[128,128]{1,0:T(8,128)(2,1)S(1)} %get-tuple-element.38), channel_id=1, source_target_pairs={{0,1},{1,2},{2,3},{3,4},{4,5},{5,6},{6,7},{7,8},{8,9},{9,10},{10,1... | collective-permute-start | bytes 98312 | tf_op jit(solution)/shard_map/ppermute | solution.py:12
  76.0 6.5 %collective-permute-start.1 = (bf16[128,128]{1,0:T(8,128)(2,1)S(1)}, bf16[128,128]{1,0:T(8,128)(2,1)S(1)}, u32[]{:S(2)}, u32[]{:S(2)}) collective-permute-start(bf16[128,128]{1,0:T(8,128)(2,1)S(1)} %get-tuple-element.39), channel_id=1, source_target_pairs={{16,0},{32,16},{48,32},{64,48},{80,64},{96,80},{112,96},{128,112},... | collective-permute-start | bytes 98312 | tf_op jit(solution)/shard_map/ppermute | solution.py:12
  77.3 5.2 %collective-permute-start = (bf16[128,128]{1,0:T(8,128)(2,1)S(1)}, bf16[128,128]{1,0:T(8,128)(2,1)S(1)}, u32[]{:S(2)}, u32[]{:S(2)}) collective-permute-start(bf16[128,128]{1,0:T(8,128)(2,1)S(1)} %get-tuple-element.37), channel_id=1, source_target_pairs={{0,16},{16,32},{32,48},{48,64},{64,80},{80,96},{96,112},{112,128},... | collective-permute-start | bytes 98312 | tf_op jit(solution)/shard_map/ppermute | solution.py:12
  82.5 2.6 copy-start.1
  82.5 2.6 copy-start.10
  101.1 16.5 %all-to-all-start.4 = ((f32[32,8,128]{2,1,0:T(8,128)}), f32[32,8,128]{2,1,0:T(8,128)S(1)}, u32[]{:S(2)}, u32[]{:S(2)}) async-start(f32[32,8,128]{2,1,0:T(8,128)} %fusion.58), calls=%async_computation.4 | async-start | bytes 262144 | tf_op jit(solution)/shard_map/all_to_all | solution.py:112
  119.1 22.2 %collective-permute-start.7 = (f32[2,128,128]{2,1,0:T(8,128)S(1)}, f32[2,128,128]{2,1,0:T(8,128)S(1)}, u32[]{:S(2)}, u32[]{:S(2)}) collective-permute-start(f32[2,128,128]{2,1,0:T(8,128)S(1)} %get-tuple-element.34), channel_id=1, source_target_pairs={{1,0},{2,1},{3,2},{4,3},{5,4},{6,5},{7,6},{8,7},{9,8},{10,9},{11,1... | collective-permute-start | bytes 393224 | tf_op jit(solution)/shard_map/ppermute | solution.py:12
  123.1 18.2 %collective-permute-start.6 = (f32[2,128,128]{2,1,0:T(8,128)S(1)}, f32[2,128,128]{2,1,0:T(8,128)S(1)}, u32[]{:S(2)}, u32[]{:S(2)}) collective-permute-start(f32[2,128,128]{2,1,0:T(8,128)S(1)} %get-tuple-element.35), channel_id=1, source_target_pairs={{0,1},{1,2},{2,3},{3,4},{4,5},{5,6},{6,7},{7,8},{8,9},{9,10},{10,1... | collective-permute-start | bytes 393224 | tf_op jit(solution)/shard_map/ppermute | solution.py:12
  125.1 16.1 %collective-permute-start.5 = (f32[2,128,128]{2,1,0:T(8,128)S(1)}, f32[2,128,128]{2,1,0:T(8,128)S(1)}, u32[]{:S(2)}, u32[]{:S(2)}) collective-permute-start(f32[2,128,128]{2,1,0:T(8,128)S(1)} %get-tuple-element.33), channel_id=1, source_target_pairs={{16,0},{32,16},{48,32},{64,48},{80,64},{96,80},{112,96},{128,112},... | collective-permute-start | bytes 393224 | tf_op jit(solution)/shard_map/ppermute | solution.py:12
  126.4 14.8 %collective-permute-start.4 = (f32[2,128,128]{2,1,0:T(8,128)S(1)}, f32[2,128,128]{2,1,0:T(8,128)S(1)}, u32[]{:S(2)}, u32[]{:S(2)}) collective-permute-start(f32[2,128,128]{2,1,0:T(8,128)S(1)} %get-tuple-element.32), channel_id=1, source_target_pairs={{0,16},{16,32},{32,48},{48,64},{64,80},{80,96},{96,112},{112,128},... | collective-permute-start | bytes 393224 | tf_op jit(solution)/shard_map/ppermute | solution.py:12
  143.2 13.6 %all-to-all-start.6 = ((f32[32,2,128]{2,1,0:T(2,128)}), f32[32,2,128]{2,1,0:T(2,128)S(1)}, u32[]{:S(2)}, u32[]{:S(2)}) async-start(f32[32,2,128]{2,1,0:T(2,128)} %broadcast_in_dim.45), calls=%async_computation.6 | async-start | bytes 65536 | tf_op jit(solution)/shard_map/all_to_all | solution.py:18
  156.8 1.4 copy-start.13
  158.3 2.1 copy-start.11
  174.0 13.0 %all-to-all-start.8 = ((f32[32,8,128]{2,1,0:T(8,128)}), f32[32,8,128]{2,1,0:T(8,128)S(1)}, u32[]{:S(2)}, u32[]{:S(2)}) async-start(f32[32,8,128]{2,1,0:T(8,128)} %fusion.56), calls=%async_computation.8 | async-start | bytes 262144 | tf_op jit(solution)/shard_map/all_to_all | solution.py:112
  188.5 22.1 %collective-permute-start.11 = (f32[2,128,128]{2,1,0:T(8,128)S(1)}, f32[2,128,128]{2,1,0:T(8,128)S(1)}, u32[]{:S(2)}, u32[]{:S(2)}) collective-permute-start(f32[2,128,128]{2,1,0:T(8,128)S(1)} %get-tuple-element.28), channel_id=1, source_target_pairs={{1,0},{2,1},{3,2},{4,3},{5,4},{6,5},{7,6},{8,7},{9,8},{10,9},{11,1... | collective-permute-start | bytes 393224 | tf_op jit(solution)/shard_map/ppermute | solution.py:12
  192.5 18.2 %collective-permute-start.10 = (f32[2,128,128]{2,1,0:T(8,128)S(1)}, f32[2,128,128]{2,1,0:T(8,128)S(1)}, u32[]{:S(2)}, u32[]{:S(2)}) collective-permute-start(f32[2,128,128]{2,1,0:T(8,128)S(1)} %get-tuple-element.29), channel_id=1, source_target_pairs={{0,1},{1,2},{2,3},{3,4},{4,5},{5,6},{6,7},{7,8},{8,9},{9,10},{10,1... | collective-permute-start | bytes 393224 | tf_op jit(solution)/shard_map/ppermute | solution.py:12
  194.5 16.1 %collective-permute-start.9 = (f32[2,128,128]{2,1,0:T(8,128)S(1)}, f32[2,128,128]{2,1,0:T(8,128)S(1)}, u32[]{:S(2)}, u32[]{:S(2)}) collective-permute-start(f32[2,128,128]{2,1,0:T(8,128)S(1)} %get-tuple-element.27), channel_id=1, source_target_pairs={{16,0},{32,16},{48,32},{64,48},{80,64},{96,80},{112,96},{128,112},... | collective-permute-start | bytes 393224 | tf_op jit(solution)/shard_map/ppermute | solution.py:12
  195.8 14.8 %collective-permute-start.8 = (f32[2,128,128]{2,1,0:T(8,128)S(1)}, f32[2,128,128]{2,1,0:T(8,128)S(1)}, u32[]{:S(2)}, u32[]{:S(2)}) collective-permute-start(f32[2,128,128]{2,1,0:T(8,128)S(1)} %get-tuple-element.26), channel_id=1, source_target_pairs={{0,16},{16,32},{32,48},{48,64},{64,80},{80,96},{96,112},{112,128},... | collective-permute-start | bytes 393224 | tf_op jit(solution)/shard_map/ppermute | solution.py:12
  212.6 13.9 %all-to-all-start.10 = ((f32[32,2,128]{2,1,0:T(2,128)}), f32[32,2,128]{2,1,0:T(2,128)S(1)}, u32[]{:S(2)}, u32[]{:S(2)}) async-start(f32[32,2,128]{2,1,0:T(2,128)} %broadcast_in_dim.48), calls=%async_computation.10 | async-start | bytes 65536 | tf_op jit(solution)/shard_map/all_to_all | solution.py:18
  226.5 1.4 copy-start.14
  228.0 2.1 copy-start.12
  243.7 17.5 %all-to-all-start.12 = ((f32[32,8,128]{2,1,0:T(8,128)}), f32[32,8,128]{2,1,0:T(8,128)S(1)}, u32[]{:S(2)}, u32[]{:S(2)}) async-start(f32[32,8,128]{2,1,0:T(8,128)} %fusion.54), calls=%async_computation.12 | async-start | bytes 262144 | tf_op jit(solution)/shard_map/all_to_all | solution.py:112
  250.3 15.5 %collective-permute-start.15 = (f32[2,128,128]{2,1,0:T(8,128)}, f32[2,128,128]{2,1,0:T(8,128)S(1)}, u32[]{:S(2)}, u32[]{:S(2)}) collective-permute-start(f32[2,128,128]{2,1,0:T(8,128)} %get-tuple-element.22), channel_id=1, source_target_pairs={{1,0},{2,1},{3,2},{4,3},{5,4},{6,5},{7,6},{8,7},{9,8},{10,9},{11,1... | collective-permute-start | bytes 393224 | tf_op jit(solution)/shard_map/ppermute | solution.py:12
  252.4 13.4 %collective-permute-start.14 = (f32[2,128,128]{2,1,0:T(8,128)S(1)}, f32[2,128,128]{2,1,0:T(8,128)S(1)}, u32[]{:S(2)}, u32[]{:S(2)}) collective-permute-start(f32[2,128,128]{2,1,0:T(8,128)S(1)} %get-tuple-element.23), channel_id=1, source_target_pairs={{0,1},{1,2},{2,3},{3,4},{4,5},{5,6},{6,7},{7,8},{8,9},{9,10},{10,1... | collective-permute-start | bytes 393224 | tf_op jit(solution)/shard_map/ppermute | solution.py:12
  255.9 9.9 %collective-permute-start.13 = (f32[2,128,128]{2,1,0:T(8,128)S(1)}, f32[2,128,128]{2,1,0:T(8,128)S(1)}, u32[]{:S(2)}, u32[]{:S(2)}) collective-permute-start(f32[2,128,128]{2,1,0:T(8,128)S(1)} %get-tuple-element.21), channel_id=1, source_target_pairs={{16,0},{32,16},{48,32},{64,48},{80,64},{96,80},{112,96},{128,112},... | collective-permute-start | bytes 393224 | tf_op jit(solution)/shard_map/ppermute | solution.py:12
  257.2 8.6 %collective-permute-start.12 = (f32[2,128,128]{2,1,0:T(8,128)S(1)}, f32[2,128,128]{2,1,0:T(8,128)S(1)}, u32[]{:S(2)}, u32[]{:S(2)}) collective-permute-start(f32[2,128,128]{2,1,0:T(8,128)S(1)} %get-tuple-element.20), channel_id=1, source_target_pairs={{0,16},{16,32},{32,48},{48,64},{64,80},{80,96},{96,112},{112,128},... | collective-permute-start | bytes 393224 | tf_op jit(solution)/shard_map/ppermute | solution.py:12
  262.3 10.9 %all-to-all-start.13 = ((f32[16,2,128]{2,1,0:T(2,128)}), f32[16,2,128]{2,1,0:T(2,128)S(1)}, u32[]{:S(2)}, u32[]{:S(2)}) async-start(f32[16,2,128]{2,1,0:T(2,128)} %broadcast_in_dim.50), calls=%async_computation.13 | async-start | bytes 32768 | tf_op jit(solution)/shard_map/all_to_all | solution.py:18
  265.9 26.8 %copy-start.2 = (bf16[896,512]{1,0:T(8,128)(2,1)S(1)}, bf16[896,512]{1,0:T(8,128)(2,1)}, u32[]{:S(2)}) copy-start(bf16[896,512]{1,0:T(8,128)(2,1)} %copy-done.1) | copy-start | bytes 2752516
  273.8 18.0 %all-to-all-start.14 = ((f32[32,2,128]{2,1,0:T(2,128)}), f32[32,2,128]{2,1,0:T(2,128)S(1)}, u32[]{:S(2)}, u32[]{:S(2)}) async-start(f32[32,2,128]{2,1,0:T(2,128)} %broadcast_in_dim.51), calls=%async_computation.14 | async-start | bytes 65536 | tf_op jit(solution)/shard_map/all_to_all | solution.py:18
  291.8 1.6 copy-start.15

commit v13 on v11

--- a/solution.py
+++ b/solution.py
@@ -19,8 +19,8 @@
 
 
 def total_over_mesh(value, tie):
-    for axis in ("gy", "gx"):
-        if axis == "gx":
+    for axis in ("gx", "gy"):
+        if axis == "gy":
             value = value + 0.0 * tie
         count = lax.axis_size(axis)
         value = jnp.sum(gather_rows(value, axis).reshape((count,) + value.shape), axis=0)

time: 297 us -> 305 us (1.027)
  starting transfers between devices: 110 us -> 119 us
  blocking collectives: 60 us -> 52.5 us
  waiting for transfers between devices: 66.6 us -> 74 us
    all_to_all x5 -> x6, starting transfers between devices: 34.5 us -> 42.9 us  [gather_rows(): lax.all_to_all(copies.reshape((-1,) + value.shape[1:]), axis, 0, 0, tiled...]
    all_to_all x5 -> x4, blocking collectives: 60 us -> 52.5 us  [gather_rows(): lax.all_to_all(copies.reshape((-1,) + value.shape[1:]), axis, 0, 0, tiled...]
    all_to_all x5 -> x6, waiting for transfers between devices: 32.1 us -> 36.6 us  [gather_rows(): lax.all_to_all(copies.reshape((-1,) + value.shape[1:]), axis, 0, 0, tiled...]
  transfers between devices with their start and end apart: 26 -> 27, of which waited for: 8 -> 11; matrix products, arithmetic and copies ran while one was open for 9% -> 8% of each run, Pallas kernels for 0% -> 0%
where the time goes in v13:
time: 305 us; the launch traced here: 304 us
  starting transfers between devices  119 us (39%)
  waiting for transfers between devices  74 us (24%)
  blocking collectives  52.5 us (17%)
  local copies, waits for them, and re-layouts  32.7 us (11%)
  matrix products  17.3 us (6%)
  other arithmetic  5.03 us (2%)
  between operations  3.44 us (1%)
    all_to_all x4, blocking collectives, gather_rows(): lax.all_to_all(copies.reshape((-1,) + value.shape[1:]), axis, 0, 0, tiled...  52.5 us
    ppermute x16, starting transfers between devices, from_behind(): lax.ppermute(value, axis, [(source, source + steps) for source in range(l...  46.7 us
    all_to_all x6, starting transfers between devices, gather_rows(): lax.all_to_all(copies.reshape((-1,) + value.shape[1:]), axis, 0, 0, tiled...  42.9 us
    all_to_all x6, waiting for transfers between devices, gather_rows(): lax.all_to_all(copies.reshape((-1,) + value.shape[1:]), axis, 0, 0, tiled...  36.6 us
    all_to_all x4, waiting for transfers between devices, apply_prec(): pieces = lax.all_to_all(partial, 'gx', 0, 0, tiled=True)  25.3 us
    all_to_all x4, starting transfers between devices, apply_prec(): pieces = lax.all_to_all(partial, 'gx', 0, 0, tiled=True)  19.5 us
    gather x2, local copies, waits for them, and re-layouts, shards(): coarse_cols = jnp.take(coarse_inverse, coarse_map, axis=1)  16.3 us
    all_to_all x1, starting transfers between devices, shards(): lax.all_to_all(coarse_cols.reshape(depth, count_x, count_y * depth), 'gx'...  9.69 us
  transfers between devices with their start and end apart: 27, of which 11 were waited for; matrix products, arithmetic and copies ran while one was open for 8% of the time, Pallas kernels for 0%

profile of v13, /device:TPU:1, one launch (start us, length us, event | category | flops | bytes accessed | tf_op | source)
XLA Modules:
  0.0 303.9 jit_solution(11763123323199082917)
XLA Ops:
  0.7 2.1 fusion.81
  3.4 11.8 %all-to-all-start.1 = ((f32[16,8,128]{2,1,0:T(8,128)}), f32[16,8,128]{2,1,0:T(8,128)S(1)}, u32[]{:S(2)}, u32[]{:S(2)}) async-start(f32[16,8,128]{2,1,0:T(8,128)} %broadcast_in_dim.42), calls=%async_computation.1 | async-start | bytes 131072 | tf_op jit(solution)/shard_map/all_to_all | solution.py:18
  16.0 14.1 %gather_fusion = f32[4096,8]{1,0:T(8,128)} fusion(f32[8,4096]{0,1:T(8,128)S(1)} %copy.80, s32[4096]{0:T(1024)S(1)} %fusion.67), kind=kCustom, calls=%fused_computation | custom fusion | bytes 278528 | tf_op jit(solution)/shard_map/jit(_take)/gather | solution.py:72
  30.1 2.2 copy.81
  32.9 9.7 %all-to-all-start = ((f32[8,32,128]{2,0,1:T(8,128)}), f32[8,32,128]{2,0,1:T(8,128)S(1)}, u32[]{:S(2)}, u32[]{:S(2)}) async-start(f32[8,32,128]{2,0,1:T(8,128)} %broadcast_select_fusion), calls=%async_computation | async-start | bytes 262144 | tf_op jit(solution)/shard_map/all_to_all | solution.py:73
  42.7 9.1 %all-to-all-done = f32[8,32,128]{2,0,1:T(8,128)S(1)} async-done(((f32[8,32,128]{2,0,1:T(8,128)}), f32[8,32,128]{2,0,1:T(8,128)S(1)}, u32[]{:S(2)}, u32[]{:S(2)}) %all-to-all-start) | async-done | bytes 131104 | tf_op jit(solution)/shard_map/all_to_all | solution.py:73
  51.8 0.9 fusion.60
  52.7 4.5 %all-to-all-start.2 = ((f32[32,8,128]{2,1,0:T(8,128)}), f32[32,8,128]{2,1,0:T(8,128)S(1)}, u32[]{:S(2)}, u32[]{:S(2)}) async-start(f32[32,8,128]{2,1,0:T(8,128)} %fusion.60), calls=%async_computation.2 | async-start | bytes 262144 | tf_op jit(solution)/shard_map/all_to_all | solution.py:112
  57.3 9.1 %all-to-all-done.2 = f32[32,8,128]{2,1,0:T(8,128)S(1)} async-done(((f32[32,8,128]{2,1,0:T(8,128)}), f32[32,8,128]{2,1,0:T(8,128)S(1)}, u32[]{:S(2)}, u32[]{:S(2)}) %all-to-all-start.2) | async-done | bytes 131104 | tf_op jit(solution)/shard_map/all_to_all | solution.py:112
  66.9 1.3 gather_fusion.1
  68.2 4.6 %collective-permute-start.3 = (bf16[128,128]{1,0:T(8,128)(2,1)S(1)}, bf16[128,128]{1,0:T(8,128)(2,1)S(1)}, u32[]{:S(2)}, u32[]{:S(2)}) collective-permute-start(bf16[128,128]{1,0:T(8,128)(2,1)S(1)} %get-tuple-element.40), channel_id=1, source_target_pairs={{1,0},{2,1},{3,2},{4,3},{5,4},{6,5},{7,6},{8,7},{9,8},{10,9},{11,1... | collective-permute-start | bytes 98312 | tf_op jit(solution)/shard_map/ppermute | solution.py:12
  72.9 3.2 %collective-permute-start.2 = (bf16[128,128]{1,0:T(8,128)(2,1)S(1)}, bf16[128,128]{1,0:T(8,128)(2,1)S(1)}, u32[]{:S(2)}, u32[]{:S(2)}) collective-permute-start(bf16[128,128]{1,0:T(8,128)(2,1)S(1)} %get-tuple-element.38), channel_id=1, source_target_pairs={{0,1},{1,2},{2,3},{3,4},{4,5},{5,6},{6,7},{7,8},{8,9},{9,10},{10,1... | collective-permute-start | bytes 98312 | tf_op jit(solution)/shard_map/ppermute | solution.py:12
  76.1 1.3 collective-permute-start.1
  77.4 4.0 %collective-permute-start = (bf16[128,128]{1,0:T(8,128)(2,1)S(1)}, bf16[128,128]{1,0:T(8,128)(2,1)S(1)}, u32[]{:S(2)}, u32[]{:S(2)}) collective-permute-start(bf16[128,128]{1,0:T(8,128)(2,1)S(1)} %get-tuple-element.37), channel_id=1, source_target_pairs={{0,16},{16,32},{32,48},{48,64},{64,80},{80,96},{96,112},{112,128},... | collective-permute-start | bytes 98312 | tf_op jit(solution)/shard_map/ppermute | solution.py:12
  82.6 2.5 fusion.9
  85.9 14.4 %all_to_all.111 = f32[16,8,128]{2,1,0:T(8,128)S(1)} all-to-all(f32[16,8,128]{2,1,0:T(8,128)S(1)} %broadcast_in_dim.43), channel_id=1, replica_groups=mesh['gx'=32,'gy'=16] {'gy'}, dimensions={0} | all-to-all | bytes 131072 | tf_op jit(solution)/shard_map/all_to_all | solution.py:18
  100.3 0.9 fusion.58
  101.2 7.3 %all-to-all-start.4 = ((f32[32,8,128]{2,1,0:T(8,128)}), f32[32,8,128]{2,1,0:T(8,128)S(1)}, u32[]{:S(2)}, u32[]{:S(2)}) async-start(f32[32,8,128]{2,1,0:T(8,128)} %fusion.58), calls=%async_computation.4 | async-start | bytes 262144 | tf_op jit(solution)/shard_map/all_to_all | solution.py:112
  108.5 1.0 gather_fusion.2
  109.6 8.1 %all-to-all-done.4 = f32[32,8,128]{2,1,0:T(8,128)S(1)} async-done(((f32[32,8,128]{2,1,0:T(8,128)}), f32[32,8,128]{2,1,0:T(8,128)S(1)}, u32[]{:S(2)}, u32[]{:S(2)}) %all-to-all-start.4) | async-done | bytes 131104 | tf_op jit(solution)/shard_map/all_to_all | solution.py:112
  118.2 1.0 gather_fusion.3
  119.2 0.7 fusion.48
  120.0 4.0 %collective-permute-start.7 = (f32[2,128,128]{2,1,0:T(8,128)}, f32[2,128,128]{2,1,0:T(8,128)S(1)}, u32[]{:S(2)}, u32[]{:S(2)}) collective-permute-start(f32[2,128,128]{2,1,0:T(8,128)} %get-tuple-element.34), channel_id=1, source_target_pairs={{1,0},{2,1},{3,2},{4,3},{5,4},{6,5},{7,6},{8,7},{9,8},{10,9},{11,1... | collective-permute-start | bytes 393224 | tf_op jit(solution)/shard_map/ppermute | solution.py:12
  124.0 2.0 collective-permute-start.6
  126.0 1.3 collective-permute-start.5
  127.3 4.0 %collective-permute-start.4 = (f32[2,128,128]{2,1,0:T(8,128)S(1)}, f32[2,128,128]{2,1,0:T(8,128)S(1)}, u32[]{:S(2)}, u32[]{:S(2)}) collective-permute-start(f32[2,128,128]{2,1,0:T(8,128)S(1)} %get-tuple-element.32), channel_id=1, source_target_pairs={{0,16},{16,32},{32,48},{48,64},{64,80},{80,96},{96,112},{112,128},... | collective-permute-start | bytes 393224 | tf_op jit(solution)/shard_map/ppermute | solution.py:12
  131.3 13.7 %all_to_all.112 = f32[32,2,128]{2,1,0:T(2,128)S(1)} all-to-all(f32[32,2,128]{2,1,0:T(2,128)S(1)} %broadcast_in_dim.44), channel_id=1, replica_groups=mesh['gx'=32,'gy'=16] {'gx'}, dimensions={0} | all-to-all | bytes 65536 | tf_op jit(solution)/shard_map/all_to_all | solution.py:18
  147.0 5.4 %all-to-all-start.6 = ((f32[16,2,128]{2,1,0:T(2,128)}), f32[16,2,128]{2,1,0:T(2,128)S(1)}, u32[]{:S(2)}, u32[]{:S(2)}) async-start(f32[16,2,128]{2,1,0:T(2,128)} %broadcast_in_dim.45), calls=%async_computation.6 | async-start | bytes 32768 | tf_op jit(solution)/shard_map/all_to_all | solution.py:18
  152.5 7.4 %all-to-all-done.6 = f32[16,2,128]{2,1,0:T(2,128)S(1)} async-done(((f32[16,2,128]{2,1,0:T(2,128)}), f32[16,2,128]{2,1,0:T(2,128)S(1)}, u32[]{:S(2)}, u32[]{:S(2)}) %all-to-all-start.6) | async-done | bytes 16416 | tf_op jit(solution)/shard_map/all_to_all | solution.py:18
  160.0 1.3 copy-done.15
  161.3 0.8 fusion.10
  163.4 10.6 %all_to_all.113 = f32[16,8,128]{2,1,0:T(8,128)S(1)} all-to-all(f32[16,8,128]{2,1,0:T(8,128)S(1)} %broadcast_in_dim.46), channel_id=1, replica_groups=mesh['gx'=32,'gy'=16] {'gy'}, dimensions={0} | all-to-all | bytes 131072 | tf_op jit(solution)/shard_map/all_to_all | solution.py:18
  174.0 0.9 fusion.56
  174.9 3.9 %all-to-all-start.8 = ((f32[32,8,128]{2,1,0:T(8,128)}), f32[32,8,128]{2,1,0:T(8,128)S(1)}, u32[]{:S(2)}, u32[]{:S(2)}) async-start(f32[32,8,128]{2,1,0:T(8,128)} %fusion.56), calls=%async_computation.8 | async-start | bytes 262144 | tf_op jit(solution)/shard_map/all_to_all | solution.py:112
  178.8 1.0 gather_fusion.4
  179.9 8.1 %all-to-all-done.8 = f32[32,8,128]{2,1,0:T(8,128)S(1)} async-done(((f32[32,8,128]{2,1,0:T(8,128)}), f32[32,8,128]{2,1,0:T(8,128)S(1)}, u32[]{:S(2)}, u32[]{:S(2)}) %all-to-all-start.8) | async-done | bytes 131104 | tf_op jit(solution)/shard_map/all_to_all | solution.py:112
  188.5 1.0 gather_fusion.5
  189.6 4.0 %collective-permute-start.11 = (f32[2,128,128]{2,1,0:T(8,128)S(1)}, f32[2,128,128]{2,1,0:T(8,128)S(1)}, u32[]{:S(2)}, u32[]{:S(2)}) collective-permute-start(f32[2,128,128]{2,1,0:T(8,128)S(1)} %get-tuple-element.28), channel_id=1, source_target_pairs={{1,0},{2,1},{3,2},{4,3},{5,4},{6,5},{7,6},{8,7},{9,8},{10,9},{11,1... | collective-permute-start | bytes 393224 | tf_op jit(solution)/shard_map/ppermute | solution.py:12
  193.5 2.2 collective-permute-start.10
  195.8 1.3 collective-permute-start.9
  197.1 4.0 %collective-permute-start.8 = (f32[2,128,128]{2,1,0:T(8,128)S(1)}, f32[2,128,128]{2,1,0:T(8,128)S(1)}, u32[]{:S(2)}, u32[]{:S(2)}) collective-permute-start(f32[2,128,128]{2,1,0:T(8,128)S(1)} %get-tuple-element.26), channel_id=1, source_target_pairs={{0,16},{16,32},{32,48},{48,64},{64,80},{80,96},{96,112},{112,128},... | collective-permute-start | bytes 393224 | tf_op jit(solution)/shard_map/ppermute | solution.py:12
  201.1 13.8 %all_to_all.114 = f32[32,2,128]{2,1,0:T(2,128)S(1)} all-to-all(f32[32,2,128]{2,1,0:T(2,128)S(1)} %broadcast_in_dim.47), channel_id=1, replica_groups=mesh['gx'=32,'gy'=16] {'gx'}, dimensions={0} | all-to-all | bytes 65536 | tf_op jit(solution)/shard_map/all_to_all | solution.py:18
  216.9 5.2 %all-to-all-start.10 = ((f32[16,2,128]{2,1,0:T(2,128)}), f32[16,2,128]{2,1,0:T(2,128)S(1)}, u32[]{:S(2)}, u32[]{:S(2)}) async-start(f32[16,2,128]{2,1,0:T(2,128)} %broadcast_in_dim.48), calls=%async_computation.10 | async-start | bytes 32768 | tf_op jit(solution)/shard_map/all_to_all | solution.py:18
  222.2 7.4 %all-to-all-done.10 = f32[16,2,128]{2,1,0:T(2,128)S(1)} async-done(((f32[16,2,128]{2,1,0:T(2,128)}), f32[16,2,128]{2,1,0:T(2,128)S(1)}, u32[]{:S(2)}, u32[]{:S(2)}) %all-to-all-start.10) | async-done | bytes 16416 | tf_op jit(solution)/shard_map/all_to_all | solution.py:18
  229.8 1.2 copy-done.16
  231.0 2.1 fusion.11
  234.5 3.7 %all-to-all-start.11 = ((f32[16,8,128]{2,1,0:T(8,128)}), f32[16,8,128]{2,1,0:T(8,128)S(1)}, u32[]{:S(2)}, u32[]{:S(2)}) async-start(f32[16,8,128]{2,1,0:T(8,128)} %broadcast_in_dim.49), calls=%async_computation.11 | async-start | bytes 131072 | tf_op jit(solution)/shard_map/all_to_all | solution.py:18
  238.2 1.0 gather_fusion.6
  239.2 1.0 gather_fusion.7
  240.2 5.8 %all-to-all-done.11 = f32[16,8,128]{2,1,0:T(8,128)S(1)} async-done(((f32[16,8,128]{2,1,0:T(8,128)}), f32[16,8,128]{2,1,0:T(8,128)S(1)}, u32[]{:S(2)}, u32[]{:S(2)}) %all-to-all-start.11) | async-done | bytes 65568 | tf_op jit(solution)/shard_map/all_to_all | solution.py:18
  246.0 0.9 fusion.54
  246.9 3.9 %all-to-all-start.12 = ((f32[32,8,128]{2,1,0:T(8,128)}), f32[32,8,128]{2,1,0:T(8,128)S(1)}, u32[]{:S(2)}, u32[]{:S(2)}) async-start(f32[32,8,128]{2,1,0:T(8,128)} %fusion.54), calls=%async_computation.12 | async-start | bytes 262144 | tf_op jit(solution)/shard_map/all_to_all | solution.py:112
  250.8 2.0 collective-permute-start.15
  252.9 3.5 %collective-permute-start.14 = (f32[2,128,128]{2,1,0:T(8,128)S(1)}, f32[2,128,128]{2,1,0:T(8,128)S(1)}, u32[]{:S(2)}, u32[]{:S(2)}) collective-permute-start(f32[2,128,128]{2,1,0:T(8,128)S(1)} %get-tuple-element.23), channel_id=1, source_target_pairs={{0,1},{1,2},{2,3},{3,4},{4,5},{5,6},{6,7},{7,8},{8,9},{9,10},{10,1... | collective-permute-start | bytes 393224 | tf_op jit(solution)/shard_map/ppermute | solution.py:12
  256.4 1.3 collective-permute-start.13
  257.7 4.0 %collective-permute-start.12 = (f32[2,128,128]{2,1,0:T(8,128)S(1)}, f32[2,128,128]{2,1,0:T(8,128)S(1)}, u32[]{:S(2)}, u32[]{:S(2)}) collective-permute-start(f32[2,128,128]{2,1,0:T(8,128)S(1)} %get-tuple-element.20), channel_id=1, source_target_pairs={{0,16},{16,32},{32,48},{48,64},{64,80},{80,96},{96,112},{112,128},... | collective-permute-start | bytes 393224 | tf_op jit(solution)/shard_map/ppermute | solution.py:12
  261.7 1.2 collective-permute-done.13
  262.9 1.8 collective-permute-done.12
  267.1 11.7 %all-to-all-start.13 = ((f32[32,2,128]{2,1,0:T(2,128)}), f32[32,2,128]{2,1,0:T(2,128)S(1)}, u32[]{:S(2)}, u32[]{:S(2)}) async-start(f32[32,2,128]{2,1,0:T(2,128)} %broadcast_in_dim.50), calls=%async_computation.13 | async-start | bytes 65536 | tf_op jit(solution)/shard_map/all_to_all | solution.py:18
  278.8 8.7 %all-to-all-done.13 = f32[32,2,128]{2,1,0:T(2,128)S(1)} async-done(((f32[32,2,128]{2,1,0:T(2,128)}), f32[32,2,128]{2,1,0:T(2,128)S(1)}, u32[]{:S(2)}, u32[]{:S(2)}) %all-to-all-start.13) | async-done | bytes 32800 | tf_op jit(solution)/shard_map/all_to_all | solution.py:18
  288.2 5.1 %all-to-all-start.14 = ((f32[16,2,128]{2,1,0:T(2,128)}), f32[16,2,128]{2,1,0:T(2,128)S(1)}, u32[]{:S(2)}, u32[]{:S(2)}) async-start(f32[16,2,128]{2,1,0:T(2,128)} %broadcast_in_dim.51), calls=%async_computation.14 | async-start | bytes 32768 | tf_op jit(solution)/shard_map/all_to_all | solution.py:18
  293.3 7.4 %all-to-all-done.14 = f32[16,2,128]{2,1,0:T(2,128)S(1)} async-done(((f32[16,2,128]{2,1,0:T(2,128)}), f32[16,2,128]{2,1,0:T(2,128)S(1)}, u32[]{:S(2)}, u32[]{:S(2)}) %all-to-all-start.14) | async-done | bytes 16416 | tf_op jit(solution)/shard_map/all_to_all | solution.py:18
  300.7 0.8 fusion.31
  302.3 1.6 fusion.4
  (118 shorter events, 14.3 us)
Async XLA Ops:
  0.6 80.8 %copy-start = (bf16[1,1,4,128,128]{4,3,2,1,0:T(8,128)(2,1)S(1)}, bf16[1,1,4,128,128]{4,3,2,1,0:T(8,128)(2,1)}, u32[]{:S(2)}) copy-start(bf16[1,1,4,128,128]{4,3,2,1,0:T(8,128)(2,1)} %param.15) | copy-start | bytes 393220
  0.6 14.6 %copy-start.8 = (s32[4096]{0:T(1024)S(1)}, s32[4096]{0:T(1024)}, u32[]{:S(2)}) copy-start(s32[4096]{0:T(1024)} %param.19) | copy-start | bytes 49156
  0.7 14.7 %copy-start.7 = (f32[8,4096]{1,0:T(8,128)S(1)}, f32[8,4096]{1,0:T(8,128)}, u32[]{:S(2)}) copy-start(f32[8,4096]{1,0:T(8,128)} %param.18) | copy-start | bytes 393220
  3.4 29.5 %all-to-all-start.1 = ((f32[16,8,128]{2,1,0:T(8,128)}), f32[16,8,128]{2,1,0:T(8,128)S(1)}, u32[]{:S(2)}, u32[]{:S(2)}) async-start(f32[16,8,128]{2,1,0:T(8,128)} %broadcast_in_dim.42), calls=%async_computation.1 | async-start | bytes 131072 | tf_op jit(solution)/shard_map/all_to_all | solution.py:18
  15.9 26.7 %copy-start.9 = (f32[1,1,896]{2,1,0:T(1,128)S(1)}, f32[1,1,896]{2,1,0:T(1,128)}, u32[]{:S(2)}) copy-start(f32[1,1,896]{2,1,0:T(1,128)} %param.14) | copy-start | bytes 10756
  15.9 41.3 %copy-start.11 = (s32[1,1,4,128]{3,2,1,0:T(4,128)S(1)}, s32[1,1,4,128]{3,2,1,0:T(4,128)}, u32[]{:S(2)}) copy-start(s32[1,1,4,128]{3,2,1,0:T(4,128)} %param.16) | copy-start | bytes 6148
  16.0 50.5 %copy-start.3 = (bf16[1,1,8,896]{3,2,1,0:T(8,128)(2,1)S(1)}, bf16[1,1,8,896]{3,2,1,0:T(8,128)(2,1)}, u32[]{:S(2)}) copy-start(bf16[1,1,8,896]{3,2,1,0:T(8,128)(2,1)} %param.17) | copy-start | bytes 43012
  16.0 50.4 %copy-start.4 = (bf16[1,1,896,128]{3,2,1,0:T(8,128)(2,1)S(1)}, bf16[1,1,896,128]{3,2,1,0:T(8,128)(2,1)}, u32[]{:S(2)}) copy-start(bf16[1,1,896,128]{3,2,1,0:T(8,128)(2,1)} %param.10) | copy-start | bytes 688132
  32.9 18.9 %all-to-all-start = ((f32[8,32,128]{2,0,1:T(8,128)}), f32[8,32,128]{2,0,1:T(8,128)S(1)}, u32[]{:S(2)}, u32[]{:S(2)}) async-start(f32[8,32,128]{2,0,1:T(8,128)} %broadcast_select_fusion), calls=%async_computation | async-start | bytes 262144 | tf_op jit(solution)/shard_map/all_to_all | solution.py:73
  52.7 13.7 %all-to-all-start.2 = ((f32[32,8,128]{2,1,0:T(8,128)}), f32[32,8,128]{2,1,0:T(8,128)S(1)}, u32[]{:S(2)}, u32[]{:S(2)}) async-start(f32[32,8,128]{2,1,0:T(8,128)} %fusion.60), calls=%async_computation.2 | async-start | bytes 262144 | tf_op jit(solution)/shard_map/all_to_all | solution.py:112
  66.4 15.6 %copy-start.10 = (f32[1,1,896]{2,1,0:T(1,128)S(1)}, f32[1,1,896]{2,1,0:T(1,128)}, u32[]{:S(2)}) copy-start(f32[1,1,896]{2,1,0:T(1,128)} %param.12) | copy-start | bytes 10756
  68.2 14.3 %collective-permute-start.3 = (bf16[128,128]{1,0:T(8,128)(2,1)S(1)}, bf16[128,128]{1,0:T(8,128)(2,1)S(1)}, u32[]{:S(2)}, u32[]{:S(2)}) collective-permute-start(bf16[128,128]{1,0:T(8,128)(2,1)S(1)} %get-tuple-element.40), channel_id=1, source_target_pairs={{1,0},{2,1},{3,2},{4,3},{5,4},{6,5},{7,6},{8,7},{9,8},{10,9},{11,1... | collective-permute-start | bytes 98312 | tf_op jit(solution)/shard_map/ppermute | solution.py:12
  72.9 9.7 %collective-permute-start.2 = (bf16[128,128]{1,0:T(8,128)(2,1)S(1)}, bf16[128,128]{1,0:T(8,128)(2,1)S(1)}, u32[]{:S(2)}, u32[]{:S(2)}) collective-permute-start(bf16[128,128]{1,0:T(8,128)(2,1)S(1)} %get-tuple-element.38), channel_id=1, source_target_pairs={{0,1},{1,2},{2,3},{3,4},{4,5},{5,6},{6,7},{7,8},{8,9},{9,10},{10,1... | collective-permute-start | bytes 98312 | tf_op jit(solution)/shard_map/ppermute | solution.py:12
  76.1 6.5 %collective-permute-start.1 = (bf16[128,128]{1,0:T(8,128)(2,1)S(1)}, bf16[128,128]{1,0:T(8,128)(2,1)S(1)}, u32[]{:S(2)}, u32[]{:S(2)}) collective-permute-start(bf16[128,128]{1,0:T(8,128)(2,1)S(1)} %get-tuple-element.39), channel_id=1, source_target_pairs={{16,0},{32,16},{48,32},{64,48},{80,64},{96,80},{112,96},{128,112},... | collective-permute-start | bytes 98312 | tf_op jit(solution)/shard_map/ppermute | solution.py:12
  77.4 5.2 %collective-permute-start = (bf16[128,128]{1,0:T(8,128)(2,1)S(1)}, bf16[128,128]{1,0:T(8,128)(2,1)S(1)}, u32[]{:S(2)}, u32[]{:S(2)}) collective-permute-start(bf16[128,128]{1,0:T(8,128)(2,1)S(1)} %get-tuple-element.37), channel_id=1, source_target_pairs={{0,16},{16,32},{32,48},{48,64},{64,80},{80,96},{96,112},{112,128},... | collective-permute-start | bytes 98312 | tf_op jit(solution)/shard_map/ppermute | solution.py:12
  82.6 77.5 %copy-start.1 = (bf16[896,512]{1,0:T(8,128)(2,1)}, bf16[896,512]{1,0:T(8,128)(2,1)S(1)}, u32[]{:S(2)}) copy-start(bf16[896,512]{1,0:T(8,128)(2,1)S(1)} %copy.84) | copy-start | bytes 2752516
  82.6 2.6 copy-start.12
  101.2 16.5 %all-to-all-start.4 = ((f32[32,8,128]{2,1,0:T(8,128)}), f32[32,8,128]{2,1,0:T(8,128)S(1)}, u32[]{:S(2)}, u32[]{:S(2)}) async-start(f32[32,8,128]{2,1,0:T(8,128)} %fusion.58), calls=%async_computation.4 | async-start | bytes 262144 | tf_op jit(solution)/shard_map/all_to_all | solution.py:112
  120.0 25.1 %collective-permute-start.7 = (f32[2,128,128]{2,1,0:T(8,128)}, f32[2,128,128]{2,1,0:T(8,128)S(1)}, u32[]{:S(2)}, u32[]{:S(2)}) collective-permute-start(f32[2,128,128]{2,1,0:T(8,128)} %get-tuple-element.34), channel_id=1, source_target_pairs={{1,0},{2,1},{3,2},{4,3},{5,4},{6,5},{7,6},{8,7},{9,8},{10,9},{11,1... | collective-permute-start | bytes 393224 | tf_op jit(solution)/shard_map/ppermute | solution.py:12
  124.0 21.1 %collective-permute-start.6 = (f32[2,128,128]{2,1,0:T(8,128)}, f32[2,128,128]{2,1,0:T(8,128)S(1)}, u32[]{:S(2)}, u32[]{:S(2)}) collective-permute-start(f32[2,128,128]{2,1,0:T(8,128)} %get-tuple-element.35), channel_id=1, source_target_pairs={{0,1},{1,2},{2,3},{3,4},{4,5},{5,6},{6,7},{7,8},{8,9},{9,10},{10,1... | collective-permute-start | bytes 393224 | tf_op jit(solution)/shard_map/ppermute | solution.py:12
  126.0 19.1 %collective-permute-start.5 = (f32[2,128,128]{2,1,0:T(8,128)S(1)}, f32[2,128,128]{2,1,0:T(8,128)S(1)}, u32[]{:S(2)}, u32[]{:S(2)}) collective-permute-start(f32[2,128,128]{2,1,0:T(8,128)S(1)} %get-tuple-element.33), channel_id=1, source_target_pairs={{16,0},{32,16},{48,32},{64,48},{80,64},{96,80},{112,96},{128,112},... | collective-permute-start | bytes 393224 | tf_op jit(solution)/shard_map/ppermute | solution.py:12
  127.3 17.8 %collective-permute-start.4 = (f32[2,128,128]{2,1,0:T(8,128)S(1)}, f32[2,128,128]{2,1,0:T(8,128)S(1)}, u32[]{:S(2)}, u32[]{:S(2)}) collective-permute-start(f32[2,128,128]{2,1,0:T(8,128)S(1)} %get-tuple-element.32), channel_id=1, source_target_pairs={{0,16},{16,32},{32,48},{48,64},{64,80},{80,96},{96,112},{112,128},... | collective-permute-start | bytes 393224 | tf_op jit(solution)/shard_map/ppermute | solution.py:12
  147.0 12.8 %all-to-all-start.6 = ((f32[16,2,128]{2,1,0:T(2,128)}), f32[16,2,128]{2,1,0:T(2,128)S(1)}, u32[]{:S(2)}, u32[]{:S(2)}) async-start(f32[16,2,128]{2,1,0:T(2,128)} %broadcast_in_dim.45), calls=%async_computation.6 | async-start | bytes 32768 | tf_op jit(solution)/shard_map/all_to_all | solution.py:18
  159.9 1.4 copy-start.15
  161.3 1.4 copy-start.13
  162.7 12.2 %copy-start.5 = (bf16[896,128]{1,0:T(8,128)(2,1)}, bf16[896,128]{1,0:T(8,128)(2,1)S(1)}, u32[]{:S(2)}) copy-start(bf16[896,128]{1,0:T(8,128)(2,1)S(1)} %fusion.10) | copy-start | bytes 688132
  174.9 13.0 %all-to-all-start.8 = ((f32[32,8,128]{2,1,0:T(8,128)}), f32[32,8,128]{2,1,0:T(8,128)S(1)}, u32[]{:S(2)}, u32[]{:S(2)}) async-start(f32[32,8,128]{2,1,0:T(8,128)} %fusion.56), calls=%async_computation.8 | async-start | bytes 262144 | tf_op jit(solution)/shard_map/all_to_all | solution.py:112
  178.8 9.2 %copy-start.6 = (bf16[896,128]{1,0:T(8,128)(2,1)S(1)}, bf16[896,128]{1,0:T(8,128)(2,1)}, u32[]{:S(2)}) copy-start(bf16[896,128]{1,0:T(8,128)(2,1)} %copy-done.5) | copy-start | bytes 688132
  189.6 25.4 %collective-permute-start.11 = (f32[2,128,128]{2,1,0:T(8,128)S(1)}, f32[2,128,128]{2,1,0:T(8,128)S(1)}, u32[]{:S(2)}, u32[]{:S(2)}) collective-permute-start(f32[2,128,128]{2,1,0:T(8,128)S(1)} %get-tuple-element.28), channel_id=1, source_target_pairs={{1,0},{2,1},{3,2},{4,3},{5,4},{6,5},{7,6},{8,7},{9,8},{10,9},{11,1... | collective-permute-start | bytes 393224 | tf_op jit(solution)/shard_map/ppermute | solution.py:12
  193.5 21.5 %collective-permute-start.10 = (f32[2,128,128]{2,1,0:T(8,128)S(1)}, f32[2,128,128]{2,1,0:T(8,128)S(1)}, u32[]{:S(2)}, u32[]{:S(2)}) collective-permute-start(f32[2,128,128]{2,1,0:T(8,128)S(1)} %get-tuple-element.29), channel_id=1, source_target_pairs={{0,1},{1,2},{2,3},{3,4},{4,5},{5,6},{6,7},{7,8},{8,9},{9,10},{10,1... | collective-permute-start | bytes 393224 | tf_op jit(solution)/shard_map/ppermute | solution.py:12
  195.8 19.2 %collective-permute-start.9 = (f32[2,128,128]{2,1,0:T(8,128)S(1)}, f32[2,128,128]{2,1,0:T(8,128)S(1)}, u32[]{:S(2)}, u32[]{:S(2)}) collective-permute-start(f32[2,128,128]{2,1,0:T(8,128)S(1)} %get-tuple-element.27), channel_id=1, source_target_pairs={{16,0},{32,16},{48,32},{64,48},{80,64},{96,80},{112,96},{128,112},... | collective-permute-start | bytes 393224 | tf_op jit(solution)/shard_map/ppermute | solution.py:12
  197.1 17.9 %collective-permute-start.8 = (f32[2,128,128]{2,1,0:T(8,128)S(1)}, f32[2,128,128]{2,1,0:T(8,128)S(1)}, u32[]{:S(2)}, u32[]{:S(2)}) collective-permute-start(f32[2,128,128]{2,1,0:T(8,128)S(1)} %get-tuple-element.26), channel_id=1, source_target_pairs={{0,16},{16,32},{32,48},{48,64},{64,80},{80,96},{96,112},{112,128},... | collective-permute-start | bytes 393224 | tf_op jit(solution)/shard_map/ppermute | solution.py:12
  216.9 12.6 %all-to-all-start.10 = ((f32[16,2,128]{2,1,0:T(2,128)}), f32[16,2,128]{2,1,0:T(2,128)S(1)}, u32[]{:S(2)}, u32[]{:S(2)}) async-start(f32[16,2,128]{2,1,0:T(2,128)} %broadcast_in_dim.48), calls=%async_computation.10 | async-start | bytes 32768 | tf_op jit(solution)/shard_map/all_to_all | solution.py:18
  229.6 1.4 copy-start.16
  231.0 2.1 copy-start.14
  234.5 11.5 %all-to-all-start.11 = ((f32[16,8,128]{2,1,0:T(8,128)}), f32[16,8,128]{2,1,0:T(8,128)S(1)}, u32[]{:S(2)}, u32[]{:S(2)}) async-start(f32[16,8,128]{2,1,0:T(8,128)} %broadcast_in_dim.49), calls=%async_computation.11 | async-start | bytes 131072 | tf_op jit(solution)/shard_map/all_to_all | solution.py:18
  246.9 19.0 %all-to-all-start.12 = ((f32[32,8,128]{2,1,0:T(8,128)}), f32[32,8,128]{2,1,0:T(8,128)S(1)}, u32[]{:S(2)}, u32[]{:S(2)}) async-start(f32[32,8,128]{2,1,0:T(8,128)} %fusion.54), calls=%async_computation.12 | async-start | bytes 262144 | tf_op jit(solution)/shard_map/all_to_all | solution.py:112
  250.8 10.9 %collective-permute-start.15 = (f32[2,128,128]{2,1,0:T(8,128)S(1)}, f32[2,128,128]{2,1,0:T(8,128)S(1)}, u32[]{:S(2)}, u32[]{:S(2)}) collective-permute-start(f32[2,128,128]{2,1,0:T(8,128)S(1)} %get-tuple-element.22), channel_id=1, source_target_pairs={{1,0},{2,1},{3,2},{4,3},{5,4},{6,5},{7,6},{8,7},{9,8},{10,9},{11,1... | collective-permute-start | bytes 393224 | tf_op jit(solution)/shard_map/ppermute | solution.py:12
  252.9 8.8 %collective-permute-start.14 = (f32[2,128,128]{2,1,0:T(8,128)S(1)}, f32[2,128,128]{2,1,0:T(8,128)S(1)}, u32[]{:S(2)}, u32[]{:S(2)}) collective-permute-start(f32[2,128,128]{2,1,0:T(8,128)S(1)} %get-tuple-element.23), channel_id=1, source_target_pairs={{0,1},{1,2},{2,3},{3,4},{4,5},{5,6},{6,7},{7,8},{8,9},{9,10},{10,1... | collective-permute-start | bytes 393224 | tf_op jit(solution)/shard_map/ppermute | solution.py:12
  256.4 6.5 %collective-permute-start.13 = (f32[2,128,128]{2,1,0:T(8,128)S(1)}, f32[2,128,128]{2,1,0:T(8,128)S(1)}, u32[]{:S(2)}, u32[]{:S(2)}) collective-permute-start(f32[2,128,128]{2,1,0:T(8,128)S(1)} %get-tuple-element.21), channel_id=1, source_target_pairs={{16,0},{32,16},{48,32},{64,48},{80,64},{96,80},{112,96},{128,112},... | collective-permute-start | bytes 393224 | tf_op jit(solution)/shard_map/ppermute | solution.py:12
  257.7 6.9 %collective-permute-start.12 = (f32[2,128,128]{2,1,0:T(8,128)S(1)}, f32[2,128,128]{2,1,0:T(8,128)S(1)}, u32[]{:S(2)}, u32[]{:S(2)}) collective-permute-start(f32[2,128,128]{2,1,0:T(8,128)S(1)} %get-tuple-element.20), channel_id=1, source_target_pairs={{0,16},{16,32},{32,48},{48,64},{64,80},{80,96},{96,112},{112,128},... | collective-permute-start | bytes 393224 | tf_op jit(solution)/shard_map/ppermute | solution.py:12
  267.1 20.5 %all-to-all-start.13 = ((f32[32,2,128]{2,1,0:T(2,128)}), f32[32,2,128]{2,1,0:T(2,128)S(1)}, u32[]{:S(2)}, u32[]{:S(2)}) async-start(f32[32,2,128]{2,1,0:T(2,128)} %broadcast_in_dim.50), calls=%async_computation.13 | async-start | bytes 65536 | tf_op jit(solution)/shard_map/all_to_all | solution.py:18
  278.8 22.8 %copy-start.2 = (bf16[896,512]{1,0:T(8,128)(2,1)S(1)}, bf16[896,512]{1,0:T(8,128)(2,1)}, u32[]{:S(2)}) copy-start(bf16[896,512]{1,0:T(8,128)(2,1)} %copy-done.1) | copy-start | bytes 2752516
  288.2 12.5 %all-to-all-start.14 = ((f32[16,2,128]{2,1,0:T(2,128)}), f32[16,2,128]{2,1,0:T(2,128)S(1)}, u32[]{:S(2)}, u32[]{:S(2)}) async-start(f32[16,2,128]{2,1,0:T(2,128)} %broadcast_in_dim.51), calls=%async_computation.14 | async-start | bytes 32768 | tf_op jit(solution)/shard_map/all_to_all | solution.py:18
  300.7 1.6 copy-start.17
